TPU v7x, 32 devices: a whole 2x2x4 slice. The times are simulated.
32 devices in a mesh: groups: 2 (over x), gx: 8 (over z, y), gy: 2 (over core).
Axes of the slice: x: 2, y: 2, z: 4, core: 2. Of those that a mesh axis runs over, the one named last changes fastest.
Arguments:
- values: float32 [96, 12, 64, 128], P(('groups', 'gx'), 'gy'), parts along dimension 0, may hold values from -6 to 6
- drift: float32 [2, 96, 12], P(None, ('groups', 'gx'), 'gy'), parts along dimension 1, may hold values from -6 to 6
- params: float32 [8], P('groups'), parts along dimension 0, may hold values from 0.5 to 1.5
Outputs:
- advanced: float32 [96, 12, 64, 128], P(('groups', 'gx'), 'gy'), parts along dimension 0
There are 2 independent parts, one for each index of `groups`. A program takes and returns all parts, laid end to end along the dimension named above; each array names one. Nothing has to cross between parts.
All inputs are finite; a program needn't handle non-finite values.
Results may differ from a plain program's by a relative error of at most 0.0003.
Values sent between devices are 32-bit elements; how exact they have to be, the bound alone decides.
No kernel may reach another device: no remote copies, remote signals or barrier semaphores. Data moves between devices by JAX's collectives and lax.ppermute only.
A program may use at most 64 MiB of HBM per device.

v0:
```python
import math

import jax
import jax.numpy as jnp
from jax import lax
from jax.sharding import PartitionSpec as P


cfl_number = 0.5
weno_eps = 1e-06
cell_span = 1.0 / 64.0


def weno_value(first, second, third, fourth, fifth):
    stencil_one = first / 3.0 - 7.0 * second / 6.0 + 11.0 * third / 6.0
    stencil_two = -second / 6.0 + 5.0 * third / 6.0 + fourth / 3.0
    stencil_three = third / 3.0 + 5.0 * fourth / 6.0 - fifth / 6.0
    smooth_one = (
        13.0 / 12.0 * (first - 2.0 * second + third) ** 2
        + 0.25 * (first - 4.0 * second + 3.0 * third) ** 2
    )
    smooth_two = 13.0 / 12.0 * (second - 2.0 * third + fourth) ** 2 + 0.25 * (second - fourth) ** 2
    smooth_three = (
        13.0 / 12.0 * (third - 2.0 * fourth + fifth) ** 2
        + 0.25 * (3.0 * third - 4.0 * fourth + fifth) ** 2
    )
    weight_one = 0.1 / (weno_eps + smooth_one) ** 2
    weight_two = 0.6 / (weno_eps + smooth_two) ** 2
    weight_three = 0.3 / (weno_eps + smooth_three) ** 2
    total = weight_one * stencil_one + weight_two * stencil_two + weight_three * stencil_three
    return total / (weight_one + weight_two + weight_three)


def both_sides(window):
    backward = weno_value(window(0), window(1), window(2), window(3), window(4))
    forward = weno_value(window(5), window(4), window(3), window(2), window(1))
    return (backward, forward)


def one_sided(padded, along, spacing, length):
    extent = padded.shape[along]
    differences = (
        lax.slice_in_dim(padded, 1, extent, axis=along)
        - lax.slice_in_dim(padded, 0, extent - 1, axis=along)
    ) / spacing

    def window(offset):
        return lax.slice_in_dim(differences, offset, offset + length, axis=along)

    return both_sides(window)


def periodic_sided(field, along, spacing):
    extent = field.shape[along]
    wrapped = jnp.concatenate(
        [
            lax.slice_in_dim(field, extent - 3, extent, axis=along),
            field,
            lax.slice_in_dim(field, 0, 3, axis=along),
        ],
        axis=along,
    )
    return one_sided(wrapped, along, spacing, extent)


def clamped_sided(field, along, spacing):
    extent = field.shape[along]
    inner = (
        lax.slice_in_dim(field, 1, extent, axis=along)
        - lax.slice_in_dim(field, 0, extent - 1, axis=along)
    ) / spacing
    differences = jnp.concatenate([lax.slice_in_dim(inner, 0, 1, axis=along), inner], axis=along)
    low_edge = lax.slice_in_dim(differences, 0, 1, axis=along)
    high_edge = lax.slice_in_dim(differences, extent - 1, extent, axis=along)

    def window(offset):
        shift_by = offset - 2
        if shift_by > 0:
            return jnp.concatenate(
                [lax.slice_in_dim(differences, shift_by, extent, axis=along)]
                + [high_edge] * shift_by,
                axis=along,
            )
        if shift_by < 0:
            return jnp.concatenate(
                [low_edge] * -shift_by
                + [lax.slice_in_dim(differences, 0, extent + shift_by, axis=along)],
                axis=along,
            )
        return differences

    return both_sides(window)


def speed_bounds(drift_field, x_coord, y_coord, turn_a, along_one, along_two):
    first_hi = jnp.max(along_one)
    first_lo = jnp.min(along_one)
    second_hi = jnp.max(along_two)
    second_lo = jnp.min(along_two)
    bound_one = jnp.max(
        jnp.maximum(drift_field[0] + first_hi, -(drift_field[0] + first_lo))
        + turn_a * jnp.abs(y_coord)[None, :]
    )
    bound_two = jnp.max(
        jnp.maximum(drift_field[1] + second_hi, -(drift_field[1] + second_lo))
        + turn_a * jnp.abs(x_coord)[:, None]
    )
    return (bound_one, bound_two)


def send_low(piece, axis):
    count = lax.axis_size(axis)
    return lax.ppermute(piece, axis, [(i, (i + 1) % count) for i in range(count - 1)])


def send_high(piece, axis):
    count = lax.axis_size(axis)
    return lax.ppermute(piece, axis, [((i + 1) % count, i) for i in range(count - 1)])


def ghost_low(field, halo, at_low, along):
    shape_dist = [1] * field.ndim
    shape_dist[along] = 3
    inner = lax.slice_in_dim(field, 0, 1, axis=along)
    after = lax.slice_in_dim(field, 1, 2, axis=along)
    dist = jnp.arange(3, 0, -1).astype(jnp.float32).reshape(tuple(shape_dist))
    return jnp.where(at_low, inner + dist * (inner - after), halo)


def ghost_high(field, halo, at_high, along):
    extent = field.shape[along]
    shape_dist = [1] * field.ndim
    shape_dist[along] = 3
    inner = lax.slice_in_dim(field, extent - 1, extent, axis=along)
    before = lax.slice_in_dim(field, extent - 2, extent - 1, axis=along)
    dist = jnp.arange(1, 4).astype(jnp.float32).reshape(tuple(shape_dist))
    return jnp.where(at_high, inner + dist * (inner - before), halo)


def spread_max(local, axes):
    count = 1
    for axis in axes:
        count *= lax.axis_size(axis)
    span = 1
    while span < count:
        moved = [
            lax.ppermute(local, axes, [(i, (i + k * span) % count) for i in range(count)])
            for k in range(1, 4)
            if k * span < count
        ]
        for item in moved:
            local = jnp.maximum(local, item)
        span *= 4
    return local


def on_device(values, drift, params):
    cells_x, cells_y, n_psi, n_speed = values.shape
    devices_x = lax.axis_size("gx")
    devices_y = lax.axis_size("gy")
    total_x = cells_x * devices_x
    total_y = cells_y * devices_y
    step_psi = 2.0 * math.pi / n_psi
    step_speed = 1.0 / n_speed
    place_x = lax.axis_index("gx")
    place_y = lax.axis_index("gy")
    first_x = place_x == 0
    last_x = place_x == devices_x - 1
    first_y = place_y == 0
    last_y = place_y == devices_y - 1
    half = cells_x // 2
    alpha_three = params[1] + params[2]
    alpha_four = params[3]

    def cut(array, side):
        return array[:half] if side == 0 else array[half:]

    def local_part(field):
        back_three, fore_three = periodic_sided(field, 2, step_psi)
        back_four, fore_four = clamped_sided(field, 3, step_speed)
        mean_three = 0.5 * (back_three + fore_three)
        mean_four = 0.5 * (back_four + fore_four)
        partial = -params[2] * jnp.abs(mean_three) + params[3] * jnp.abs(mean_four)
        partial = partial + 0.5 * (
            alpha_three * (fore_three - back_three) + alpha_four * (fore_four - back_four)
        )
        return mean_three, partial

    def local_halves(field):
        pieces = []
        for side in (0, 1):
            pieces.append(lax.optimization_barrier(local_part(cut(field, side))))
        return pieces

    def y_halo(field):
        tail = lax.slice_in_dim(field, cells_y - 3, cells_y, axis=1)
        head = lax.slice_in_dim(field, 0, 3, axis=1)
        if devices_y == 2:
            piece = lax.optimization_barrier(jnp.where(first_y, tail, head))
            swapped = lax.ppermute(piece, "gy", [(0, 1), (1, 0)])
            return swapped, swapped
        tail, head = lax.optimization_barrier((tail, head))
        return send_low(tail, "gy"), send_high(head, "gy")

    def local_whole(field):
        mean_three, partial = lax.optimization_barrier(local_part(field))
        return [(cut(mean_three, side), cut(partial, side)) for side in (0, 1)]

    x_halos = (send_low(values[cells_x - 3 :], "gx"), send_high(values[:3], "gx"))
    y_halos = y_halo(values)
    psi_grid = jnp.arange(n_psi).astype(jnp.float32) * step_psi - math.pi
    speed_grid = 0.5 + (jnp.arange(n_speed).astype(jnp.float32) + 0.5) * step_speed
    along_one = -speed_grid[None, :] + params[0] * jnp.cos(psi_grid)[:, None]
    along_two = params[0] * jnp.sin(psi_grid)[:, None]
    y_coord = (
        (place_y * cells_y + jnp.arange(cells_y)).astype(jnp.float32) + 0.5 - 0.5 * total_y
    ) * cell_span
    x_coord = (
        (place_x * cells_x + jnp.arange(cells_x)).astype(jnp.float32) + 0.5 - 0.5 * total_x
    ) * cell_span
    local_one, local_two = speed_bounds(drift, x_coord, y_coord, params[1], along_one, along_two)
    bounds = spread_max(jnp.stack([local_one, local_two]), ("gx", "gy"))
    locals_now = local_halves(values)
    bound_one = bounds[0]
    bound_two = bounds[1]
    step_time = cfl_number / (
        bound_one / cell_span
        + bound_two / cell_span
        + alpha_three / step_psi
        + alpha_four / step_speed
    )
    x_col = x_coord[:, None, None, None]
    y_col = y_coord[None, :, None, None]
    flow_x = drift[0][:, :, None, None]
    flow_y = drift[1][:, :, None, None]

    def half_parts(field, side, x_halo, y_low, y_high, mean_three, partial):
        if side == 0:
            start, stop = 0, half
            ghost = ghost_low(field, x_halo, first_x, 0)
            wide_x = jnp.concatenate([ghost, field[: half + 3]], axis=0)
        else:
            start, stop = half, cells_x
            ghost = ghost_high(field, x_halo, last_x, 0)
            wide_x = jnp.concatenate([field[half - 3 :], ghost], axis=0)
        back_one, fore_one = one_sided(wide_x, 0, cell_span, stop - start)
        part = field[start:stop]
        wide_y = jnp.concatenate(
            [
                ghost_low(part, y_low[start:stop], first_y, 1),
                part,
                ghost_high(part, y_high[start:stop], last_y, 1),
            ],
            axis=1,
        )
        back_two, fore_two = one_sided(wide_y, 1, cell_span, cells_y)
        mean_one = 0.5 * (back_one + fore_one)
        mean_two = 0.5 * (back_two + fore_two)
        ham = mean_one * (along_one[None, None] + flow_x[start:stop])
        ham = ham + mean_two * (along_two[None, None] + flow_y[start:stop])
        ham = ham + params[1] * jnp.abs(mean_one * y_col - mean_two * x_col[start:stop] - mean_three)
        ham = ham + partial
        spread = 0.5 * (bound_one * (fore_one - back_one) + bound_two * (fore_two - back_two))
        return ham + spread

    def stage(field, x_halos, y_halos, local_pieces, order, update, last):
        results = [None, None]
        sent = [None, None]
        for side in order:
            rate = half_parts(field, side, x_halos[side], *y_halos, *local_pieces[side])
            results[side] = update(side, rate)
            if last:
                continue
            if side == 0:
                piece = lax.optimization_barrier(results[side][:3])
                sent[side] = send_high(piece, "gx")
            else:
                piece = lax.optimization_barrier(results[side][results[side].shape[0] - 3 :])
                sent[side] = send_low(piece, "gx")
        merged = jnp.concatenate(results, axis=0)
        if last:
            return merged, None, None, None
        next_y = y_halo(merged)
        next_pieces = local_whole(merged)
        return merged, (sent[1], sent[0]), next_y, next_pieces

    first, x_halos, y_halos, locals_now = stage(
        values, x_halos, y_halos, locals_now, (1, 0),
        lambda side, rate: cut(values, side) + step_time * rate, False,
    )
    second, x_halos, y_halos, locals_now = stage(
        first, x_halos, y_halos, locals_now, (0, 1),
        lambda side, rate: 0.75 * cut(values, side) + 0.25 * (cut(first, side) + step_time * rate),
        False,
    )
    result, _, _, _ = stage(
        second, x_halos, y_halos, locals_now, (1, 0),
        lambda side, rate: cut(values, side) * (1.0 / 3.0)
        + 2.0 / 3.0 * (cut(second, side) + step_time * rate),
        True,
    )
    return result


def solution(mesh):
    in_specs = (P(("groups", "gx"), "gy", None, None), P(None, ("groups", "gx"), "gy"), P("groups"))
    out_specs = P(("groups", "gx"), "gy", None, None)
    return jax.shard_map(
        on_device, mesh=mesh, in_specs=in_specs, out_specs=out_specs, check_vma=False
    )
```

profile of v0, /device:TPU:0, one launch (start us, length us, event | category | flops | bytes accessed | tf_op | source)
XLA Modules:
  0.0 225.2 jit_solution(8755103993769991976)
XLA Ops:
  0.0 1.5 fusion.114
  1.5 0.7 cosine_multiply_fusion
  2.2 1.4 fusion.103
  3.5 1.4 fusion.104
  4.9 0.8 fusion.112
  5.7 0.6 abs_multiply_fusion.1
  6.3 0.6 abs_multiply_fusion
  6.9 0.8 add_reduce_fusion.1
  7.7 3.3 %fusion.95 = (f32[]{:T(128)}, f32[]{:T(128)}) fusion(f32[1,6,6]{2,0,1:T(1,128)S(1)} %get-tuple-element.127, f32[6]{0:T(128)S(1)} %abs_multiply_fusion.1, f32[]{:T(128)} %get-tuple-element.22, f32[]{:T(128)} %get-tuple-element.21, f32[6]{0:T(128)S(1)} %abs_multiply_fusion, f32[]{:T(128)} %fusion.103, f32[]{:T(128)} %fusion.104, ...), kind=kLoop, calls=%fused_computation.268 | loop fusion | flops 430 | bytes 360 | tf_op jit(solution)/shard_map/reduce_max | solution.py:100
  11.0 1.8 pad_maximum_fusion.31
  12.8 2.4 %collective-permute-start.2 = (f32[2]{0:T(128)}, f32[2]{0:T(128)}, u32[]{:S(2)}, u32[]{:S(2)}) collective-permute-start(f32[2]{0:T(128)} %pad_maximum_fusion.31), channel_id=1, source_target_pairs={{0,3},{1,4},{2,5},{3,6},{4,7},{5,8},{6,9},{7,10},{8,11},{9,12},{10... | collective-permute-start | bytes 32 | tf_op jit(solution)/shard_map/ppermute | solution.py:147
  15.2 1.5 collective-permute-start.1
  17.2 2.4 %fusion.108 = (f32[3,6,64,128]{3,2,1,0:T(8,128)}, f32[3,6,64,128]{3,2,1,0:T(8,128)}) fusion(f32[6,6,64,128]{3,2,1,0:T(8,128)} %param.3), kind=kLoop, calls=%fused_computation.300 | loop fusion | bytes 2359296 | tf_op jit(solution)/shard_map/slice | solution.py:176
  19.6 4.2 %collective-permute-start.6 = (f32[3,6,64,128]{3,2,1,0:T(8,128)}, f32[3,6,64,128]{3,2,1,0:T(8,128)}, u32[]{:S(2)}, u32[]{:S(2)}) collective-permute-start(f32[3,6,64,128]{3,2,1,0:T(8,128)} %get-tuple-element.72), channel_id=1, source_target_pairs={{0,2},{2,4},{4,6},{6,8},{8,10},{10,12},{12,14},{1,3},{3,5},{5,7},{... | collective-permute-start | bytes 1769480 | tf_op jit(solution)/shard_map/ppermute | solution.py:113
  23.8 1.3 collective-permute-start.8
  25.5 1.1 fusion.110
  26.6 1.0 slice.1173
  27.6 1.1 fusion.109
  28.7 2.1 slice_maximum_fusion.5
  30.8 1.4 slice_maximum_fusion.4
  34.1 0.9 slice_bitcast_fusion.17
  35.0 0.8 slice_bitcast_fusion.5
  35.8 0.6 add_multiply_fusion.12
  36.4 0.6 fusion.111
  37.0 1.2 sine_multiply_fusion
  38.2 1.1 slice.1138
  39.3 2.2 pad_maximum_fusion.23
  41.6 0.9 slice_select_fusion
  42.5 1.4 slice_multiply_fusion.1
  44.1 8.8 %multiply_add_fusion.2 = (f32[3,6,64,128]{3,2,1,0:T(8,128)}, f32[3,6,64,128]{3,2,1,0:T(8,128)S(1)}, f32[3,6,64,128]{3,2,1,0:T(8,128)S(1)}) fusion(f32[3,6,64,1]{3,2,1,0:T(8,128)} %get-tuple-element.122, f32[3,6,64,125]{3,2,1,0:T(8,128)S(1)} %copy-done.13, f32[3,6,64,126]{3,2,1,0:T(8,128)S(1)} %copy-done.10, f32[3,6,64,127]{3,2,1,0:T(8,128)S(1)} %get-tuple-element.70, ...), kind=kLoop, calls=%fused_computation.178 | loop fusion | flops 40402944 | bytes 8225292 | tf_op jit(solution)/shard_map/add | solution.py:184
  53.0 0.6 copy-done.28
  54.3 6.9 %multiply_add_fusion.3 = (f32[3,6,64,128]{3,2,1,0:T(8,128)S(1)}, f32[3,6,64,128]{3,2,1,0:T(8,128)S(1)}, f32[3,6,64,128]{3,2,1,0:T(8,128)S(1)}) fusion(f32[3,6,64,1]{3,2,1,0:T(8,128)S(1)} %copy-done.15, f32[3,6,64,125]{3,2,1,0:T(8,128)S(1)} %copy-done.14, f32[3,6,64,126]{3,2,1,0:T(8,128)S(1)} %copy-done.7, f32[3,6,64,127]{3,2,1,0:T(8,128)S(1)} %get-tuple-element.69, ...), kind=kLoop, calls=%fused_computation.185 | loop fusion | flops 40402944 | bytes 8225292 | tf_op jit(solution)/shard_map/add | solution.py:184
  62.5 1.0 collective-permute-start.7
  63.5 1.9 maximum_maximum_fusion.9
  65.4 3.2 %collective-permute-start.5 = (f32[2]{0:T(128)S(1)}, f32[2]{0:T(128)S(1)}, u32[]{:S(2)}, u32[]{:S(2)}) collective-permute-start(f32[2]{0:T(128)S(1)} %maximum_maximum_fusion.9), channel_id=1, source_target_pairs={{0,12},{1,13},{2,14},{3,15},{4,0},{5,1},{6,2},{7,3},{8,4},{9,5},{1... | collective-permute-start | bytes 32 | tf_op jit(solution)/shard_map/ppermute | solution.py:147
  68.6 0.8 collective-permute-start.4
  69.9 1.6 collective-permute-start.3
  71.5 1.6 collective-permute-done.4
  73.0 2.4 %collective-permute-done.3 = f32[2]{0:T(128)S(1)} collective-permute-done((f32[2]{0:T(128)S(1)}, f32[2]{0:T(128)S(1)}, u32[]{:S(2)}, u32[]{:S(2)}) %collective-permute-start.3) | collective-permute-done | bytes 40 | tf_op jit(solution)/shard_map/ppermute | solution.py:147
  75.5 0.7 fusion.113
  77.5 1.3 add_select_fusion.5
  78.9 1.3 add_select_fusion.17
  80.2 1.5 pad_maximum_fusion.10
  82.0 1.2 add_select_fusion.3
  83.7 0.6 copy-done.6
  84.3 7.4 %fusion.53 = f32[3,6,64,128]{3,2,1,0:T(8,128)S(1)} fusion(f32[3,6,64,128]{3,2,1,0:T(8,128)S(1)} %copy-done.6, f32[3,6,64,128]{3,2,1,0:T(8,128)S(1)} %add_multiply_fusion.8, f32[3,11,64,128]{3,2,1,0:T(8,128)S(1)} %fusion.22, f32[8,6,64,128]{3,2,1,0:T(8,128)S(1)} %get-tuple-element.52, f32[3]{0:T(128)S(1)} %copy-done.25, ...), kind=kLoop, calls=%fused_computation.138 | loop fusion | flops 40108032 | bytes 9474684 | tf_op jit(solution)/shard_map/add | solution.py:289
  91.7 7.4 %fusion.31 = f32[3,6,64,128]{3,2,1,0:T(8,128)S(1)} fusion(f32[3,6,64,128]{3,2,1,0:T(8,128)S(1)} %get-tuple-element.14, f32[3,6,64,128]{3,2,1,0:T(8,128)S(1)} %add_multiply_fusion.9, f32[3,11,64,128]{3,2,1,0:T(8,128)S(1)} %fusion.23, f32[8,6,64,128]{3,2,1,0:T(8,128)S(1)} %get-tuple-element.51, f32[]{:T(128)} %bitcast.7, f32[]{:T(128)} %bitcast.6, ...), kind=kLoop, calls=%fused_computation.116 | loop fusion | flops 40108032 | bytes 9474684 | tf_op jit(solution)/shard_map/add | solution.py:289
  100.3 0.7 slice_maximum_fusion.3
  101.9 13.1 %multiply_add_fusion.1 = (f32[6,6,64,128]{3,2,1,0:T(8,128)S(1)}, f32[6,6,64,128]{3,2,1,0:T(8,128)S(1)}, f32[6,6,64,128]{3,2,1,0:T(8,128)S(1)}) fusion(f32[6,6,64,1]{3,2,1,0:T(8,128)S(1)} %get-tuple-element.50, f32[6,6,64,125]{3,2,1,0:T(8,128)S(1)} %slice.1220, f32[6,6,64,126]{3,2,1,0:T(8,128)S(1)} %get-tuple-element.48, f32[6,6,64,127]{3,2,1,0:T(8,128)S(1)} %fusion.17, ...), kind=kLoop, calls=%fused_computation.83 | loop fusion | flops 80805888 | bytes 16450572 | tf_op jit(solution)/shard_map/add | solution.py:184
  115.3 3.5 %collective-permute-start.9 = (f32[3,6,64,128]{3,2,1,0:T(8,128)S(1)}, f32[3,6,64,128]{3,2,1,0:T(8,128)S(1)}, u32[]{:S(2)}, u32[]{:S(2)}) collective-permute-start(f32[3,6,64,128]{3,2,1,0:T(8,128)S(1)} %fusion.53), channel_id=1, source_target_pairs={{0,2},{2,4},{4,6},{6,8},{8,10},{10,12},{12,14},{1,3},{3,5},{5,7},{... | collective-permute-start | bytes 1769480 | tf_op jit(solution)/shard_map/ppermute | solution.py:113
  118.8 1.5 collective-permute-start.11
  120.8 23.9 %collective-permute-done.9 = f32[3,6,64,128]{3,2,1,0:T(8,128)S(1)} collective-permute-done((f32[3,6,64,128]{3,2,1,0:T(8,128)S(1)}, f32[3,6,64,128]{3,2,1,0:T(8,128)S(1)}, u32[]{:S(2)}, u32[]{:S(2)}) %collective-permute-start.9) | collective-permute-done | bytes 589856 | tf_op jit(solution)/shard_map/ppermute | solution.py:113
  145.1 0.5 pad_maximum_fusion
  146.2 7.5 %fusion.61 = f32[3,6,64,128]{3,2,1,0:T(8,128)S(1)} fusion(f32[3,6,64,128]{3,2,1,0:T(8,128)S(1)} %fusion.53, f32[6,6,64,128]{3,2,1,0:T(8,128)S(1)} %get-tuple-element.18, f32[6,6,64,128]{3,2,1,0:T(8,128)S(1)} %add_multiply_fusion.1, f32[3,11,64,128]{3,2,1,0:T(8,128)S(1)} %fusion.20, f32[8,6,64,128]{3,2,1,0:T(8,128)S(1)} %fusion.8, f32[3]{0:T(128)S(1)} %copy-done.25, ...), kind=kLoop, calls=%fused_computation.146 | loop fusion | flops 40550400 | bytes 10064508 | tf_op jit(solution)/shard_map/add | solution.py:293
  153.7 7.5 %fusion.39 = f32[3,6,64,128]{3,2,1,0:T(8,128)S(1)} fusion(f32[3,6,64,128]{3,2,1,0:T(8,128)S(1)} %fusion.31, f32[6,6,64,128]{3,2,1,0:T(8,128)S(1)} %get-tuple-element.18, f32[6,6,64,128]{3,2,1,0:T(8,128)S(1)} %add_multiply_fusion.1, f32[3,11,64,128]{3,2,1,0:T(8,128)S(1)} %fusion.21, f32[8,6,64,128]{3,2,1,0:T(8,128)S(1)} %fusion.9, f32[]{:T(128)} %bitcast.7, ...), kind=kLoop, calls=%fused_computation.124 | loop fusion | flops 40550400 | bytes 10064508 | tf_op jit(solution)/shard_map/add | solution.py:293
  162.3 0.7 slice_maximum_fusion.1
  164.0 13.1 %multiply_add_fusion = (f32[6,6,64,128]{3,2,1,0:T(8,128)S(1)}, f32[6,6,64,128]{3,2,1,0:T(8,128)S(1)}, f32[6,6,64,128]{3,2,1,0:T(8,128)S(1)}) fusion(f32[6,6,64,1]{3,2,1,0:T(8,128)S(1)} %get-tuple-element.42, f32[6,6,64,125]{3,2,1,0:T(8,128)S(1)} %slice.1292, f32[6,6,64,126]{3,2,1,0:T(8,128)S(1)} %get-tuple-element.40, f32[6,6,64,127]{3,2,1,0:T(8,128)S(1)} %fusion.14, ...), kind=kLoop, calls=%fused_computation.79 | loop fusion | flops 80805888 | bytes 16450572 | tf_op jit(solution)/shard_map/add | solution.py:184
  177.3 4.4 %collective-permute-start.12 = (f32[3,6,64,128]{3,2,1,0:T(8,128)S(1)}, f32[3,6,64,128]{3,2,1,0:T(8,128)S(1)}, u32[]{:S(2)}, u32[]{:S(2)}) collective-permute-start(f32[3,6,64,128]{3,2,1,0:T(8,128)S(1)} %fusion.61), channel_id=1, source_target_pairs={{0,2},{2,4},{4,6},{6,8},{8,10},{10,12},{12,14},{1,3},{3,5},{5,7},{... | collective-permute-start | bytes 1769480 | tf_op jit(solution)/shard_map/ppermute | solution.py:113
  181.7 1.6 collective-permute-start.14
  183.7 23.8 %collective-permute-done.12 = f32[3,6,64,128]{3,2,1,0:T(8,128)S(1)} collective-permute-done((f32[3,6,64,128]{3,2,1,0:T(8,128)S(1)}, f32[3,6,64,128]{3,2,1,0:T(8,128)S(1)}, u32[]{:S(2)}, u32[]{:S(2)}) %collective-permute-start.12) | collective-permute-done | bytes 589856 | tf_op jit(solution)/shard_map/ppermute | solution.py:113
  208.0 0.5 pad_maximum_fusion.2
  209.1 7.5 %fusion.69 = f32[3,6,64,128]{3,2,1,0:T(8,128)S(1)} fusion(f32[3,6,64,128]{3,2,1,0:T(8,128)S(1)} %fusion.61, f32[6,6,64,128]{3,2,1,0:T(8,128)S(1)} %get-tuple-element.20, f32[6,6,64,128]{3,2,1,0:T(8,128)S(1)} %add_multiply_fusion, f32[3,11,64,128]{3,2,1,0:T(8,128)S(1)} %fusion.18, f32[8,6,64,128]{3,2,1,0:T(8,128)S(1)} %fusion.6, f32[3]{0:T(128)S(1)} %copy-done.25, ...), kind=kLoop, calls=%fused_computation.154 | loop fusion | flops 40550400 | bytes 10064508 | tf_op jit(solution)/shard_map/add | solution.py:298
  216.6 7.5 %fusion.47 = f32[3,6,64,128]{3,2,1,0:T(8,128)S(1)} fusion(f32[3,6,64,128]{3,2,1,0:T(8,128)S(1)} %fusion.39, f32[6,6,64,128]{3,2,1,0:T(8,128)S(1)} %get-tuple-element.20, f32[6,6,64,128]{3,2,1,0:T(8,128)S(1)} %add_multiply_fusion, f32[3,11,64,128]{3,2,1,0:T(8,128)S(1)} %fusion.19, f32[8,6,64,128]{3,2,1,0:T(8,128)S(1)} %fusion.7, f32[]{:T(128)} %bitcast.7, ...), kind=kLoop, calls=%fused_computation.132 | loop fusion | flops 40550400 | bytes 10064508 | tf_op jit(solution)/shard_map/add | solution.py:298
  224.1 1.1 pad_maximum_fusion.22
  (136 shorter events, 11.3 us)
Async XLA Ops:
  12.8 12.4 %copy-start = (f32[6,6,64,128]{3,2,1,0:T(8,128)S(1)}, f32[6,6,64,128]{3,2,1,0:T(8,128)}, u32[]{:S(2)}) copy-start(f32[6,6,64,128]{3,2,1,0:T(8,128)} %param.3) | copy-start | bytes 3538948
  12.8 49.7 %collective-permute-start.2 = (f32[2]{0:T(128)}, f32[2]{0:T(128)}, u32[]{:S(2)}, u32[]{:S(2)}) collective-permute-start(f32[2]{0:T(128)} %pad_maximum_fusion.31), channel_id=1, source_target_pairs={{0,3},{1,4},{2,5},{3,6},{4,7},{5,8},{6,9},{7,10},{8,11},{9,12},{10... | collective-permute-start | bytes 32 | tf_op jit(solution)/shard_map/ppermute | solution.py:147
  15.2 48.3 %collective-permute-start.1 = (f32[2]{0:T(128)}, f32[2]{0:T(128)}, u32[]{:S(2)}, u32[]{:S(2)}) collective-permute-start(f32[2]{0:T(128)} %pad_maximum_fusion.31), channel_id=1, source_target_pairs={{0,2},{1,3},{2,4},{3,5},{4,6},{5,7},{6,8},{7,9},{8,10},{9,11},{10,... | collective-permute-start | bytes 32 | tf_op jit(solution)/shard_map/ppermute | solution.py:147
  16.7 46.8 %collective-permute-start = (f32[2]{0:T(128)}, f32[2]{0:T(128)}, u32[]{:S(2)}, u32[]{:S(2)}) collective-permute-start(f32[2]{0:T(128)} %pad_maximum_fusion.31), channel_id=1, source_target_pairs={{0,1},{1,2},{2,3},{3,4},{4,5},{5,6},{6,7},{7,8},{8,9},{9,10},{10,1... | collective-permute-start | bytes 32 | tf_op jit(solution)/shard_map/ppermute | solution.py:147
  19.6 57.9 %collective-permute-start.6 = (f32[3,6,64,128]{3,2,1,0:T(8,128)}, f32[3,6,64,128]{3,2,1,0:T(8,128)}, u32[]{:S(2)}, u32[]{:S(2)}) collective-permute-start(f32[3,6,64,128]{3,2,1,0:T(8,128)} %get-tuple-element.72), channel_id=1, source_target_pairs={{0,2},{2,4},{4,6},{6,8},{8,10},{10,12},{12,14},{1,3},{3,5},{5,7},{... | collective-permute-start | bytes 1769480 | tf_op jit(solution)/shard_map/ppermute | solution.py:113
  23.8 58.2 %collective-permute-start.8 = (f32[3,6,64,128]{3,2,1,0:T(8,128)}, f32[3,6,64,128]{3,2,1,0:T(8,128)}, u32[]{:S(2)}, u32[]{:S(2)}) collective-permute-start(f32[3,6,64,128]{3,2,1,0:T(8,128)} %get-tuple-element.71), channel_id=1, source_target_pairs={{2,0},{4,2},{6,4},{8,6},{10,8},{12,10},{14,12},{3,1},{5,3},{7,5},{... | collective-permute-start | bytes 1769480 | tf_op jit(solution)/shard_map/ppermute | solution.py:118
  26.6 4.2 %copy-start.3 = (f32[3,6,64,1]{3,2,1,0:T(8,128)}, f32[3,6,64,1]{3,2,1,0:T(8,128)S(1)}, u32[]{:S(2)}) copy-start(f32[3,6,64,1]{3,2,1,0:T(8,128)S(1)} %get-tuple-element.121) | copy-start | bytes 13828
  28.7 2.1 copy-start.1
  35.0 1.4 copy-start.23
  41.6 2.3 %copy-start.5 = (f32[3,6,70,128]{3,2,1,0:T(8,128)S(1)}, f32[3,6,70,128]{3,2,1,0:T(8,128)}, u32[]{:S(2)}) copy-start(f32[3,6,70,128]{3,2,1,0:T(8,128)} %get-tuple-element.146) | copy-start | bytes 1935364
  41.6 2.4 %copy-start.12 = (f32[3,6,64,127]{3,2,1,0:T(8,128)S(1)}, f32[3,6,64,127]{3,2,1,0:T(8,128)}, u32[]{:S(2)}) copy-start(f32[3,6,64,127]{3,2,1,0:T(8,128)} %get-tuple-element.142) | copy-start | bytes 1755652
  41.6 2.4 %copy-start.13 = (f32[3,6,64,125]{3,2,1,0:T(8,128)S(1)}, f32[3,6,64,125]{3,2,1,0:T(8,128)}, u32[]{:S(2)}) copy-start(f32[3,6,64,125]{3,2,1,0:T(8,128)} %slice.1173) | copy-start | bytes 1728004
  42.5 1.5 copy-start.4
  42.5 1.5 copy-start.9
  42.5 1.6 copy-start.10
  44.1 9.5 %copy-start.11 = (f32[3,6,64,127]{3,2,1,0:T(8,128)S(1)}, f32[3,6,64,127]{3,2,1,0:T(8,128)}, u32[]{:S(2)}) copy-start(f32[3,6,64,127]{3,2,1,0:T(8,128)} %get-tuple-element.143) | copy-start | bytes 1755652
  44.1 9.5 %copy-start.14 = (f32[3,6,64,125]{3,2,1,0:T(8,128)S(1)}, f32[3,6,64,125]{3,2,1,0:T(8,128)}, u32[]{:S(2)}) copy-start(f32[3,6,64,125]{3,2,1,0:T(8,128)} %slice.1138) | copy-start | bytes 1728004
  44.1 9.5 %copy-start.15 = (f32[3,6,64,1]{3,2,1,0:T(8,128)S(1)}, f32[3,6,64,1]{3,2,1,0:T(8,128)}, u32[]{:S(2)}) copy-start(f32[3,6,64,1]{3,2,1,0:T(8,128)} %get-tuple-element.118) | copy-start | bytes 13828
  52.9 0.7 copy-start.28
  52.9 0.7 copy-start.29
  52.9 1.1 copy-start.2
  52.9 1.2 copy-start.7
  52.9 1.4 copy-start.8
  61.2 0.6 copy-start.30
  61.2 0.7 copy-start.27
  61.2 1.3 copy-start.26
  62.5 16.3 %collective-permute-start.7 = (f32[6,3,64,128]{3,2,1,0:T(8,128)}, f32[6,3,64,128]{3,2,1,0:T(8,128)}, u32[]{:S(2)}, u32[]{:S(2)}) collective-permute-start(f32[6,3,64,128]{3,2,1,0:T(8,128)} %slice_select_fusion), channel_id=1, source_target_pairs={{0,1},{1,0},{2,3},{3,2},{4,5},{5,4},{6,7},{7,6},{8,9},{9,8},{10,11... | collective-permute-start | bytes 1769480 | tf_op jit(solution)/shard_map/ppermute | solution.py:200
  65.4 4.5 %collective-permute-start.5 = (f32[2]{0:T(128)S(1)}, f32[2]{0:T(128)S(1)}, u32[]{:S(2)}, u32[]{:S(2)}) collective-permute-start(f32[2]{0:T(128)S(1)} %maximum_maximum_fusion.9), channel_id=1, source_target_pairs={{0,12},{1,13},{2,14},{3,15},{4,0},{5,1},{6,2},{7,3},{8,4},{9,5},{1... | collective-permute-start | bytes 32 | tf_op jit(solution)/shard_map/ppermute | solution.py:147
  68.6 4.5 %collective-permute-start.4 = (f32[2]{0:T(128)S(1)}, f32[2]{0:T(128)S(1)}, u32[]{:S(2)}, u32[]{:S(2)}) collective-permute-start(f32[2]{0:T(128)S(1)} %maximum_maximum_fusion.9), channel_id=1, source_target_pairs={{0,8},{1,9},{2,10},{3,11},{4,12},{5,13},{6,14},{7,15},{8,0},{9,1},... | collective-permute-start | bytes 32 | tf_op jit(solution)/shard_map/ppermute | solution.py:147
  69.9 5.6 %collective-permute-start.3 = (f32[2]{0:T(128)S(1)}, f32[2]{0:T(128)S(1)}, u32[]{:S(2)}, u32[]{:S(2)}) collective-permute-start(f32[2]{0:T(128)S(1)} %maximum_maximum_fusion.9), channel_id=1, source_target_pairs={{0,4},{1,5},{2,6},{3,7},{4,8},{5,9},{6,10},{7,11},{8,12},{9,13},{1... | collective-permute-start | bytes 32 | tf_op jit(solution)/shard_map/ppermute | solution.py:147
  77.4 1.4 copy-start.16
  77.5 1.4 copy-start.17
  77.5 1.4 copy-start.18
  77.5 1.4 copy-start.19
  77.5 1.4 copy-start.20
  77.5 1.4 copy-start.21
  77.5 1.4 copy-start.22
  83.3 1.1 copy-start.6
  83.3 1.1 copy-start.25
  84.3 7.4 %copy-start.24 = (f32[3]{0:T(128)S(1)}, f32[3]{0:T(128)}, u32[]{:S(2)}) copy-start(f32[3]{0:T(128)} %get-tuple-element.132) | copy-start | bytes 40
  101.9 18.5 %collective-permute-start.10 = (f32[6,3,64,128]{3,2,1,0:T(8,128)S(1)}, f32[6,3,64,128]{3,2,1,0:T(8,128)S(1)}, u32[]{:S(2)}, u32[]{:S(2)}) collective-permute-start(f32[6,3,64,128]{3,2,1,0:T(8,128)S(1)} %fusion.74), channel_id=1, source_target_pairs={{0,1},{1,0},{2,3},{3,2},{4,5},{5,4},{6,7},{7,6},{8,9},{9,8},{10,11... | collective-permute-start | bytes 1769480 | tf_op jit(solution)/shard_map/ppermute | solution.py:200
  115.3 29.4 %collective-permute-start.9 = (f32[3,6,64,128]{3,2,1,0:T(8,128)S(1)}, f32[3,6,64,128]{3,2,1,0:T(8,128)S(1)}, u32[]{:S(2)}, u32[]{:S(2)}) collective-permute-start(f32[3,6,64,128]{3,2,1,0:T(8,128)S(1)} %fusion.53), channel_id=1, source_target_pairs={{0,2},{2,4},{4,6},{6,8},{8,10},{10,12},{12,14},{1,3},{3,5},{5,7},{... | collective-permute-start | bytes 1769480 | tf_op jit(solution)/shard_map/ppermute | solution.py:113
  118.8 26.1 %collective-permute-start.11 = (f32[3,6,64,128]{3,2,1,0:T(8,128)S(1)}, f32[3,6,64,128]{3,2,1,0:T(8,128)S(1)}, u32[]{:S(2)}, u32[]{:S(2)}) collective-permute-start(f32[3,6,64,128]{3,2,1,0:T(8,128)S(1)} %fusion.31), channel_id=1, source_target_pairs={{2,0},{4,2},{6,4},{8,6},{10,8},{12,10},{14,12},{3,1},{5,3},{7,5},{... | collective-permute-start | bytes 1769480 | tf_op jit(solution)/shard_map/ppermute | solution.py:118
  163.9 19.5 %collective-permute-start.13 = (f32[6,3,64,128]{3,2,1,0:T(8,128)S(1)}, f32[6,3,64,128]{3,2,1,0:T(8,128)S(1)}, u32[]{:S(2)}, u32[]{:S(2)}) collective-permute-start(f32[6,3,64,128]{3,2,1,0:T(8,128)S(1)} %fusion.71), channel_id=1, source_target_pairs={{0,1},{1,0},{2,3},{3,2},{4,5},{5,4},{6,7},{7,6},{8,9},{9,8},{10,11... | collective-permute-start | bytes 1769480 | tf_op jit(solution)/shard_map/ppermute | solution.py:200
  177.3 30.3 %collective-permute-start.12 = (f32[3,6,64,128]{3,2,1,0:T(8,128)S(1)}, f32[3,6,64,128]{3,2,1,0:T(8,128)S(1)}, u32[]{:S(2)}, u32[]{:S(2)}) collective-permute-start(f32[3,6,64,128]{3,2,1,0:T(8,128)S(1)} %fusion.61), channel_id=1, source_target_pairs={{0,2},{2,4},{4,6},{6,8},{8,10},{10,12},{12,14},{1,3},{3,5},{5,7},{... | collective-permute-start | bytes 1769480 | tf_op jit(solution)/shard_map/ppermute | solution.py:113
  181.7 26.1 %collective-permute-start.14 = (f32[3,6,64,128]{3,2,1,0:T(8,128)S(1)}, f32[3,6,64,128]{3,2,1,0:T(8,128)S(1)}, u32[]{:S(2)}, u32[]{:S(2)}) collective-permute-start(f32[3,6,64,128]{3,2,1,0:T(8,128)S(1)} %fusion.39), channel_id=1, source_target_pairs={{2,0},{4,2},{6,4},{8,6},{10,8},{12,10},{14,12},{3,1},{5,3},{7,5},{... | collective-permute-start | bytes 1769480 | tf_op jit(solution)/shard_map/ppermute | solution.py:118
where the time goes:
time: 226 us; the launch traced here: 225 us
  other arithmetic  126 us (56%)
  waiting for transfers between devices  52.2 us (23%)
  starting transfers between devices  27.6 us (12%)
  local copies, waits for them, and re-layouts  14.2 us (6%)
  between operations  4.74 us (2%)
    ppermute x3, waiting for transfers between devices, send_low(): lax.ppermute(piece, axis, [(i, (i + 1) % count) for i in range(count - 1)])  47.7 us
    add x4, other arithmetic, local_part(): partial + 0.5 * (alpha_three * (fore_three - back_three) + alpha_four * (...  41.7 us
    add x2, other arithmetic, on_device(): 0.75 * cut(values, side) + 0.25 * (cut(first, side) + step_time * rate)  14.9 us
    add x2, other arithmetic, on_device(): cut(values, side) * (1.0 / 3.0)  14.9 us
    add x2, other arithmetic, on_device(): cut(values, side) + step_time * rate  14.8 us
    ppermute x3, starting transfers between devices, send_low(): lax.ppermute(piece, axis, [(i, (i + 1) % count) for i in range(count - 1)])  12.2 us
    ppermute x6, starting transfers between devices, spread_max(): lax.ppermute(local, axes, [(i, (i + k * span) % count) for i in range(cou...  9.99 us
    concatenate x6, other arithmetic, clamped_sided(): jnp.concatenate([lax.slice_in_dim(inner, 0, 1, axis=along), inner], axis=...  5.67 us
  transfers between devices with their start and end apart: 15, of which 5 were waited for; matrix products, arithmetic and copies ran while one was open for 31% of the time, Pallas kernels for 0%

commit v1 on v0

--- a/solution.py
+++ b/solution.py
@@ -173,7 +173,11 @@
     alpha_four = params[3]
 
     def cut(array, side):
-        return array[:half] if side == 0 else array[half:]
+        if side == 0:
+            return array[:half]
+        if side == 1:
+            return array[half:]
+        return array
 
     def local_part(field):
         back_three, fore_three = periodic_sided(field, 2, step_psi)
@@ -186,12 +190,6 @@
         )
         return mean_three, partial
 
-    def local_halves(field):
-        pieces = []
-        for side in (0, 1):
-            pieces.append(lax.optimization_barrier(local_part(cut(field, side))))
-        return pieces
-
     def y_halo(field):
         tail = lax.slice_in_dim(field, cells_y - 3, cells_y, axis=1)
         head = lax.slice_in_dim(field, 0, 3, axis=1)
@@ -203,8 +201,7 @@
         return send_low(tail, "gy"), send_high(head, "gy")
 
     def local_whole(field):
-        mean_three, partial = lax.optimization_barrier(local_part(field))
-        return [(cut(mean_three, side), cut(partial, side)) for side in (0, 1)]
+        return lax.optimization_barrier(local_part(field))
 
     x_halos = (send_low(values[cells_x - 3 :], "gx"), send_high(values[:3], "gx"))
     y_halos = y_halo(values)
@@ -219,8 +216,8 @@
         (place_x * cells_x + jnp.arange(cells_x)).astype(jnp.float32) + 0.5 - 0.5 * total_x
     ) * cell_span
     local_one, local_two = speed_bounds(drift, x_coord, y_coord, params[1], along_one, along_two)
+    locals_now = local_whole(values)
     bounds = spread_max(jnp.stack([local_one, local_two]), ("gx", "gy"))
-    locals_now = local_halves(values)
     bound_one = bounds[0]
     bound_two = bounds[1]
     step_time = cfl_number / (
@@ -234,15 +231,27 @@
     flow_x = drift[0][:, :, None, None]
     flow_y = drift[1][:, :, None, None]
 
-    def half_parts(field, side, x_halo, y_low, y_high, mean_three, partial):
+    def half_parts(field, side, x_halos, y_low, y_high, mean_three, partial):
         if side == 0:
             start, stop = 0, half
-            ghost = ghost_low(field, x_halo, first_x, 0)
+            ghost = ghost_low(field, x_halos[0], first_x, 0)
             wide_x = jnp.concatenate([ghost, field[: half + 3]], axis=0)
+        elif side == 1:
+            start, stop = half, cells_x
+            ghost = ghost_high(field, x_halos[1], last_x, 0)
+            wide_x = jnp.concatenate([field[half - 3 :], ghost], axis=0)
         else:
-            start, stop = half, cells_x
-            ghost = ghost_high(field, x_halo, last_x, 0)
-            wide_x = jnp.concatenate([field[half - 3 :], ghost], axis=0)
+            start, stop = 0, cells_x
+            wide_x = jnp.concatenate(
+                [
+                    ghost_low(field, x_halos[0], first_x, 0),
+                    field,
+                    ghost_high(field, x_halos[1], last_x, 0),
+                ],
+                axis=0,
+            )
+        mean_three = mean_three[start:stop]
+        partial = partial[start:stop]
         back_one, fore_one = one_sided(wide_x, 0, cell_span, stop - start)
         part = field[start:stop]
         wide_y = jnp.concatenate(
@@ -260,15 +269,22 @@
         ham = ham + mean_two * (along_two[None, None] + flow_y[start:stop])
         ham = ham + params[1] * jnp.abs(mean_one * y_col - mean_two * x_col[start:stop] - mean_three)
         ham = ham + partial
-        spread = 0.5 * (bound_one * (fore_one - back_one) + bound_two * (fore_two - back_two))
-        return ham + spread
-
-    def stage(field, x_halos, y_halos, local_pieces, order, update, last):
+        return ham, fore_one - back_one, fore_two - back_two
+
+    def combine(ham, spread_one, spread_two):
+        return ham + 0.5 * (bound_one * spread_one + bound_two * spread_two)
+
+    def stage(layer, field, x_halos, y_halos, local_pieces, order, update, last):
         results = [None, None]
         sent = [None, None]
-        for side in order:
-            rate = half_parts(field, side, x_halos[side], *y_halos, *local_pieces[side])
-            results[side] = update(side, rate)
+        if last:
+            rate = combine(*half_parts(field, 2, x_halos, *y_halos, *local_pieces))
+            return update(2, rate), None, None, None
+        for position, side in enumerate(order):
+            parts = half_parts(field, side, x_halos, *y_halos, *local_pieces)
+            if layer == 1 and position == 0:
+                parts = lax.optimization_barrier(parts)
+            results[side] = update(side, combine(*parts))
             if last:
                 continue
             if side == 0:
@@ -285,16 +301,16 @@
         return merged, (sent[1], sent[0]), next_y, next_pieces
 
     first, x_halos, y_halos, locals_now = stage(
-        values, x_halos, y_halos, locals_now, (1, 0),
+        1, values, x_halos, y_halos, locals_now, (1, 0),
         lambda side, rate: cut(values, side) + step_time * rate, False,
     )
     second, x_halos, y_halos, locals_now = stage(
-        first, x_halos, y_halos, locals_now, (0, 1),
+        2, first, x_halos, y_halos, locals_now, (0, 1),
         lambda side, rate: 0.75 * cut(values, side) + 0.25 * (cut(first, side) + step_time * rate),
         False,
     )
     result, _, _, _ = stage(
-        second, x_halos, y_halos, locals_now, (1, 0),
+        3, second, x_halos, y_halos, locals_now, (1, 0),
         lambda side, rate: cut(values, side) * (1.0 / 3.0)
         + 2.0 / 3.0 * (cut(second, side) + step_time * rate),
         True,

time: 226 us -> 227 us (level)
  waiting for transfers between devices: 52.2 us -> 60.8 us
  other arithmetic: 126 us -> 121 us
    ppermute x3, waiting for transfers between devices: 47.7 us -> 36.4 us  [send_low(): lax.ppermute(piece, axis, [(i, (i + 1) % count) for i in range(count - 1)])]
    ppermute x3, waiting for transfers between devices: 0.01 us -> 11.1 us  [send_high(): lax.ppermute(piece, axis, [((i + 1) % count, i) for i in range(count - 1)])]
    ppermute x6, waiting for transfers between devices: 4.53 us -> 13.3 us  [spread_max(): lax.ppermute(local, axes, [(i, (i + k * span) % count) for i in range(cou...]
    add x2, other arithmetic: 14.8 us -> 8.81 us  [on_device(): cut(values, side) + step_time * rate]
    sub x0 -> x2, other arithmetic: none -> 5.1 us  [half_parts(): return (ham, fore_one - back_one, fore_two - back_two)]
    add x4 -> x3, other arithmetic: 41.7 us -> 39.9 us  [local_part(): partial + 0.5 * (alpha_three * (fore_three - back_three) + alpha_four * (...]
    add x2 -> x1, other arithmetic: 14.9 us -> 14.1 us  [on_device(): cut(values, side) * (1.0 / 3.0)]
  transfers between devices with their start and end apart: 15 -> 15, of which waited for: 5 -> 5; matrix products, arithmetic and copies ran while one was open for 31% -> 24% of each run, Pallas kernels for 0% -> 0%
where the time goes in v1:
time: 227 us; the launch traced here: 226 us
  other arithmetic  121 us (53%)
  waiting for transfers between devices  60.8 us (27%)
  starting transfers between devices  26.5 us (12%)
  local copies, waits for them, and re-layouts  13.8 us (6%)
  between operations  4.69 us (2%)
    add x3, other arithmetic, local_part(): partial + 0.5 * (alpha_three * (fore_three - back_three) + alpha_four * (...  39.9 us
    ppermute x3, waiting for transfers between devices, send_low(): lax.ppermute(piece, axis, [(i, (i + 1) % count) for i in range(count - 1)])  36.4 us
    add x2, other arithmetic, on_device(): 0.75 * cut(values, side) + 0.25 * (cut(first, side) + step_time * rate)  14.8 us
    add x1, other arithmetic, on_device(): cut(values, side) * (1.0 / 3.0)  14.1 us
    ppermute x6, waiting for transfers between devices, spread_max(): lax.ppermute(local, axes, [(i, (i + k * span) % count) for i in range(cou...  13.3 us
    ppermute x3, waiting for transfers between devices, send_high(): lax.ppermute(piece, axis, [((i + 1) % count, i) for i in range(count - 1)])  11.1 us
    ppermute x3, starting transfers between devices, send_low(): lax.ppermute(piece, axis, [(i, (i + 1) % count) for i in range(count - 1)])  10.9 us
    ppermute x6, starting transfers between devices, spread_max(): lax.ppermute(local, axes, [(i, (i + k * span) % count) for i in range(cou...  10.2 us
  transfers between devices with their start and end apart: 15, of which 5 were waited for; matrix products, arithmetic and copies ran while one was open for 24% of the time, Pallas kernels for 0%

profile of v1, /device:TPU:0, one launch (start us, length us, event | category | flops | bytes accessed | tf_op | source)
XLA Modules:
  0.0 226.4 jit_solution(4674132104510872251)
XLA Ops:
  0.0 1.4 fusion.95
  1.5 1.3 sine_multiply_fusion
  2.7 1.3 fusion.81
  4.0 1.1 abs_multiply_fusion
  5.1 1.1 abs_multiply_fusion.1
  6.3 0.8 fusion.93
  7.0 1.3 add_reduce_fusion.1
  8.3 1.9 add_reduce_fusion.2
  10.2 1.8 add_reduce_fusion.3
  12.0 1.8 pad_maximum_fusion.24
  13.8 2.4 %collective-permute-start.2 = (f32[2]{0:T(128)}, f32[2]{0:T(128)}, u32[]{:S(2)}, u32[]{:S(2)}) collective-permute-start(f32[2]{0:T(128)} %pad_maximum_fusion.24), channel_id=1, source_target_pairs={{0,3},{1,4},{2,5},{3,6},{4,7},{5,8},{6,9},{7,10},{8,11},{9,12},{10... | collective-permute-start | bytes 32 | tf_op jit(solution)/shard_map/ppermute | solution.py:147
  16.2 1.5 collective-permute-start.1
  18.2 2.1 slice_select_fusion
  20.4 1.2 collective-permute-start.7
  21.5 1.2 fusion.89
  22.7 4.2 %collective-permute-start.6 = (f32[3,6,64,128]{3,2,1,0:T(8,128)}, f32[3,6,64,128]{3,2,1,0:T(8,128)}, u32[]{:S(2)}, u32[]{:S(2)}) collective-permute-start(f32[3,6,64,128]{3,2,1,0:T(8,128)} %get-tuple-element.73), channel_id=1, source_target_pairs={{0,2},{2,4},{4,6},{6,8},{8,10},{10,12},{12,14},{1,3},{3,5},{5,7},{... | collective-permute-start | bytes 1769480 | tf_op jit(solution)/shard_map/ppermute | solution.py:113
  27.4 1.4 fusion.91
  28.8 1.4 slice.941
  30.2 2.0 slice_maximum_fusion.5
  32.2 1.4 slice_maximum_fusion.4
  35.6 0.9 slice_bitcast_fusion.13
  36.6 0.6 add_convert_fusion
  37.1 1.0 slice_bitcast_fusion.5
  38.1 0.5 fusion.92
  38.7 0.6 copy_bitcast_fusion
  39.6 0.5 copy-done.22
  40.2 0.7 slice_multiply_fusion.1
  42.0 13.7 %multiply_add_fusion.2 = (f32[6,6,64,128]{3,2,1,0:T(8,128)}, f32[6,6,64,128]{3,2,1,0:T(8,128)S(1)}, f32[6,6,64,128]{3,2,1,0:T(8,128)S(1)}) fusion(f32[6,6,64,1]{3,2,1,0:T(8,128)S(1)} %copy-done.4, f32[6,6,64,125]{3,2,1,0:T(8,128)S(1)} %copy-done.3, f32[6,6,64,126]{3,2,1,0:T(8,128)S(1)} %copy-done.6, f32[6,6,64,127]{3,2,1,0:T(8,128)S(1)} %subtract_multiply_fusion, ...), kind=kLoop, calls=%fused_computation.108 | loop fusion | flops 80805888 | bytes 16450572 | tf_op jit(solution)/shard_map/add | solution.py:188
  55.9 0.6 copy_bitcast_fusion.2
  56.5 0.7 add_multiply_fusion.7
  57.2 0.7 add_multiply_fusion.9
  57.9 0.6 fusion.79
  59.1 0.6 copy.25
  59.7 1.3 collective-permute-start.8
  61.0 1.9 maximum_maximum_fusion.7
  62.9 3.5 %collective-permute-start.5 = (f32[2]{0:T(128)S(1)}, f32[2]{0:T(128)S(1)}, u32[]{:S(2)}, u32[]{:S(2)}) collective-permute-start(f32[2]{0:T(128)S(1)} %maximum_maximum_fusion.7), channel_id=1, source_target_pairs={{0,12},{1,13},{2,14},{3,15},{4,0},{5,1},{6,2},{7,3},{8,4},{9,5},{1... | collective-permute-start | bytes 32 | tf_op jit(solution)/shard_map/ppermute | solution.py:147
  66.4 0.8 collective-permute-start.4
  67.2 9.5 %collective-permute-done.5 = f32[2]{0:T(128)S(1)} collective-permute-done((f32[2]{0:T(128)S(1)}, f32[2]{0:T(128)S(1)}, u32[]{:S(2)}, u32[]{:S(2)}) %collective-permute-start.5) | collective-permute-done | bytes 40 | tf_op jit(solution)/shard_map/ppermute | solution.py:147
  76.7 1.6 collective-permute-start.3
  78.3 3.8 %collective-permute-done.3 = f32[2]{0:T(128)S(1)} collective-permute-done((f32[2]{0:T(128)S(1)}, f32[2]{0:T(128)S(1)}, u32[]{:S(2)}, u32[]{:S(2)}) %collective-permute-start.3) | collective-permute-done | bytes 40 | tf_op jit(solution)/shard_map/ppermute | solution.py:147
  82.0 0.7 fusion.94
  84.0 1.6 add_select_fusion.15
  85.6 1.3 pad_maximum_fusion.11
  87.0 2.6 %fusion.85 = (f32[3,6,64,128]{3,2,1,0:T(8,128)S(1)}, f32[3,6,64,128]{3,2,1,0:T(8,128)S(1)}, f32[3,6,64,128]{3,2,1,0:T(8,128)S(1)}) fusion(f32[3,11,64,128]{3,2,1,0:T(8,128)S(1)} %fusion.25), kind=kLoop, calls=%fused_computation.262 | loop fusion | flops 18432000 | bytes 5308416 | tf_op jit(solution)/shard_map/sub | solution.py:272
  89.8 0.7 copy-done.9
  91.2 2.5 %fusion.86 = (f32[3,6,64,128]{3,2,1,0:T(8,128)S(1)}, f32[3,6,64,128]{3,2,1,0:T(8,128)S(1)}, f32[3,6,64,128]{3,2,1,0:T(8,128)S(1)}) fusion(f32[8,6,64,128]{3,2,1,0:T(8,128)S(1)} %get-tuple-element.59), kind=kLoop, calls=%fused_computation.263 | loop fusion | flops 18432000 | bytes 5308416 | tf_op jit(solution)/shard_map/sub | solution.py:272
  93.8 1.1 fusion.43
  95.1 1.5 multiply_add_fusion.3
  96.6 7.3 %fusion.32 = f32[3,6,64,128]{3,2,1,0:T(8,128)S(1)} fusion(f32[6,6,64,128]{3,2,1,0:T(8,128)S(1)} %copy-done.1, f32[6,6,64,128]{3,2,1,0:T(8,128)S(1)} %add_multiply_fusion.2, f32[3,11,64,128]{3,2,1,0:T(8,128)S(1)} %fusion.26, f32[8,6,64,128]{3,2,1,0:T(8,128)S(1)} %get-tuple-element.58, f32[]{:T(128)} %bitcast.7, f32[]{:T(128)} %bitcast.6, ...), kind=kLoop, calls=%fused_computation.130 | loop fusion | flops 40108032 | bytes 9474684 | tf_op jit(solution)/shard_map/add | solution.py:305
  105.1 0.7 slice_maximum_fusion.3
  106.7 13.1 %multiply_add_fusion.1 = (f32[6,6,64,128]{3,2,1,0:T(8,128)S(1)}, f32[6,6,64,128]{3,2,1,0:T(8,128)S(1)}, f32[6,6,64,128]{3,2,1,0:T(8,128)S(1)}) fusion(f32[6,6,64,1]{3,2,1,0:T(8,128)S(1)} %get-tuple-element.57, f32[6,6,64,125]{3,2,1,0:T(8,128)S(1)} %slice.1007, f32[6,6,64,126]{3,2,1,0:T(8,128)S(1)} %get-tuple-element.55, f32[6,6,64,127]{3,2,1,0:T(8,128)S(1)} %fusion.15, ...), kind=kLoop, calls=%fused_computation.104 | loop fusion | flops 80805888 | bytes 16450572 | tf_op jit(solution)/shard_map/add | solution.py:188
  120.1 1.3 collective-permute-start.9
  121.4 1.5 collective-permute-start.11
  123.4 24.1 %collective-permute-done.9 = f32[3,6,64,128]{3,2,1,0:T(8,128)S(1)} collective-permute-done((f32[3,6,64,128]{3,2,1,0:T(8,128)S(1)}, f32[3,6,64,128]{3,2,1,0:T(8,128)S(1)}, u32[]{:S(2)}, u32[]{:S(2)}) %collective-permute-start.9) | collective-permute-done | bytes 589856 | tf_op jit(solution)/shard_map/ppermute | solution.py:113
  148.0 0.5 pad_maximum_fusion.3
  149.1 7.4 %fusion.51 = f32[3,6,64,128]{3,2,1,0:T(8,128)S(1)} fusion(f32[3,6,64,128]{3,2,1,0:T(8,128)S(1)} %multiply_add_fusion.3, f32[6,6,64,128]{3,2,1,0:T(8,128)S(1)} %get-tuple-element.20, f32[6,6,64,128]{3,2,1,0:T(8,128)S(1)} %add_multiply_fusion.1, f32[3,11,64,128]{3,2,1,0:T(8,128)S(1)} %fusion.23, f32[8,6,64,128]{3,2,1,0:T(8,128)S(1)} %fusion.8, ...), kind=kLoop, calls=%fused_computation.149 | loop fusion | flops 40550400 | bytes 10064508 | tf_op jit(solution)/shard_map/add | solution.py:309
  156.6 7.4 %fusion.40 = f32[3,6,64,128]{3,2,1,0:T(8,128)S(1)} fusion(f32[3,6,64,128]{3,2,1,0:T(8,128)S(1)} %fusion.32, f32[6,6,64,128]{3,2,1,0:T(8,128)S(1)} %get-tuple-element.20, f32[6,6,64,128]{3,2,1,0:T(8,128)S(1)} %add_multiply_fusion.1, f32[3,11,64,128]{3,2,1,0:T(8,128)S(1)} %fusion.24, f32[8,6,64,128]{3,2,1,0:T(8,128)S(1)} %fusion.9, f32[]{:T(128)} %bitcast.7, ...), kind=kLoop, calls=%fused_computation.138 | loop fusion | flops 40550400 | bytes 10064508 | tf_op jit(solution)/shard_map/add | solution.py:309
  165.1 0.7 slice_maximum_fusion.1
  166.7 13.1 %multiply_add_fusion = (f32[6,6,64,128]{3,2,1,0:T(8,128)S(1)}, f32[6,6,64,128]{3,2,1,0:T(8,128)S(1)}, f32[6,6,64,128]{3,2,1,0:T(8,128)S(1)}) fusion(f32[6,6,64,1]{3,2,1,0:T(8,128)S(1)} %get-tuple-element.49, f32[6,6,64,125]{3,2,1,0:T(8,128)S(1)} %slice.1086, f32[6,6,64,126]{3,2,1,0:T(8,128)S(1)} %get-tuple-element.47, f32[6,6,64,127]{3,2,1,0:T(8,128)S(1)} %fusion.18, ...), kind=kLoop, calls=%fused_computation.100 | loop fusion | flops 80805888 | bytes 16450572 | tf_op jit(solution)/shard_map/add | solution.py:188
  180.1 1.3 collective-permute-start.13
  181.4 5.3 %collective-permute-start.12 = (f32[3,6,64,128]{3,2,1,0:T(8,128)S(1)}, f32[3,6,64,128]{3,2,1,0:T(8,128)S(1)}, u32[]{:S(2)}, u32[]{:S(2)}) collective-permute-start(f32[3,6,64,128]{3,2,1,0:T(8,128)S(1)} %fusion.51), channel_id=1, source_target_pairs={{0,2},{2,4},{4,6},{6,8},{8,10},{10,12},{12,14},{1,3},{3,5},{5,7},{... | collective-permute-start | bytes 1769480 | tf_op jit(solution)/shard_map/ppermute | solution.py:113
  187.3 11.1 %collective-permute-done.13 = f32[3,6,64,128]{3,2,1,0:T(8,128)S(1)} collective-permute-done((f32[3,6,64,128]{3,2,1,0:T(8,128)S(1)}, f32[3,6,64,128]{3,2,1,0:T(8,128)S(1)}, u32[]{:S(2)}, u32[]{:S(2)}) %collective-permute-start.13) | collective-permute-done | bytes 589856 | tf_op jit(solution)/shard_map/ppermute | solution.py:118
  199.0 12.2 %collective-permute-done.12 = f32[3,6,64,128]{3,2,1,0:T(8,128)S(1)} collective-permute-done((f32[3,6,64,128]{3,2,1,0:T(8,128)S(1)}, f32[3,6,64,128]{3,2,1,0:T(8,128)S(1)}, u32[]{:S(2)}, u32[]{:S(2)}) %collective-permute-start.12) | collective-permute-done | bytes 589856 | tf_op jit(solution)/shard_map/ppermute | solution.py:113
  212.3 14.1 %fusion.22 = f32[6,6,64,128]{3,2,1,0:T(8,128)} fusion(f32[3,6,64,128]{3,2,1,0:T(8,128)S(1)} %fusion.51, f32[3,6,64,128]{3,2,1,0:T(8,128)S(1)} %fusion.40, f32[6,6,64,128]{3,2,1,0:T(8,128)S(1)} %get-tuple-element.22, f32[6,6,64,128]{3,2,1,0:T(8,128)S(1)} %add_multiply_fusion, f32[6,11,64,128]{3,2,1,0:T(8,128)S(1)} %fusion, f32[11,6,64,128]{3,2,1,0:T(8,128)S(1)} %fusion.1, ...), kind=kLoop, calls=%fused_computation.73 | loop fusion | flops 81395712 | bytes 20096208 | tf_op jit(solution)/shard_map/add | solution.py:314
  (120 shorter events, 12.0 us)
Async XLA Ops:
  0.0 21.5 %copy-start = (f32[6,6,64,128]{3,2,1,0:T(8,128)S(1)}, f32[6,6,64,128]{3,2,1,0:T(8,128)}, u32[]{:S(2)}) copy-start(f32[6,6,64,128]{3,2,1,0:T(8,128)} %param.3) | copy-start | bytes 3538948
  13.8 45.9 %collective-permute-start.2 = (f32[2]{0:T(128)}, f32[2]{0:T(128)}, u32[]{:S(2)}, u32[]{:S(2)}) collective-permute-start(f32[2]{0:T(128)} %pad_maximum_fusion.24), channel_id=1, source_target_pairs={{0,3},{1,4},{2,5},{3,6},{4,7},{5,8},{6,9},{7,10},{8,11},{9,12},{10... | collective-permute-start | bytes 32 | tf_op jit(solution)/shard_map/ppermute | solution.py:147
  16.2 44.7 %collective-permute-start.1 = (f32[2]{0:T(128)}, f32[2]{0:T(128)}, u32[]{:S(2)}, u32[]{:S(2)}) collective-permute-start(f32[2]{0:T(128)} %pad_maximum_fusion.24), channel_id=1, source_target_pairs={{0,2},{1,3},{2,4},{3,5},{4,6},{5,7},{6,8},{7,9},{8,10},{9,11},{10,... | collective-permute-start | bytes 32 | tf_op jit(solution)/shard_map/ppermute | solution.py:147
  17.8 43.2 %collective-permute-start = (f32[2]{0:T(128)}, f32[2]{0:T(128)}, u32[]{:S(2)}, u32[]{:S(2)}) collective-permute-start(f32[2]{0:T(128)} %pad_maximum_fusion.24), channel_id=1, source_target_pairs={{0,1},{1,2},{2,3},{3,4},{4,5},{5,6},{6,7},{7,8},{8,9},{9,10},{10,1... | collective-permute-start | bytes 32 | tf_op jit(solution)/shard_map/ppermute | solution.py:147
  20.4 63.6 %collective-permute-start.7 = (f32[6,3,64,128]{3,2,1,0:T(8,128)}, f32[6,3,64,128]{3,2,1,0:T(8,128)}, u32[]{:S(2)}, u32[]{:S(2)}) collective-permute-start(f32[6,3,64,128]{3,2,1,0:T(8,128)} %slice_select_fusion), channel_id=1, source_target_pairs={{0,1},{1,0},{2,3},{3,2},{4,5},{5,4},{6,7},{7,6},{8,9},{9,8},{10,11... | collective-permute-start | bytes 1769480 | tf_op jit(solution)/shard_map/ppermute | solution.py:198
  22.7 66.9 %collective-permute-start.6 = (f32[3,6,64,128]{3,2,1,0:T(8,128)}, f32[3,6,64,128]{3,2,1,0:T(8,128)}, u32[]{:S(2)}, u32[]{:S(2)}) collective-permute-start(f32[3,6,64,128]{3,2,1,0:T(8,128)} %get-tuple-element.73), channel_id=1, source_target_pairs={{0,2},{2,4},{4,6},{6,8},{8,10},{10,12},{12,14},{1,3},{3,5},{5,7},{... | collective-permute-start | bytes 1769480 | tf_op jit(solution)/shard_map/ppermute | solution.py:113
  36.6 1.6 copy-start.15
  39.3 1.6 copy-start.5
  39.3 1.6 copy-start.6
  39.4 0.7 copy-start.22
  39.4 1.9 copy-start.2
  39.4 2.2 copy-start.3
  39.4 2.6 %copy-start.4 = (f32[6,6,64,1]{3,2,1,0:T(8,128)S(1)}, f32[6,6,64,1]{3,2,1,0:T(8,128)}, u32[]{:S(2)}) copy-start(f32[6,6,64,1]{3,2,1,0:T(8,128)} %get-tuple-element.79) | copy-start | bytes 27652
  55.7 0.8 copy-start.25
  55.8 3.3 %copy-start.21 = (f32[1,3,6]{2,0,1:T(1,128)S(1)}, f32[1,3,6]{2,0,1:T(1,128)}, u32[]{:S(2)}) copy-start(f32[1,3,6]{2,0,1:T(1,128)} %get-tuple-element.110) | copy-start | bytes 220
  55.8 3.9 %copy-start.7 = (f32[3,6,64,128]{3,2,1,0:T(8,128)S(1)}, f32[3,6,64,128]{3,2,1,0:T(8,128)}, u32[]{:S(2)}) copy-start(f32[3,6,64,128]{3,2,1,0:T(8,128)} %get-tuple-element.72) | copy-start | bytes 1769476
  59.7 30.1 %collective-permute-start.8 = (f32[3,6,64,128]{3,2,1,0:T(8,128)S(1)}, f32[3,6,64,128]{3,2,1,0:T(8,128)S(1)}, u32[]{:S(2)}, u32[]{:S(2)}) collective-permute-start(f32[3,6,64,128]{3,2,1,0:T(8,128)S(1)} %copy-done.7), channel_id=1, source_target_pairs={{2,0},{4,2},{6,4},{8,6},{10,8},{12,10},{14,12},{3,1},{5,3},{7,5},{... | collective-permute-start | bytes 1769480 | tf_op jit(solution)/shard_map/ppermute | solution.py:118
  62.9 13.7 %collective-permute-start.5 = (f32[2]{0:T(128)S(1)}, f32[2]{0:T(128)S(1)}, u32[]{:S(2)}, u32[]{:S(2)}) collective-permute-start(f32[2]{0:T(128)S(1)} %maximum_maximum_fusion.7), channel_id=1, source_target_pairs={{0,12},{1,13},{2,14},{3,15},{4,0},{5,1},{6,2},{7,3},{8,4},{9,5},{1... | collective-permute-start | bytes 32 | tf_op jit(solution)/shard_map/ppermute | solution.py:147
  66.4 11.9 %collective-permute-start.4 = (f32[2]{0:T(128)S(1)}, f32[2]{0:T(128)S(1)}, u32[]{:S(2)}, u32[]{:S(2)}) collective-permute-start(f32[2]{0:T(128)S(1)} %maximum_maximum_fusion.7), channel_id=1, source_target_pairs={{0,8},{1,9},{2,10},{3,11},{4,12},{5,13},{6,14},{7,15},{8,0},{9,1},... | collective-permute-start | bytes 32 | tf_op jit(solution)/shard_map/ppermute | solution.py:147
  76.7 5.4 %collective-permute-start.3 = (f32[2]{0:T(128)S(1)}, f32[2]{0:T(128)S(1)}, u32[]{:S(2)}, u32[]{:S(2)}) collective-permute-start(f32[2]{0:T(128)S(1)} %maximum_maximum_fusion.7), channel_id=1, source_target_pairs={{0,4},{1,5},{2,6},{3,7},{4,8},{5,9},{6,10},{7,11},{8,12},{9,13},{1... | collective-permute-start | bytes 32 | tf_op jit(solution)/shard_map/ppermute | solution.py:147
  87.0 2.6 %copy-start.11 = (f32[6,64,128]{2,1,0:T(8,128)S(1)}, f32[6,64,128]{2,1,0:T(8,128)}, u32[]{:S(2)}) copy-start(f32[6,64,128]{2,1,0:T(8,128)} %get-tuple-element.60) | copy-start | bytes 589828
  87.0 2.6 %copy-start.12 = (f32[6,64,128]{2,1,0:T(8,128)S(1)}, f32[6,64,128]{2,1,0:T(8,128)}, u32[]{:S(2)}) copy-start(f32[6,64,128]{2,1,0:T(8,128)} %get-tuple-element.63) | copy-start | bytes 589828
  89.6 0.9 copy-start.9
  89.6 1.0 copy-start.10
  89.6 1.0 copy-start.16
  91.2 2.6 %copy-start.1 = (f32[6,6,64,128]{3,2,1,0:T(8,128)S(1)}, f32[6,6,64,128]{3,2,1,0:T(8,128)}, u32[]{:S(2)}) copy-start(f32[6,6,64,128]{3,2,1,0:T(8,128)} %get-tuple-element.15) | copy-start | bytes 3538948
  91.2 2.6 %copy-start.8 = (f32[64,128]{1,0:T(8,128)S(1)}, f32[64,128]{1,0:T(8,128)}, u32[]{:S(2)}) copy-start(f32[64,128]{1,0:T(8,128)} %get-tuple-element.116) | copy-start | bytes 98308
  91.2 2.6 %copy-start.13 = (f32[3,6,64]{2,1,0:T(8,128)S(1)}, f32[3,6,64]{2,1,0:T(8,128)}, u32[]{:S(2)}) copy-start(f32[3,6,64]{2,1,0:T(8,128)} %get-tuple-element.118) | copy-start | bytes 13828
  91.2 2.6 %copy-start.17 = (f32[6]{0:T(128)S(1)}, f32[6]{0:T(128)}, u32[]{:S(2)}) copy-start(f32[6]{0:T(128)} %get-tuple-element.136) | copy-start | bytes 76
  91.2 2.6 %copy-start.18 = (f32[3,6]{1,0:T(4,128)S(1)}, f32[3,6]{1,0:T(4,128)}, u32[]{:S(2)}) copy-start(f32[3,6]{1,0:T(4,128)} %get-tuple-element.140) | copy-start | bytes 220
  91.2 2.6 %copy-start.24 = (f32[3]{0:T(128)S(1)}, f32[3]{0:T(128)}, u32[]{:S(2)}) copy-start(f32[3]{0:T(128)} %get-tuple-element.120) | copy-start | bytes 40
  95.1 1.5 copy-start.19
  95.1 1.5 copy-start.23
  106.7 16.4 %collective-permute-start.10 = (f32[6,3,64,128]{3,2,1,0:T(8,128)S(1)}, f32[6,3,64,128]{3,2,1,0:T(8,128)S(1)}, u32[]{:S(2)}, u32[]{:S(2)}) collective-permute-start(f32[6,3,64,128]{3,2,1,0:T(8,128)S(1)} %fusion.53), channel_id=1, source_target_pairs={{0,1},{1,0},{2,3},{3,2},{4,5},{5,4},{6,7},{7,6},{8,9},{9,8},{10,11... | collective-permute-start | bytes 1769480 | tf_op jit(solution)/shard_map/ppermute | solution.py:198
  120.1 27.4 %collective-permute-start.9 = (f32[3,6,64,128]{3,2,1,0:T(8,128)S(1)}, f32[3,6,64,128]{3,2,1,0:T(8,128)S(1)}, u32[]{:S(2)}, u32[]{:S(2)}) collective-permute-start(f32[3,6,64,128]{3,2,1,0:T(8,128)S(1)} %multiply_add_fusion.3), channel_id=1, source_target_pairs={{0,2},{2,4},{4,6},{6,8},{8,10},{10,12},{12,14},{1,3},{3,5},{5,7},{... | collective-permute-start | bytes 1769480 | tf_op jit(solution)/shard_map/ppermute | solution.py:113
  121.4 26.4 %collective-permute-start.11 = (f32[3,6,64,128]{3,2,1,0:T(8,128)S(1)}, f32[3,6,64,128]{3,2,1,0:T(8,128)S(1)}, u32[]{:S(2)}, u32[]{:S(2)}) collective-permute-start(f32[3,6,64,128]{3,2,1,0:T(8,128)S(1)} %fusion.32), channel_id=1, source_target_pairs={{2,0},{4,2},{6,4},{8,6},{10,8},{12,10},{14,12},{3,1},{5,3},{7,5},{... | collective-permute-start | bytes 1769480 | tf_op jit(solution)/shard_map/ppermute | solution.py:118
  180.0 6.8 %collective-permute-start.14 = (f32[6,3,64,128]{3,2,1,0:T(8,128)S(1)}, f32[6,3,64,128]{3,2,1,0:T(8,128)S(1)}, u32[]{:S(2)}, u32[]{:S(2)}) collective-permute-start(f32[6,3,64,128]{3,2,1,0:T(8,128)S(1)} %fusion.56), channel_id=1, source_target_pairs={{0,1},{1,0},{2,3},{3,2},{4,5},{5,4},{6,7},{7,6},{8,9},{9,8},{10,11... | collective-permute-start | bytes 1769480 | tf_op jit(solution)/shard_map/ppermute | solution.py:198
  180.1 18.4 %collective-permute-start.13 = (f32[3,6,64,128]{3,2,1,0:T(8,128)S(1)}, f32[3,6,64,128]{3,2,1,0:T(8,128)S(1)}, u32[]{:S(2)}, u32[]{:S(2)}) collective-permute-start(f32[3,6,64,128]{3,2,1,0:T(8,128)S(1)} %fusion.40), channel_id=1, source_target_pairs={{2,0},{4,2},{6,4},{8,6},{10,8},{12,10},{14,12},{3,1},{5,3},{7,5},{... | collective-permute-start | bytes 1769480 | tf_op jit(solution)/shard_map/ppermute | solution.py:118
  181.4 29.9 %collective-permute-start.12 = (f32[3,6,64,128]{3,2,1,0:T(8,128)S(1)}, f32[3,6,64,128]{3,2,1,0:T(8,128)S(1)}, u32[]{:S(2)}, u32[]{:S(2)}) collective-permute-start(f32[3,6,64,128]{3,2,1,0:T(8,128)S(1)} %fusion.51), channel_id=1, source_target_pairs={{0,2},{2,4},{4,6},{6,8},{8,10},{10,12},{12,14},{1,3},{3,5},{5,7},{... | collective-permute-start | bytes 1769480 | tf_op jit(solution)/shard_map/ppermute | solution.py:113
  211.6 0.7 copy-start.14
  211.6 0.7 copy-start.20
  211.6 0.7 copy-start.26

commit v2 on v1

--- a/solution.py
+++ b/solution.py
@@ -90,22 +90,6 @@
         return differences
 
     return both_sides(window)
-
-
-def speed_bounds(drift_field, x_coord, y_coord, turn_a, along_one, along_two):
-    first_hi = jnp.max(along_one)
-    first_lo = jnp.min(along_one)
-    second_hi = jnp.max(along_two)
-    second_lo = jnp.min(along_two)
-    bound_one = jnp.max(
-        jnp.maximum(drift_field[0] + first_hi, -(drift_field[0] + first_lo))
-        + turn_a * jnp.abs(y_coord)[None, :]
-    )
-    bound_two = jnp.max(
-        jnp.maximum(drift_field[1] + second_hi, -(drift_field[1] + second_lo))
-        + turn_a * jnp.abs(x_coord)[:, None]
-    )
-    return (bound_one, bound_two)
 
 
 def send_low(piece, axis):
@@ -215,7 +199,18 @@
     x_coord = (
         (place_x * cells_x + jnp.arange(cells_x)).astype(jnp.float32) + 0.5 - 0.5 * total_x
     ) * cell_span
-    local_one, local_two = speed_bounds(drift, x_coord, y_coord, params[1], along_one, along_two)
+    turn_speed = params[0] * jnp.cos(psi_grid)
+    side_speed = params[0] * jnp.sin(psi_grid)
+    first_hi = jnp.max(turn_speed) - speed_grid[0]
+    first_lo = jnp.min(turn_speed) - speed_grid[n_speed - 1]
+    local_one = jnp.max(
+        jnp.maximum(drift[0] + first_hi, -(drift[0] + first_lo))
+        + params[1] * jnp.abs(y_coord)[None, :]
+    )
+    local_two = jnp.max(
+        jnp.maximum(drift[1] + jnp.max(side_speed), -(drift[1] + jnp.min(side_speed)))
+        + params[1] * jnp.abs(x_coord)[:, None]
+    )
     locals_now = local_whole(values)
     bounds = spread_max(jnp.stack([local_one, local_two]), ("gx", "gy"))
     bound_one = bounds[0]

time: 227 us -> 229 us (level)
  between operations: 4.69 us -> 7.07 us
    mul x3 -> x4, other arithmetic: 3.47 us -> 4.8 us  [the longest x1 1.79 us: on_device(): side_speed = params[0] * jnp.sin(psi_grid)]
  transfers between devices with their start and end apart: 15 -> 15, of which waited for: 5 -> 5; matrix products, arithmetic and copies ran while one was open for 24% -> 23% of each run, Pallas kernels for 0% -> 0%
where the time goes in v2:
time: 229 us; the launch traced here: 227 us
  other arithmetic  120 us (52%)
  waiting for transfers between devices  60.7 us (27%)
  starting transfers between devices  26.5 us (12%)
  local copies, waits for them, and re-layouts  13.6 us (6%)
  between operations  7.07 us (3%)
    add x3, other arithmetic, local_part(): partial + 0.5 * (alpha_three * (fore_three - back_three) + alpha_four * (...  40.1 us
    ppermute x3, waiting for transfers between devices, send_low(): lax.ppermute(piece, axis, [(i, (i + 1) % count) for i in range(count - 1)])  36.4 us
    add x2, other arithmetic, on_device(): 0.75 * cut(values, side) + 0.25 * (cut(first, side) + step_time * rate)  14.8 us
    add x1, other arithmetic, on_device(): cut(values, side) * (1.0 / 3.0)  14.1 us
    ppermute x6, waiting for transfers between devices, spread_max(): lax.ppermute(local, axes, [(i, (i + k * span) % count) for i in range(cou...  13.3 us
    ppermute x3, waiting for transfers between devices, send_high(): lax.ppermute(piece, axis, [((i + 1) % count, i) for i in range(count - 1)])  11 us
    ppermute x3, starting transfers between devices, send_low(): lax.ppermute(piece, axis, [(i, (i + 1) % count) for i in range(count - 1)])  10.9 us
    ppermute x6, starting transfers between devices, spread_max(): lax.ppermute(local, axes, [(i, (i + k * span) % count) for i in range(cou...  10.2 us
  transfers between devices with their start and end apart: 15, of which 5 were waited for; matrix products, arithmetic and copies ran while one was open for 23% of the time, Pallas kernels for 0%

profile of v2, /device:TPU:0, one launch (start us, length us, event | category | flops | bytes accessed | tf_op | source)
XLA Modules:
  0.0 227.5 jit_solution(3260310484102746316)
XLA Ops:
  0.0 1.5 fusion.99
  1.5 1.8 sine_multiply_fusion
  3.3 1.3 fusion.82
  4.5 1.3 fusion.85
  5.8 1.2 abs_multiply_fusion
  7.0 1.1 abs_multiply_fusion.1
  8.2 0.8 fusion.96
  8.9 0.6 fusion.98
  12.1 1.8 add_reduce_fusion
  14.0 0.6 add_reduce_fusion.1
  14.6 1.7 pad_maximum_fusion.24
  16.2 2.4 %collective-permute-start.2 = (f32[2]{0:T(128)}, f32[2]{0:T(128)}, u32[]{:S(2)}, u32[]{:S(2)}) collective-permute-start(f32[2]{0:T(128)} %pad_maximum_fusion.24), channel_id=1, source_target_pairs={{0,3},{1,4},{2,5},{3,6},{4,7},{5,8},{6,9},{7,10},{8,11},{9,12},{10... | collective-permute-start | bytes 32 | tf_op jit(solution)/shard_map/ppermute | solution.py:131
  18.7 1.5 collective-permute-start.1
  20.2 0.5 collective-permute-start
  20.6 2.1 slice_select_fusion
  22.8 1.2 collective-permute-start.7
  24.0 1.2 fusion.92
  25.2 4.2 %collective-permute-start.6 = (f32[3,6,64,128]{3,2,1,0:T(8,128)}, f32[3,6,64,128]{3,2,1,0:T(8,128)}, u32[]{:S(2)}, u32[]{:S(2)}) collective-permute-start(f32[3,6,64,128]{3,2,1,0:T(8,128)} %get-tuple-element.71), channel_id=1, source_target_pairs={{0,2},{2,4},{4,6},{6,8},{8,10},{10,12},{12,14},{1,3},{3,5},{5,7},{... | collective-permute-start | bytes 1769480 | tf_op jit(solution)/shard_map/ppermute | solution.py:97
  29.8 1.4 fusion.94
  31.2 1.4 slice.952
  32.7 2.1 slice_maximum_fusion.5
  34.7 1.4 slice_maximum_fusion.4
  37.9 0.9 slice_bitcast_fusion.13
  38.8 1.0 slice_bitcast_fusion.5
  39.8 0.5 fusion.95
  40.4 0.7 cosine_multiply_fusion
  41.0 0.6 copy_bitcast_fusion
  42.0 0.6 copy-done.21
  42.6 0.6 slice_multiply_fusion.1
  44.4 13.8 %multiply_add_fusion.2 = (f32[6,6,64,128]{3,2,1,0:T(8,128)}, f32[6,6,64,128]{3,2,1,0:T(8,128)S(1)}, f32[6,6,64,128]{3,2,1,0:T(8,128)S(1)}) fusion(f32[6,6,64,1]{3,2,1,0:T(8,128)S(1)} %copy-done.4, f32[6,6,64,125]{3,2,1,0:T(8,128)S(1)} %copy-done.3, f32[6,6,64,126]{3,2,1,0:T(8,128)S(1)} %copy-done.6, f32[6,6,64,127]{3,2,1,0:T(8,128)S(1)} %subtract_multiply_fusion, ...), kind=kLoop, calls=%fused_computation.108 | loop fusion | flops 80805888 | bytes 16450572 | tf_op jit(solution)/shard_map/add | solution.py:172
  59.8 1.3 collective-permute-start.8
  61.1 1.9 maximum_maximum_fusion.7
  63.0 3.5 %collective-permute-start.5 = (f32[2]{0:T(128)S(1)}, f32[2]{0:T(128)S(1)}, u32[]{:S(2)}, u32[]{:S(2)}) collective-permute-start(f32[2]{0:T(128)S(1)} %maximum_maximum_fusion.7), channel_id=1, source_target_pairs={{0,12},{1,13},{2,14},{3,15},{4,0},{5,1},{6,2},{7,3},{8,4},{9,5},{1... | collective-permute-start | bytes 32 | tf_op jit(solution)/shard_map/ppermute | solution.py:131
  66.4 0.8 collective-permute-start.4
  67.2 9.6 %collective-permute-done.5 = f32[2]{0:T(128)S(1)} collective-permute-done((f32[2]{0:T(128)S(1)}, f32[2]{0:T(128)S(1)}, u32[]{:S(2)}, u32[]{:S(2)}) %collective-permute-start.5) | collective-permute-done | bytes 40 | tf_op jit(solution)/shard_map/ppermute | solution.py:131
  76.8 1.6 collective-permute-start.3
  78.4 3.8 %collective-permute-done.3 = f32[2]{0:T(128)S(1)} collective-permute-done((f32[2]{0:T(128)S(1)}, f32[2]{0:T(128)S(1)}, u32[]{:S(2)}, u32[]{:S(2)}) %collective-permute-start.3) | collective-permute-done | bytes 40 | tf_op jit(solution)/shard_map/ppermute | solution.py:131
  82.2 0.6 fusion.97
  84.1 1.4 add_select_fusion.15
  85.5 1.3 pad_maximum_fusion.11
  86.9 2.6 %fusion.88 = (f32[3,6,64,128]{3,2,1,0:T(8,128)S(1)}, f32[3,6,64,128]{3,2,1,0:T(8,128)S(1)}, f32[3,6,64,128]{3,2,1,0:T(8,128)S(1)}) fusion(f32[3,11,64,128]{3,2,1,0:T(8,128)S(1)} %fusion.25), kind=kLoop, calls=%fused_computation.263 | loop fusion | flops 18432000 | bytes 5308416 | tf_op jit(solution)/shard_map/sub | solution.py:267
  89.7 0.7 copy-done.8
  90.5 1.2 add_select_fusion.5
  91.7 0.5 fusion.7
  92.2 2.5 %fusion.89 = (f32[3,6,64,128]{3,2,1,0:T(8,128)S(1)}, f32[3,6,64,128]{3,2,1,0:T(8,128)S(1)}, f32[3,6,64,128]{3,2,1,0:T(8,128)S(1)}) fusion(f32[8,6,64,128]{3,2,1,0:T(8,128)S(1)} %get-tuple-element.57), kind=kLoop, calls=%fused_computation.264 | loop fusion | flops 18432000 | bytes 5308416 | tf_op jit(solution)/shard_map/sub | solution.py:267
  94.8 1.1 fusion.43
  96.1 1.4 multiply_add_fusion.3
  97.5 7.3 %fusion.32 = f32[3,6,64,128]{3,2,1,0:T(8,128)S(1)} fusion(f32[6,6,64,128]{3,2,1,0:T(8,128)S(1)} %copy-done.1, f32[6,6,64,128]{3,2,1,0:T(8,128)S(1)} %add_multiply_fusion.2, f32[3,11,64,128]{3,2,1,0:T(8,128)S(1)} %fusion.26, f32[8,6,64,128]{3,2,1,0:T(8,128)S(1)} %get-tuple-element.56, f32[]{:T(128)} %bitcast.9, f32[]{:T(128)} %bitcast.8, ...), kind=kLoop, calls=%fused_computation.130 | loop fusion | flops 40108032 | bytes 9474684 | tf_op jit(solution)/shard_map/add | solution.py:300
  106.0 0.7 slice_maximum_fusion.3
  107.6 13.1 %multiply_add_fusion.1 = (f32[6,6,64,128]{3,2,1,0:T(8,128)S(1)}, f32[6,6,64,128]{3,2,1,0:T(8,128)S(1)}, f32[6,6,64,128]{3,2,1,0:T(8,128)S(1)}) fusion(f32[6,6,64,1]{3,2,1,0:T(8,128)S(1)} %get-tuple-element.55, f32[6,6,64,125]{3,2,1,0:T(8,128)S(1)} %slice.1018, f32[6,6,64,126]{3,2,1,0:T(8,128)S(1)} %get-tuple-element.53, f32[6,6,64,127]{3,2,1,0:T(8,128)S(1)} %fusion.15, ...), kind=kLoop, calls=%fused_computation.104 | loop fusion | flops 80805888 | bytes 16450572 | tf_op jit(solution)/shard_map/add | solution.py:172
  121.1 1.3 collective-permute-start.9
  122.4 1.5 collective-permute-start.11
  124.4 24.1 %collective-permute-done.9 = f32[3,6,64,128]{3,2,1,0:T(8,128)S(1)} collective-permute-done((f32[3,6,64,128]{3,2,1,0:T(8,128)S(1)}, f32[3,6,64,128]{3,2,1,0:T(8,128)S(1)}, u32[]{:S(2)}, u32[]{:S(2)}) %collective-permute-start.9) | collective-permute-done | bytes 589856 | tf_op jit(solution)/shard_map/ppermute | solution.py:97
  149.0 0.5 pad_maximum_fusion.3
  150.1 7.4 %fusion.51 = f32[3,6,64,128]{3,2,1,0:T(8,128)S(1)} fusion(f32[3,6,64,128]{3,2,1,0:T(8,128)S(1)} %multiply_add_fusion.3, f32[6,6,64,128]{3,2,1,0:T(8,128)S(1)} %get-tuple-element.20, f32[6,6,64,128]{3,2,1,0:T(8,128)S(1)} %add_multiply_fusion.1, f32[3,11,64,128]{3,2,1,0:T(8,128)S(1)} %fusion.23, f32[8,6,64,128]{3,2,1,0:T(8,128)S(1)} %fusion.8, ...), kind=kLoop, calls=%fused_computation.149 | loop fusion | flops 40550400 | bytes 10064508 | tf_op jit(solution)/shard_map/add | solution.py:304
  157.5 7.4 %fusion.40 = f32[3,6,64,128]{3,2,1,0:T(8,128)S(1)} fusion(f32[3,6,64,128]{3,2,1,0:T(8,128)S(1)} %fusion.32, f32[6,6,64,128]{3,2,1,0:T(8,128)S(1)} %get-tuple-element.20, f32[6,6,64,128]{3,2,1,0:T(8,128)S(1)} %add_multiply_fusion.1, f32[3,11,64,128]{3,2,1,0:T(8,128)S(1)} %fusion.24, f32[8,6,64,128]{3,2,1,0:T(8,128)S(1)} %fusion.9, f32[]{:T(128)} %bitcast.9, ...), kind=kLoop, calls=%fused_computation.138 | loop fusion | flops 40550400 | bytes 10064508 | tf_op jit(solution)/shard_map/add | solution.py:304
  166.1 0.7 slice_maximum_fusion.1
  167.6 13.2 %multiply_add_fusion = (f32[6,6,64,128]{3,2,1,0:T(8,128)S(1)}, f32[6,6,64,128]{3,2,1,0:T(8,128)S(1)}, f32[6,6,64,128]{3,2,1,0:T(8,128)S(1)}) fusion(f32[6,6,64,1]{3,2,1,0:T(8,128)S(1)} %get-tuple-element.47, f32[6,6,64,125]{3,2,1,0:T(8,128)S(1)} %slice.1097, f32[6,6,64,126]{3,2,1,0:T(8,128)S(1)} %get-tuple-element.45, f32[6,6,64,127]{3,2,1,0:T(8,128)S(1)} %fusion.18, ...), kind=kLoop, calls=%fused_computation.100 | loop fusion | flops 80805888 | bytes 16450572 | tf_op jit(solution)/shard_map/add | solution.py:172
  181.1 1.3 collective-permute-start.13
  182.4 5.3 %collective-permute-start.12 = (f32[3,6,64,128]{3,2,1,0:T(8,128)S(1)}, f32[3,6,64,128]{3,2,1,0:T(8,128)S(1)}, u32[]{:S(2)}, u32[]{:S(2)}) collective-permute-start(f32[3,6,64,128]{3,2,1,0:T(8,128)S(1)} %fusion.51), channel_id=1, source_target_pairs={{0,2},{2,4},{4,6},{6,8},{8,10},{10,12},{12,14},{1,3},{3,5},{5,7},{... | collective-permute-start | bytes 1769480 | tf_op jit(solution)/shard_map/ppermute | solution.py:97
  188.5 11.0 %collective-permute-done.13 = f32[3,6,64,128]{3,2,1,0:T(8,128)S(1)} collective-permute-done((f32[3,6,64,128]{3,2,1,0:T(8,128)S(1)}, f32[3,6,64,128]{3,2,1,0:T(8,128)S(1)}, u32[]{:S(2)}, u32[]{:S(2)}) %collective-permute-start.13) | collective-permute-done | bytes 589856 | tf_op jit(solution)/shard_map/ppermute | solution.py:102
  199.6 0.4 fusion
  200.1 12.2 %collective-permute-done.12 = f32[3,6,64,128]{3,2,1,0:T(8,128)S(1)} collective-permute-done((f32[3,6,64,128]{3,2,1,0:T(8,128)S(1)}, f32[3,6,64,128]{3,2,1,0:T(8,128)S(1)}, u32[]{:S(2)}, u32[]{:S(2)}) %collective-permute-start.12) | collective-permute-done | bytes 589856 | tf_op jit(solution)/shard_map/ppermute | solution.py:97
  213.4 14.1 %fusion.22 = f32[6,6,64,128]{3,2,1,0:T(8,128)} fusion(f32[3,6,64,128]{3,2,1,0:T(8,128)S(1)} %fusion.51, f32[3,6,64,128]{3,2,1,0:T(8,128)S(1)} %fusion.40, f32[6,6,64,128]{3,2,1,0:T(8,128)S(1)} %get-tuple-element.22, f32[6,6,64,128]{3,2,1,0:T(8,128)S(1)} %add_multiply_fusion, f32[6,11,64,128]{3,2,1,0:T(8,128)S(1)} %fusion, f32[11,6,64,128]{3,2,1,0:T(8,128)S(1)} %fusion.1, ...), kind=kLoop, calls=%fused_computation.73 | loop fusion | flops 81395712 | bytes 20096208 | tf_op jit(solution)/shard_map/add | solution.py:309
  (118 shorter events, 11.3 us)
Async XLA Ops:
  0.0 24.0 %copy-start = (f32[6,6,64,128]{3,2,1,0:T(8,128)S(1)}, f32[6,6,64,128]{3,2,1,0:T(8,128)}, u32[]{:S(2)}) copy-start(f32[6,6,64,128]{3,2,1,0:T(8,128)} %param.3) | copy-start | bytes 3538948
  16.2 43.5 %collective-permute-start.2 = (f32[2]{0:T(128)}, f32[2]{0:T(128)}, u32[]{:S(2)}, u32[]{:S(2)}) collective-permute-start(f32[2]{0:T(128)} %pad_maximum_fusion.24), channel_id=1, source_target_pairs={{0,3},{1,4},{2,5},{3,6},{4,7},{5,8},{6,9},{7,10},{8,11},{9,12},{10... | collective-permute-start | bytes 32 | tf_op jit(solution)/shard_map/ppermute | solution.py:131
  18.7 42.4 %collective-permute-start.1 = (f32[2]{0:T(128)}, f32[2]{0:T(128)}, u32[]{:S(2)}, u32[]{:S(2)}) collective-permute-start(f32[2]{0:T(128)} %pad_maximum_fusion.24), channel_id=1, source_target_pairs={{0,2},{1,3},{2,4},{3,5},{4,6},{5,7},{6,8},{7,9},{8,10},{9,11},{10,... | collective-permute-start | bytes 32 | tf_op jit(solution)/shard_map/ppermute | solution.py:131
  20.2 40.9 %collective-permute-start = (f32[2]{0:T(128)}, f32[2]{0:T(128)}, u32[]{:S(2)}, u32[]{:S(2)}) collective-permute-start(f32[2]{0:T(128)} %pad_maximum_fusion.24), channel_id=1, source_target_pairs={{0,1},{1,2},{2,3},{3,4},{4,5},{5,6},{6,7},{7,8},{8,9},{9,10},{10,1... | collective-permute-start | bytes 32 | tf_op jit(solution)/shard_map/ppermute | solution.py:131
  22.8 61.2 %collective-permute-start.7 = (f32[6,3,64,128]{3,2,1,0:T(8,128)}, f32[6,3,64,128]{3,2,1,0:T(8,128)}, u32[]{:S(2)}, u32[]{:S(2)}) collective-permute-start(f32[6,3,64,128]{3,2,1,0:T(8,128)} %slice_select_fusion), channel_id=1, source_target_pairs={{0,1},{1,0},{2,3},{3,2},{4,5},{5,4},{6,7},{7,6},{8,9},{9,8},{10,11... | collective-permute-start | bytes 1769480 | tf_op jit(solution)/shard_map/ppermute | solution.py:182
  25.2 64.3 %collective-permute-start.6 = (f32[3,6,64,128]{3,2,1,0:T(8,128)}, f32[3,6,64,128]{3,2,1,0:T(8,128)}, u32[]{:S(2)}, u32[]{:S(2)}) collective-permute-start(f32[3,6,64,128]{3,2,1,0:T(8,128)} %get-tuple-element.71), channel_id=1, source_target_pairs={{0,2},{2,4},{4,6},{6,8},{8,10},{10,12},{12,14},{1,3},{3,5},{5,7},{... | collective-permute-start | bytes 1769480 | tf_op jit(solution)/shard_map/ppermute | solution.py:97
  38.8 1.0 copy-start.17
  41.6 1.6 copy-start.5
  41.6 1.6 copy-start.6
  41.8 0.8 copy-start.21
  41.8 1.9 copy-start.2
  41.8 2.2 copy-start.3
  41.8 2.6 %copy-start.4 = (f32[6,6,64,1]{3,2,1,0:T(8,128)S(1)}, f32[6,6,64,1]{3,2,1,0:T(8,128)}, u32[]{:S(2)}) copy-start(f32[6,6,64,1]{3,2,1,0:T(8,128)} %get-tuple-element.77) | copy-start | bytes 27652
  58.2 0.6 copy-start.23
  58.2 1.6 copy-start.20
  58.2 1.6 copy-start.7
  58.2 25.8 %copy-start.12 = (f32[3,64,128]{2,1,0:T(8,128)S(1)}, f32[3,64,128]{2,1,0:T(8,128)}, u32[]{:S(2)}) copy-start(f32[3,64,128]{2,1,0:T(8,128)} %get-tuple-element.62) | copy-start | bytes 294916
  58.2 25.8 %copy-start.13 = (f32[3,64,128]{2,1,0:T(8,128)S(1)}, f32[3,64,128]{2,1,0:T(8,128)}, u32[]{:S(2)}) copy-start(f32[3,64,128]{2,1,0:T(8,128)} %get-tuple-element.63) | copy-start | bytes 294916
  58.2 25.8 %copy-start.14 = (f32[3,64,128]{2,1,0:T(8,128)S(1)}, f32[3,64,128]{2,1,0:T(8,128)}, u32[]{:S(2)}) copy-start(f32[3,64,128]{2,1,0:T(8,128)} %get-tuple-element.64) | copy-start | bytes 294916
  58.2 25.8 %copy-start.15 = (f32[3,64,128]{2,1,0:T(8,128)S(1)}, f32[3,64,128]{2,1,0:T(8,128)}, u32[]{:S(2)}) copy-start(f32[3,64,128]{2,1,0:T(8,128)} %get-tuple-element.65) | copy-start | bytes 294916
  58.2 25.8 %copy-start.16 = (f32[3,64,128]{2,1,0:T(8,128)S(1)}, f32[3,64,128]{2,1,0:T(8,128)}, u32[]{:S(2)}) copy-start(f32[3,64,128]{2,1,0:T(8,128)} %get-tuple-element.66) | copy-start | bytes 294916
  59.8 29.9 %collective-permute-start.8 = (f32[3,6,64,128]{3,2,1,0:T(8,128)S(1)}, f32[3,6,64,128]{3,2,1,0:T(8,128)}, u32[]{:S(2)}, u32[]{:S(2)}) collective-permute-start(f32[3,6,64,128]{3,2,1,0:T(8,128)S(1)} %copy-done.7), channel_id=1, source_target_pairs={{2,0},{4,2},{6,4},{8,6},{10,8},{12,10},{14,12},{3,1},{5,3},{7,5},{... | collective-permute-start | bytes 1769480 | tf_op jit(solution)/shard_map/ppermute | solution.py:102
  63.0 13.8 %collective-permute-start.5 = (f32[2]{0:T(128)S(1)}, f32[2]{0:T(128)S(1)}, u32[]{:S(2)}, u32[]{:S(2)}) collective-permute-start(f32[2]{0:T(128)S(1)} %maximum_maximum_fusion.7), channel_id=1, source_target_pairs={{0,12},{1,13},{2,14},{3,15},{4,0},{5,1},{6,2},{7,3},{8,4},{9,5},{1... | collective-permute-start | bytes 32 | tf_op jit(solution)/shard_map/ppermute | solution.py:131
  66.4 11.9 %collective-permute-start.4 = (f32[2]{0:T(128)S(1)}, f32[2]{0:T(128)S(1)}, u32[]{:S(2)}, u32[]{:S(2)}) collective-permute-start(f32[2]{0:T(128)S(1)} %maximum_maximum_fusion.7), channel_id=1, source_target_pairs={{0,8},{1,9},{2,10},{3,11},{4,12},{5,13},{6,14},{7,15},{8,0},{9,1},... | collective-permute-start | bytes 32 | tf_op jit(solution)/shard_map/ppermute | solution.py:131
  76.8 5.4 %collective-permute-start.3 = (f32[2]{0:T(128)S(1)}, f32[2]{0:T(128)S(1)}, u32[]{:S(2)}, u32[]{:S(2)}) collective-permute-start(f32[2]{0:T(128)S(1)} %maximum_maximum_fusion.7), channel_id=1, source_target_pairs={{0,4},{1,5},{2,6},{3,7},{4,8},{5,9},{6,10},{7,11},{8,12},{9,13},{1... | collective-permute-start | bytes 32 | tf_op jit(solution)/shard_map/ppermute | solution.py:131
  86.9 2.6 %copy-start.10 = (f32[6,64,128]{2,1,0:T(8,128)S(1)}, f32[6,64,128]{2,1,0:T(8,128)}, u32[]{:S(2)}) copy-start(f32[6,64,128]{2,1,0:T(8,128)} %get-tuple-element.58) | copy-start | bytes 589828
  86.9 2.6 %copy-start.11 = (f32[6,64,128]{2,1,0:T(8,128)S(1)}, f32[6,64,128]{2,1,0:T(8,128)}, u32[]{:S(2)}) copy-start(f32[6,64,128]{2,1,0:T(8,128)} %get-tuple-element.61) | copy-start | bytes 589828
  89.5 0.9 copy-start.8
  89.5 1.0 copy-start.9
  92.2 2.6 %copy-start.1 = (f32[6,6,64,128]{3,2,1,0:T(8,128)S(1)}, f32[6,6,64,128]{3,2,1,0:T(8,128)}, u32[]{:S(2)}) copy-start(f32[6,6,64,128]{3,2,1,0:T(8,128)} %get-tuple-element.15) | copy-start | bytes 3538948
  92.2 2.6 %copy-start.18 = (f32[6]{0:T(128)S(1)}, f32[6]{0:T(128)}, u32[]{:S(2)}) copy-start(f32[6]{0:T(128)} %get-tuple-element.135) | copy-start | bytes 76
  92.2 2.6 %copy-start.22 = (f32[3]{0:T(128)S(1)}, f32[3]{0:T(128)}, u32[]{:S(2)}) copy-start(f32[3]{0:T(128)} %get-tuple-element.117) | copy-start | bytes 40
  107.5 16.5 %collective-permute-start.10 = (f32[6,3,64,128]{3,2,1,0:T(8,128)S(1)}, f32[6,3,64,128]{3,2,1,0:T(8,128)S(1)}, u32[]{:S(2)}, u32[]{:S(2)}) collective-permute-start(f32[6,3,64,128]{3,2,1,0:T(8,128)S(1)} %fusion.53), channel_id=1, source_target_pairs={{0,1},{1,0},{2,3},{3,2},{4,5},{5,4},{6,7},{7,6},{8,9},{9,8},{10,11... | collective-permute-start | bytes 1769480 | tf_op jit(solution)/shard_map/ppermute | solution.py:182
  121.1 27.4 %collective-permute-start.9 = (f32[3,6,64,128]{3,2,1,0:T(8,128)S(1)}, f32[3,6,64,128]{3,2,1,0:T(8,128)S(1)}, u32[]{:S(2)}, u32[]{:S(2)}) collective-permute-start(f32[3,6,64,128]{3,2,1,0:T(8,128)S(1)} %multiply_add_fusion.3), channel_id=1, source_target_pairs={{0,2},{2,4},{4,6},{6,8},{8,10},{10,12},{12,14},{1,3},{3,5},{5,7},{... | collective-permute-start | bytes 1769480 | tf_op jit(solution)/shard_map/ppermute | solution.py:97
  122.4 26.4 %collective-permute-start.11 = (f32[3,6,64,128]{3,2,1,0:T(8,128)S(1)}, f32[3,6,64,128]{3,2,1,0:T(8,128)S(1)}, u32[]{:S(2)}, u32[]{:S(2)}) collective-permute-start(f32[3,6,64,128]{3,2,1,0:T(8,128)S(1)} %fusion.32), channel_id=1, source_target_pairs={{2,0},{4,2},{6,4},{8,6},{10,8},{12,10},{14,12},{3,1},{5,3},{7,5},{... | collective-permute-start | bytes 1769480 | tf_op jit(solution)/shard_map/ppermute | solution.py:102
  181.0 6.9 %collective-permute-start.14 = (f32[6,3,64,128]{3,2,1,0:T(8,128)S(1)}, f32[6,3,64,128]{3,2,1,0:T(8,128)S(1)}, u32[]{:S(2)}, u32[]{:S(2)}) collective-permute-start(f32[6,3,64,128]{3,2,1,0:T(8,128)S(1)} %fusion.56), channel_id=1, source_target_pairs={{0,1},{1,0},{2,3},{3,2},{4,5},{5,4},{6,7},{7,6},{8,9},{9,8},{10,11... | collective-permute-start | bytes 1769480 | tf_op jit(solution)/shard_map/ppermute | solution.py:182
  181.1 18.4 %collective-permute-start.13 = (f32[3,6,64,128]{3,2,1,0:T(8,128)S(1)}, f32[3,6,64,128]{3,2,1,0:T(8,128)S(1)}, u32[]{:S(2)}, u32[]{:S(2)}) collective-permute-start(f32[3,6,64,128]{3,2,1,0:T(8,128)S(1)} %fusion.40), channel_id=1, source_target_pairs={{2,0},{4,2},{6,4},{8,6},{10,8},{12,10},{14,12},{3,1},{5,3},{7,5},{... | collective-permute-start | bytes 1769480 | tf_op jit(solution)/shard_map/ppermute | solution.py:102
  182.4 29.9 %collective-permute-start.12 = (f32[3,6,64,128]{3,2,1,0:T(8,128)S(1)}, f32[3,6,64,128]{3,2,1,0:T(8,128)S(1)}, u32[]{:S(2)}, u32[]{:S(2)}) collective-permute-start(f32[3,6,64,128]{3,2,1,0:T(8,128)S(1)} %fusion.51), channel_id=1, source_target_pairs={{0,2},{2,4},{4,6},{6,8},{8,10},{10,12},{12,14},{1,3},{3,5},{5,7},{... | collective-permute-start | bytes 1769480 | tf_op jit(solution)/shard_map/ppermute | solution.py:97
  212.7 0.7 copy-start.19

commit v3 on v2

--- a/solution.py
+++ b/solution.py
@@ -173,6 +173,12 @@
             alpha_three * (fore_three - back_three) + alpha_four * (fore_four - back_four)
         )
         return mean_three, partial
+
+    def local_halves(field):
+        pieces = []
+        for side in (0, 1):
+            pieces.append(lax.optimization_barrier(local_part(cut(field, side))))
+        return pieces
 
     def y_halo(field):
         tail = lax.slice_in_dim(field, cells_y - 3, cells_y, axis=1)
@@ -211,7 +217,7 @@
         jnp.maximum(drift[1] + jnp.max(side_speed), -(drift[1] + jnp.min(side_speed)))
         + params[1] * jnp.abs(x_coord)[:, None]
     )
-    locals_now = local_whole(values)
+    locals_now = local_halves(values)
     bounds = spread_max(jnp.stack([local_one, local_two]), ("gx", "gy"))
     bound_one = bounds[0]
     bound_two = bounds[1]
@@ -245,8 +251,9 @@
                 ],
                 axis=0,
             )
-        mean_three = mean_three[start:stop]
-        partial = partial[start:stop]
+        if mean_three.shape[0] != stop - start:
+            mean_three = mean_three[start:stop]
+            partial = partial[start:stop]
         back_one, fore_one = one_sided(wide_x, 0, cell_span, stop - start)
         part = field[start:stop]
         wide_y = jnp.concatenate(
@@ -269,16 +276,15 @@
     def combine(ham, spread_one, spread_two):
         return ham + 0.5 * (bound_one * spread_one + bound_two * spread_two)
 
-    def stage(layer, field, x_halos, y_halos, local_pieces, order, update, last):
+    def stage(field, x_halos, y_halos, local_pieces, order, update, last):
         results = [None, None]
         sent = [None, None]
         if last:
             rate = combine(*half_parts(field, 2, x_halos, *y_halos, *local_pieces))
             return update(2, rate), None, None, None
-        for position, side in enumerate(order):
-            parts = half_parts(field, side, x_halos, *y_halos, *local_pieces)
-            if layer == 1 and position == 0:
-                parts = lax.optimization_barrier(parts)
+        for side in order:
+            pieces = local_pieces[side] if isinstance(local_pieces, list) else local_pieces
+            parts = half_parts(field, side, x_halos, *y_halos, *pieces)
             results[side] = update(side, combine(*parts))
             if last:
                 continue
@@ -296,16 +302,16 @@
         return merged, (sent[1], sent[0]), next_y, next_pieces
 
     first, x_halos, y_halos, locals_now = stage(
-        1, values, x_halos, y_halos, locals_now, (1, 0),
+        values, x_halos, y_halos, locals_now, (1, 0),
         lambda side, rate: cut(values, side) + step_time * rate, False,
     )
     second, x_halos, y_halos, locals_now = stage(
-        2, first, x_halos, y_halos, locals_now, (0, 1),
+        first, x_halos, y_halos, locals_now, (0, 1),
         lambda side, rate: 0.75 * cut(values, side) + 0.25 * (cut(first, side) + step_time * rate),
         False,
     )
     result, _, _, _ = stage(
-        3, second, x_halos, y_halos, locals_now, (1, 0),
+        second, x_halos, y_halos, locals_now, (1, 0),
         lambda side, rate: cut(values, side) * (1.0 / 3.0)
         + 2.0 / 3.0 * (cut(second, side) + step_time * rate),
         True,

time: 229 us -> 227 us (level)
  waiting for transfers between devices: 60.7 us -> 51.6 us
  other arithmetic: 120 us -> 123 us
    ppermute x6, waiting for transfers between devices: 13.3 us -> 4.53 us  [spread_max(): lax.ppermute(local, axes, [(i, (i + k * span) % count) for i in range(cou...]
    add x2, other arithmetic: 8.73 us -> 14.6 us  [on_device(): cut(values, side) + step_time * rate]
    sub x2 -> x0, other arithmetic: 5.1 us -> none  [half_parts(): return (ham, fore_one - back_one, fore_two - back_two)]
    add x3 -> x4, other arithmetic: 40.1 us -> 41.6 us  [local_part(): partial + 0.5 * (alpha_three * (fore_three - back_three) + alpha_four * (...]
  transfers between devices with their start and end apart: 15 -> 15, of which waited for: 5 -> 6; matrix products, arithmetic and copies ran while one was open for 23% -> 26% of each run, Pallas kernels for 0% -> 0%
where the time goes in v3:
time: 227 us; the launch traced here: 226 us
  other arithmetic  123 us (54%)
  waiting for transfers between devices  51.6 us (23%)
  starting transfers between devices  28.3 us (12%)
  local copies, waits for them, and re-layouts  15.7 us (7%)
  between operations  6.98 us (3%)
    add x4, other arithmetic, local_part(): partial + 0.5 * (alpha_three * (fore_three - back_three) + alpha_four * (...  41.6 us
    ppermute x3, waiting for transfers between devices, send_low(): lax.ppermute(piece, axis, [(i, (i + 1) % count) for i in range(count - 1)])  36.1 us
    add x2, other arithmetic, on_device(): 0.75 * cut(values, side) + 0.25 * (cut(first, side) + step_time * rate)  14.8 us
    add x2, other arithmetic, on_device(): cut(values, side) + step_time * rate  14.6 us
    add x1, other arithmetic, on_device(): cut(values, side) * (1.0 / 3.0)  14.1 us
    ppermute x3, starting transfers between devices, send_low(): lax.ppermute(piece, axis, [(i, (i + 1) % count) for i in range(count - 1)])  13.1 us
    ppermute x3, waiting for transfers between devices, send_high(): lax.ppermute(piece, axis, [((i + 1) % count, i) for i in range(count - 1)])  11 us
    ppermute x6, starting transfers between devices, spread_max(): lax.ppermute(local, axes, [(i, (i + k * span) % count) for i in range(cou...  9.98 us
  transfers between devices with their start and end apart: 15, of which 6 were waited for; matrix products, arithmetic and copies ran while one was open for 26% of the time, Pallas kernels for 0%

profile of v3, /device:TPU:0, one launch (start us, length us, event | category | flops | bytes accessed | tf_op | source)
XLA Modules:
  0.0 225.9 jit_solution(2917048902383779078)
XLA Ops:
  0.0 1.4 fusion.102
  1.5 1.8 sine_multiply_fusion
  3.3 1.3 fusion.86
  4.5 1.3 fusion.89
  5.8 0.8 fusion.99
  6.6 0.6 abs_multiply_fusion
  7.2 0.6 abs_multiply_fusion.1
  7.8 0.7 fusion.101
  10.9 1.8 add_reduce_fusion
  12.8 0.6 add_reduce_fusion.1
  13.3 1.8 pad_maximum_fusion.28
  15.2 2.4 %collective-permute-start.2 = (f32[2]{0:T(128)}, f32[2]{0:T(128)}, u32[]{:S(2)}, u32[]{:S(2)}) collective-permute-start(f32[2]{0:T(128)} %pad_maximum_fusion.28), channel_id=1, source_target_pairs={{0,3},{1,4},{2,5},{3,6},{4,7},{5,8},{6,9},{7,10},{8,11},{9,12},{10... | collective-permute-start | bytes 32 | tf_op jit(solution)/shard_map/ppermute | solution.py:131
  17.6 1.5 collective-permute-start.1
  19.6 2.4 %fusion.95 = (f32[3,6,64,128]{3,2,1,0:T(8,128)}, f32[3,6,64,128]{3,2,1,0:T(8,128)}) fusion(f32[6,6,64,128]{3,2,1,0:T(8,128)} %param.3), kind=kLoop, calls=%fused_computation.279 | loop fusion | bytes 2359296 | tf_op jit(solution)/shard_map/slice | solution.py:161
  22.0 4.2 %collective-permute-start.6 = (f32[3,6,64,128]{3,2,1,0:T(8,128)}, f32[3,6,64,128]{3,2,1,0:T(8,128)}, u32[]{:S(2)}, u32[]{:S(2)}) collective-permute-start(f32[3,6,64,128]{3,2,1,0:T(8,128)} %get-tuple-element.72), channel_id=1, source_target_pairs={{0,2},{2,4},{4,6},{6,8},{8,10},{10,12},{12,14},{1,3},{3,5},{5,7},{... | collective-permute-start | bytes 1769480 | tf_op jit(solution)/shard_map/ppermute | solution.py:97
  26.2 1.3 collective-permute-start.8
  27.9 1.1 fusion.97
  29.0 1.1 slice.1061
  30.0 1.1 fusion.96
  31.1 2.1 slice_maximum_fusion.5
  33.2 1.5 slice_maximum_fusion.4
  36.6 0.9 slice_bitcast_fusion.13
  37.5 0.8 slice_bitcast_fusion.5
  38.3 0.6 fusion.98
  38.9 1.3 cosine_multiply_fusion
  40.2 0.6 fusion.85
  40.7 1.0 slice.1026
  41.8 0.6 copy_bitcast_fusion
  42.4 2.2 pad_maximum_fusion.20
  44.7 0.9 slice_select_fusion
  45.6 0.6 slice_multiply_fusion.1
  47.2 8.8 %multiply_add_fusion.2 = (f32[3,6,64,128]{3,2,1,0:T(8,128)}, f32[3,6,64,128]{3,2,1,0:T(8,128)S(1)}, f32[3,6,64,128]{3,2,1,0:T(8,128)S(1)}) fusion(f32[3,6,64,1]{3,2,1,0:T(8,128)} %get-tuple-element.110, f32[3,6,64,125]{3,2,1,0:T(8,128)S(1)} %copy-done.13, f32[3,6,64,126]{3,2,1,0:T(8,128)S(1)} %copy-done.10, f32[3,6,64,127]{3,2,1,0:T(8,128)S(1)} %get-tuple-element.70, ...), kind=kLoop, calls=%fused_computation.169 | loop fusion | flops 40402944 | bytes 8225292 | tf_op jit(solution)/shard_map/add | solution.py:172
  56.1 0.5 copy-done.24
  57.4 6.8 %multiply_add_fusion.3 = (f32[3,6,64,128]{3,2,1,0:T(8,128)S(1)}, f32[3,6,64,128]{3,2,1,0:T(8,128)S(1)}, f32[3,6,64,128]{3,2,1,0:T(8,128)S(1)}) fusion(f32[3,6,64,1]{3,2,1,0:T(8,128)S(1)} %copy-done.15, f32[3,6,64,125]{3,2,1,0:T(8,128)S(1)} %copy-done.14, f32[3,6,64,126]{3,2,1,0:T(8,128)S(1)} %copy-done.7, f32[3,6,64,127]{3,2,1,0:T(8,128)S(1)} %get-tuple-element.69, ...), kind=kLoop, calls=%fused_computation.176 | loop fusion | flops 40402944 | bytes 8225292 | tf_op jit(solution)/shard_map/add | solution.py:172
  64.3 0.5 fusion.83
  65.5 1.0 collective-permute-start.7
  66.4 1.9 maximum_maximum_fusion.9
  68.3 3.2 %collective-permute-start.5 = (f32[2]{0:T(128)S(1)}, f32[2]{0:T(128)S(1)}, u32[]{:S(2)}, u32[]{:S(2)}) collective-permute-start(f32[2]{0:T(128)S(1)} %maximum_maximum_fusion.9), channel_id=1, source_target_pairs={{0,12},{1,13},{2,14},{3,15},{4,0},{5,1},{6,2},{7,3},{8,4},{9,5},{1... | collective-permute-start | bytes 32 | tf_op jit(solution)/shard_map/ppermute | solution.py:131
  71.5 0.8 collective-permute-start.4
  72.8 1.6 collective-permute-start.3
  74.4 1.6 collective-permute-done.4
  76.0 2.4 %collective-permute-done.3 = f32[2]{0:T(128)S(1)} collective-permute-done((f32[2]{0:T(128)S(1)}, f32[2]{0:T(128)S(1)}, u32[]{:S(2)}, u32[]{:S(2)}) %collective-permute-start.3) | collective-permute-done | bytes 40 | tf_op jit(solution)/shard_map/ppermute | solution.py:131
  78.4 0.6 fusion.100
  80.3 1.3 add_select_fusion.7
  81.7 1.3 add_select_fusion.15
  83.0 1.5 pad_maximum_fusion.10
  84.8 1.2 add_select_fusion.5
  86.5 0.6 copy-done.6
  87.1 7.3 %fusion.47 = f32[3,6,64,128]{3,2,1,0:T(8,128)S(1)} fusion(f32[3,6,64,128]{3,2,1,0:T(8,128)S(1)} %copy-done.6, f32[3,6,64,128]{3,2,1,0:T(8,128)S(1)} %add_multiply_fusion.6, f32[3,11,64,128]{3,2,1,0:T(8,128)S(1)} %fusion.24, f32[8,6,64,128]{3,2,1,0:T(8,128)S(1)} %get-tuple-element.52, f32[3]{0:T(128)S(1)} %copy-done.28, ...), kind=kLoop, calls=%fused_computation.135 | loop fusion | flops 40108032 | bytes 9474684 | tf_op jit(solution)/shard_map/add | solution.py:306
  94.4 7.3 %fusion.33 = f32[3,6,64,128]{3,2,1,0:T(8,128)S(1)} fusion(f32[3,6,64,128]{3,2,1,0:T(8,128)S(1)} %get-tuple-element.14, f32[3,6,64,128]{3,2,1,0:T(8,128)S(1)} %add_multiply_fusion.7, f32[3,11,64,128]{3,2,1,0:T(8,128)S(1)} %fusion.25, f32[8,6,64,128]{3,2,1,0:T(8,128)S(1)} %get-tuple-element.51, f32[]{:T(128)} %bitcast.9, f32[]{:T(128)} %bitcast.8, ...), kind=kLoop, calls=%fused_computation.121 | loop fusion | flops 40108032 | bytes 9474684 | tf_op jit(solution)/shard_map/add | solution.py:306
  102.9 0.7 slice_maximum_fusion.3
  104.6 13.0 %multiply_add_fusion.1 = (f32[6,6,64,128]{3,2,1,0:T(8,128)S(1)}, f32[6,6,64,128]{3,2,1,0:T(8,128)S(1)}, f32[6,6,64,128]{3,2,1,0:T(8,128)S(1)}) fusion(f32[6,6,64,1]{3,2,1,0:T(8,128)S(1)} %get-tuple-element.50, f32[6,6,64,125]{3,2,1,0:T(8,128)S(1)} %slice.1108, f32[6,6,64,126]{3,2,1,0:T(8,128)S(1)} %get-tuple-element.48, f32[6,6,64,127]{3,2,1,0:T(8,128)S(1)} %fusion.14, ...), kind=kLoop, calls=%fused_computation.94 | loop fusion | flops 80805888 | bytes 16450572 | tf_op jit(solution)/shard_map/add | solution.py:172
  117.8 3.5 %collective-permute-start.9 = (f32[3,6,64,128]{3,2,1,0:T(8,128)S(1)}, f32[3,6,64,128]{3,2,1,0:T(8,128)S(1)}, u32[]{:S(2)}, u32[]{:S(2)}) collective-permute-start(f32[3,6,64,128]{3,2,1,0:T(8,128)S(1)} %fusion.47), channel_id=1, source_target_pairs={{0,2},{2,4},{4,6},{6,8},{8,10},{10,12},{12,14},{1,3},{3,5},{5,7},{... | collective-permute-start | bytes 1769480 | tf_op jit(solution)/shard_map/ppermute | solution.py:97
  121.4 1.5 collective-permute-start.11
  123.4 23.9 %collective-permute-done.9 = f32[3,6,64,128]{3,2,1,0:T(8,128)S(1)} collective-permute-done((f32[3,6,64,128]{3,2,1,0:T(8,128)S(1)}, f32[3,6,64,128]{3,2,1,0:T(8,128)S(1)}, u32[]{:S(2)}, u32[]{:S(2)}) %collective-permute-start.9) | collective-permute-done | bytes 589856 | tf_op jit(solution)/shard_map/ppermute | solution.py:97
  148.8 7.4 %fusion.55 = f32[3,6,64,128]{3,2,1,0:T(8,128)S(1)} fusion(f32[3,6,64,128]{3,2,1,0:T(8,128)S(1)} %fusion.47, f32[6,6,64,128]{3,2,1,0:T(8,128)S(1)} %get-tuple-element.18, f32[6,6,64,128]{3,2,1,0:T(8,128)S(1)} %add_multiply_fusion.1, f32[3,11,64,128]{3,2,1,0:T(8,128)S(1)} %fusion.22, f32[8,6,64,128]{3,2,1,0:T(8,128)S(1)} %fusion.8, f32[3]{0:T(128)S(1)} %copy-done.28, ...), kind=kLoop, calls=%fused_computation.143 | loop fusion | flops 40550400 | bytes 10064508 | tf_op jit(solution)/shard_map/add | solution.py:310
  156.2 7.4 %fusion.41 = f32[3,6,64,128]{3,2,1,0:T(8,128)S(1)} fusion(f32[3,6,64,128]{3,2,1,0:T(8,128)S(1)} %fusion.33, f32[6,6,64,128]{3,2,1,0:T(8,128)S(1)} %get-tuple-element.18, f32[6,6,64,128]{3,2,1,0:T(8,128)S(1)} %add_multiply_fusion.1, f32[3,11,64,128]{3,2,1,0:T(8,128)S(1)} %fusion.23, f32[8,6,64,128]{3,2,1,0:T(8,128)S(1)} %fusion.9, f32[]{:T(128)} %bitcast.9, ...), kind=kLoop, calls=%fused_computation.129 | loop fusion | flops 40550400 | bytes 10064508 | tf_op jit(solution)/shard_map/add | solution.py:310
  164.8 0.7 slice_maximum_fusion.1
  166.3 13.0 %multiply_add_fusion = (f32[6,6,64,128]{3,2,1,0:T(8,128)S(1)}, f32[6,6,64,128]{3,2,1,0:T(8,128)S(1)}, f32[6,6,64,128]{3,2,1,0:T(8,128)S(1)}) fusion(f32[6,6,64,1]{3,2,1,0:T(8,128)S(1)} %get-tuple-element.42, f32[6,6,64,125]{3,2,1,0:T(8,128)S(1)} %slice.1187, f32[6,6,64,126]{3,2,1,0:T(8,128)S(1)} %get-tuple-element.40, f32[6,6,64,127]{3,2,1,0:T(8,128)S(1)} %fusion.17, ...), kind=kLoop, calls=%fused_computation.90 | loop fusion | flops 80805888 | bytes 16450572 | tf_op jit(solution)/shard_map/add | solution.py:172
  179.6 1.3 collective-permute-start.13
  180.9 5.3 %collective-permute-start.12 = (f32[3,6,64,128]{3,2,1,0:T(8,128)S(1)}, f32[3,6,64,128]{3,2,1,0:T(8,128)S(1)}, u32[]{:S(2)}, u32[]{:S(2)}) collective-permute-start(f32[3,6,64,128]{3,2,1,0:T(8,128)S(1)} %fusion.55), channel_id=1, source_target_pairs={{0,2},{2,4},{4,6},{6,8},{8,10},{10,12},{12,14},{1,3},{3,5},{5,7},{... | collective-permute-start | bytes 1769480 | tf_op jit(solution)/shard_map/ppermute | solution.py:97
  187.0 11.0 %collective-permute-done.13 = f32[3,6,64,128]{3,2,1,0:T(8,128)S(1)} collective-permute-done((f32[3,6,64,128]{3,2,1,0:T(8,128)S(1)}, f32[3,6,64,128]{3,2,1,0:T(8,128)S(1)}, u32[]{:S(2)}, u32[]{:S(2)}) %collective-permute-start.13) | collective-permute-done | bytes 589856 | tf_op jit(solution)/shard_map/ppermute | solution.py:102
  198.5 12.2 %collective-permute-done.12 = f32[3,6,64,128]{3,2,1,0:T(8,128)S(1)} collective-permute-done((f32[3,6,64,128]{3,2,1,0:T(8,128)S(1)}, f32[3,6,64,128]{3,2,1,0:T(8,128)S(1)}, u32[]{:S(2)}, u32[]{:S(2)}) %collective-permute-start.12) | collective-permute-done | bytes 589856 | tf_op jit(solution)/shard_map/ppermute | solution.py:97
  211.8 14.1 %fusion.21 = f32[6,6,64,128]{3,2,1,0:T(8,128)} fusion(f32[3,6,64,128]{3,2,1,0:T(8,128)S(1)} %fusion.55, f32[3,6,64,128]{3,2,1,0:T(8,128)S(1)} %fusion.41, f32[6,6,64,128]{3,2,1,0:T(8,128)S(1)} %get-tuple-element.20, f32[6,6,64,128]{3,2,1,0:T(8,128)S(1)} %add_multiply_fusion, f32[6,11,64,128]{3,2,1,0:T(8,128)S(1)} %fusion, f32[11,6,64,128]{3,2,1,0:T(8,128)S(1)} %fusion.1, ...), kind=kLoop, calls=%fused_computation.70 | loop fusion | flops 81395712 | bytes 20096208 | tf_op jit(solution)/shard_map/add | solution.py:315
  (138 shorter events, 12.9 us)
Async XLA Ops:
  15.2 12.3 %copy-start = (f32[6,6,64,128]{3,2,1,0:T(8,128)S(1)}, f32[6,6,64,128]{3,2,1,0:T(8,128)}, u32[]{:S(2)}) copy-start(f32[6,6,64,128]{3,2,1,0:T(8,128)} %param.3) | copy-start | bytes 3538948
  15.2 50.3 %collective-permute-start.2 = (f32[2]{0:T(128)}, f32[2]{0:T(128)}, u32[]{:S(2)}, u32[]{:S(2)}) collective-permute-start(f32[2]{0:T(128)} %pad_maximum_fusion.28), channel_id=1, source_target_pairs={{0,3},{1,4},{2,5},{3,6},{4,7},{5,8},{6,9},{7,10},{8,11},{9,12},{10... | collective-permute-start | bytes 32 | tf_op jit(solution)/shard_map/ppermute | solution.py:131
  17.6 48.8 %collective-permute-start.1 = (f32[2]{0:T(128)}, f32[2]{0:T(128)}, u32[]{:S(2)}, u32[]{:S(2)}) collective-permute-start(f32[2]{0:T(128)} %pad_maximum_fusion.28), channel_id=1, source_target_pairs={{0,2},{1,3},{2,4},{3,5},{4,6},{5,7},{6,8},{7,9},{8,10},{9,11},{10,... | collective-permute-start | bytes 32 | tf_op jit(solution)/shard_map/ppermute | solution.py:131
  19.1 47.3 %collective-permute-start = (f32[2]{0:T(128)}, f32[2]{0:T(128)}, u32[]{:S(2)}, u32[]{:S(2)}) collective-permute-start(f32[2]{0:T(128)} %pad_maximum_fusion.28), channel_id=1, source_target_pairs={{0,1},{1,2},{2,3},{3,4},{4,5},{5,6},{6,7},{7,8},{8,9},{9,10},{10,1... | collective-permute-start | bytes 32 | tf_op jit(solution)/shard_map/ppermute | solution.py:131
  22.0 58.3 %collective-permute-start.6 = (f32[3,6,64,128]{3,2,1,0:T(8,128)}, f32[3,6,64,128]{3,2,1,0:T(8,128)}, u32[]{:S(2)}, u32[]{:S(2)}) collective-permute-start(f32[3,6,64,128]{3,2,1,0:T(8,128)} %get-tuple-element.72), channel_id=1, source_target_pairs={{0,2},{2,4},{4,6},{6,8},{8,10},{10,12},{12,14},{1,3},{3,5},{5,7},{... | collective-permute-start | bytes 1769480 | tf_op jit(solution)/shard_map/ppermute | solution.py:97
  26.2 58.6 %collective-permute-start.8 = (f32[3,6,64,128]{3,2,1,0:T(8,128)}, f32[3,6,64,128]{3,2,1,0:T(8,128)}, u32[]{:S(2)}, u32[]{:S(2)}) collective-permute-start(f32[3,6,64,128]{3,2,1,0:T(8,128)} %get-tuple-element.71), channel_id=1, source_target_pairs={{2,0},{4,2},{6,4},{8,6},{10,8},{12,10},{14,12},{3,1},{5,3},{7,5},{... | collective-permute-start | bytes 1769480 | tf_op jit(solution)/shard_map/ppermute | solution.py:102
  29.0 4.3 %copy-start.3 = (f32[3,6,64,1]{3,2,1,0:T(8,128)}, f32[3,6,64,1]{3,2,1,0:T(8,128)S(1)}, u32[]{:S(2)}) copy-start(f32[3,6,64,1]{3,2,1,0:T(8,128)S(1)} %get-tuple-element.109) | copy-start | bytes 13828
  31.1 2.1 copy-start.1
  37.5 0.8 copy-start.23
  44.7 1.5 copy-start.5
  44.7 1.6 copy-start.12
  44.7 1.6 copy-start.13
  45.6 1.2 copy-start.4
  45.6 1.4 copy-start.9
  45.6 1.6 copy-start.10
  47.2 9.8 %copy-start.11 = (f32[3,6,64,127]{3,2,1,0:T(8,128)S(1)}, f32[3,6,64,127]{3,2,1,0:T(8,128)}, u32[]{:S(2)}) copy-start(f32[3,6,64,127]{3,2,1,0:T(8,128)} %get-tuple-element.140) | copy-start | bytes 1755652
  47.2 9.8 %copy-start.14 = (f32[3,6,64,125]{3,2,1,0:T(8,128)S(1)}, f32[3,6,64,125]{3,2,1,0:T(8,128)}, u32[]{:S(2)}) copy-start(f32[3,6,64,125]{3,2,1,0:T(8,128)} %slice.1026) | copy-start | bytes 1728004
  47.2 9.8 %copy-start.15 = (f32[3,6,64,1]{3,2,1,0:T(8,128)S(1)}, f32[3,6,64,1]{3,2,1,0:T(8,128)}, u32[]{:S(2)}) copy-start(f32[3,6,64,1]{3,2,1,0:T(8,128)} %get-tuple-element.106) | copy-start | bytes 13828
  56.0 0.7 copy-start.24
  56.0 0.7 copy-start.29
  56.0 0.8 copy-start.31
  56.0 0.8 copy-start.32
  56.0 1.1 copy-start.2
  56.0 1.2 copy-start.7
  56.0 1.4 copy-start.8
  64.2 0.6 copy-start.26
  64.3 1.2 copy-start.25
  65.5 16.1 %collective-permute-start.7 = (f32[6,3,64,128]{3,2,1,0:T(8,128)}, f32[6,3,64,128]{3,2,1,0:T(8,128)}, u32[]{:S(2)}, u32[]{:S(2)}) collective-permute-start(f32[6,3,64,128]{3,2,1,0:T(8,128)} %slice_select_fusion), channel_id=1, source_target_pairs={{0,1},{1,0},{2,3},{3,2},{4,5},{5,4},{6,7},{7,6},{8,9},{9,8},{10,11... | collective-permute-start | bytes 1769480 | tf_op jit(solution)/shard_map/ppermute | solution.py:188
  68.3 4.5 %collective-permute-start.5 = (f32[2]{0:T(128)S(1)}, f32[2]{0:T(128)S(1)}, u32[]{:S(2)}, u32[]{:S(2)}) collective-permute-start(f32[2]{0:T(128)S(1)} %maximum_maximum_fusion.9), channel_id=1, source_target_pairs={{0,12},{1,13},{2,14},{3,15},{4,0},{5,1},{6,2},{7,3},{8,4},{9,5},{1... | collective-permute-start | bytes 32 | tf_op jit(solution)/shard_map/ppermute | solution.py:131
  71.5 4.5 %collective-permute-start.4 = (f32[2]{0:T(128)S(1)}, f32[2]{0:T(128)S(1)}, u32[]{:S(2)}, u32[]{:S(2)}) collective-permute-start(f32[2]{0:T(128)S(1)} %maximum_maximum_fusion.9), channel_id=1, source_target_pairs={{0,8},{1,9},{2,10},{3,11},{4,12},{5,13},{6,14},{7,15},{8,0},{9,1},... | collective-permute-start | bytes 32 | tf_op jit(solution)/shard_map/ppermute | solution.py:131
  72.8 5.6 %collective-permute-start.3 = (f32[2]{0:T(128)S(1)}, f32[2]{0:T(128)S(1)}, u32[]{:S(2)}, u32[]{:S(2)}) collective-permute-start(f32[2]{0:T(128)S(1)} %maximum_maximum_fusion.9), channel_id=1, source_target_pairs={{0,4},{1,5},{2,6},{3,7},{4,8},{5,9},{6,10},{7,11},{8,12},{9,13},{1... | collective-permute-start | bytes 32 | tf_op jit(solution)/shard_map/ppermute | solution.py:131
  80.2 1.4 copy-start.16
  80.2 1.4 copy-start.17
  80.2 1.4 copy-start.18
  80.3 1.4 copy-start.19
  80.3 1.4 copy-start.20
  80.3 1.4 copy-start.21
  80.3 1.4 copy-start.22
  86.0 1.1 copy-start.6
  86.1 1.1 copy-start.28
  87.1 7.3 %copy-start.27 = (f32[3]{0:T(128)S(1)}, f32[3]{0:T(128)}, u32[]{:S(2)}) copy-start(f32[3]{0:T(128)} %get-tuple-element.119) | copy-start | bytes 40
  104.5 18.5 %collective-permute-start.10 = (f32[6,3,64,128]{3,2,1,0:T(8,128)S(1)}, f32[6,3,64,128]{3,2,1,0:T(8,128)S(1)}, u32[]{:S(2)}, u32[]{:S(2)}) collective-permute-start(f32[6,3,64,128]{3,2,1,0:T(8,128)S(1)} %fusion.57), channel_id=1, source_target_pairs={{0,1},{1,0},{2,3},{3,2},{4,5},{5,4},{6,7},{7,6},{8,9},{9,8},{10,11... | collective-permute-start | bytes 1769480 | tf_op jit(solution)/shard_map/ppermute | solution.py:188
  117.8 29.4 %collective-permute-start.9 = (f32[3,6,64,128]{3,2,1,0:T(8,128)S(1)}, f32[3,6,64,128]{3,2,1,0:T(8,128)S(1)}, u32[]{:S(2)}, u32[]{:S(2)}) collective-permute-start(f32[3,6,64,128]{3,2,1,0:T(8,128)S(1)} %fusion.47), channel_id=1, source_target_pairs={{0,2},{2,4},{4,6},{6,8},{8,10},{10,12},{12,14},{1,3},{3,5},{5,7},{... | collective-permute-start | bytes 1769480 | tf_op jit(solution)/shard_map/ppermute | solution.py:97
  121.4 26.1 %collective-permute-start.11 = (f32[3,6,64,128]{3,2,1,0:T(8,128)S(1)}, f32[3,6,64,128]{3,2,1,0:T(8,128)S(1)}, u32[]{:S(2)}, u32[]{:S(2)}) collective-permute-start(f32[3,6,64,128]{3,2,1,0:T(8,128)S(1)} %fusion.33), channel_id=1, source_target_pairs={{2,0},{4,2},{6,4},{8,6},{10,8},{12,10},{14,12},{3,1},{5,3},{7,5},{... | collective-permute-start | bytes 1769480 | tf_op jit(solution)/shard_map/ppermute | solution.py:102
  179.5 6.9 %collective-permute-start.14 = (f32[6,3,64,128]{3,2,1,0:T(8,128)S(1)}, f32[6,3,64,128]{3,2,1,0:T(8,128)S(1)}, u32[]{:S(2)}, u32[]{:S(2)}) collective-permute-start(f32[6,3,64,128]{3,2,1,0:T(8,128)S(1)} %fusion.60), channel_id=1, source_target_pairs={{0,1},{1,0},{2,3},{3,2},{4,5},{5,4},{6,7},{7,6},{8,9},{9,8},{10,11... | collective-permute-start | bytes 1769480 | tf_op jit(solution)/shard_map/ppermute | solution.py:188
  179.6 18.4 %collective-permute-start.13 = (f32[3,6,64,128]{3,2,1,0:T(8,128)S(1)}, f32[3,6,64,128]{3,2,1,0:T(8,128)S(1)}, u32[]{:S(2)}, u32[]{:S(2)}) collective-permute-start(f32[3,6,64,128]{3,2,1,0:T(8,128)S(1)} %fusion.41), channel_id=1, source_target_pairs={{2,0},{4,2},{6,4},{8,6},{10,8},{12,10},{14,12},{3,1},{5,3},{7,5},{... | collective-permute-start | bytes 1769480 | tf_op jit(solution)/shard_map/ppermute | solution.py:102
  180.9 29.9 %collective-permute-start.12 = (f32[3,6,64,128]{3,2,1,0:T(8,128)S(1)}, f32[3,6,64,128]{3,2,1,0:T(8,128)S(1)}, u32[]{:S(2)}, u32[]{:S(2)}) collective-permute-start(f32[3,6,64,128]{3,2,1,0:T(8,128)S(1)} %fusion.55), channel_id=1, source_target_pairs={{0,2},{2,4},{4,6},{6,8},{8,10},{10,12},{12,14},{1,3},{3,5},{5,7},{... | collective-permute-start | bytes 1769480 | tf_op jit(solution)/shard_map/ppermute | solution.py:97
  211.2 0.6 copy-start.30

commit v4 on v3

--- a/solution.py
+++ b/solution.py
@@ -1,6 +1,7 @@
 import math
 
 import jax
+import numpy as np
 import jax.numpy as jnp
 from jax import lax
 from jax.sharding import PartitionSpec as P
@@ -195,26 +196,30 @@
 
     x_halos = (send_low(values[cells_x - 3 :], "gx"), send_high(values[:3], "gx"))
     y_halos = y_halo(values)
-    psi_grid = jnp.arange(n_psi).astype(jnp.float32) * step_psi - math.pi
-    speed_grid = 0.5 + (jnp.arange(n_speed).astype(jnp.float32) + 0.5) * step_speed
-    along_one = -speed_grid[None, :] + params[0] * jnp.cos(psi_grid)[:, None]
-    along_two = params[0] * jnp.sin(psi_grid)[:, None]
+    psi_grid = np.arange(n_psi).astype(np.float32) * np.float32(step_psi) - np.float32(math.pi)
+    cos_table = np.cos(psi_grid.astype(np.float64)).astype(np.float32)
+    sin_table = np.sin(psi_grid.astype(np.float64)).astype(np.float32)
+    speed_grid = np.float32(0.5) + (
+        np.arange(n_speed).astype(np.float32) + np.float32(0.5)
+    ) * np.float32(step_speed)
+    along_one = -jnp.asarray(speed_grid)[None, :] + params[0] * jnp.asarray(cos_table)[:, None]
+    along_two = params[0] * jnp.asarray(sin_table)[:, None]
     y_coord = (
         (place_y * cells_y + jnp.arange(cells_y)).astype(jnp.float32) + 0.5 - 0.5 * total_y
     ) * cell_span
     x_coord = (
         (place_x * cells_x + jnp.arange(cells_x)).astype(jnp.float32) + 0.5 - 0.5 * total_x
     ) * cell_span
-    turn_speed = params[0] * jnp.cos(psi_grid)
-    side_speed = params[0] * jnp.sin(psi_grid)
-    first_hi = jnp.max(turn_speed) - speed_grid[0]
-    first_lo = jnp.min(turn_speed) - speed_grid[n_speed - 1]
+    first_hi = params[0] * cos_table.max() - speed_grid[0]
+    first_lo = params[0] * cos_table.min() - speed_grid[n_speed - 1]
+    second_hi = params[0] * sin_table.max()
+    second_lo = params[0] * sin_table.min()
     local_one = jnp.max(
         jnp.maximum(drift[0] + first_hi, -(drift[0] + first_lo))
         + params[1] * jnp.abs(y_coord)[None, :]
     )
     local_two = jnp.max(
-        jnp.maximum(drift[1] + jnp.max(side_speed), -(drift[1] + jnp.min(side_speed)))
+        jnp.maximum(drift[1] + second_hi, -(drift[1] + second_lo))
         + params[1] * jnp.abs(x_coord)[:, None]
     )
     locals_now = local_halves(values)

time: 227 us -> 220 us (0.969)
  other arithmetic: 123 us -> 118 us
where the time goes in v4:
time: 220 us; the launch traced here: 219 us
  other arithmetic  118 us (54%)
  waiting for transfers between devices  51.6 us (23%)
  starting transfers between devices  28.3 us (13%)
  local copies, waits for them, and re-layouts  14.4 us (7%)
  between operations  5.91 us (3%)
    add x4, other arithmetic, local_part(): partial + 0.5 * (alpha_three * (fore_three - back_three) + alpha_four * (...  41.7 us
    ppermute x3, waiting for transfers between devices, send_low(): lax.ppermute(piece, axis, [(i, (i + 1) % count) for i in range(count - 1)])  36.1 us
    add x2, other arithmetic, on_device(): 0.75 * cut(values, side) + 0.25 * (cut(first, side) + step_time * rate)  14.9 us
    add x2, other arithmetic, on_device(): cut(values, side) + step_time * rate  14.8 us
    add x1, other arithmetic, on_device(): cut(values, side) * (1.0 / 3.0)  14.1 us
    ppermute x3, starting transfers between devices, send_low(): lax.ppermute(piece, axis, [(i, (i + 1) % count) for i in range(count - 1)])  13.1 us
    ppermute x3, waiting for transfers between devices, send_high(): lax.ppermute(piece, axis, [((i + 1) % count, i) for i in range(count - 1)])  11 us
    ppermute x6, starting transfers between devices, spread_max(): lax.ppermute(local, axes, [(i, (i + k * span) % count) for i in range(cou...  9.99 us
  transfers between devices with their start and end apart: 15, of which 6 were waited for; matrix products, arithmetic and copies ran while one was open for 26% of the time, Pallas kernels for 0%

profile of v4, /device:TPU:0, one launch (start us, length us, event | category | flops | bytes accessed | tf_op | source)
XLA Modules:
  0.0 218.6 jit_solution(5771607543044835046)
XLA Ops:
  0.0 1.4 fusion.96
  1.5 0.8 fusion.94
  2.2 0.6 abs_multiply_fusion
  2.9 0.6 abs_multiply_fusion.1
  4.6 1.3 add_reduce_fusion
  5.9 0.7 add_reduce_fusion.1
  6.5 1.8 pad_maximum_fusion.28
  8.4 2.4 %collective-permute-start.2 = (f32[2]{0:T(128)}, f32[2]{0:T(128)}, u32[]{:S(2)}, u32[]{:S(2)}) collective-permute-start(f32[2]{0:T(128)} %pad_maximum_fusion.28), channel_id=1, source_target_pairs={{0,3},{1,4},{2,5},{3,6},{4,7},{5,8},{6,9},{7,10},{8,11},{9,12},{10... | collective-permute-start | bytes 32 | tf_op jit(solution)/shard_map/ppermute | solution.py:132
  10.8 1.5 collective-permute-start.1
  12.3 0.5 collective-permute-start
  12.8 2.4 %fusion.90 = (f32[3,6,64,128]{3,2,1,0:T(8,128)}, f32[3,6,64,128]{3,2,1,0:T(8,128)}) fusion(f32[6,6,64,128]{3,2,1,0:T(8,128)} %param.6), kind=kLoop, calls=%fused_computation.272 | loop fusion | bytes 2359296 | tf_op jit(solution)/shard_map/slice | solution.py:162
  15.2 4.2 %collective-permute-start.6 = (f32[3,6,64,128]{3,2,1,0:T(8,128)}, f32[3,6,64,128]{3,2,1,0:T(8,128)}, u32[]{:S(2)}, u32[]{:S(2)}) collective-permute-start(f32[3,6,64,128]{3,2,1,0:T(8,128)} %get-tuple-element.72), channel_id=1, source_target_pairs={{0,2},{2,4},{4,6},{6,8},{8,10},{10,12},{12,14},{1,3},{3,5},{5,7},{... | collective-permute-start | bytes 1769480 | tf_op jit(solution)/shard_map/ppermute | solution.py:98
  19.4 1.3 collective-permute-start.8
  21.1 1.1 fusion.92
  22.2 1.1 slice.1055
  23.3 1.0 fusion.91
  24.3 2.1 slice_maximum_fusion.5
  26.5 1.5 slice_maximum_fusion.4
  29.9 0.9 slice_bitcast_fusion.13
  30.8 0.8 slice_bitcast_fusion.5
  31.6 0.6 fusion.93
  32.2 1.0 slice.1020
  33.3 0.6 copy_bitcast_fusion
  33.8 2.2 %pad_maximum_fusion.20 = (f32[3,6,70,128]{3,2,1,0:T(8,128)}, f32[3,6,70,128]{3,2,1,0:T(8,128)S(1)}) fusion(f32[3,6,3,128]{3,2,1,0:T(4,128)S(1)} %get-tuple-element.67, f32[3,6,64,128]{3,2,1,0:T(8,128)} %get-tuple-element.71, f32[3,6,3,128]{3,2,1,0:T(4,128)S(1)} %get-tuple-element.65, f32[3,6,3,128]{3,2,1,0:T(4,128)S(1)} %get-tuple-element.68, ...), kind=kLoop, calls=%fused_computation.114 | loop fusion | flops 645120 | bytes 2580480 | tf_op jit(solution)/shard_map/concatenate | solution.py:56
  36.2 0.9 slice_select_fusion
  37.1 0.6 slice_multiply_fusion.1
  37.7 0.5 broadcast_multiply_fusion
  38.3 0.5 broadcast_multiply_fusion.1
  39.0 8.8 %multiply_add_fusion.2 = (f32[3,6,64,128]{3,2,1,0:T(8,128)}, f32[3,6,64,128]{3,2,1,0:T(8,128)S(1)}, f32[3,6,64,128]{3,2,1,0:T(8,128)S(1)}) fusion(f32[3,6,64,1]{3,2,1,0:T(8,128)} %get-tuple-element.110, f32[3,6,64,125]{3,2,1,0:T(8,128)S(1)} %copy-done.13, f32[3,6,64,126]{3,2,1,0:T(8,128)S(1)} %copy-done.10, f32[3,6,64,127]{3,2,1,0:T(8,128)S(1)} %get-tuple-element.70, ...), kind=kLoop, calls=%fused_computation.169 | loop fusion | flops 40402944 | bytes 8225292 | tf_op jit(solution)/shard_map/add | solution.py:173
  47.9 0.6 copy-done.24
  49.2 6.8 %multiply_add_fusion.3 = (f32[3,6,64,128]{3,2,1,0:T(8,128)S(1)}, f32[3,6,64,128]{3,2,1,0:T(8,128)S(1)}, f32[3,6,64,128]{3,2,1,0:T(8,128)S(1)}) fusion(f32[3,6,64,1]{3,2,1,0:T(8,128)S(1)} %copy-done.15, f32[3,6,64,125]{3,2,1,0:T(8,128)S(1)} %copy-done.14, f32[3,6,64,126]{3,2,1,0:T(8,128)S(1)} %copy-done.7, f32[3,6,64,127]{3,2,1,0:T(8,128)S(1)} %get-tuple-element.69, ...), kind=kLoop, calls=%fused_computation.176 | loop fusion | flops 40402944 | bytes 8225292 | tf_op jit(solution)/shard_map/add | solution.py:173
  56.2 0.5 fusion.83
  57.4 1.0 collective-permute-start.7
  58.4 2.0 maximum_maximum_fusion.9
  60.4 3.2 %collective-permute-start.5 = (f32[2]{0:T(128)S(1)}, f32[2]{0:T(128)S(1)}, u32[]{:S(2)}, u32[]{:S(2)}) collective-permute-start(f32[2]{0:T(128)S(1)} %maximum_maximum_fusion.9), channel_id=1, source_target_pairs={{0,12},{1,13},{2,14},{3,15},{4,0},{5,1},{6,2},{7,3},{8,4},{9,5},{1... | collective-permute-start | bytes 32 | tf_op jit(solution)/shard_map/ppermute | solution.py:132
  63.6 0.8 collective-permute-start.4
  64.4 0.5 collective-permute-done.5
  64.9 1.6 collective-permute-start.3
  66.5 1.6 collective-permute-done.4
  68.1 2.4 %collective-permute-done.3 = f32[2]{0:T(128)S(1)} collective-permute-done((f32[2]{0:T(128)S(1)}, f32[2]{0:T(128)S(1)}, u32[]{:S(2)}, u32[]{:S(2)}) %collective-permute-start.3) | collective-permute-done | bytes 40 | tf_op jit(solution)/shard_map/ppermute | solution.py:132
  70.5 0.7 fusion.95
  72.6 1.3 add_select_fusion.7
  74.0 1.3 add_select_fusion.15
  75.3 1.5 pad_maximum_fusion.10
  77.1 1.2 add_select_fusion.5
  78.3 0.5 fusion.7
  78.8 0.6 copy-done.6
  79.4 7.4 %fusion.47 = f32[3,6,64,128]{3,2,1,0:T(8,128)S(1)} fusion(f32[3,6,64,128]{3,2,1,0:T(8,128)S(1)} %copy-done.6, f32[3,6,64,128]{3,2,1,0:T(8,128)S(1)} %add_multiply_fusion.6, f32[3,11,64,128]{3,2,1,0:T(8,128)S(1)} %fusion.24, f32[8,6,64,128]{3,2,1,0:T(8,128)S(1)} %get-tuple-element.52, f32[3]{0:T(128)S(1)} %copy-done.28, ...), kind=kLoop, calls=%fused_computation.135 | loop fusion | flops 40108032 | bytes 9474684 | tf_op jit(solution)/shard_map/add | solution.py:311
  86.8 7.4 %fusion.33 = f32[3,6,64,128]{3,2,1,0:T(8,128)S(1)} fusion(f32[3,6,64,128]{3,2,1,0:T(8,128)S(1)} %get-tuple-element.14, f32[3,6,64,128]{3,2,1,0:T(8,128)S(1)} %add_multiply_fusion.7, f32[3,11,64,128]{3,2,1,0:T(8,128)S(1)} %fusion.25, f32[8,6,64,128]{3,2,1,0:T(8,128)S(1)} %get-tuple-element.51, f32[]{:T(128)} %bitcast.7, f32[]{:T(128)} %bitcast.6, ...), kind=kLoop, calls=%fused_computation.121 | loop fusion | flops 40108032 | bytes 9474684 | tf_op jit(solution)/shard_map/add | solution.py:311
  95.4 0.7 slice_maximum_fusion.3
  97.0 13.0 %multiply_add_fusion.1 = (f32[6,6,64,128]{3,2,1,0:T(8,128)S(1)}, f32[6,6,64,128]{3,2,1,0:T(8,128)S(1)}, f32[6,6,64,128]{3,2,1,0:T(8,128)S(1)}) fusion(f32[6,6,64,1]{3,2,1,0:T(8,128)S(1)} %get-tuple-element.50, f32[6,6,64,125]{3,2,1,0:T(8,128)S(1)} %slice.1102, f32[6,6,64,126]{3,2,1,0:T(8,128)S(1)} %get-tuple-element.48, f32[6,6,64,127]{3,2,1,0:T(8,128)S(1)} %fusion.14, ...), kind=kLoop, calls=%fused_computation.94 | loop fusion | flops 80805888 | bytes 16450572 | tf_op jit(solution)/shard_map/add | solution.py:173
  110.3 3.6 %collective-permute-start.9 = (f32[3,6,64,128]{3,2,1,0:T(8,128)S(1)}, f32[3,6,64,128]{3,2,1,0:T(8,128)S(1)}, u32[]{:S(2)}, u32[]{:S(2)}) collective-permute-start(f32[3,6,64,128]{3,2,1,0:T(8,128)S(1)} %fusion.47), channel_id=1, source_target_pairs={{0,2},{2,4},{4,6},{6,8},{8,10},{10,12},{12,14},{1,3},{3,5},{5,7},{... | collective-permute-start | bytes 1769480 | tf_op jit(solution)/shard_map/ppermute | solution.py:98
  113.9 1.5 collective-permute-start.11
  115.8 23.9 %collective-permute-done.9 = f32[3,6,64,128]{3,2,1,0:T(8,128)S(1)} collective-permute-done((f32[3,6,64,128]{3,2,1,0:T(8,128)S(1)}, f32[3,6,64,128]{3,2,1,0:T(8,128)S(1)}, u32[]{:S(2)}, u32[]{:S(2)}) %collective-permute-start.9) | collective-permute-done | bytes 589856 | tf_op jit(solution)/shard_map/ppermute | solution.py:98
  140.2 0.5 pad_maximum_fusion.3
  141.3 7.5 %fusion.55 = f32[3,6,64,128]{3,2,1,0:T(8,128)S(1)} fusion(f32[3,6,64,128]{3,2,1,0:T(8,128)S(1)} %fusion.47, f32[6,6,64,128]{3,2,1,0:T(8,128)S(1)} %get-tuple-element.18, f32[6,6,64,128]{3,2,1,0:T(8,128)S(1)} %add_multiply_fusion.1, f32[3,11,64,128]{3,2,1,0:T(8,128)S(1)} %fusion.22, f32[8,6,64,128]{3,2,1,0:T(8,128)S(1)} %fusion.8, f32[3]{0:T(128)S(1)} %copy-done.28, ...), kind=kLoop, calls=%fused_computation.143 | loop fusion | flops 40550400 | bytes 10064508 | tf_op jit(solution)/shard_map/add | solution.py:315
  148.7 7.5 %fusion.41 = f32[3,6,64,128]{3,2,1,0:T(8,128)S(1)} fusion(f32[3,6,64,128]{3,2,1,0:T(8,128)S(1)} %fusion.33, f32[6,6,64,128]{3,2,1,0:T(8,128)S(1)} %get-tuple-element.18, f32[6,6,64,128]{3,2,1,0:T(8,128)S(1)} %add_multiply_fusion.1, f32[3,11,64,128]{3,2,1,0:T(8,128)S(1)} %fusion.23, f32[8,6,64,128]{3,2,1,0:T(8,128)S(1)} %fusion.9, f32[]{:T(128)} %bitcast.7, ...), kind=kLoop, calls=%fused_computation.129 | loop fusion | flops 40550400 | bytes 10064508 | tf_op jit(solution)/shard_map/add | solution.py:315
  157.4 0.7 slice_maximum_fusion.1
  158.9 13.1 %multiply_add_fusion = (f32[6,6,64,128]{3,2,1,0:T(8,128)S(1)}, f32[6,6,64,128]{3,2,1,0:T(8,128)S(1)}, f32[6,6,64,128]{3,2,1,0:T(8,128)S(1)}) fusion(f32[6,6,64,1]{3,2,1,0:T(8,128)S(1)} %get-tuple-element.42, f32[6,6,64,125]{3,2,1,0:T(8,128)S(1)} %slice.1181, f32[6,6,64,126]{3,2,1,0:T(8,128)S(1)} %get-tuple-element.40, f32[6,6,64,127]{3,2,1,0:T(8,128)S(1)} %fusion.17, ...), kind=kLoop, calls=%fused_computation.90 | loop fusion | flops 80805888 | bytes 16450572 | tf_op jit(solution)/shard_map/add | solution.py:173
  172.3 1.3 collective-permute-start.13
  173.6 5.3 %collective-permute-start.12 = (f32[3,6,64,128]{3,2,1,0:T(8,128)S(1)}, f32[3,6,64,128]{3,2,1,0:T(8,128)S(1)}, u32[]{:S(2)}, u32[]{:S(2)}) collective-permute-start(f32[3,6,64,128]{3,2,1,0:T(8,128)S(1)} %fusion.55), channel_id=1, source_target_pairs={{0,2},{2,4},{4,6},{6,8},{8,10},{10,12},{12,14},{1,3},{3,5},{5,7},{... | collective-permute-start | bytes 1769480 | tf_op jit(solution)/shard_map/ppermute | solution.py:98
  179.6 11.0 %collective-permute-done.13 = f32[3,6,64,128]{3,2,1,0:T(8,128)S(1)} collective-permute-done((f32[3,6,64,128]{3,2,1,0:T(8,128)S(1)}, f32[3,6,64,128]{3,2,1,0:T(8,128)S(1)}, u32[]{:S(2)}, u32[]{:S(2)}) %collective-permute-start.13) | collective-permute-done | bytes 589856 | tf_op jit(solution)/shard_map/ppermute | solution.py:103
  191.2 12.2 %collective-permute-done.12 = f32[3,6,64,128]{3,2,1,0:T(8,128)S(1)} collective-permute-done((f32[3,6,64,128]{3,2,1,0:T(8,128)S(1)}, f32[3,6,64,128]{3,2,1,0:T(8,128)S(1)}, u32[]{:S(2)}, u32[]{:S(2)}) %collective-permute-start.12) | collective-permute-done | bytes 589856 | tf_op jit(solution)/shard_map/ppermute | solution.py:98
  204.5 14.1 %fusion.21 = f32[6,6,64,128]{3,2,1,0:T(8,128)} fusion(f32[3,6,64,128]{3,2,1,0:T(8,128)S(1)} %fusion.55, f32[3,6,64,128]{3,2,1,0:T(8,128)S(1)} %fusion.41, f32[6,6,64,128]{3,2,1,0:T(8,128)S(1)} %get-tuple-element.20, f32[6,6,64,128]{3,2,1,0:T(8,128)S(1)} %add_multiply_fusion, f32[6,11,64,128]{3,2,1,0:T(8,128)S(1)} %fusion, f32[11,6,64,128]{3,2,1,0:T(8,128)S(1)} %fusion.1, ...), kind=kLoop, calls=%fused_computation.70 | loop fusion | flops 81395712 | bytes 20096208 | tf_op jit(solution)/shard_map/add | solution.py:320
  (133 shorter events, 10.2 us)
Async XLA Ops:
  8.4 12.3 %copy-start = (f32[6,6,64,128]{3,2,1,0:T(8,128)S(1)}, f32[6,6,64,128]{3,2,1,0:T(8,128)}, u32[]{:S(2)}) copy-start(f32[6,6,64,128]{3,2,1,0:T(8,128)} %param.6) | copy-start | bytes 3538948
  8.4 49.0 %collective-permute-start.2 = (f32[2]{0:T(128)}, f32[2]{0:T(128)}, u32[]{:S(2)}, u32[]{:S(2)}) collective-permute-start(f32[2]{0:T(128)} %pad_maximum_fusion.28), channel_id=1, source_target_pairs={{0,3},{1,4},{2,5},{3,6},{4,7},{5,8},{6,9},{7,10},{8,11},{9,12},{10... | collective-permute-start | bytes 32 | tf_op jit(solution)/shard_map/ppermute | solution.py:132
  10.8 47.5 %collective-permute-start.1 = (f32[2]{0:T(128)}, f32[2]{0:T(128)}, u32[]{:S(2)}, u32[]{:S(2)}) collective-permute-start(f32[2]{0:T(128)} %pad_maximum_fusion.28), channel_id=1, source_target_pairs={{0,2},{1,3},{2,4},{3,5},{4,6},{5,7},{6,8},{7,9},{8,10},{9,11},{10,... | collective-permute-start | bytes 32 | tf_op jit(solution)/shard_map/ppermute | solution.py:132
  12.3 46.0 %collective-permute-start = (f32[2]{0:T(128)}, f32[2]{0:T(128)}, u32[]{:S(2)}, u32[]{:S(2)}) collective-permute-start(f32[2]{0:T(128)} %pad_maximum_fusion.28), channel_id=1, source_target_pairs={{0,1},{1,2},{2,3},{3,4},{4,5},{5,6},{6,7},{7,8},{8,9},{9,10},{10,1... | collective-permute-start | bytes 32 | tf_op jit(solution)/shard_map/ppermute | solution.py:132
  15.2 57.4 %collective-permute-start.6 = (f32[3,6,64,128]{3,2,1,0:T(8,128)}, f32[3,6,64,128]{3,2,1,0:T(8,128)}, u32[]{:S(2)}, u32[]{:S(2)}) collective-permute-start(f32[3,6,64,128]{3,2,1,0:T(8,128)} %get-tuple-element.72), channel_id=1, source_target_pairs={{0,2},{2,4},{4,6},{6,8},{8,10},{10,12},{12,14},{1,3},{3,5},{5,7},{... | collective-permute-start | bytes 1769480 | tf_op jit(solution)/shard_map/ppermute | solution.py:98
  19.4 57.7 %collective-permute-start.8 = (f32[3,6,64,128]{3,2,1,0:T(8,128)}, f32[3,6,64,128]{3,2,1,0:T(8,128)}, u32[]{:S(2)}, u32[]{:S(2)}) collective-permute-start(f32[3,6,64,128]{3,2,1,0:T(8,128)} %get-tuple-element.71), channel_id=1, source_target_pairs={{2,0},{4,2},{6,4},{8,6},{10,8},{12,10},{14,12},{3,1},{5,3},{7,5},{... | collective-permute-start | bytes 1769480 | tf_op jit(solution)/shard_map/ppermute | solution.py:103
  22.2 4.3 %copy-start.3 = (f32[3,6,64,1]{3,2,1,0:T(8,128)}, f32[3,6,64,1]{3,2,1,0:T(8,128)S(1)}, u32[]{:S(2)}) copy-start(f32[3,6,64,1]{3,2,1,0:T(8,128)S(1)} %get-tuple-element.109) | copy-start | bytes 13828
  24.3 2.1 copy-start.1
  30.8 0.8 copy-start.23
  36.1 1.6 copy-start.32
  36.2 2.1 copy-start.31
  36.2 2.7 %copy-start.5 = (f32[3,6,70,128]{3,2,1,0:T(8,128)S(1)}, f32[3,6,70,128]{3,2,1,0:T(8,128)}, u32[]{:S(2)}) copy-start(f32[3,6,70,128]{3,2,1,0:T(8,128)} %get-tuple-element.137) | copy-start | bytes 1935364
  36.2 2.8 %copy-start.12 = (f32[3,6,64,127]{3,2,1,0:T(8,128)S(1)}, f32[3,6,64,127]{3,2,1,0:T(8,128)}, u32[]{:S(2)}) copy-start(f32[3,6,64,127]{3,2,1,0:T(8,128)} %get-tuple-element.133) | copy-start | bytes 1755652
  36.2 2.8 %copy-start.13 = (f32[3,6,64,125]{3,2,1,0:T(8,128)S(1)}, f32[3,6,64,125]{3,2,1,0:T(8,128)}, u32[]{:S(2)}) copy-start(f32[3,6,64,125]{3,2,1,0:T(8,128)} %slice.1055) | copy-start | bytes 1728004
  37.1 1.9 copy-start.4
  37.1 1.9 copy-start.9
  37.1 1.9 copy-start.10
  39.0 9.7 %copy-start.11 = (f32[3,6,64,127]{3,2,1,0:T(8,128)S(1)}, f32[3,6,64,127]{3,2,1,0:T(8,128)}, u32[]{:S(2)}) copy-start(f32[3,6,64,127]{3,2,1,0:T(8,128)} %get-tuple-element.134) | copy-start | bytes 1755652
  39.0 9.7 %copy-start.14 = (f32[3,6,64,125]{3,2,1,0:T(8,128)S(1)}, f32[3,6,64,125]{3,2,1,0:T(8,128)}, u32[]{:S(2)}) copy-start(f32[3,6,64,125]{3,2,1,0:T(8,128)} %slice.1020) | copy-start | bytes 1728004
  39.0 9.7 %copy-start.15 = (f32[3,6,64,1]{3,2,1,0:T(8,128)S(1)}, f32[3,6,64,1]{3,2,1,0:T(8,128)}, u32[]{:S(2)}) copy-start(f32[3,6,64,1]{3,2,1,0:T(8,128)} %get-tuple-element.106) | copy-start | bytes 13828
  47.8 0.7 copy-start.24
  47.8 0.8 copy-start.30
  47.8 1.1 copy-start.2
  47.8 1.3 copy-start.7
  47.8 1.4 copy-start.8
  56.1 0.7 copy-start.26
  56.1 1.3 copy-start.25
  57.4 16.5 %collective-permute-start.7 = (f32[6,3,64,128]{3,2,1,0:T(8,128)}, f32[6,3,64,128]{3,2,1,0:T(8,128)}, u32[]{:S(2)}, u32[]{:S(2)}) collective-permute-start(f32[6,3,64,128]{3,2,1,0:T(8,128)} %slice_select_fusion), channel_id=1, source_target_pairs={{0,1},{1,0},{2,3},{3,2},{4,5},{5,4},{6,7},{7,6},{8,9},{9,8},{10,11... | collective-permute-start | bytes 1769480 | tf_op jit(solution)/shard_map/ppermute | solution.py:189
  60.4 4.5 %collective-permute-start.5 = (f32[2]{0:T(128)S(1)}, f32[2]{0:T(128)S(1)}, u32[]{:S(2)}, u32[]{:S(2)}) collective-permute-start(f32[2]{0:T(128)S(1)} %maximum_maximum_fusion.9), channel_id=1, source_target_pairs={{0,12},{1,13},{2,14},{3,15},{4,0},{5,1},{6,2},{7,3},{8,4},{9,5},{1... | collective-permute-start | bytes 32 | tf_op jit(solution)/shard_map/ppermute | solution.py:132
  63.6 4.5 %collective-permute-start.4 = (f32[2]{0:T(128)S(1)}, f32[2]{0:T(128)S(1)}, u32[]{:S(2)}, u32[]{:S(2)}) collective-permute-start(f32[2]{0:T(128)S(1)} %maximum_maximum_fusion.9), channel_id=1, source_target_pairs={{0,8},{1,9},{2,10},{3,11},{4,12},{5,13},{6,14},{7,15},{8,0},{9,1},... | collective-permute-start | bytes 32 | tf_op jit(solution)/shard_map/ppermute | solution.py:132
  64.9 5.6 %collective-permute-start.3 = (f32[2]{0:T(128)S(1)}, f32[2]{0:T(128)S(1)}, u32[]{:S(2)}, u32[]{:S(2)}) collective-permute-start(f32[2]{0:T(128)S(1)} %maximum_maximum_fusion.9), channel_id=1, source_target_pairs={{0,4},{1,5},{2,6},{3,7},{4,8},{5,9},{6,10},{7,11},{8,12},{9,13},{1... | collective-permute-start | bytes 32 | tf_op jit(solution)/shard_map/ppermute | solution.py:132
  72.5 1.4 copy-start.16
  72.5 1.4 copy-start.17
  72.5 1.4 copy-start.18
  72.5 1.4 copy-start.19
  72.5 1.4 copy-start.20
  72.6 1.4 copy-start.21
  72.6 1.4 copy-start.22
  78.3 1.1 copy-start.6
  78.3 1.1 copy-start.28
  79.4 7.4 %copy-start.27 = (f32[3]{0:T(128)S(1)}, f32[3]{0:T(128)}, u32[]{:S(2)}) copy-start(f32[3]{0:T(128)} %get-tuple-element.119) | copy-start | bytes 40
  96.9 18.5 %collective-permute-start.10 = (f32[6,3,64,128]{3,2,1,0:T(8,128)S(1)}, f32[6,3,64,128]{3,2,1,0:T(8,128)S(1)}, u32[]{:S(2)}, u32[]{:S(2)}) collective-permute-start(f32[6,3,64,128]{3,2,1,0:T(8,128)S(1)} %fusion.57), channel_id=1, source_target_pairs={{0,1},{1,0},{2,3},{3,2},{4,5},{5,4},{6,7},{7,6},{8,9},{9,8},{10,11... | collective-permute-start | bytes 1769480 | tf_op jit(solution)/shard_map/ppermute | solution.py:189
  110.3 29.4 %collective-permute-start.9 = (f32[3,6,64,128]{3,2,1,0:T(8,128)S(1)}, f32[3,6,64,128]{3,2,1,0:T(8,128)S(1)}, u32[]{:S(2)}, u32[]{:S(2)}) collective-permute-start(f32[3,6,64,128]{3,2,1,0:T(8,128)S(1)} %fusion.47), channel_id=1, source_target_pairs={{0,2},{2,4},{4,6},{6,8},{8,10},{10,12},{12,14},{1,3},{3,5},{5,7},{... | collective-permute-start | bytes 1769480 | tf_op jit(solution)/shard_map/ppermute | solution.py:98
  113.9 26.1 %collective-permute-start.11 = (f32[3,6,64,128]{3,2,1,0:T(8,128)S(1)}, f32[3,6,64,128]{3,2,1,0:T(8,128)S(1)}, u32[]{:S(2)}, u32[]{:S(2)}) collective-permute-start(f32[3,6,64,128]{3,2,1,0:T(8,128)S(1)} %fusion.33), channel_id=1, source_target_pairs={{2,0},{4,2},{6,4},{8,6},{10,8},{12,10},{14,12},{3,1},{5,3},{7,5},{... | collective-permute-start | bytes 1769480 | tf_op jit(solution)/shard_map/ppermute | solution.py:103
  172.2 6.9 %collective-permute-start.14 = (f32[6,3,64,128]{3,2,1,0:T(8,128)S(1)}, f32[6,3,64,128]{3,2,1,0:T(8,128)S(1)}, u32[]{:S(2)}, u32[]{:S(2)}) collective-permute-start(f32[6,3,64,128]{3,2,1,0:T(8,128)S(1)} %fusion.60), channel_id=1, source_target_pairs={{0,1},{1,0},{2,3},{3,2},{4,5},{5,4},{6,7},{7,6},{8,9},{9,8},{10,11... | collective-permute-start | bytes 1769480 | tf_op jit(solution)/shard_map/ppermute | solution.py:189
  172.3 18.4 %collective-permute-start.13 = (f32[3,6,64,128]{3,2,1,0:T(8,128)S(1)}, f32[3,6,64,128]{3,2,1,0:T(8,128)S(1)}, u32[]{:S(2)}, u32[]{:S(2)}) collective-permute-start(f32[3,6,64,128]{3,2,1,0:T(8,128)S(1)} %fusion.41), channel_id=1, source_target_pairs={{2,0},{4,2},{6,4},{8,6},{10,8},{12,10},{14,12},{3,1},{5,3},{7,5},{... | collective-permute-start | bytes 1769480 | tf_op jit(solution)/shard_map/ppermute | solution.py:103
  173.6 29.9 %collective-permute-start.12 = (f32[3,6,64,128]{3,2,1,0:T(8,128)S(1)}, f32[3,6,64,128]{3,2,1,0:T(8,128)S(1)}, u32[]{:S(2)}, u32[]{:S(2)}) collective-permute-start(f32[3,6,64,128]{3,2,1,0:T(8,128)S(1)} %fusion.55), channel_id=1, source_target_pairs={{0,2},{2,4},{4,6},{6,8},{8,10},{10,12},{12,14},{1,3},{3,5},{5,7},{... | collective-permute-start | bytes 1769480 | tf_op jit(solution)/shard_map/ppermute | solution.py:98
  203.9 0.6 copy-start.29

commit v5 on v4

--- a/solution.py
+++ b/solution.py
@@ -1,9 +1,12 @@
+import functools
 import math
 
 import jax
 import numpy as np
 import jax.numpy as jnp
 from jax import lax
+from jax.experimental import pallas as pl
+from jax.experimental.pallas import tpu as pltpu
 from jax.sharding import PartitionSpec as P
 
 
@@ -91,6 +94,59 @@
         return differences
 
     return both_sides(window)
+
+
+def local_kernel(params_ref, field_ref, mean_ref, partial_ref, *, step_psi, step_speed):
+    rows, n_psi, n_speed = field_ref.shape[1:]
+    turn_b = params_ref[2]
+    accel = params_ref[3]
+    alpha_three = params_ref[1] + params_ref[2]
+    alpha_four = params_ref[3]
+    lane = lax.broadcasted_iota(jnp.int32, (n_psi, n_speed), 1)
+
+    def body(row, carry):
+        cells = field_ref[0, row]
+        diff = (cells - pltpu.roll(cells, 1, 0)) / step_psi
+        psi = [pltpu.roll(diff, (2 - offset) % n_psi, 0) for offset in range(6)]
+        back_three = weno_value(psi[0], psi[1], psi[2], psi[3], psi[4])
+        fore_three = weno_value(psi[5], psi[4], psi[3], psi[2], psi[1])
+        raw = (cells - pltpu.roll(cells, 1, 1)) / step_speed
+        diff_v = jnp.where(lane == 0, pltpu.roll(raw, n_speed - 1, 1), raw)
+        up_one = jnp.where(lane == n_speed - 1, diff_v, pltpu.roll(diff_v, n_speed - 1, 1))
+        up_two = jnp.where(lane >= n_speed - 2, up_one, pltpu.roll(diff_v, n_speed - 2, 1))
+        up_three = jnp.where(lane >= n_speed - 3, up_two, pltpu.roll(diff_v, n_speed - 3, 1))
+        down_one = jnp.where(lane == 0, diff_v, pltpu.roll(diff_v, 1, 1))
+        down_two = jnp.where(lane <= 1, down_one, pltpu.roll(diff_v, 2, 1))
+        back_four = weno_value(down_two, down_one, diff_v, up_one, up_two)
+        fore_four = weno_value(up_three, up_two, up_one, diff_v, down_one)
+        mean_three = 0.5 * (back_three + fore_three)
+        mean_four = 0.5 * (back_four + fore_four)
+        partial = -turn_b * jnp.abs(mean_three) + accel * jnp.abs(mean_four)
+        partial = partial + 0.5 * (
+            alpha_three * (fore_three - back_three) + alpha_four * (fore_four - back_four)
+        )
+        mean_ref[0, row] = mean_three
+        partial_ref[0, row] = partial
+        return carry
+
+    lax.fori_loop(0, rows, body, 0)
+
+
+def local_pallas(field, params, start, planes):
+    rows, n_psi, n_speed = field.shape[1:]
+    kernel = functools.partial(
+        local_kernel, step_psi=2.0 * math.pi / n_psi, step_speed=1.0 / n_speed
+    )
+    source = pl.BlockSpec((1, rows, n_psi, n_speed), lambda i: (i + start, 0, 0, 0))
+    block = pl.BlockSpec((1, rows, n_psi, n_speed), lambda i: (i, 0, 0, 0))
+    shape = jax.ShapeDtypeStruct((planes, rows, n_psi, n_speed), jnp.float32)
+    return pl.pallas_call(
+        kernel,
+        grid=(planes,),
+        in_specs=[pl.BlockSpec(memory_space=pltpu.SMEM), source],
+        out_specs=[block, block],
+        out_shape=[shape, shape],
+    )(params, field)
 
 
 def send_low(piece, axis):
@@ -174,12 +230,6 @@
             alpha_three * (fore_three - back_three) + alpha_four * (fore_four - back_four)
         )
         return mean_three, partial
-
-    def local_halves(field):
-        pieces = []
-        for side in (0, 1):
-            pieces.append(lax.optimization_barrier(local_part(cut(field, side))))
-        return pieces
 
     def y_halo(field):
         tail = lax.slice_in_dim(field, cells_y - 3, cells_y, axis=1)
@@ -222,7 +272,11 @@
         jnp.maximum(drift[1] + second_hi, -(drift[1] + second_lo))
         + params[1] * jnp.abs(x_coord)[:, None]
     )
-    locals_now = local_halves(values)
+    locals_now = []
+    for side in (0, 1):
+        start = 0 if side == 0 else half
+        count = half if side == 0 else cells_x - half
+        locals_now.append(tuple(local_pallas(values, params, start, count)))
     bounds = spread_max(jnp.stack([local_one, local_two]), ("gx", "gy"))
     bound_one = bounds[0]
     bound_two = bounds[1]

time: 220 us -> 220 us (level)
  Pallas kernels: 0 us -> 23.7 us
  other arithmetic: 118 us -> 95.7 us
  waiting for transfers between devices: 51.6 us -> 61.3 us
  local copies, waits for them, and re-layouts: 14.4 us -> 6 us
    pallas_call x0 -> x2, Pallas kernels: none -> 23.7 us  [local_pallas(): pl.pallas_call(kernel, grid=(planes,), in_specs=[pl.BlockSpec(memory_spac...]
    add x4 -> x2, other arithmetic: 41.7 us -> 26.2 us  [local_part(): partial + 0.5 * (alpha_three * (fore_three - back_three) + alpha_four * (...]
    ppermute x6, waiting for transfers between devices: 4.53 us -> 13.2 us  [spread_max(): lax.ppermute(local, axes, [(i, (i + k * span) % count) for i in range(cou...]
    concatenate x6 -> x4, other arithmetic: 5.72 us -> 2.1 us  [clamped_sided(): jnp.concatenate([lax.slice_in_dim(inner, 0, 1, axis=along), inner], axis=...]
    slice x1, local copies, waits for them, and re-layouts: 2.39 us -> 0.11 us  [cut(): return array[:half]]
    concatenate x3 -> x2, other arithmetic: 2.51 us -> 0.29 us  [periodic_sided(): jnp.concatenate([lax.slice_in_dim(field, extent - 3, extent, axis=along),...]
  transfers between devices with their start and end apart: 15 -> 15, of which waited for: 6 -> 5; matrix products, arithmetic and copies ran while one was open for 26% -> 12% of each run, Pallas kernels for 0% -> 11%
where the time goes in v5:
time: 220 us; the launch traced here: 219 us
  other arithmetic  95.7 us (44%)
  waiting for transfers between devices  61.3 us (28%)
  starting transfers between devices  26.5 us (12%)
  Pallas kernels  23.7 us (11%)
  local copies, waits for them, and re-layouts  6 us (3%)
  between operations  5.98 us (3%)
    ppermute x3, waiting for transfers between devices, send_low(): lax.ppermute(piece, axis, [(i, (i + 1) % count) for i in range(count - 1)])  37 us
    add x2, other arithmetic, local_part(): partial + 0.5 * (alpha_three * (fore_three - back_three) + alpha_four * (...  26.2 us
    pallas_call x2, Pallas kernels, local_pallas(): pl.pallas_call(kernel, grid=(planes,), in_specs=[pl.BlockSpec(memory_spac...  23.7 us
    add x2, other arithmetic, on_device(): 0.75 * cut(values, side) + 0.25 * (cut(first, side) + step_time * rate)  15 us
    add x2, other arithmetic, on_device(): cut(values, side) + step_time * rate  15 us
    add x1, other arithmetic, on_device(): cut(values, side) * (1.0 / 3.0)  14.2 us
    ppermute x6, waiting for transfers between devices, spread_max(): lax.ppermute(local, axes, [(i, (i + k * span) % count) for i in range(cou...  13.2 us
    ppermute x3, waiting for transfers between devices, send_high(): lax.ppermute(piece, axis, [((i + 1) % count, i) for i in range(count - 1)])  11 us
  transfers between devices with their start and end apart: 15, of which 5 were waited for; matrix products, arithmetic and copies ran while one was open for 12% of the time, Pallas kernels for 11%

profile of v5, /device:TPU:0, one launch (start us, length us, event | category | flops | bytes accessed | tf_op | source)
XLA Modules:
  0.0 219.1 jit_solution(8903195565279416668)
XLA Ops:
  0.0 1.4 fusion.90
  1.5 0.8 fusion.89
  2.2 1.1 abs_multiply_fusion
  3.4 1.2 abs_multiply_fusion.1
  5.9 1.3 add_reduce_fusion
  7.2 0.7 add_reduce_fusion.1
  7.9 1.9 pad_maximum_fusion.20
  9.8 2.4 %collective-permute-start.2 = (f32[2]{0:T(128)}, f32[2]{0:T(128)}, u32[]{:S(2)}, u32[]{:S(2)}) collective-permute-start(f32[2]{0:T(128)} %pad_maximum_fusion.20), channel_id=1, source_target_pairs={{0,3},{1,4},{2,5},{3,6},{4,7},{5,8},{6,9},{7,10},{8,11},{9,12},{10... | collective-permute-start | bytes 32 | tf_op jit(solution)/shard_map/ppermute | solution.py:188
  12.2 1.5 collective-permute-start.1
  13.7 0.5 collective-permute-start
  14.2 2.1 slice_select_fusion
  16.3 1.2 collective-permute-start.7
  17.6 4.2 %collective-permute-start.6 = (f32[3,6,64,128]{3,2,1,0:T(8,128)S(1)}, f32[3,6,64,128]{3,2,1,0:T(8,128)}, u32[]{:S(2)}, u32[]{:S(2)}) collective-permute-start(f32[3,6,64,128]{3,2,1,0:T(8,128)S(1)} %get-tuple-element.60), channel_id=1, source_target_pairs={{0,2},{2,4},{4,6},{6,8},{8,10},{10,12},{12,14},{1,3},{3,5},{5,7},{... | collective-permute-start | bytes 1769480 | tf_op jit(solution)/shard_map/ppermute | solution.py:154
  21.9 0.8 slice_bitcast_fusion.13
  22.8 0.6 copy-done.8
  23.4 0.6 slice_multiply_fusion.1
  24.0 0.6 broadcast_multiply_fusion
  24.7 0.7 broadcast_multiply_fusion.1
  25.6 11.8 %shard_map.65 = (f32[3,6,64,128]{3,2,1,0:T(8,128)}, f32[3,6,64,128]{3,2,1,0:T(8,128)}) custom-call(f32[4]{0:T(128)} %params_ref.3, f32[6,6,64,128]{3,2,1,0:T(8,128)} %field_ref.3), custom_call_target="tpu_custom_call" | custom-call | tf_op jit(solution)/shard_map/pallas_call | solution.py:143
  37.4 11.8 %shard_map.64 = (f32[3,6,64,128]{3,2,1,0:T(8,128)}, f32[3,6,64,128]{3,2,1,0:T(8,128)}) custom-call(f32[4]{0:T(128)} %params_ref.3, f32[6,6,64,128]{3,2,1,0:T(8,128)} %field_ref.3), custom_call_target="tpu_custom_call" | custom-call | tf_op jit(solution)/shard_map/pallas_call | solution.py:143
  51.9 1.3 collective-permute-start.8
  53.2 2.1 maximum_maximum_fusion.5
  55.3 3.5 %collective-permute-start.5 = (f32[2]{0:T(128)S(1)}, f32[2]{0:T(128)S(1)}, u32[]{:S(2)}, u32[]{:S(2)}) collective-permute-start(f32[2]{0:T(128)S(1)} %maximum_maximum_fusion.5), channel_id=1, source_target_pairs={{0,12},{1,13},{2,14},{3,15},{4,0},{5,1},{6,2},{7,3},{8,4},{9,5},{1... | collective-permute-start | bytes 32 | tf_op jit(solution)/shard_map/ppermute | solution.py:188
  58.7 0.8 collective-permute-start.4
  59.5 9.4 %collective-permute-done.5 = f32[2]{0:T(128)S(1)} collective-permute-done((f32[2]{0:T(128)S(1)}, f32[2]{0:T(128)S(1)}, u32[]{:S(2)}, u32[]{:S(2)}) %collective-permute-start.5) | collective-permute-done | bytes 40 | tf_op jit(solution)/shard_map/ppermute | solution.py:188
  68.9 1.6 collective-permute-start.3
  70.5 3.8 %collective-permute-done.3 = f32[2]{0:T(128)S(1)} collective-permute-done((f32[2]{0:T(128)S(1)}, f32[2]{0:T(128)S(1)}, u32[]{:S(2)}, u32[]{:S(2)}) %collective-permute-start.3) | collective-permute-done | bytes 40 | tf_op jit(solution)/shard_map/ppermute | solution.py:188
  74.3 0.7 fusion.91
  76.5 1.3 add_select_fusion.15
  77.8 0.3 pad_maximum_fusion.10
  78.5 1.3 add_select_fusion.5
  79.9 0.5 fusion.7
  80.5 0.5 copy-done.4
  81.2 7.5 %fusion.45 = f32[3,6,64,128]{3,2,1,0:T(8,128)S(1)} fusion(f32[3,6,64,128]{3,2,1,0:T(8,128)S(1)} %copy-done.5, f32[3,6,64,128]{3,2,1,0:T(8,128)S(1)} %copy-done.4, f32[3,11,64,128]{3,2,1,0:T(8,128)S(1)} %fusion.24, f32[8,6,64,128]{3,2,1,0:T(8,128)S(1)} %get-tuple-element.46, f32[3]{0:T(128)S(1)} %copy-done.12, f32[3,6,64]{2,1,0:T(8,128)S(1)} %get-tuple-element.98, ...), kind=kLoop, calls=%fused_computation.129 | loop fusion | flops 40108032 | bytes 9474684 | tf_op jit(solution)/shard_map/add | solution.py:365
  88.7 7.4 %fusion.31 = f32[3,6,64,128]{3,2,1,0:T(8,128)S(1)} fusion(f32[3,6,64,128]{3,2,1,0:T(8,128)S(1)} %copy-done.3, f32[3,6,64,128]{3,2,1,0:T(8,128)S(1)} %copy-done.2, f32[3,11,64,128]{3,2,1,0:T(8,128)S(1)} %fusion.25, f32[8,6,64,128]{3,2,1,0:T(8,128)S(1)} %get-tuple-element.45, f32[]{:T(128)} %bitcast.7, f32[]{:T(128)} %bitcast.6, f32[3]{0:T(128)S(1)} %copy-done.11, ...), kind=kLoop, calls=%fused_computation.115 | loop fusion | flops 40108032 | bytes 9474684 | tf_op jit(solution)/shard_map/add | solution.py:365
  96.2 0.4 fusion.14
  96.6 0.4 fusion.86
  97.0 0.4 slice.900
  97.4 0.7 slice_maximum_fusion.3
  98.0 0.4 slice_maximum_fusion.2
  99.0 13.1 %multiply_add_fusion.1 = (f32[6,6,64,128]{3,2,1,0:T(8,128)S(1)}, f32[6,6,64,128]{3,2,1,0:T(8,128)S(1)}, f32[6,6,64,128]{3,2,1,0:T(8,128)S(1)}) fusion(f32[6,6,64,1]{3,2,1,0:T(8,128)S(1)} %get-tuple-element.44, f32[6,6,64,125]{3,2,1,0:T(8,128)S(1)} %slice.900, f32[6,6,64,126]{3,2,1,0:T(8,128)S(1)} %get-tuple-element.42, f32[6,6,64,127]{3,2,1,0:T(8,128)S(1)} %fusion.14, ...), kind=kLoop, calls=%fused_computation.94 | loop fusion | flops 80805888 | bytes 16450572 | tf_op jit(solution)/shard_map/add | solution.py:229
  112.3 1.5 collective-permute-start.9
  113.8 1.3 collective-permute-start.11
  115.2 0.2 add_select_fusion.11
  115.6 24.2 %collective-permute-done.9 = f32[3,6,64,128]{3,2,1,0:T(8,128)S(1)} collective-permute-done((f32[3,6,64,128]{3,2,1,0:T(8,128)S(1)}, f32[3,6,64,128]{3,2,1,0:T(8,128)S(1)}, u32[]{:S(2)}, u32[]{:S(2)}) %collective-permute-start.9) | collective-permute-done | bytes 589856 | tf_op jit(solution)/shard_map/ppermute | solution.py:154
  140.2 0.4 pad_maximum_fusion.3
  141.3 7.5 %fusion.53 = f32[3,6,64,128]{3,2,1,0:T(8,128)S(1)} fusion(f32[3,6,64,128]{3,2,1,0:T(8,128)S(1)} %fusion.45, f32[6,6,64,128]{3,2,1,0:T(8,128)S(1)} %get-tuple-element.18, f32[6,6,64,128]{3,2,1,0:T(8,128)S(1)} %add_multiply_fusion.1, f32[3,11,64,128]{3,2,1,0:T(8,128)S(1)} %fusion.22, f32[8,6,64,128]{3,2,1,0:T(8,128)S(1)} %fusion.8, f32[3]{0:T(128)S(1)} %copy-done.12, ...), kind=kLoop, calls=%fused_computation.137 | loop fusion | flops 40550400 | bytes 10064508 | tf_op jit(solution)/shard_map/add | solution.py:369
  148.8 7.5 %fusion.39 = f32[3,6,64,128]{3,2,1,0:T(8,128)S(1)} fusion(f32[3,6,64,128]{3,2,1,0:T(8,128)S(1)} %fusion.31, f32[6,6,64,128]{3,2,1,0:T(8,128)S(1)} %get-tuple-element.18, f32[6,6,64,128]{3,2,1,0:T(8,128)S(1)} %add_multiply_fusion.1, f32[3,11,64,128]{3,2,1,0:T(8,128)S(1)} %fusion.23, f32[8,6,64,128]{3,2,1,0:T(8,128)S(1)} %fusion.9, f32[]{:T(128)} %bitcast.7, ...), kind=kLoop, calls=%fused_computation.123 | loop fusion | flops 40550400 | bytes 10064508 | tf_op jit(solution)/shard_map/add | solution.py:369
  156.3 0.4 fusion.17
  156.7 0.4 fusion.85
  157.1 0.4 slice.979
  157.5 0.7 slice_maximum_fusion.1
  158.2 0.4 slice_maximum_fusion
  159.0 13.1 %multiply_add_fusion = (f32[6,6,64,128]{3,2,1,0:T(8,128)S(1)}, f32[6,6,64,128]{3,2,1,0:T(8,128)S(1)}, f32[6,6,64,128]{3,2,1,0:T(8,128)S(1)}) fusion(f32[6,6,64,1]{3,2,1,0:T(8,128)S(1)} %get-tuple-element.36, f32[6,6,64,125]{3,2,1,0:T(8,128)S(1)} %slice.979, f32[6,6,64,126]{3,2,1,0:T(8,128)S(1)} %get-tuple-element.34, f32[6,6,64,127]{3,2,1,0:T(8,128)S(1)} %fusion.17, ...), kind=kLoop, calls=%fused_computation.90 | loop fusion | flops 80805888 | bytes 16450572 | tf_op jit(solution)/shard_map/add | solution.py:229
  172.4 1.3 collective-permute-start.13
  173.7 5.3 %collective-permute-start.12 = (f32[3,6,64,128]{3,2,1,0:T(8,128)S(1)}, f32[3,6,64,128]{3,2,1,0:T(8,128)S(1)}, u32[]{:S(2)}, u32[]{:S(2)}) collective-permute-start(f32[3,6,64,128]{3,2,1,0:T(8,128)S(1)} %fusion.53), channel_id=1, source_target_pairs={{0,2},{2,4},{4,6},{6,8},{8,10},{10,12},{12,14},{1,3},{3,5},{5,7},{... | collective-permute-start | bytes 1769480 | tf_op jit(solution)/shard_map/ppermute | solution.py:154
  179.1 0.3 add_select_fusion.1
  179.4 0.3 pad_maximum_fusion.2
  179.7 11.0 %collective-permute-done.13 = f32[3,6,64,128]{3,2,1,0:T(8,128)S(1)} collective-permute-done((f32[3,6,64,128]{3,2,1,0:T(8,128)S(1)}, f32[3,6,64,128]{3,2,1,0:T(8,128)S(1)}, u32[]{:S(2)}, u32[]{:S(2)}) %collective-permute-start.13) | collective-permute-done | bytes 589856 | tf_op jit(solution)/shard_map/ppermute | solution.py:159
  190.9 0.4 fusion
  191.3 12.8 %collective-permute-done.12 = f32[3,6,64,128]{3,2,1,0:T(8,128)S(1)} collective-permute-done((f32[3,6,64,128]{3,2,1,0:T(8,128)S(1)}, f32[3,6,64,128]{3,2,1,0:T(8,128)S(1)}, u32[]{:S(2)}, u32[]{:S(2)}) %collective-permute-start.12) | collective-permute-done | bytes 589856 | tf_op jit(solution)/shard_map/ppermute | solution.py:154
  204.3 0.2 pad_maximum_fusion.1
  204.6 0.3 fusion.1
  204.9 14.2 %fusion.21 = f32[6,6,64,128]{3,2,1,0:T(8,128)} fusion(f32[3,6,64,128]{3,2,1,0:T(8,128)S(1)} %fusion.53, f32[3,6,64,128]{3,2,1,0:T(8,128)S(1)} %fusion.39, f32[6,6,64,128]{3,2,1,0:T(8,128)S(1)} %get-tuple-element.20, f32[6,6,64,128]{3,2,1,0:T(8,128)S(1)} %add_multiply_fusion, f32[6,11,64,128]{3,2,1,0:T(8,128)S(1)} %fusion, f32[11,6,64,128]{3,2,1,0:T(8,128)S(1)} %fusion.1, ...), kind=kLoop, calls=%fused_computation.70 | loop fusion | flops 81395712 | bytes 20096208 | tf_op jit(solution)/shard_map/add | solution.py:374
  (86 shorter events, 4.3 us)
Async XLA Ops:
  0.0 17.5 %copy-start = (f32[6,6,64,128]{3,2,1,0:T(8,128)S(1)}, f32[6,6,64,128]{3,2,1,0:T(8,128)}, u32[]{:S(2)}) copy-start(f32[6,6,64,128]{3,2,1,0:T(8,128)} %field_ref.3) | copy-start | bytes 3538948
  9.8 42.1 %collective-permute-start.2 = (f32[2]{0:T(128)}, f32[2]{0:T(128)}, u32[]{:S(2)}, u32[]{:S(2)}) collective-permute-start(f32[2]{0:T(128)} %pad_maximum_fusion.20), channel_id=1, source_target_pairs={{0,3},{1,4},{2,5},{3,6},{4,7},{5,8},{6,9},{7,10},{8,11},{9,12},{10... | collective-permute-start | bytes 32 | tf_op jit(solution)/shard_map/ppermute | solution.py:188
  12.2 41.0 %collective-permute-start.1 = (f32[2]{0:T(128)}, f32[2]{0:T(128)}, u32[]{:S(2)}, u32[]{:S(2)}) collective-permute-start(f32[2]{0:T(128)} %pad_maximum_fusion.20), channel_id=1, source_target_pairs={{0,2},{1,3},{2,4},{3,5},{4,6},{5,7},{6,8},{7,9},{8,10},{9,11},{10,... | collective-permute-start | bytes 32 | tf_op jit(solution)/shard_map/ppermute | solution.py:188
  13.7 39.5 %collective-permute-start = (f32[2]{0:T(128)}, f32[2]{0:T(128)}, u32[]{:S(2)}, u32[]{:S(2)}) collective-permute-start(f32[2]{0:T(128)} %pad_maximum_fusion.20), channel_id=1, source_target_pairs={{0,1},{1,2},{2,3},{3,4},{4,5},{5,6},{6,7},{7,8},{8,9},{9,10},{10,1... | collective-permute-start | bytes 32 | tf_op jit(solution)/shard_map/ppermute | solution.py:188
  16.3 60.2 %collective-permute-start.7 = (f32[6,3,64,128]{3,2,1,0:T(8,128)}, f32[6,3,64,128]{3,2,1,0:T(8,128)}, u32[]{:S(2)}, u32[]{:S(2)}) collective-permute-start(f32[6,3,64,128]{3,2,1,0:T(8,128)} %slice_select_fusion), channel_id=1, source_target_pairs={{0,1},{1,0},{2,3},{3,2},{4,5},{5,4},{6,7},{7,6},{8,9},{9,8},{10,11... | collective-permute-start | bytes 1769480 | tf_op jit(solution)/shard_map/ppermute | solution.py:239
  17.6 58.7 %collective-permute-start.6 = (f32[3,6,64,128]{3,2,1,0:T(8,128)S(1)}, f32[3,6,64,128]{3,2,1,0:T(8,128)}, u32[]{:S(2)}, u32[]{:S(2)}) collective-permute-start(f32[3,6,64,128]{3,2,1,0:T(8,128)S(1)} %get-tuple-element.60), channel_id=1, source_target_pairs={{0,2},{2,4},{4,6},{6,8},{8,10},{10,12},{12,14},{1,3},{3,5},{5,7},{... | collective-permute-start | bytes 1769480 | tf_op jit(solution)/shard_map/ppermute | solution.py:154
  22.7 0.7 copy-start.8
  22.7 0.7 copy-start.10
  22.7 1.4 copy-start.15
  22.7 2.0 copy-start.14
  22.7 2.8 %copy-start.13 = (f32[128]{0:T(128)S(1)}, f32[128]{0:T(128)}, u32[]{:S(2)}) copy-start(f32[128]{0:T(128)} %constant.418) | copy-start | bytes 1540
  37.4 39.1 %copy-start.6 = (f32[3,64,128]{2,1,0:T(8,128)S(1)}, f32[3,64,128]{2,1,0:T(8,128)}, u32[]{:S(2)}) copy-start(f32[3,64,128]{2,1,0:T(8,128)} %get-tuple-element.55) | copy-start | bytes 294916
  37.4 39.1 %copy-start.7 = (f32[3,64,128]{2,1,0:T(8,128)S(1)}, f32[3,64,128]{2,1,0:T(8,128)}, u32[]{:S(2)}) copy-start(f32[3,64,128]{2,1,0:T(8,128)} %get-tuple-element.56) | copy-start | bytes 294916
  51.9 26.6 %collective-permute-start.8 = (f32[3,6,64,128]{3,2,1,0:T(8,128)S(1)}, f32[3,6,64,128]{3,2,1,0:T(8,128)}, u32[]{:S(2)}, u32[]{:S(2)}) collective-permute-start(f32[3,6,64,128]{3,2,1,0:T(8,128)S(1)} %get-tuple-element.59), channel_id=1, source_target_pairs={{2,0},{4,2},{6,4},{8,6},{10,8},{12,10},{14,12},{3,1},{5,3},{7,5},{... | collective-permute-start | bytes 1769480 | tf_op jit(solution)/shard_map/ppermute | solution.py:159
  55.3 13.7 %collective-permute-start.5 = (f32[2]{0:T(128)S(1)}, f32[2]{0:T(128)S(1)}, u32[]{:S(2)}, u32[]{:S(2)}) collective-permute-start(f32[2]{0:T(128)S(1)} %maximum_maximum_fusion.5), channel_id=1, source_target_pairs={{0,12},{1,13},{2,14},{3,15},{4,0},{5,1},{6,2},{7,3},{8,4},{9,5},{1... | collective-permute-start | bytes 32 | tf_op jit(solution)/shard_map/ppermute | solution.py:188
  58.7 11.8 %collective-permute-start.4 = (f32[2]{0:T(128)S(1)}, f32[2]{0:T(128)S(1)}, u32[]{:S(2)}, u32[]{:S(2)}) collective-permute-start(f32[2]{0:T(128)S(1)} %maximum_maximum_fusion.5), channel_id=1, source_target_pairs={{0,8},{1,9},{2,10},{3,11},{4,12},{5,13},{6,14},{7,15},{8,0},{9,1},... | collective-permute-start | bytes 32 | tf_op jit(solution)/shard_map/ppermute | solution.py:188
  68.9 5.4 %collective-permute-start.3 = (f32[2]{0:T(128)S(1)}, f32[2]{0:T(128)S(1)}, u32[]{:S(2)}, u32[]{:S(2)}) collective-permute-start(f32[2]{0:T(128)S(1)} %maximum_maximum_fusion.5), channel_id=1, source_target_pairs={{0,4},{1,5},{2,6},{3,7},{4,8},{5,9},{6,10},{7,11},{8,12},{9,13},{1... | collective-permute-start | bytes 32 | tf_op jit(solution)/shard_map/ppermute | solution.py:188
  78.5 1.5 copy-start.1
  79.9 1.1 copy-start.4
  79.9 1.2 copy-start.5
  79.9 1.2 copy-start.9
  79.9 1.2 copy-start.12
  81.2 7.6 %copy-start.2 = (f32[3,6,64,128]{3,2,1,0:T(8,128)S(1)}, f32[3,6,64,128]{3,2,1,0:T(8,128)}, u32[]{:S(2)}) copy-start(f32[3,6,64,128]{3,2,1,0:T(8,128)} %get-tuple-element.13) | copy-start | bytes 1769476
  81.2 7.6 %copy-start.3 = (f32[3,6,64,128]{3,2,1,0:T(8,128)S(1)}, f32[3,6,64,128]{3,2,1,0:T(8,128)}, u32[]{:S(2)}) copy-start(f32[3,6,64,128]{3,2,1,0:T(8,128)} %get-tuple-element.14) | copy-start | bytes 1769476
  81.2 7.6 %copy-start.11 = (f32[3]{0:T(128)S(1)}, f32[3]{0:T(128)}, u32[]{:S(2)}) copy-start(f32[3]{0:T(128)} %get-tuple-element.99) | copy-start | bytes 40
  98.9 16.3 %collective-permute-start.10 = (f32[6,3,64,128]{3,2,1,0:T(8,128)S(1)}, f32[6,3,64,128]{3,2,1,0:T(8,128)S(1)}, u32[]{:S(2)}, u32[]{:S(2)}) collective-permute-start(f32[6,3,64,128]{3,2,1,0:T(8,128)S(1)} %fusion.55), channel_id=1, source_target_pairs={{0,1},{1,0},{2,3},{3,2},{4,5},{5,4},{6,7},{7,6},{8,9},{9,8},{10,11... | collective-permute-start | bytes 1769480 | tf_op jit(solution)/shard_map/ppermute | solution.py:239
  112.3 27.4 %collective-permute-start.9 = (f32[3,6,64,128]{3,2,1,0:T(8,128)S(1)}, f32[3,6,64,128]{3,2,1,0:T(8,128)S(1)}, u32[]{:S(2)}, u32[]{:S(2)}) collective-permute-start(f32[3,6,64,128]{3,2,1,0:T(8,128)S(1)} %fusion.45), channel_id=1, source_target_pairs={{0,2},{2,4},{4,6},{6,8},{8,10},{10,12},{12,14},{1,3},{3,5},{5,7},{... | collective-permute-start | bytes 1769480 | tf_op jit(solution)/shard_map/ppermute | solution.py:154
  113.8 26.2 %collective-permute-start.11 = (f32[3,6,64,128]{3,2,1,0:T(8,128)S(1)}, f32[3,6,64,128]{3,2,1,0:T(8,128)S(1)}, u32[]{:S(2)}, u32[]{:S(2)}) collective-permute-start(f32[3,6,64,128]{3,2,1,0:T(8,128)S(1)} %fusion.31), channel_id=1, source_target_pairs={{2,0},{4,2},{6,4},{8,6},{10,8},{12,10},{14,12},{3,1},{5,3},{7,5},{... | collective-permute-start | bytes 1769480 | tf_op jit(solution)/shard_map/ppermute | solution.py:159
  172.3 6.8 %collective-permute-start.14 = (f32[6,3,64,128]{3,2,1,0:T(8,128)S(1)}, f32[6,3,64,128]{3,2,1,0:T(8,128)S(1)}, u32[]{:S(2)}, u32[]{:S(2)}) collective-permute-start(f32[6,3,64,128]{3,2,1,0:T(8,128)S(1)} %fusion.58), channel_id=1, source_target_pairs={{0,1},{1,0},{2,3},{3,2},{4,5},{5,4},{6,7},{7,6},{8,9},{9,8},{10,11... | collective-permute-start | bytes 1769480 | tf_op jit(solution)/shard_map/ppermute | solution.py:239
  172.4 18.4 %collective-permute-start.13 = (f32[3,6,64,128]{3,2,1,0:T(8,128)S(1)}, f32[3,6,64,128]{3,2,1,0:T(8,128)S(1)}, u32[]{:S(2)}, u32[]{:S(2)}) collective-permute-start(f32[3,6,64,128]{3,2,1,0:T(8,128)S(1)} %fusion.39), channel_id=1, source_target_pairs={{2,0},{4,2},{6,4},{8,6},{10,8},{12,10},{14,12},{3,1},{5,3},{7,5},{... | collective-permute-start | bytes 1769480 | tf_op jit(solution)/shard_map/ppermute | solution.py:159
  173.7 30.5 %collective-permute-start.12 = (f32[3,6,64,128]{3,2,1,0:T(8,128)S(1)}, f32[3,6,64,128]{3,2,1,0:T(8,128)S(1)}, u32[]{:S(2)}, u32[]{:S(2)}) collective-permute-start(f32[3,6,64,128]{3,2,1,0:T(8,128)S(1)} %fusion.53), channel_id=1, source_target_pairs={{0,2},{2,4},{4,6},{6,8},{8,10},{10,12},{12,14},{1,3},{3,5},{5,7},{... | collective-permute-start | bytes 1769480 | tf_op jit(solution)/shard_map/ppermute | solution.py:154

commit v6 on v4

--- a/solution.py
+++ b/solution.py
@@ -70,25 +70,12 @@
         lax.slice_in_dim(field, 1, extent, axis=along)
         - lax.slice_in_dim(field, 0, extent - 1, axis=along)
     ) / spacing
-    differences = jnp.concatenate([lax.slice_in_dim(inner, 0, 1, axis=along), inner], axis=along)
-    low_edge = lax.slice_in_dim(differences, 0, 1, axis=along)
-    high_edge = lax.slice_in_dim(differences, extent - 1, extent, axis=along)
+    low_edge = lax.slice_in_dim(inner, 0, 1, axis=along)
+    high_edge = lax.slice_in_dim(inner, extent - 2, extent - 1, axis=along)
+    padded = jnp.concatenate([low_edge] * 3 + [inner] + [high_edge] * 3, axis=along)
 
     def window(offset):
-        shift_by = offset - 2
-        if shift_by > 0:
-            return jnp.concatenate(
-                [lax.slice_in_dim(differences, shift_by, extent, axis=along)]
-                + [high_edge] * shift_by,
-                axis=along,
-            )
-        if shift_by < 0:
-            return jnp.concatenate(
-                [low_edge] * -shift_by
-                + [lax.slice_in_dim(differences, 0, extent + shift_by, axis=along)],
-                axis=along,
-            )
-        return differences
+        return lax.slice_in_dim(padded, offset, offset + extent, axis=along)
 
     return both_sides(window)
 

time: 220 us -> 209 us (0.950)
  local copies, waits for them, and re-layouts: 14.4 us -> 9.13 us
  other arithmetic: 118 us -> 113 us
    concatenate x6 -> x0, other arithmetic: 5.72 us -> none  [clamped_sided(): jnp.concatenate([lax.slice_in_dim(inner, 0, 1, axis=along), inner], axis=...]
    slice x8 -> x3, local copies, waits for them, and re-layouts: 5.82 us -> 1.23 us  [clamped_sided(): low_edge = lax.slice_in_dim(inner, 0, 1, axis=along)]
  transfers between devices with their start and end apart: 15 -> 15, of which waited for: 6 -> 6; matrix products, arithmetic and copies ran while one was open for 26% -> 24% of each run, Pallas kernels for 0% -> 0%
where the time goes in v6:
time: 209 us; the launch traced here: 208 us
  other arithmetic  113 us (54%)
  waiting for transfers between devices  51.9 us (25%)
  starting transfers between devices  28 us (13%)
  local copies, waits for them, and re-layouts  9.13 us (4%)
  between operations  6.05 us (3%)
    add x4, other arithmetic, local_part(): partial + 0.5 * (alpha_three * (fore_three - back_three) + alpha_four * (...  40.3 us
    ppermute x3, waiting for transfers between devices, send_low(): lax.ppermute(piece, axis, [(i, (i + 1) % count) for i in range(count - 1)])  36.1 us
    add x2, other arithmetic, on_device(): 0.75 * cut(values, side) + 0.25 * (cut(first, side) + step_time * rate)  14.9 us
    add x2, other arithmetic, on_device(): cut(values, side) + step_time * rate  14.8 us
    add x1, other arithmetic, on_device(): cut(values, side) * (1.0 / 3.0)  14.1 us
    ppermute x3, starting transfers between devices, send_low(): lax.ppermute(piece, axis, [(i, (i + 1) % count) for i in range(count - 1)])  12.8 us
    ppermute x3, waiting for transfers between devices, send_high(): lax.ppermute(piece, axis, [((i + 1) % count, i) for i in range(count - 1)])  11.3 us
    ppermute x6, starting transfers between devices, spread_max(): lax.ppermute(local, axes, [(i, (i + k * span) % count) for i in range(cou...  9.99 us
  transfers between devices with their start and end apart: 15, of which 6 were waited for; matrix products, arithmetic and copies ran while one was open for 24% of the time, Pallas kernels for 0%

profile of v6, /device:TPU:0, one launch (start us, length us, event | category | flops | bytes accessed | tf_op | source)
XLA Modules:
  0.0 208.4 jit_solution(17808018214883480737)
XLA Ops:
  0.0 1.4 fusion.132
  1.4 0.8 fusion.130
  2.2 0.6 abs_multiply_fusion
  2.8 1.1 abs_multiply_fusion.1
  5.1 1.4 add_reduce_fusion
  6.5 0.6 add_reduce_fusion.1
  7.1 1.9 pad_maximum_fusion.48
  9.0 2.4 %collective-permute-start.2 = (f32[2]{0:T(128)}, f32[2]{0:T(128)}, u32[]{:S(2)}, u32[]{:S(2)}) collective-permute-start(f32[2]{0:T(128)} %pad_maximum_fusion.48), channel_id=1, source_target_pairs={{0,3},{1,4},{2,5},{3,6},{4,7},{5,8},{6,9},{7,10},{8,11},{9,12},{10... | collective-permute-start | bytes 32 | tf_op jit(solution)/shard_map/ppermute | solution.py:119
  11.4 1.5 collective-permute-start.1
  13.0 0.5 collective-permute-start
  13.4 2.4 %fusion.126 = (f32[3,6,64,128]{3,2,1,0:T(8,128)}, f32[3,6,64,128]{3,2,1,0:T(8,128)}) fusion(f32[6,6,64,128]{3,2,1,0:T(8,128)} %param.6), kind=kLoop, calls=%fused_computation.312 | loop fusion | bytes 2359296 | tf_op jit(solution)/shard_map/slice | solution.py:149
  15.8 4.2 %collective-permute-start.6 = (f32[3,6,64,128]{3,2,1,0:T(8,128)}, f32[3,6,64,128]{3,2,1,0:T(8,128)}, u32[]{:S(2)}, u32[]{:S(2)}) collective-permute-start(f32[3,6,64,128]{3,2,1,0:T(8,128)} %get-tuple-element.68), channel_id=1, source_target_pairs={{0,2},{2,4},{4,6},{6,8},{8,10},{10,12},{12,14},{1,3},{3,5},{5,7},{... | collective-permute-start | bytes 1769480 | tf_op jit(solution)/shard_map/ppermute | solution.py:85
  20.1 1.3 collective-permute-start.8
  21.4 0.4 subtract_multiply_fusion.1
  23.7 0.9 slice_bitcast_fusion.13
  24.5 0.8 slice_bitcast_fusion.5
  25.4 0.6 fusion.129
  26.0 0.6 copy_bitcast_fusion
  26.6 2.2 %pad_maximum_fusion.30 = (f32[3,6,70,128]{3,2,1,0:T(8,128)}, f32[3,6,70,128]{3,2,1,0:T(8,128)S(1)}) fusion(f32[3,6,3,128]{3,2,1,0:T(4,128)S(1)} %get-tuple-element.63, f32[3,6,64,128]{3,2,1,0:T(8,128)} %get-tuple-element.67, f32[3,6,3,128]{3,2,1,0:T(4,128)S(1)} %get-tuple-element.61, f32[3,6,3,128]{3,2,1,0:T(4,128)S(1)} %get-tuple-element.64, ...), kind=kLoop, calls=%fused_computation.134 | loop fusion | flops 645120 | bytes 2580480 | tf_op jit(solution)/shard_map/concatenate | solution.py:56
  28.9 0.9 slice_select_fusion
  29.8 0.6 slice_multiply_fusion.1
  30.4 0.6 broadcast_multiply_fusion
  31.0 0.6 broadcast_multiply_fusion.1
  31.8 0.4 fusion.127
  32.2 7.5 %multiply_add_fusion.2 = (f32[3,6,64,128]{3,2,1,0:T(8,128)}, f32[3,6,64,128]{3,2,1,0:T(8,128)S(1)}, f32[3,6,64,128]{3,2,1,0:T(8,128)S(1)}) fusion(f32[3,6,64,1]{3,2,1,0:T(8,128)S(1)} %get-tuple-element.125, f32[3,6,64,127]{3,2,1,0:T(8,128)S(1)} %get-tuple-element.66, f32[3,6,64,1]{3,2,1,0:T(8,128)S(1)} %get-tuple-element.126, f32[]{:T(128)S(6)} %add.2741, ...), kind=kLoop, calls=%fused_computation.197 | loop fusion | flops 40550400 | bytes 5902860 | tf_op jit(solution)/shard_map/add | solution.py:160
  39.7 0.7 add_multiply_fusion.8
  40.4 0.7 add_multiply_fusion.10
  41.2 6.8 %multiply_add_fusion.3 = (f32[3,6,64,128]{3,2,1,0:T(8,128)S(1)}, f32[3,6,64,128]{3,2,1,0:T(8,128)S(1)}, f32[3,6,64,128]{3,2,1,0:T(8,128)S(1)}) fusion(f32[3,6,64,1]{3,2,1,0:T(8,128)S(1)} %get-tuple-element.100, f32[3,6,64,127]{3,2,1,0:T(8,128)S(1)} %get-tuple-element.65, f32[3,6,64,1]{3,2,1,0:T(8,128)S(1)} %get-tuple-element.99, f32[]{:T(128)S(6)} %add.2741, ...), kind=kLoop, calls=%fused_computation.210 | loop fusion | flops 40550400 | bytes 5902860 | tf_op jit(solution)/shard_map/add | solution.py:160
  48.1 0.5 fusion.119
  49.3 1.0 collective-permute-start.7
  50.3 2.1 maximum_maximum_fusion.1
  52.3 3.2 %collective-permute-start.5 = (f32[2]{0:T(128)S(1)}, f32[2]{0:T(128)S(1)}, u32[]{:S(2)}, u32[]{:S(2)}) collective-permute-start(f32[2]{0:T(128)S(1)} %maximum_maximum_fusion.1), channel_id=1, source_target_pairs={{0,12},{1,13},{2,14},{3,15},{4,0},{5,1},{6,2},{7,3},{8,4},{9,5},{1... | collective-permute-start | bytes 32 | tf_op jit(solution)/shard_map/ppermute | solution.py:119
  55.5 0.8 collective-permute-start.4
  56.3 0.5 collective-permute-done.5
  56.8 1.6 collective-permute-start.3
  58.4 1.6 collective-permute-done.4
  60.0 2.4 %collective-permute-done.3 = f32[2]{0:T(128)S(1)} collective-permute-done((f32[2]{0:T(128)S(1)}, f32[2]{0:T(128)S(1)}, u32[]{:S(2)}, u32[]{:S(2)}) %collective-permute-start.3) | collective-permute-done | bytes 40 | tf_op jit(solution)/shard_map/ppermute | solution.py:119
  62.5 0.6 fusion.131
  64.5 1.3 add_select_fusion.7
  65.9 1.3 add_select_fusion.15
  67.2 1.5 pad_maximum_fusion.22
  69.0 1.2 add_select_fusion.5
  70.3 0.5 fusion.7
  70.7 0.6 copy-done.2
  71.3 7.4 %fusion.65 = f32[3,6,64,128]{3,2,1,0:T(8,128)S(1)} fusion(f32[3,6,64,128]{3,2,1,0:T(8,128)S(1)} %copy-done.2, f32[3,6,64,128]{3,2,1,0:T(8,128)S(1)} %add_multiply_fusion.6, f32[3,11,64,128]{3,2,1,0:T(8,128)S(1)} %fusion.42, f32[8,6,64,128]{3,2,1,0:T(8,128)S(1)} %get-tuple-element.48, f32[3]{0:T(128)S(1)} %copy-done.23, f32[3,6,64]{2,1,0:T(8,128)S(1)} %copy-done.11, ...), kind=kLoop, calls=%fused_computation.155 | loop fusion | flops 40108032 | bytes 9474684 | tf_op jit(solution)/shard_map/add | solution.py:298
  78.8 7.4 %fusion.51 = f32[3,6,64,128]{3,2,1,0:T(8,128)S(1)} fusion(f32[3,6,64,128]{3,2,1,0:T(8,128)S(1)} %get-tuple-element.14, f32[3,6,64,128]{3,2,1,0:T(8,128)S(1)} %add_multiply_fusion.7, f32[3,11,64,128]{3,2,1,0:T(8,128)S(1)} %fusion.43, f32[8,6,64,128]{3,2,1,0:T(8,128)S(1)} %get-tuple-element.47, f32[]{:T(128)} %bitcast.7, f32[]{:T(128)} %bitcast.6, ...), kind=kLoop, calls=%fused_computation.141 | loop fusion | flops 40108032 | bytes 9474684 | tf_op jit(solution)/shard_map/add | solution.py:298
  86.2 0.4 fusion.14
  86.7 0.4 fusion.124
  87.5 13.0 %multiply_add_fusion.1 = (f32[6,6,64,128]{3,2,1,0:T(8,128)S(1)}, f32[6,6,64,128]{3,2,1,0:T(8,128)S(1)}, f32[6,6,64,128]{3,2,1,0:T(8,128)S(1)}) fusion(f32[6,6,64,1]{3,2,1,0:T(8,128)S(1)} %get-tuple-element.46, f32[6,6,64,127]{3,2,1,0:T(8,128)S(1)} %fusion.14, f32[6,6,64,1]{3,2,1,0:T(8,128)S(1)} %get-tuple-element.45, f32[]{:T(128)S(6)} %add.2741, ...), kind=kLoop, calls=%fused_computation.108 | loop fusion | flops 81100800 | bytes 11805708 | tf_op jit(solution)/shard_map/add | solution.py:160
  100.9 3.5 %collective-permute-start.9 = (f32[3,6,64,128]{3,2,1,0:T(8,128)S(1)}, f32[3,6,64,128]{3,2,1,0:T(8,128)S(1)}, u32[]{:S(2)}, u32[]{:S(2)}) collective-permute-start(f32[3,6,64,128]{3,2,1,0:T(8,128)S(1)} %fusion.65), channel_id=1, source_target_pairs={{0,2},{2,4},{4,6},{6,8},{8,10},{10,12},{12,14},{1,3},{3,5},{5,7},{... | collective-permute-start | bytes 1769480 | tf_op jit(solution)/shard_map/ppermute | solution.py:85
  104.4 1.5 collective-permute-start.11
  106.4 23.9 %collective-permute-done.9 = f32[3,6,64,128]{3,2,1,0:T(8,128)S(1)} collective-permute-done((f32[3,6,64,128]{3,2,1,0:T(8,128)S(1)}, f32[3,6,64,128]{3,2,1,0:T(8,128)S(1)}, u32[]{:S(2)}, u32[]{:S(2)}) %collective-permute-start.9) | collective-permute-done | bytes 589856 | tf_op jit(solution)/shard_map/ppermute | solution.py:85
  130.7 0.5 pad_maximum_fusion.3
  131.8 0.5 copy-done.16
  132.3 7.5 %fusion.73 = f32[3,6,64,128]{3,2,1,0:T(8,128)S(1)} fusion(f32[3,6,64,128]{3,2,1,0:T(8,128)S(1)} %fusion.65, f32[6,6,64,128]{3,2,1,0:T(8,128)S(1)} %get-tuple-element.18, f32[6,6,64,128]{3,2,1,0:T(8,128)S(1)} %add_multiply_fusion.1, f32[3,11,64,128]{3,2,1,0:T(8,128)S(1)} %fusion.40, f32[8,6,64,128]{3,2,1,0:T(8,128)S(1)} %fusion.8, f32[3]{0:T(128)S(1)} %copy-done.23, ...), kind=kLoop, calls=%fused_computation.163 | loop fusion | flops 40550400 | bytes 10064508 | tf_op jit(solution)/shard_map/add | solution.py:302
  139.8 7.5 %fusion.59 = f32[3,6,64,128]{3,2,1,0:T(8,128)S(1)} fusion(f32[3,6,64,128]{3,2,1,0:T(8,128)S(1)} %fusion.51, f32[6,6,64,128]{3,2,1,0:T(8,128)S(1)} %get-tuple-element.18, f32[6,6,64,128]{3,2,1,0:T(8,128)S(1)} %add_multiply_fusion.1, f32[3,11,64,128]{3,2,1,0:T(8,128)S(1)} %fusion.41, f32[8,6,64,128]{3,2,1,0:T(8,128)S(1)} %fusion.9, f32[]{:T(128)} %bitcast.7, ...), kind=kLoop, calls=%fused_computation.149 | loop fusion | flops 40550400 | bytes 10064508 | tf_op jit(solution)/shard_map/add | solution.py:302
  147.7 0.4 fusion.123
  148.5 13.0 %multiply_add_fusion = (f32[6,6,64,128]{3,2,1,0:T(8,128)S(1)}, f32[6,6,64,128]{3,2,1,0:T(8,128)S(1)}, f32[6,6,64,128]{3,2,1,0:T(8,128)S(1)}) fusion(f32[6,6,64,1]{3,2,1,0:T(8,128)S(1)} %get-tuple-element.40, f32[6,6,64,127]{3,2,1,0:T(8,128)S(1)} %fusion.17, f32[6,6,64,1]{3,2,1,0:T(8,128)S(1)} %get-tuple-element.39, f32[]{:T(128)S(6)} %add.2741, f32[]{:T(128)} %bitcast.9, ...), kind=kLoop, calls=%fused_computation.98 | loop fusion | flops 81100800 | bytes 11805708 | tf_op jit(solution)/shard_map/add | solution.py:160
  161.9 1.3 collective-permute-start.13
  163.2 5.1 %collective-permute-start.12 = (f32[3,6,64,128]{3,2,1,0:T(8,128)S(1)}, f32[3,6,64,128]{3,2,1,0:T(8,128)S(1)}, u32[]{:S(2)}, u32[]{:S(2)}) collective-permute-start(f32[3,6,64,128]{3,2,1,0:T(8,128)S(1)} %fusion.73), channel_id=1, source_target_pairs={{0,2},{2,4},{4,6},{6,8},{8,10},{10,12},{12,14},{1,3},{3,5},{5,7},{... | collective-permute-start | bytes 1769480 | tf_op jit(solution)/shard_map/ppermute | solution.py:85
  169.0 11.3 %collective-permute-done.13 = f32[3,6,64,128]{3,2,1,0:T(8,128)S(1)} collective-permute-done((f32[3,6,64,128]{3,2,1,0:T(8,128)S(1)}, f32[3,6,64,128]{3,2,1,0:T(8,128)S(1)}, u32[]{:S(2)}, u32[]{:S(2)}) %collective-permute-start.13) | collective-permute-done | bytes 589856 | tf_op jit(solution)/shard_map/ppermute | solution.py:90
  180.4 0.4 fusion
  180.8 12.2 %collective-permute-done.12 = f32[3,6,64,128]{3,2,1,0:T(8,128)S(1)} collective-permute-done((f32[3,6,64,128]{3,2,1,0:T(8,128)S(1)}, f32[3,6,64,128]{3,2,1,0:T(8,128)S(1)}, u32[]{:S(2)}, u32[]{:S(2)}) %collective-permute-start.12) | collective-permute-done | bytes 589856 | tf_op jit(solution)/shard_map/ppermute | solution.py:85
  194.2 14.1 %fusion.21 = f32[6,6,64,128]{3,2,1,0:T(8,128)} fusion(f32[3,6,64,128]{3,2,1,0:T(8,128)S(1)} %fusion.73, f32[3,6,64,128]{3,2,1,0:T(8,128)S(1)} %fusion.59, f32[6,6,64,128]{3,2,1,0:T(8,128)S(1)} %get-tuple-element.20, f32[6,6,64,128]{3,2,1,0:T(8,128)S(1)} %add_multiply_fusion, f32[6,11,64,128]{3,2,1,0:T(8,128)S(1)} %fusion, f32[11,6,64,128]{3,2,1,0:T(8,128)S(1)} %fusion.1, ...), kind=kLoop, calls=%fused_computation.70 | loop fusion | flops 81395712 | bytes 20096208 | tf_op jit(solution)/shard_map/add | solution.py:307
  (112 shorter events, 6.2 us)
Async XLA Ops:
  9.0 12.3 %copy-start = (f32[6,6,64,128]{3,2,1,0:T(8,128)S(1)}, f32[6,6,64,128]{3,2,1,0:T(8,128)}, u32[]{:S(2)}) copy-start(f32[6,6,64,128]{3,2,1,0:T(8,128)} %param.6) | copy-start | bytes 3538948
  9.0 40.3 %collective-permute-start.2 = (f32[2]{0:T(128)}, f32[2]{0:T(128)}, u32[]{:S(2)}, u32[]{:S(2)}) collective-permute-start(f32[2]{0:T(128)} %pad_maximum_fusion.48), channel_id=1, source_target_pairs={{0,3},{1,4},{2,5},{3,6},{4,7},{5,8},{6,9},{7,10},{8,11},{9,12},{10... | collective-permute-start | bytes 32 | tf_op jit(solution)/shard_map/ppermute | solution.py:119
  11.4 38.8 %collective-permute-start.1 = (f32[2]{0:T(128)}, f32[2]{0:T(128)}, u32[]{:S(2)}, u32[]{:S(2)}) collective-permute-start(f32[2]{0:T(128)} %pad_maximum_fusion.48), channel_id=1, source_target_pairs={{0,2},{1,3},{2,4},{3,5},{4,6},{5,7},{6,8},{7,9},{8,10},{9,11},{10,... | collective-permute-start | bytes 32 | tf_op jit(solution)/shard_map/ppermute | solution.py:119
  13.0 37.3 %collective-permute-start = (f32[2]{0:T(128)}, f32[2]{0:T(128)}, u32[]{:S(2)}, u32[]{:S(2)}) collective-permute-start(f32[2]{0:T(128)} %pad_maximum_fusion.48), channel_id=1, source_target_pairs={{0,1},{1,2},{2,3},{3,4},{4,5},{5,6},{6,7},{7,8},{8,9},{9,10},{10,1... | collective-permute-start | bytes 32 | tf_op jit(solution)/shard_map/ppermute | solution.py:119
  15.8 48.7 %collective-permute-start.6 = (f32[3,6,64,128]{3,2,1,0:T(8,128)}, f32[3,6,64,128]{3,2,1,0:T(8,128)}, u32[]{:S(2)}, u32[]{:S(2)}) collective-permute-start(f32[3,6,64,128]{3,2,1,0:T(8,128)} %get-tuple-element.68), channel_id=1, source_target_pairs={{0,2},{2,4},{4,6},{6,8},{8,10},{10,12},{12,14},{1,3},{3,5},{5,7},{... | collective-permute-start | bytes 1769480 | tf_op jit(solution)/shard_map/ppermute | solution.py:85
  20.1 48.9 %collective-permute-start.8 = (f32[3,6,64,128]{3,2,1,0:T(8,128)}, f32[3,6,64,128]{3,2,1,0:T(8,128)}, u32[]{:S(2)}, u32[]{:S(2)}) collective-permute-start(f32[3,6,64,128]{3,2,1,0:T(8,128)} %get-tuple-element.67), channel_id=1, source_target_pairs={{2,0},{4,2},{6,4},{8,6},{10,8},{12,10},{14,12},{3,1},{5,3},{7,5},{... | collective-permute-start | bytes 1769480 | tf_op jit(solution)/shard_map/ppermute | solution.py:90
  24.5 0.8 copy-start.13
  28.9 1.5 copy-start.27
  28.9 2.1 %copy-start.26 = (f32[64]{0:T(128)S(1)}, f32[64]{0:T(128)}, u32[]{:S(2)}) copy-start(f32[64]{0:T(128)} %constant.500.clone) | copy-start | bytes 772
  28.9 2.8 %copy-start.1 = (f32[3,6,70,128]{3,2,1,0:T(8,128)S(1)}, f32[3,6,70,128]{3,2,1,0:T(8,128)}, u32[]{:S(2)}) copy-start(f32[3,6,70,128]{3,2,1,0:T(8,128)} %get-tuple-element.127) | copy-start | bytes 1935364
  39.7 1.4 copy-start.25
  48.0 0.6 copy-start.21
  48.0 1.3 copy-start.20
  48.6 22.1 %copy-start.15 = (f32[1,3,6]{2,1,0:T(4,128)}, f32[1,3,6]{2,1,0:T(4,128)S(1)}, u32[]{:S(2)}) copy-start(f32[1,3,6]{2,1,0:T(4,128)S(1)} %copy.27) | copy-start | bytes 220
  49.3 29.5 %copy-start.17 = (f32[1,3,6]{2,1,0:T(4,128)}, f32[1,3,6]{2,1,0:T(4,128)S(1)}, u32[]{:S(2)}) copy-start(f32[1,3,6]{2,1,0:T(4,128)S(1)} %copy.28) | copy-start | bytes 220
  49.3 16.5 %collective-permute-start.7 = (f32[6,3,64,128]{3,2,1,0:T(8,128)}, f32[6,3,64,128]{3,2,1,0:T(8,128)}, u32[]{:S(2)}, u32[]{:S(2)}) collective-permute-start(f32[6,3,64,128]{3,2,1,0:T(8,128)} %slice_select_fusion), channel_id=1, source_target_pairs={{0,1},{1,0},{2,3},{3,2},{4,5},{5,4},{6,7},{7,6},{8,9},{9,8},{10,11... | collective-permute-start | bytes 1769480 | tf_op jit(solution)/shard_map/ppermute | solution.py:176
  52.3 4.5 %collective-permute-start.5 = (f32[2]{0:T(128)S(1)}, f32[2]{0:T(128)S(1)}, u32[]{:S(2)}, u32[]{:S(2)}) collective-permute-start(f32[2]{0:T(128)S(1)} %maximum_maximum_fusion.1), channel_id=1, source_target_pairs={{0,12},{1,13},{2,14},{3,15},{4,0},{5,1},{6,2},{7,3},{8,4},{9,5},{1... | collective-permute-start | bytes 32 | tf_op jit(solution)/shard_map/ppermute | solution.py:119
  55.5 4.5 %collective-permute-start.4 = (f32[2]{0:T(128)S(1)}, f32[2]{0:T(128)S(1)}, u32[]{:S(2)}, u32[]{:S(2)}) collective-permute-start(f32[2]{0:T(128)S(1)} %maximum_maximum_fusion.1), channel_id=1, source_target_pairs={{0,8},{1,9},{2,10},{3,11},{4,12},{5,13},{6,14},{7,15},{8,0},{9,1},... | collective-permute-start | bytes 32 | tf_op jit(solution)/shard_map/ppermute | solution.py:119
  56.8 5.6 %collective-permute-start.3 = (f32[2]{0:T(128)S(1)}, f32[2]{0:T(128)S(1)}, u32[]{:S(2)}, u32[]{:S(2)}) collective-permute-start(f32[2]{0:T(128)S(1)} %maximum_maximum_fusion.1), channel_id=1, source_target_pairs={{0,4},{1,5},{2,6},{3,7},{4,8},{5,9},{6,10},{7,11},{8,12},{9,13},{1... | collective-permute-start | bytes 32 | tf_op jit(solution)/shard_map/ppermute | solution.py:119
  64.4 1.4 copy-start.3
  64.4 1.4 copy-start.4
  64.4 1.4 copy-start.5
  64.5 1.4 copy-start.6
  64.5 1.4 copy-start.7
  64.5 1.4 copy-start.8
  64.5 1.4 copy-start.9
  70.2 1.1 copy-start.2
  70.2 1.1 copy-start.11
  70.3 1.1 copy-start.14
  70.3 1.0 copy-start.23
  71.3 7.4 %copy-start.10 = (f32[3,6,64]{2,1,0:T(8,128)S(1)}, f32[3,6,64]{2,1,0:T(8,128)}, u32[]{:S(2)}) copy-start(f32[3,6,64]{2,1,0:T(8,128)} %get-tuple-element.109) | copy-start | bytes 13828
  71.3 7.4 %copy-start.22 = (f32[3]{0:T(128)S(1)}, f32[3]{0:T(128)}, u32[]{:S(2)}) copy-start(f32[3]{0:T(128)} %get-tuple-element.111) | copy-start | bytes 40
  87.5 18.5 %collective-permute-start.10 = (f32[6,3,64,128]{3,2,1,0:T(8,128)S(1)}, f32[6,3,64,128]{3,2,1,0:T(8,128)S(1)}, u32[]{:S(2)}, u32[]{:S(2)}) collective-permute-start(f32[6,3,64,128]{3,2,1,0:T(8,128)S(1)} %fusion.75), channel_id=1, source_target_pairs={{0,1},{1,0},{2,3},{3,2},{4,5},{5,4},{6,7},{7,6},{8,9},{9,8},{10,11... | collective-permute-start | bytes 1769480 | tf_op jit(solution)/shard_map/ppermute | solution.py:176
  100.9 29.4 %collective-permute-start.9 = (f32[3,6,64,128]{3,2,1,0:T(8,128)S(1)}, f32[3,6,64,128]{3,2,1,0:T(8,128)S(1)}, u32[]{:S(2)}, u32[]{:S(2)}) collective-permute-start(f32[3,6,64,128]{3,2,1,0:T(8,128)S(1)} %fusion.65), channel_id=1, source_target_pairs={{0,2},{2,4},{4,6},{6,8},{8,10},{10,12},{12,14},{1,3},{3,5},{5,7},{... | collective-permute-start | bytes 1769480 | tf_op jit(solution)/shard_map/ppermute | solution.py:85
  104.4 26.1 %collective-permute-start.11 = (f32[3,6,64,128]{3,2,1,0:T(8,128)S(1)}, f32[3,6,64,128]{3,2,1,0:T(8,128)S(1)}, u32[]{:S(2)}, u32[]{:S(2)}) collective-permute-start(f32[3,6,64,128]{3,2,1,0:T(8,128)S(1)} %fusion.51), channel_id=1, source_target_pairs={{2,0},{4,2},{6,4},{8,6},{10,8},{12,10},{14,12},{3,1},{5,3},{7,5},{... | collective-permute-start | bytes 1769480 | tf_op jit(solution)/shard_map/ppermute | solution.py:90
  131.6 0.6 copy-start.16
  132.3 7.5 %copy-start.18 = (f32[1,3,6]{2,1,0:T(4,128)S(1)}, f32[1,3,6]{2,1,0:T(4,128)}, u32[]{:S(2)}) copy-start(f32[1,3,6]{2,1,0:T(4,128)} %copy-done.17) | copy-start | bytes 220
  161.8 6.6 %collective-permute-start.14 = (f32[6,3,64,128]{3,2,1,0:T(8,128)S(1)}, f32[6,3,64,128]{3,2,1,0:T(8,128)S(1)}, u32[]{:S(2)}, u32[]{:S(2)}) collective-permute-start(f32[6,3,64,128]{3,2,1,0:T(8,128)S(1)} %fusion.78), channel_id=1, source_target_pairs={{0,1},{1,0},{2,3},{3,2},{4,5},{5,4},{6,7},{7,6},{8,9},{9,8},{10,11... | collective-permute-start | bytes 1769480 | tf_op jit(solution)/shard_map/ppermute | solution.py:176
  161.9 18.4 %collective-permute-start.13 = (f32[3,6,64,128]{3,2,1,0:T(8,128)S(1)}, f32[3,6,64,128]{3,2,1,0:T(8,128)S(1)}, u32[]{:S(2)}, u32[]{:S(2)}) collective-permute-start(f32[3,6,64,128]{3,2,1,0:T(8,128)S(1)} %fusion.59), channel_id=1, source_target_pairs={{2,0},{4,2},{6,4},{8,6},{10,8},{12,10},{14,12},{3,1},{5,3},{7,5},{... | collective-permute-start | bytes 1769480 | tf_op jit(solution)/shard_map/ppermute | solution.py:90
  163.2 29.9 %collective-permute-start.12 = (f32[3,6,64,128]{3,2,1,0:T(8,128)S(1)}, f32[3,6,64,128]{3,2,1,0:T(8,128)S(1)}, u32[]{:S(2)}, u32[]{:S(2)}) collective-permute-start(f32[3,6,64,128]{3,2,1,0:T(8,128)S(1)} %fusion.73), channel_id=1, source_target_pairs={{0,2},{2,4},{4,6},{6,8},{8,10},{10,12},{12,14},{1,3},{3,5},{5,7},{... | collective-permute-start | bytes 1769480 | tf_op jit(solution)/shard_map/ppermute | solution.py:85
  193.5 0.7 copy-start.12
  193.5 0.7 copy-start.19
  193.5 0.7 copy-start.24

commit v7 on v6

--- a/solution.py
+++ b/solution.py
@@ -172,7 +172,9 @@
         tail = lax.slice_in_dim(field, cells_y - 3, cells_y, axis=1)
         head = lax.slice_in_dim(field, 0, 3, axis=1)
         if devices_y == 2:
-            piece = lax.optimization_barrier(jnp.where(first_y, tail, head))
+            offset = jnp.where(first_y, cells_y - 3, 0)
+            piece = lax.dynamic_slice_in_dim(field, offset, 3, axis=1)
+            piece = lax.optimization_barrier(piece)
             swapped = lax.ppermute(piece, "gy", [(0, 1), (1, 0)])
             return swapped, swapped
         tail, head = lax.optimization_barrier((tail, head))
@@ -201,16 +203,17 @@
     first_lo = params[0] * cos_table.min() - speed_grid[n_speed - 1]
     second_hi = params[0] * sin_table.max()
     second_lo = params[0] * sin_table.min()
-    local_one = jnp.max(
-        jnp.maximum(drift[0] + first_hi, -(drift[0] + first_lo))
-        + params[1] * jnp.abs(y_coord)[None, :]
-    )
-    local_two = jnp.max(
-        jnp.maximum(drift[1] + second_hi, -(drift[1] + second_lo))
-        + params[1] * jnp.abs(x_coord)[:, None]
-    )
+    terms = jnp.stack(
+        [
+            jnp.maximum(drift[0] + first_hi, -(drift[0] + first_lo))
+            + params[1] * jnp.abs(y_coord)[None, :],
+            jnp.maximum(drift[1] + second_hi, -(drift[1] + second_lo))
+            + params[1] * jnp.abs(x_coord)[:, None],
+        ]
+    )
+    local_bounds = jnp.max(terms, axis=(1, 2))
     locals_now = local_halves(values)
-    bounds = spread_max(jnp.stack([local_one, local_two]), ("gx", "gy"))
+    bounds = spread_max(local_bounds, ("gx", "gy"))
     bound_one = bounds[0]
     bound_two = bounds[1]
     step_time = cfl_number / (

time: 209 us -> 205 us (0.981)
  other arithmetic: 113 us -> 109 us
where the time goes in v7:
time: 205 us; the launch traced here: 204 us
  other arithmetic  109 us (53%)
  waiting for transfers between devices  51.9 us (25%)
  starting transfers between devices  28 us (14%)
  local copies, waits for them, and re-layouts  9.53 us (5%)
  between operations  6.02 us (3%)
    add x4, other arithmetic, local_part(): partial + 0.5 * (alpha_three * (fore_three - back_three) + alpha_four * (...  40.3 us
    ppermute x3, waiting for transfers between devices, send_low(): lax.ppermute(piece, axis, [(i, (i + 1) % count) for i in range(count - 1)])  36.1 us
    add x2, other arithmetic, on_device(): 0.75 * cut(values, side) + 0.25 * (cut(first, side) + step_time * rate)  14.9 us
    add x2, other arithmetic, on_device(): cut(values, side) + step_time * rate  14.8 us
    add x1, other arithmetic, on_device(): cut(values, side) * (1.0 / 3.0)  14.1 us
    ppermute x3, starting transfers between devices, send_low(): lax.ppermute(piece, axis, [(i, (i + 1) % count) for i in range(count - 1)])  12.8 us
    ppermute x3, waiting for transfers between devices, send_high(): lax.ppermute(piece, axis, [((i + 1) % count, i) for i in range(count - 1)])  11.3 us
    ppermute x6, starting transfers between devices, spread_max(): lax.ppermute(local, axes, [(i, (i + k * span) % count) for i in range(cou...  9.98 us
  transfers between devices with their start and end apart: 15, of which 6 were waited for; matrix products, arithmetic and copies ran while one was open for 24% of the time, Pallas kernels for 0%

profile of v7, /device:TPU:0, one launch (start us, length us, event | category | flops | bytes accessed | tf_op | source)
XLA Modules:
  0.0 204.5 jit_solution(15133526762475849442)
XLA Ops:
  0.0 1.4 fusion.134
  1.4 0.8 fusion.132
  2.2 0.6 abs_multiply_fusion
  2.8 0.6 abs_multiply_fusion.1
  4.7 1.2 copy_bitcast_fusion
  5.9 0.6 maximum_reduce_fusion
  6.5 2.4 %collective-permute-start.2 = (f32[2]{0:T(128)}, f32[2]{0:T(128)}, u32[]{:S(2)}, u32[]{:S(2)}) collective-permute-start(f32[2]{0:T(128)} %maximum_reduce_fusion), channel_id=1, source_target_pairs={{0,3},{1,4},{2,5},{3,6},{4,7},{5,8},{6,9},{7,10},{8,11},{9,12},{10... | collective-permute-start | bytes 32 | tf_op jit(solution)/shard_map/ppermute | solution.py:119
  9.0 1.5 collective-permute-start.1
  10.5 0.5 collective-permute-start
  11.0 2.4 %fusion.128 = (f32[3,6,64,128]{3,2,1,0:T(8,128)}, f32[3,6,64,128]{3,2,1,0:T(8,128)}) fusion(f32[6,6,64,128]{3,2,1,0:T(8,128)} %param.6), kind=kLoop, calls=%fused_computation.312 | loop fusion | bytes 2359296 | tf_op jit(solution)/shard_map/slice | solution.py:149
  13.4 4.2 %collective-permute-start.6 = (f32[3,6,64,128]{3,2,1,0:T(8,128)}, f32[3,6,64,128]{3,2,1,0:T(8,128)}, u32[]{:S(2)}, u32[]{:S(2)}) collective-permute-start(f32[3,6,64,128]{3,2,1,0:T(8,128)} %get-tuple-element.68), channel_id=1, source_target_pairs={{0,2},{2,4},{4,6},{6,8},{8,10},{10,12},{12,14},{1,3},{3,5},{5,7},{... | collective-permute-start | bytes 1769480 | tf_op jit(solution)/shard_map/ppermute | solution.py:85
  17.6 1.3 collective-permute-start.8
  18.9 0.4 subtract_multiply_fusion.1
  21.2 0.9 slice_bitcast_fusion.13
  22.1 0.8 slice_bitcast_fusion.5
  23.0 0.6 fusion.131
  23.6 0.5 fusion.120
  24.1 2.2 %pad_maximum_fusion.30 = (f32[3,6,70,128]{3,2,1,0:T(8,128)}, f32[3,6,70,128]{3,2,1,0:T(8,128)S(1)}) fusion(f32[3,6,3,128]{3,2,1,0:T(4,128)S(1)} %get-tuple-element.63, f32[3,6,64,128]{3,2,1,0:T(8,128)} %get-tuple-element.67, f32[3,6,3,128]{3,2,1,0:T(4,128)S(1)} %get-tuple-element.61, f32[3,6,3,128]{3,2,1,0:T(4,128)S(1)} %get-tuple-element.64, ...), kind=kLoop, calls=%fused_computation.130 | loop fusion | flops 645120 | bytes 2580480 | tf_op jit(solution)/shard_map/concatenate | solution.py:56
  26.4 0.9 constant_dynamic-slice_fusion
  27.3 0.7 slice_multiply_fusion.1
  28.0 0.6 broadcast_multiply_fusion
  28.6 0.6 broadcast_multiply_fusion.1
  29.3 0.4 fusion.129
  29.8 7.5 %multiply_add_fusion.2 = (f32[3,6,64,128]{3,2,1,0:T(8,128)}, f32[3,6,64,128]{3,2,1,0:T(8,128)S(1)}, f32[3,6,64,128]{3,2,1,0:T(8,128)S(1)}) fusion(f32[3,6,64,1]{3,2,1,0:T(8,128)S(1)} %get-tuple-element.125, f32[3,6,64,127]{3,2,1,0:T(8,128)S(1)} %get-tuple-element.66, f32[3,6,64,1]{3,2,1,0:T(8,128)S(1)} %get-tuple-element.126, f32[]{:T(128)S(6)} %add.2754, ...), kind=kLoop, calls=%fused_computation.189 | loop fusion | flops 40550400 | bytes 5902860 | tf_op jit(solution)/shard_map/add | solution.py:160
  37.3 0.7 add_multiply_fusion.8
  38.0 0.7 add_multiply_fusion.10
  38.8 6.8 %multiply_add_fusion.3 = (f32[3,6,64,128]{3,2,1,0:T(8,128)S(1)}, f32[3,6,64,128]{3,2,1,0:T(8,128)S(1)}, f32[3,6,64,128]{3,2,1,0:T(8,128)S(1)}) fusion(f32[3,6,64,1]{3,2,1,0:T(8,128)S(1)} %get-tuple-element.100, f32[3,6,64,127]{3,2,1,0:T(8,128)S(1)} %get-tuple-element.65, f32[3,6,64,1]{3,2,1,0:T(8,128)S(1)} %get-tuple-element.99, f32[]{:T(128)S(6)} %add.2754, ...), kind=kLoop, calls=%fused_computation.202 | loop fusion | flops 40550400 | bytes 5902860 | tf_op jit(solution)/shard_map/add | solution.py:160
  45.7 0.5 fusion.121
  46.9 1.0 collective-permute-start.7
  47.9 0.7 maximum_maximum_fusion.1
  48.6 3.2 %collective-permute-start.5 = (f32[2]{0:T(128)S(1)}, f32[2]{0:T(128)S(1)}, u32[]{:S(2)}, u32[]{:S(2)}) collective-permute-start(f32[2]{0:T(128)S(1)} %maximum_maximum_fusion.1), channel_id=1, source_target_pairs={{0,12},{1,13},{2,14},{3,15},{4,0},{5,1},{6,2},{7,3},{8,4},{9,5},{1... | collective-permute-start | bytes 32 | tf_op jit(solution)/shard_map/ppermute | solution.py:119
  51.8 0.8 collective-permute-start.4
  52.6 0.5 collective-permute-done.5
  53.1 1.6 collective-permute-start.3
  54.7 1.6 collective-permute-done.4
  56.2 2.4 %collective-permute-done.3 = f32[2]{0:T(128)S(1)} collective-permute-done((f32[2]{0:T(128)S(1)}, f32[2]{0:T(128)S(1)}, u32[]{:S(2)}, u32[]{:S(2)}) %collective-permute-start.3) | collective-permute-done | bytes 40 | tf_op jit(solution)/shard_map/ppermute | solution.py:119
  58.7 0.6 fusion.133
  60.7 1.3 add_select_fusion.7
  62.1 1.3 add_select_fusion.15
  63.4 1.5 pad_maximum_fusion.22
  65.2 1.2 add_select_fusion.5
  66.5 0.5 fusion.7
  66.9 0.6 copy-done.2
  67.5 7.4 %fusion.65 = f32[3,6,64,128]{3,2,1,0:T(8,128)S(1)} fusion(f32[3,6,64,128]{3,2,1,0:T(8,128)S(1)} %copy-done.2, f32[3,6,64,128]{3,2,1,0:T(8,128)S(1)} %add_multiply_fusion.6, f32[3,11,64,128]{3,2,1,0:T(8,128)S(1)} %fusion.42, f32[8,6,64,128]{3,2,1,0:T(8,128)S(1)} %get-tuple-element.48, f32[3]{0:T(128)S(1)} %copy-done.23, f32[3,6,64]{2,1,0:T(8,128)S(1)} %copy-done.11, ...), kind=kLoop, calls=%fused_computation.151 | loop fusion | flops 40108032 | bytes 9474684 | tf_op jit(solution)/shard_map/add | solution.py:301
  74.9 7.4 %fusion.51 = f32[3,6,64,128]{3,2,1,0:T(8,128)S(1)} fusion(f32[3,6,64,128]{3,2,1,0:T(8,128)S(1)} %get-tuple-element.14, f32[3,6,64,128]{3,2,1,0:T(8,128)S(1)} %add_multiply_fusion.7, f32[3,11,64,128]{3,2,1,0:T(8,128)S(1)} %fusion.43, f32[8,6,64,128]{3,2,1,0:T(8,128)S(1)} %get-tuple-element.47, f32[]{:T(128)} %bitcast.3, f32[]{:T(128)} %bitcast.2, ...), kind=kLoop, calls=%fused_computation.137 | loop fusion | flops 40108032 | bytes 9474684 | tf_op jit(solution)/shard_map/add | solution.py:301
  82.3 0.4 fusion.14
  82.8 0.4 fusion.126
  83.7 13.0 %multiply_add_fusion.1 = (f32[6,6,64,128]{3,2,1,0:T(8,128)S(1)}, f32[6,6,64,128]{3,2,1,0:T(8,128)S(1)}, f32[6,6,64,128]{3,2,1,0:T(8,128)S(1)}) fusion(f32[6,6,64,1]{3,2,1,0:T(8,128)S(1)} %get-tuple-element.46, f32[6,6,64,127]{3,2,1,0:T(8,128)S(1)} %fusion.14, f32[6,6,64,1]{3,2,1,0:T(8,128)S(1)} %get-tuple-element.45, f32[]{:T(128)S(6)} %add.2754, ...), kind=kLoop, calls=%fused_computation.104 | loop fusion | flops 81100800 | bytes 11805708 | tf_op jit(solution)/shard_map/add | solution.py:160
  97.0 3.5 %collective-permute-start.9 = (f32[3,6,64,128]{3,2,1,0:T(8,128)S(1)}, f32[3,6,64,128]{3,2,1,0:T(8,128)S(1)}, u32[]{:S(2)}, u32[]{:S(2)}) collective-permute-start(f32[3,6,64,128]{3,2,1,0:T(8,128)S(1)} %fusion.65), channel_id=1, source_target_pairs={{0,2},{2,4},{4,6},{6,8},{8,10},{10,12},{12,14},{1,3},{3,5},{5,7},{... | collective-permute-start | bytes 1769480 | tf_op jit(solution)/shard_map/ppermute | solution.py:85
  100.6 1.5 collective-permute-start.11
  102.5 23.9 %collective-permute-done.9 = f32[3,6,64,128]{3,2,1,0:T(8,128)S(1)} collective-permute-done((f32[3,6,64,128]{3,2,1,0:T(8,128)S(1)}, f32[3,6,64,128]{3,2,1,0:T(8,128)S(1)}, u32[]{:S(2)}, u32[]{:S(2)}) %collective-permute-start.9) | collective-permute-done | bytes 589856 | tf_op jit(solution)/shard_map/ppermute | solution.py:85
  126.9 0.5 pad_maximum_fusion.3
  128.0 0.5 copy-done.15
  128.5 7.5 %fusion.73 = f32[3,6,64,128]{3,2,1,0:T(8,128)S(1)} fusion(f32[3,6,64,128]{3,2,1,0:T(8,128)S(1)} %fusion.65, f32[6,6,64,128]{3,2,1,0:T(8,128)S(1)} %get-tuple-element.18, f32[6,6,64,128]{3,2,1,0:T(8,128)S(1)} %add_multiply_fusion.1, f32[3,11,64,128]{3,2,1,0:T(8,128)S(1)} %fusion.40, f32[8,6,64,128]{3,2,1,0:T(8,128)S(1)} %fusion.8, f32[3]{0:T(128)S(1)} %copy-done.23, ...), kind=kLoop, calls=%fused_computation.159 | loop fusion | flops 40550400 | bytes 10064508 | tf_op jit(solution)/shard_map/add | solution.py:305
  135.9 7.4 %fusion.59 = f32[3,6,64,128]{3,2,1,0:T(8,128)S(1)} fusion(f32[3,6,64,128]{3,2,1,0:T(8,128)S(1)} %fusion.51, f32[6,6,64,128]{3,2,1,0:T(8,128)S(1)} %get-tuple-element.18, f32[6,6,64,128]{3,2,1,0:T(8,128)S(1)} %add_multiply_fusion.1, f32[3,11,64,128]{3,2,1,0:T(8,128)S(1)} %fusion.41, f32[8,6,64,128]{3,2,1,0:T(8,128)S(1)} %fusion.9, f32[]{:T(128)} %bitcast.3, ...), kind=kLoop, calls=%fused_computation.145 | loop fusion | flops 40550400 | bytes 10064508 | tf_op jit(solution)/shard_map/add | solution.py:305
  143.4 0.4 fusion.17
  143.9 0.4 fusion.125
  144.6 13.0 %multiply_add_fusion = (f32[6,6,64,128]{3,2,1,0:T(8,128)S(1)}, f32[6,6,64,128]{3,2,1,0:T(8,128)S(1)}, f32[6,6,64,128]{3,2,1,0:T(8,128)S(1)}) fusion(f32[6,6,64,1]{3,2,1,0:T(8,128)S(1)} %get-tuple-element.40, f32[6,6,64,127]{3,2,1,0:T(8,128)S(1)} %fusion.17, f32[6,6,64,1]{3,2,1,0:T(8,128)S(1)} %get-tuple-element.39, f32[]{:T(128)S(6)} %add.2754, f32[]{:T(128)} %bitcast.5, ...), kind=kLoop, calls=%fused_computation.94 | loop fusion | flops 81100800 | bytes 11805708 | tf_op jit(solution)/shard_map/add | solution.py:160
  158.0 1.3 collective-permute-start.13
  159.3 5.1 %collective-permute-start.12 = (f32[3,6,64,128]{3,2,1,0:T(8,128)S(1)}, f32[3,6,64,128]{3,2,1,0:T(8,128)S(1)}, u32[]{:S(2)}, u32[]{:S(2)}) collective-permute-start(f32[3,6,64,128]{3,2,1,0:T(8,128)S(1)} %fusion.73), channel_id=1, source_target_pairs={{0,2},{2,4},{4,6},{6,8},{8,10},{10,12},{12,14},{1,3},{3,5},{5,7},{... | collective-permute-start | bytes 1769480 | tf_op jit(solution)/shard_map/ppermute | solution.py:85
  165.1 11.3 %collective-permute-done.13 = f32[3,6,64,128]{3,2,1,0:T(8,128)S(1)} collective-permute-done((f32[3,6,64,128]{3,2,1,0:T(8,128)S(1)}, f32[3,6,64,128]{3,2,1,0:T(8,128)S(1)}, u32[]{:S(2)}, u32[]{:S(2)}) %collective-permute-start.13) | collective-permute-done | bytes 589856 | tf_op jit(solution)/shard_map/ppermute | solution.py:90
  176.5 0.4 fusion
  176.9 12.2 %collective-permute-done.12 = f32[3,6,64,128]{3,2,1,0:T(8,128)S(1)} collective-permute-done((f32[3,6,64,128]{3,2,1,0:T(8,128)S(1)}, f32[3,6,64,128]{3,2,1,0:T(8,128)S(1)}, u32[]{:S(2)}, u32[]{:S(2)}) %collective-permute-start.12) | collective-permute-done | bytes 589856 | tf_op jit(solution)/shard_map/ppermute | solution.py:85
  190.4 14.1 %fusion.21 = f32[6,6,64,128]{3,2,1,0:T(8,128)} fusion(f32[3,6,64,128]{3,2,1,0:T(8,128)S(1)} %fusion.73, f32[3,6,64,128]{3,2,1,0:T(8,128)S(1)} %fusion.59, f32[6,6,64,128]{3,2,1,0:T(8,128)S(1)} %get-tuple-element.20, f32[6,6,64,128]{3,2,1,0:T(8,128)S(1)} %add_multiply_fusion, f32[6,11,64,128]{3,2,1,0:T(8,128)S(1)} %fusion, f32[11,6,64,128]{3,2,1,0:T(8,128)S(1)} %fusion.1, ...), kind=kLoop, calls=%fused_computation.66 | loop fusion | flops 81395712 | bytes 20096208 | tf_op jit(solution)/shard_map/add | solution.py:310
  (112 shorter events, 5.8 us)
Async XLA Ops:
  6.5 12.3 %copy-start = (f32[6,6,64,128]{3,2,1,0:T(8,128)S(1)}, f32[6,6,64,128]{3,2,1,0:T(8,128)}, u32[]{:S(2)}) copy-start(f32[6,6,64,128]{3,2,1,0:T(8,128)} %param.6) | copy-start | bytes 3538948
  6.5 40.4 %collective-permute-start.2 = (f32[2]{0:T(128)}, f32[2]{0:T(128)}, u32[]{:S(2)}, u32[]{:S(2)}) collective-permute-start(f32[2]{0:T(128)} %maximum_reduce_fusion), channel_id=1, source_target_pairs={{0,3},{1,4},{2,5},{3,6},{4,7},{5,8},{6,9},{7,10},{8,11},{9,12},{10... | collective-permute-start | bytes 32 | tf_op jit(solution)/shard_map/ppermute | solution.py:119
  9.0 38.9 %collective-permute-start.1 = (f32[2]{0:T(128)}, f32[2]{0:T(128)}, u32[]{:S(2)}, u32[]{:S(2)}) collective-permute-start(f32[2]{0:T(128)} %maximum_reduce_fusion), channel_id=1, source_target_pairs={{0,2},{1,3},{2,4},{3,5},{4,6},{5,7},{6,8},{7,9},{8,10},{9,11},{10,... | collective-permute-start | bytes 32 | tf_op jit(solution)/shard_map/ppermute | solution.py:119
  10.5 37.4 %collective-permute-start = (f32[2]{0:T(128)}, f32[2]{0:T(128)}, u32[]{:S(2)}, u32[]{:S(2)}) collective-permute-start(f32[2]{0:T(128)} %maximum_reduce_fusion), channel_id=1, source_target_pairs={{0,1},{1,2},{2,3},{3,4},{4,5},{5,6},{6,7},{7,8},{8,9},{9,10},{10,1... | collective-permute-start | bytes 32 | tf_op jit(solution)/shard_map/ppermute | solution.py:119
  13.4 47.3 %collective-permute-start.6 = (f32[3,6,64,128]{3,2,1,0:T(8,128)}, f32[3,6,64,128]{3,2,1,0:T(8,128)}, u32[]{:S(2)}, u32[]{:S(2)}) collective-permute-start(f32[3,6,64,128]{3,2,1,0:T(8,128)} %get-tuple-element.68), channel_id=1, source_target_pairs={{0,2},{2,4},{4,6},{6,8},{8,10},{10,12},{12,14},{1,3},{3,5},{5,7},{... | collective-permute-start | bytes 1769480 | tf_op jit(solution)/shard_map/ppermute | solution.py:85
  17.6 47.6 %collective-permute-start.8 = (f32[3,6,64,128]{3,2,1,0:T(8,128)}, f32[3,6,64,128]{3,2,1,0:T(8,128)}, u32[]{:S(2)}, u32[]{:S(2)}) collective-permute-start(f32[3,6,64,128]{3,2,1,0:T(8,128)} %get-tuple-element.67), channel_id=1, source_target_pairs={{2,0},{4,2},{6,4},{8,6},{10,8},{12,10},{14,12},{3,1},{5,3},{7,5},{... | collective-permute-start | bytes 1769480 | tf_op jit(solution)/shard_map/ppermute | solution.py:90
  22.1 0.9 copy-start.13
  26.3 1.7 copy-start.27
  26.3 2.3 %copy-start.26 = (f32[64]{0:T(128)S(1)}, f32[64]{0:T(128)}, u32[]{:S(2)}) copy-start(f32[64]{0:T(128)} %constant.502.clone) | copy-start | bytes 772
  26.4 2.8 %copy-start.1 = (f32[3,6,70,128]{3,2,1,0:T(8,128)S(1)}, f32[3,6,70,128]{3,2,1,0:T(8,128)}, u32[]{:S(2)}) copy-start(f32[3,6,70,128]{3,2,1,0:T(8,128)} %get-tuple-element.127) | copy-start | bytes 1935364
  37.2 1.5 copy-start.25
  45.6 0.7 copy-start.21
  45.6 1.3 copy-start.20
  46.3 20.7 %copy-start.14 = (f32[1,3,6]{2,1,0:T(4,128)}, f32[1,3,6]{2,1,0:T(4,128)S(1)}, u32[]{:S(2)}) copy-start(f32[1,3,6]{2,1,0:T(4,128)S(1)} %copy.43) | copy-start | bytes 220
  46.9 28.0 %copy-start.16 = (f32[1,3,6]{2,1,0:T(4,128)}, f32[1,3,6]{2,1,0:T(4,128)S(1)}, u32[]{:S(2)}) copy-start(f32[1,3,6]{2,1,0:T(4,128)S(1)} %copy.44) | copy-start | bytes 220
  46.9 15.1 %collective-permute-start.7 = (f32[6,3,64,128]{3,2,1,0:T(8,128)}, f32[6,3,64,128]{3,2,1,0:T(8,128)}, u32[]{:S(2)}, u32[]{:S(2)}) collective-permute-start(f32[6,3,64,128]{3,2,1,0:T(8,128)} %constant_dynamic-slice_fusion), channel_id=1, source_target_pairs={{0,1},{1,0},{2,3},{3,2},{4,5},{5,4},{6,7},{7,6},{8,9},{9,8},{10,11... | collective-permute-start | bytes 1769480 | tf_op jit(solution)/shard_map/ppermute | solution.py:178
  48.6 4.5 %collective-permute-start.5 = (f32[2]{0:T(128)S(1)}, f32[2]{0:T(128)S(1)}, u32[]{:S(2)}, u32[]{:S(2)}) collective-permute-start(f32[2]{0:T(128)S(1)} %maximum_maximum_fusion.1), channel_id=1, source_target_pairs={{0,12},{1,13},{2,14},{3,15},{4,0},{5,1},{6,2},{7,3},{8,4},{9,5},{1... | collective-permute-start | bytes 32 | tf_op jit(solution)/shard_map/ppermute | solution.py:119
  51.8 4.5 %collective-permute-start.4 = (f32[2]{0:T(128)S(1)}, f32[2]{0:T(128)S(1)}, u32[]{:S(2)}, u32[]{:S(2)}) collective-permute-start(f32[2]{0:T(128)S(1)} %maximum_maximum_fusion.1), channel_id=1, source_target_pairs={{0,8},{1,9},{2,10},{3,11},{4,12},{5,13},{6,14},{7,15},{8,0},{9,1},... | collective-permute-start | bytes 32 | tf_op jit(solution)/shard_map/ppermute | solution.py:119
  53.1 5.6 %collective-permute-start.3 = (f32[2]{0:T(128)S(1)}, f32[2]{0:T(128)S(1)}, u32[]{:S(2)}, u32[]{:S(2)}) collective-permute-start(f32[2]{0:T(128)S(1)} %maximum_maximum_fusion.1), channel_id=1, source_target_pairs={{0,4},{1,5},{2,6},{3,7},{4,8},{5,9},{6,10},{7,11},{8,12},{9,13},{1... | collective-permute-start | bytes 32 | tf_op jit(solution)/shard_map/ppermute | solution.py:119
  60.6 1.4 copy-start.3
  60.6 1.4 copy-start.4
  60.6 1.4 copy-start.5
  60.7 1.4 copy-start.6
  60.7 1.4 copy-start.7
  60.7 1.4 copy-start.8
  60.7 1.4 copy-start.9
  66.4 1.1 copy-start.2
  66.4 1.1 copy-start.11
  66.5 1.1 copy-start.19
  66.5 1.0 copy-start.23
  67.5 7.4 %copy-start.10 = (f32[3,6,64]{2,1,0:T(8,128)S(1)}, f32[3,6,64]{2,1,0:T(8,128)}, u32[]{:S(2)}) copy-start(f32[3,6,64]{2,1,0:T(8,128)} %get-tuple-element.113) | copy-start | bytes 13828
  67.5 7.4 %copy-start.22 = (f32[3]{0:T(128)S(1)}, f32[3]{0:T(128)}, u32[]{:S(2)}) copy-start(f32[3]{0:T(128)} %get-tuple-element.115) | copy-start | bytes 40
  83.6 18.5 %collective-permute-start.10 = (f32[6,3,64,128]{3,2,1,0:T(8,128)S(1)}, f32[6,3,64,128]{3,2,1,0:T(8,128)S(1)}, u32[]{:S(2)}, u32[]{:S(2)}) collective-permute-start(f32[6,3,64,128]{3,2,1,0:T(8,128)S(1)} %fusion.74), channel_id=1, source_target_pairs={{0,1},{1,0},{2,3},{3,2},{4,5},{5,4},{6,7},{7,6},{8,9},{9,8},{10,11... | collective-permute-start | bytes 1769480 | tf_op jit(solution)/shard_map/ppermute | solution.py:178
  97.0 29.4 %collective-permute-start.9 = (f32[3,6,64,128]{3,2,1,0:T(8,128)S(1)}, f32[3,6,64,128]{3,2,1,0:T(8,128)S(1)}, u32[]{:S(2)}, u32[]{:S(2)}) collective-permute-start(f32[3,6,64,128]{3,2,1,0:T(8,128)S(1)} %fusion.65), channel_id=1, source_target_pairs={{0,2},{2,4},{4,6},{6,8},{8,10},{10,12},{12,14},{1,3},{3,5},{5,7},{... | collective-permute-start | bytes 1769480 | tf_op jit(solution)/shard_map/ppermute | solution.py:85
  100.6 26.1 %collective-permute-start.11 = (f32[3,6,64,128]{3,2,1,0:T(8,128)S(1)}, f32[3,6,64,128]{3,2,1,0:T(8,128)S(1)}, u32[]{:S(2)}, u32[]{:S(2)}) collective-permute-start(f32[3,6,64,128]{3,2,1,0:T(8,128)S(1)} %fusion.51), channel_id=1, source_target_pairs={{2,0},{4,2},{6,4},{8,6},{10,8},{12,10},{14,12},{3,1},{5,3},{7,5},{... | collective-permute-start | bytes 1769480 | tf_op jit(solution)/shard_map/ppermute | solution.py:90
  127.8 0.7 copy-start.15
  128.5 7.5 %copy-start.17 = (f32[1,3,6]{2,1,0:T(4,128)S(1)}, f32[1,3,6]{2,1,0:T(4,128)}, u32[]{:S(2)}) copy-start(f32[1,3,6]{2,1,0:T(4,128)} %copy-done.16) | copy-start | bytes 220
  157.9 6.6 %collective-permute-start.14 = (f32[6,3,64,128]{3,2,1,0:T(8,128)S(1)}, f32[6,3,64,128]{3,2,1,0:T(8,128)S(1)}, u32[]{:S(2)}, u32[]{:S(2)}) collective-permute-start(f32[6,3,64,128]{3,2,1,0:T(8,128)S(1)} %fusion.75), channel_id=1, source_target_pairs={{0,1},{1,0},{2,3},{3,2},{4,5},{5,4},{6,7},{7,6},{8,9},{9,8},{10,11... | collective-permute-start | bytes 1769480 | tf_op jit(solution)/shard_map/ppermute | solution.py:178
  158.0 18.4 %collective-permute-start.13 = (f32[3,6,64,128]{3,2,1,0:T(8,128)S(1)}, f32[3,6,64,128]{3,2,1,0:T(8,128)S(1)}, u32[]{:S(2)}, u32[]{:S(2)}) collective-permute-start(f32[3,6,64,128]{3,2,1,0:T(8,128)S(1)} %fusion.59), channel_id=1, source_target_pairs={{2,0},{4,2},{6,4},{8,6},{10,8},{12,10},{14,12},{3,1},{5,3},{7,5},{... | collective-permute-start | bytes 1769480 | tf_op jit(solution)/shard_map/ppermute | solution.py:90
  159.3 29.9 %collective-permute-start.12 = (f32[3,6,64,128]{3,2,1,0:T(8,128)S(1)}, f32[3,6,64,128]{3,2,1,0:T(8,128)S(1)}, u32[]{:S(2)}, u32[]{:S(2)}) collective-permute-start(f32[3,6,64,128]{3,2,1,0:T(8,128)S(1)} %fusion.73), channel_id=1, source_target_pairs={{0,2},{2,4},{4,6},{6,8},{8,10},{10,12},{12,14},{1,3},{3,5},{5,7},{... | collective-permute-start | bytes 1769480 | tf_op jit(solution)/shard_map/ppermute | solution.py:85
  189.6 0.7 copy-start.12
  189.6 0.7 copy-start.18
  189.6 0.7 copy-start.24

commit v8 on v7

--- a/solution.py
+++ b/solution.py
@@ -272,26 +272,30 @@
         return ham + 0.5 * (bound_one * spread_one + bound_two * spread_two)
 
     def stage(field, x_halos, y_halos, local_pieces, order, update, last):
-        results = [None, None]
-        sent = [None, None]
         if last:
             rate = combine(*half_parts(field, 2, x_halos, *y_halos, *local_pieces))
             return update(2, rate), None, None, None
-        for side in order:
+        results = [None, None]
+        sent = [None, None]
+
+        def half(side):
             pieces = local_pieces[side] if isinstance(local_pieces, list) else local_pieces
             parts = half_parts(field, side, x_halos, *y_halos, *pieces)
             results[side] = update(side, combine(*parts))
-            if last:
-                continue
+
+        def send(side):
             if side == 0:
                 piece = lax.optimization_barrier(results[side][:3])
                 sent[side] = send_high(piece, "gx")
             else:
                 piece = lax.optimization_barrier(results[side][results[side].shape[0] - 3 :])
                 sent[side] = send_low(piece, "gx")
+
+        half(order[0])
+        send(order[0])
+        half(order[1])
+        send(order[1])
         merged = jnp.concatenate(results, axis=0)
-        if last:
-            return merged, None, None, None
         next_y = y_halo(merged)
         next_pieces = local_whole(merged)
         return merged, (sent[1], sent[0]), next_y, next_pieces

time: 205 us -> 205 us (level)
  no operation moved by 1% of the time
where the time goes in v8:
time: 205 us; the launch traced here: 204 us
  other arithmetic  109 us (53%)
  waiting for transfers between devices  51.9 us (25%)
  starting transfers between devices  28 us (14%)
  local copies, waits for them, and re-layouts  9.53 us (5%)
  between operations  6.02 us (3%)
    add x4, other arithmetic, local_part(): partial + 0.5 * (alpha_three * (fore_three - back_three) + alpha_four * (...  40.3 us
    ppermute x3, waiting for transfers between devices, send_low(): lax.ppermute(piece, axis, [(i, (i + 1) % count) for i in range(count - 1)])  36.1 us
    add x2, other arithmetic, on_device(): 0.75 * cut(values, side) + 0.25 * (cut(first, side) + step_time * rate)  14.9 us
    add x2, other arithmetic, on_device(): cut(values, side) + step_time * rate  14.8 us
    add x1, other arithmetic, on_device(): cut(values, side) * (1.0 / 3.0)  14.1 us
    ppermute x3, starting transfers between devices, send_low(): lax.ppermute(piece, axis, [(i, (i + 1) % count) for i in range(count - 1)])  12.8 us
    ppermute x3, waiting for transfers between devices, send_high(): lax.ppermute(piece, axis, [((i + 1) % count, i) for i in range(count - 1)])  11.3 us
    ppermute x6, starting transfers between devices, spread_max(): lax.ppermute(local, axes, [(i, (i + k * span) % count) for i in range(cou...  9.98 us
  transfers between devices with their start and end apart: 15, of which 6 were waited for; matrix products, arithmetic and copies ran while one was open for 24% of the time, Pallas kernels for 0%

profile of v8, /device:TPU:0, one launch (start us, length us, event | category | flops | bytes accessed | tf_op | source)
XLA Modules:
  0.0 204.5 jit_solution(15133526762475849442)
XLA Ops:
  0.0 1.4 fusion.134
  1.4 0.8 fusion.132
  2.2 0.6 abs_multiply_fusion
  2.8 0.6 abs_multiply_fusion.1
  4.7 1.2 copy_bitcast_fusion
  5.9 0.6 maximum_reduce_fusion
  6.5 2.4 %collective-permute-start.2 = (f32[2]{0:T(128)}, f32[2]{0:T(128)}, u32[]{:S(2)}, u32[]{:S(2)}) collective-permute-start(f32[2]{0:T(128)} %maximum_reduce_fusion), channel_id=1, source_target_pairs={{0,3},{1,4},{2,5},{3,6},{4,7},{5,8},{6,9},{7,10},{8,11},{9,12},{10... | collective-permute-start | bytes 32 | tf_op jit(solution)/shard_map/ppermute | solution.py:119
  9.0 1.5 collective-permute-start.1
  10.5 0.5 collective-permute-start
  11.0 2.4 %fusion.128 = (f32[3,6,64,128]{3,2,1,0:T(8,128)}, f32[3,6,64,128]{3,2,1,0:T(8,128)}) fusion(f32[6,6,64,128]{3,2,1,0:T(8,128)} %param.6), kind=kLoop, calls=%fused_computation.312 | loop fusion | bytes 2359296 | tf_op jit(solution)/shard_map/slice | solution.py:149
  13.4 4.2 %collective-permute-start.6 = (f32[3,6,64,128]{3,2,1,0:T(8,128)}, f32[3,6,64,128]{3,2,1,0:T(8,128)}, u32[]{:S(2)}, u32[]{:S(2)}) collective-permute-start(f32[3,6,64,128]{3,2,1,0:T(8,128)} %get-tuple-element.68), channel_id=1, source_target_pairs={{0,2},{2,4},{4,6},{6,8},{8,10},{10,12},{12,14},{1,3},{3,5},{5,7},{... | collective-permute-start | bytes 1769480 | tf_op jit(solution)/shard_map/ppermute | solution.py:85
  17.6 1.3 collective-permute-start.8
  18.9 0.4 subtract_multiply_fusion.1
  21.2 0.9 slice_bitcast_fusion.13
  22.1 0.8 slice_bitcast_fusion.5
  23.0 0.6 fusion.131
  23.6 0.5 fusion.120
  24.1 2.2 %pad_maximum_fusion.30 = (f32[3,6,70,128]{3,2,1,0:T(8,128)}, f32[3,6,70,128]{3,2,1,0:T(8,128)S(1)}) fusion(f32[3,6,3,128]{3,2,1,0:T(4,128)S(1)} %get-tuple-element.63, f32[3,6,64,128]{3,2,1,0:T(8,128)} %get-tuple-element.67, f32[3,6,3,128]{3,2,1,0:T(4,128)S(1)} %get-tuple-element.61, f32[3,6,3,128]{3,2,1,0:T(4,128)S(1)} %get-tuple-element.64, ...), kind=kLoop, calls=%fused_computation.130 | loop fusion | flops 645120 | bytes 2580480 | tf_op jit(solution)/shard_map/concatenate | solution.py:56
  26.4 0.9 constant_dynamic-slice_fusion
  27.3 0.7 slice_multiply_fusion.1
  28.0 0.6 broadcast_multiply_fusion
  28.6 0.6 broadcast_multiply_fusion.1
  29.3 0.4 fusion.129
  29.8 7.5 %multiply_add_fusion.2 = (f32[3,6,64,128]{3,2,1,0:T(8,128)}, f32[3,6,64,128]{3,2,1,0:T(8,128)S(1)}, f32[3,6,64,128]{3,2,1,0:T(8,128)S(1)}) fusion(f32[3,6,64,1]{3,2,1,0:T(8,128)S(1)} %get-tuple-element.125, f32[3,6,64,127]{3,2,1,0:T(8,128)S(1)} %get-tuple-element.66, f32[3,6,64,1]{3,2,1,0:T(8,128)S(1)} %get-tuple-element.126, f32[]{:T(128)S(6)} %add.2754, ...), kind=kLoop, calls=%fused_computation.189 | loop fusion | flops 40550400 | bytes 5902860 | tf_op jit(solution)/shard_map/add | solution.py:160
  37.3 0.7 add_multiply_fusion.8
  38.0 0.7 add_multiply_fusion.10
  38.8 6.8 %multiply_add_fusion.3 = (f32[3,6,64,128]{3,2,1,0:T(8,128)S(1)}, f32[3,6,64,128]{3,2,1,0:T(8,128)S(1)}, f32[3,6,64,128]{3,2,1,0:T(8,128)S(1)}) fusion(f32[3,6,64,1]{3,2,1,0:T(8,128)S(1)} %get-tuple-element.100, f32[3,6,64,127]{3,2,1,0:T(8,128)S(1)} %get-tuple-element.65, f32[3,6,64,1]{3,2,1,0:T(8,128)S(1)} %get-tuple-element.99, f32[]{:T(128)S(6)} %add.2754, ...), kind=kLoop, calls=%fused_computation.202 | loop fusion | flops 40550400 | bytes 5902860 | tf_op jit(solution)/shard_map/add | solution.py:160
  45.7 0.5 fusion.121
  46.9 1.0 collective-permute-start.7
  47.9 0.7 maximum_maximum_fusion.1
  48.6 3.2 %collective-permute-start.5 = (f32[2]{0:T(128)S(1)}, f32[2]{0:T(128)S(1)}, u32[]{:S(2)}, u32[]{:S(2)}) collective-permute-start(f32[2]{0:T(128)S(1)} %maximum_maximum_fusion.1), channel_id=1, source_target_pairs={{0,12},{1,13},{2,14},{3,15},{4,0},{5,1},{6,2},{7,3},{8,4},{9,5},{1... | collective-permute-start | bytes 32 | tf_op jit(solution)/shard_map/ppermute | solution.py:119
  51.8 0.8 collective-permute-start.4
  52.6 0.5 collective-permute-done.5
  53.1 1.6 collective-permute-start.3
  54.7 1.6 collective-permute-done.4
  56.2 2.4 %collective-permute-done.3 = f32[2]{0:T(128)S(1)} collective-permute-done((f32[2]{0:T(128)S(1)}, f32[2]{0:T(128)S(1)}, u32[]{:S(2)}, u32[]{:S(2)}) %collective-permute-start.3) | collective-permute-done | bytes 40 | tf_op jit(solution)/shard_map/ppermute | solution.py:119
  58.7 0.6 fusion.133
  60.7 1.3 add_select_fusion.7
  62.1 1.3 add_select_fusion.15
  63.4 1.5 pad_maximum_fusion.22
  65.2 1.2 add_select_fusion.5
  66.5 0.5 fusion.7
  66.9 0.6 copy-done.2
  67.5 7.4 %fusion.65 = f32[3,6,64,128]{3,2,1,0:T(8,128)S(1)} fusion(f32[3,6,64,128]{3,2,1,0:T(8,128)S(1)} %copy-done.2, f32[3,6,64,128]{3,2,1,0:T(8,128)S(1)} %add_multiply_fusion.6, f32[3,11,64,128]{3,2,1,0:T(8,128)S(1)} %fusion.42, f32[8,6,64,128]{3,2,1,0:T(8,128)S(1)} %get-tuple-element.48, f32[3]{0:T(128)S(1)} %copy-done.23, f32[3,6,64]{2,1,0:T(8,128)S(1)} %copy-done.11, ...), kind=kLoop, calls=%fused_computation.151 | loop fusion | flops 40108032 | bytes 9474684 | tf_op jit(solution)/shard_map/add | solution.py:305
  74.9 7.4 %fusion.51 = f32[3,6,64,128]{3,2,1,0:T(8,128)S(1)} fusion(f32[3,6,64,128]{3,2,1,0:T(8,128)S(1)} %get-tuple-element.14, f32[3,6,64,128]{3,2,1,0:T(8,128)S(1)} %add_multiply_fusion.7, f32[3,11,64,128]{3,2,1,0:T(8,128)S(1)} %fusion.43, f32[8,6,64,128]{3,2,1,0:T(8,128)S(1)} %get-tuple-element.47, f32[]{:T(128)} %bitcast.3, f32[]{:T(128)} %bitcast.2, ...), kind=kLoop, calls=%fused_computation.137 | loop fusion | flops 40108032 | bytes 9474684 | tf_op jit(solution)/shard_map/add | solution.py:305
  82.3 0.4 fusion.14
  82.8 0.4 fusion.126
  83.7 13.0 %multiply_add_fusion.1 = (f32[6,6,64,128]{3,2,1,0:T(8,128)S(1)}, f32[6,6,64,128]{3,2,1,0:T(8,128)S(1)}, f32[6,6,64,128]{3,2,1,0:T(8,128)S(1)}) fusion(f32[6,6,64,1]{3,2,1,0:T(8,128)S(1)} %get-tuple-element.46, f32[6,6,64,127]{3,2,1,0:T(8,128)S(1)} %fusion.14, f32[6,6,64,1]{3,2,1,0:T(8,128)S(1)} %get-tuple-element.45, f32[]{:T(128)S(6)} %add.2754, ...), kind=kLoop, calls=%fused_computation.104 | loop fusion | flops 81100800 | bytes 11805708 | tf_op jit(solution)/shard_map/add | solution.py:160
  97.0 3.5 %collective-permute-start.9 = (f32[3,6,64,128]{3,2,1,0:T(8,128)S(1)}, f32[3,6,64,128]{3,2,1,0:T(8,128)S(1)}, u32[]{:S(2)}, u32[]{:S(2)}) collective-permute-start(f32[3,6,64,128]{3,2,1,0:T(8,128)S(1)} %fusion.65), channel_id=1, source_target_pairs={{0,2},{2,4},{4,6},{6,8},{8,10},{10,12},{12,14},{1,3},{3,5},{5,7},{... | collective-permute-start | bytes 1769480 | tf_op jit(solution)/shard_map/ppermute | solution.py:85
  100.6 1.5 collective-permute-start.11
  102.5 23.9 %collective-permute-done.9 = f32[3,6,64,128]{3,2,1,0:T(8,128)S(1)} collective-permute-done((f32[3,6,64,128]{3,2,1,0:T(8,128)S(1)}, f32[3,6,64,128]{3,2,1,0:T(8,128)S(1)}, u32[]{:S(2)}, u32[]{:S(2)}) %collective-permute-start.9) | collective-permute-done | bytes 589856 | tf_op jit(solution)/shard_map/ppermute | solution.py:85
  126.9 0.5 pad_maximum_fusion.3
  128.0 0.5 copy-done.15
  128.5 7.5 %fusion.73 = f32[3,6,64,128]{3,2,1,0:T(8,128)S(1)} fusion(f32[3,6,64,128]{3,2,1,0:T(8,128)S(1)} %fusion.65, f32[6,6,64,128]{3,2,1,0:T(8,128)S(1)} %get-tuple-element.18, f32[6,6,64,128]{3,2,1,0:T(8,128)S(1)} %add_multiply_fusion.1, f32[3,11,64,128]{3,2,1,0:T(8,128)S(1)} %fusion.40, f32[8,6,64,128]{3,2,1,0:T(8,128)S(1)} %fusion.8, f32[3]{0:T(128)S(1)} %copy-done.23, ...), kind=kLoop, calls=%fused_computation.159 | loop fusion | flops 40550400 | bytes 10064508 | tf_op jit(solution)/shard_map/add | solution.py:309
  135.9 7.4 %fusion.59 = f32[3,6,64,128]{3,2,1,0:T(8,128)S(1)} fusion(f32[3,6,64,128]{3,2,1,0:T(8,128)S(1)} %fusion.51, f32[6,6,64,128]{3,2,1,0:T(8,128)S(1)} %get-tuple-element.18, f32[6,6,64,128]{3,2,1,0:T(8,128)S(1)} %add_multiply_fusion.1, f32[3,11,64,128]{3,2,1,0:T(8,128)S(1)} %fusion.41, f32[8,6,64,128]{3,2,1,0:T(8,128)S(1)} %fusion.9, f32[]{:T(128)} %bitcast.3, ...), kind=kLoop, calls=%fused_computation.145 | loop fusion | flops 40550400 | bytes 10064508 | tf_op jit(solution)/shard_map/add | solution.py:309
  143.4 0.4 fusion.17
  143.9 0.4 fusion.125
  144.6 13.0 %multiply_add_fusion = (f32[6,6,64,128]{3,2,1,0:T(8,128)S(1)}, f32[6,6,64,128]{3,2,1,0:T(8,128)S(1)}, f32[6,6,64,128]{3,2,1,0:T(8,128)S(1)}) fusion(f32[6,6,64,1]{3,2,1,0:T(8,128)S(1)} %get-tuple-element.40, f32[6,6,64,127]{3,2,1,0:T(8,128)S(1)} %fusion.17, f32[6,6,64,1]{3,2,1,0:T(8,128)S(1)} %get-tuple-element.39, f32[]{:T(128)S(6)} %add.2754, f32[]{:T(128)} %bitcast.5, ...), kind=kLoop, calls=%fused_computation.94 | loop fusion | flops 81100800 | bytes 11805708 | tf_op jit(solution)/shard_map/add | solution.py:160
  158.0 1.3 collective-permute-start.13
  159.3 5.1 %collective-permute-start.12 = (f32[3,6,64,128]{3,2,1,0:T(8,128)S(1)}, f32[3,6,64,128]{3,2,1,0:T(8,128)S(1)}, u32[]{:S(2)}, u32[]{:S(2)}) collective-permute-start(f32[3,6,64,128]{3,2,1,0:T(8,128)S(1)} %fusion.73), channel_id=1, source_target_pairs={{0,2},{2,4},{4,6},{6,8},{8,10},{10,12},{12,14},{1,3},{3,5},{5,7},{... | collective-permute-start | bytes 1769480 | tf_op jit(solution)/shard_map/ppermute | solution.py:85
  165.1 11.3 %collective-permute-done.13 = f32[3,6,64,128]{3,2,1,0:T(8,128)S(1)} collective-permute-done((f32[3,6,64,128]{3,2,1,0:T(8,128)S(1)}, f32[3,6,64,128]{3,2,1,0:T(8,128)S(1)}, u32[]{:S(2)}, u32[]{:S(2)}) %collective-permute-start.13) | collective-permute-done | bytes 589856 | tf_op jit(solution)/shard_map/ppermute | solution.py:90
  176.5 0.4 fusion
  176.9 12.2 %collective-permute-done.12 = f32[3,6,64,128]{3,2,1,0:T(8,128)S(1)} collective-permute-done((f32[3,6,64,128]{3,2,1,0:T(8,128)S(1)}, f32[3,6,64,128]{3,2,1,0:T(8,128)S(1)}, u32[]{:S(2)}, u32[]{:S(2)}) %collective-permute-start.12) | collective-permute-done | bytes 589856 | tf_op jit(solution)/shard_map/ppermute | solution.py:85
  190.4 14.1 %fusion.21 = f32[6,6,64,128]{3,2,1,0:T(8,128)} fusion(f32[3,6,64,128]{3,2,1,0:T(8,128)S(1)} %fusion.73, f32[3,6,64,128]{3,2,1,0:T(8,128)S(1)} %fusion.59, f32[6,6,64,128]{3,2,1,0:T(8,128)S(1)} %get-tuple-element.20, f32[6,6,64,128]{3,2,1,0:T(8,128)S(1)} %add_multiply_fusion, f32[6,11,64,128]{3,2,1,0:T(8,128)S(1)} %fusion, f32[11,6,64,128]{3,2,1,0:T(8,128)S(1)} %fusion.1, ...), kind=kLoop, calls=%fused_computation.66 | loop fusion | flops 81395712 | bytes 20096208 | tf_op jit(solution)/shard_map/add | solution.py:314
  (112 shorter events, 5.8 us)
Async XLA Ops:
  6.5 12.3 %copy-start = (f32[6,6,64,128]{3,2,1,0:T(8,128)S(1)}, f32[6,6,64,128]{3,2,1,0:T(8,128)}, u32[]{:S(2)}) copy-start(f32[6,6,64,128]{3,2,1,0:T(8,128)} %param.6) | copy-start | bytes 3538948
  6.5 40.4 %collective-permute-start.2 = (f32[2]{0:T(128)}, f32[2]{0:T(128)}, u32[]{:S(2)}, u32[]{:S(2)}) collective-permute-start(f32[2]{0:T(128)} %maximum_reduce_fusion), channel_id=1, source_target_pairs={{0,3},{1,4},{2,5},{3,6},{4,7},{5,8},{6,9},{7,10},{8,11},{9,12},{10... | collective-permute-start | bytes 32 | tf_op jit(solution)/shard_map/ppermute | solution.py:119
  9.0 38.9 %collective-permute-start.1 = (f32[2]{0:T(128)}, f32[2]{0:T(128)}, u32[]{:S(2)}, u32[]{:S(2)}) collective-permute-start(f32[2]{0:T(128)} %maximum_reduce_fusion), channel_id=1, source_target_pairs={{0,2},{1,3},{2,4},{3,5},{4,6},{5,7},{6,8},{7,9},{8,10},{9,11},{10,... | collective-permute-start | bytes 32 | tf_op jit(solution)/shard_map/ppermute | solution.py:119
  10.5 37.4 %collective-permute-start = (f32[2]{0:T(128)}, f32[2]{0:T(128)}, u32[]{:S(2)}, u32[]{:S(2)}) collective-permute-start(f32[2]{0:T(128)} %maximum_reduce_fusion), channel_id=1, source_target_pairs={{0,1},{1,2},{2,3},{3,4},{4,5},{5,6},{6,7},{7,8},{8,9},{9,10},{10,1... | collective-permute-start | bytes 32 | tf_op jit(solution)/shard_map/ppermute | solution.py:119
  13.4 47.3 %collective-permute-start.6 = (f32[3,6,64,128]{3,2,1,0:T(8,128)}, f32[3,6,64,128]{3,2,1,0:T(8,128)}, u32[]{:S(2)}, u32[]{:S(2)}) collective-permute-start(f32[3,6,64,128]{3,2,1,0:T(8,128)} %get-tuple-element.68), channel_id=1, source_target_pairs={{0,2},{2,4},{4,6},{6,8},{8,10},{10,12},{12,14},{1,3},{3,5},{5,7},{... | collective-permute-start | bytes 1769480 | tf_op jit(solution)/shard_map/ppermute | solution.py:85
  17.6 47.6 %collective-permute-start.8 = (f32[3,6,64,128]{3,2,1,0:T(8,128)}, f32[3,6,64,128]{3,2,1,0:T(8,128)}, u32[]{:S(2)}, u32[]{:S(2)}) collective-permute-start(f32[3,6,64,128]{3,2,1,0:T(8,128)} %get-tuple-element.67), channel_id=1, source_target_pairs={{2,0},{4,2},{6,4},{8,6},{10,8},{12,10},{14,12},{3,1},{5,3},{7,5},{... | collective-permute-start | bytes 1769480 | tf_op jit(solution)/shard_map/ppermute | solution.py:90
  22.1 0.9 copy-start.13
  26.3 1.7 copy-start.27
  26.3 2.3 %copy-start.26 = (f32[64]{0:T(128)S(1)}, f32[64]{0:T(128)}, u32[]{:S(2)}) copy-start(f32[64]{0:T(128)} %constant.502.clone) | copy-start | bytes 772
  26.4 2.8 %copy-start.1 = (f32[3,6,70,128]{3,2,1,0:T(8,128)S(1)}, f32[3,6,70,128]{3,2,1,0:T(8,128)}, u32[]{:S(2)}) copy-start(f32[3,6,70,128]{3,2,1,0:T(8,128)} %get-tuple-element.127) | copy-start | bytes 1935364
  37.2 1.5 copy-start.25
  45.6 0.7 copy-start.21
  45.6 1.3 copy-start.20
  46.3 20.7 %copy-start.14 = (f32[1,3,6]{2,1,0:T(4,128)}, f32[1,3,6]{2,1,0:T(4,128)S(1)}, u32[]{:S(2)}) copy-start(f32[1,3,6]{2,1,0:T(4,128)S(1)} %copy.43) | copy-start | bytes 220
  46.9 28.0 %copy-start.16 = (f32[1,3,6]{2,1,0:T(4,128)}, f32[1,3,6]{2,1,0:T(4,128)S(1)}, u32[]{:S(2)}) copy-start(f32[1,3,6]{2,1,0:T(4,128)S(1)} %copy.44) | copy-start | bytes 220
  46.9 15.1 %collective-permute-start.7 = (f32[6,3,64,128]{3,2,1,0:T(8,128)}, f32[6,3,64,128]{3,2,1,0:T(8,128)}, u32[]{:S(2)}, u32[]{:S(2)}) collective-permute-start(f32[6,3,64,128]{3,2,1,0:T(8,128)} %constant_dynamic-slice_fusion), channel_id=1, source_target_pairs={{0,1},{1,0},{2,3},{3,2},{4,5},{5,4},{6,7},{7,6},{8,9},{9,8},{10,11... | collective-permute-start | bytes 1769480 | tf_op jit(solution)/shard_map/ppermute | solution.py:178
  48.6 4.5 %collective-permute-start.5 = (f32[2]{0:T(128)S(1)}, f32[2]{0:T(128)S(1)}, u32[]{:S(2)}, u32[]{:S(2)}) collective-permute-start(f32[2]{0:T(128)S(1)} %maximum_maximum_fusion.1), channel_id=1, source_target_pairs={{0,12},{1,13},{2,14},{3,15},{4,0},{5,1},{6,2},{7,3},{8,4},{9,5},{1... | collective-permute-start | bytes 32 | tf_op jit(solution)/shard_map/ppermute | solution.py:119
  51.8 4.5 %collective-permute-start.4 = (f32[2]{0:T(128)S(1)}, f32[2]{0:T(128)S(1)}, u32[]{:S(2)}, u32[]{:S(2)}) collective-permute-start(f32[2]{0:T(128)S(1)} %maximum_maximum_fusion.1), channel_id=1, source_target_pairs={{0,8},{1,9},{2,10},{3,11},{4,12},{5,13},{6,14},{7,15},{8,0},{9,1},... | collective-permute-start | bytes 32 | tf_op jit(solution)/shard_map/ppermute | solution.py:119
  53.1 5.6 %collective-permute-start.3 = (f32[2]{0:T(128)S(1)}, f32[2]{0:T(128)S(1)}, u32[]{:S(2)}, u32[]{:S(2)}) collective-permute-start(f32[2]{0:T(128)S(1)} %maximum_maximum_fusion.1), channel_id=1, source_target_pairs={{0,4},{1,5},{2,6},{3,7},{4,8},{5,9},{6,10},{7,11},{8,12},{9,13},{1... | collective-permute-start | bytes 32 | tf_op jit(solution)/shard_map/ppermute | solution.py:119
  60.6 1.4 copy-start.3
  60.6 1.4 copy-start.4
  60.6 1.4 copy-start.5
  60.7 1.4 copy-start.6
  60.7 1.4 copy-start.7
  60.7 1.4 copy-start.8
  60.7 1.4 copy-start.9
  66.4 1.1 copy-start.2
  66.4 1.1 copy-start.11
  66.5 1.1 copy-start.19
  66.5 1.0 copy-start.23
  67.5 7.4 %copy-start.10 = (f32[3,6,64]{2,1,0:T(8,128)S(1)}, f32[3,6,64]{2,1,0:T(8,128)}, u32[]{:S(2)}) copy-start(f32[3,6,64]{2,1,0:T(8,128)} %get-tuple-element.113) | copy-start | bytes 13828
  67.5 7.4 %copy-start.22 = (f32[3]{0:T(128)S(1)}, f32[3]{0:T(128)}, u32[]{:S(2)}) copy-start(f32[3]{0:T(128)} %get-tuple-element.115) | copy-start | bytes 40
  83.6 18.5 %collective-permute-start.10 = (f32[6,3,64,128]{3,2,1,0:T(8,128)S(1)}, f32[6,3,64,128]{3,2,1,0:T(8,128)S(1)}, u32[]{:S(2)}, u32[]{:S(2)}) collective-permute-start(f32[6,3,64,128]{3,2,1,0:T(8,128)S(1)} %fusion.74), channel_id=1, source_target_pairs={{0,1},{1,0},{2,3},{3,2},{4,5},{5,4},{6,7},{7,6},{8,9},{9,8},{10,11... | collective-permute-start | bytes 1769480 | tf_op jit(solution)/shard_map/ppermute | solution.py:178
  97.0 29.4 %collective-permute-start.9 = (f32[3,6,64,128]{3,2,1,0:T(8,128)S(1)}, f32[3,6,64,128]{3,2,1,0:T(8,128)S(1)}, u32[]{:S(2)}, u32[]{:S(2)}) collective-permute-start(f32[3,6,64,128]{3,2,1,0:T(8,128)S(1)} %fusion.65), channel_id=1, source_target_pairs={{0,2},{2,4},{4,6},{6,8},{8,10},{10,12},{12,14},{1,3},{3,5},{5,7},{... | collective-permute-start | bytes 1769480 | tf_op jit(solution)/shard_map/ppermute | solution.py:85
  100.6 26.1 %collective-permute-start.11 = (f32[3,6,64,128]{3,2,1,0:T(8,128)S(1)}, f32[3,6,64,128]{3,2,1,0:T(8,128)S(1)}, u32[]{:S(2)}, u32[]{:S(2)}) collective-permute-start(f32[3,6,64,128]{3,2,1,0:T(8,128)S(1)} %fusion.51), channel_id=1, source_target_pairs={{2,0},{4,2},{6,4},{8,6},{10,8},{12,10},{14,12},{3,1},{5,3},{7,5},{... | collective-permute-start | bytes 1769480 | tf_op jit(solution)/shard_map/ppermute | solution.py:90
  127.8 0.7 copy-start.15
  128.5 7.5 %copy-start.17 = (f32[1,3,6]{2,1,0:T(4,128)S(1)}, f32[1,3,6]{2,1,0:T(4,128)}, u32[]{:S(2)}) copy-start(f32[1,3,6]{2,1,0:T(4,128)} %copy-done.16) | copy-start | bytes 220
  157.9 6.6 %collective-permute-start.14 = (f32[6,3,64,128]{3,2,1,0:T(8,128)S(1)}, f32[6,3,64,128]{3,2,1,0:T(8,128)S(1)}, u32[]{:S(2)}, u32[]{:S(2)}) collective-permute-start(f32[6,3,64,128]{3,2,1,0:T(8,128)S(1)} %fusion.75), channel_id=1, source_target_pairs={{0,1},{1,0},{2,3},{3,2},{4,5},{5,4},{6,7},{7,6},{8,9},{9,8},{10,11... | collective-permute-start | bytes 1769480 | tf_op jit(solution)/shard_map/ppermute | solution.py:178
  158.0 18.4 %collective-permute-start.13 = (f32[3,6,64,128]{3,2,1,0:T(8,128)S(1)}, f32[3,6,64,128]{3,2,1,0:T(8,128)S(1)}, u32[]{:S(2)}, u32[]{:S(2)}) collective-permute-start(f32[3,6,64,128]{3,2,1,0:T(8,128)S(1)} %fusion.59), channel_id=1, source_target_pairs={{2,0},{4,2},{6,4},{8,6},{10,8},{12,10},{14,12},{3,1},{5,3},{7,5},{... | collective-permute-start | bytes 1769480 | tf_op jit(solution)/shard_map/ppermute | solution.py:90
  159.3 29.9 %collective-permute-start.12 = (f32[3,6,64,128]{3,2,1,0:T(8,128)S(1)}, f32[3,6,64,128]{3,2,1,0:T(8,128)S(1)}, u32[]{:S(2)}, u32[]{:S(2)}) collective-permute-start(f32[3,6,64,128]{3,2,1,0:T(8,128)S(1)} %fusion.73), channel_id=1, source_target_pairs={{0,2},{2,4},{4,6},{6,8},{8,10},{10,12},{12,14},{1,3},{3,5},{5,7},{... | collective-permute-start | bytes 1769480 | tf_op jit(solution)/shard_map/ppermute | solution.py:85
  189.6 0.7 copy-start.12
  189.6 0.7 copy-start.18
  189.6 0.7 copy-start.24

commit v9 on v8

--- a/solution.py
+++ b/solution.py
@@ -109,20 +109,20 @@
     return jnp.where(at_high, inner + dist * (inner - before), halo)
 
 
-def spread_max(local, axes):
-    count = 1
-    for axis in axes:
-        count *= lax.axis_size(axis)
+def spread_max(local, axis, first_level):
+    count = lax.axis_size(axis)
     span = 1
+    level = first_level
     while span < count:
         moved = [
-            lax.ppermute(local, axes, [(i, (i + k * span) % count) for i in range(count)])
+            lax.ppermute(local, axis, [(i, (i + k * span) % count) for i in range(count)])
             for k in range(1, 4)
             if k * span < count
         ]
         for item in moved:
             local = jnp.maximum(local, item)
         span *= 4
+        level += 1
     return local
 
 
@@ -168,9 +168,14 @@
             pieces.append(lax.optimization_barrier(local_part(cut(field, side))))
         return pieces
 
-    def y_halo(field):
+    def y_halo(field, whole=False):
         tail = lax.slice_in_dim(field, cells_y - 3, cells_y, axis=1)
         head = lax.slice_in_dim(field, 0, 3, axis=1)
+        if devices_y == 2 and whole:
+            swapped = lax.ppermute(field, "gy", [(0, 1), (1, 0)])
+            offset = jnp.where(first_y, 0, cells_y - 3)
+            piece = lax.dynamic_slice_in_dim(swapped, offset, 3, axis=1)
+            return piece, piece
         if devices_y == 2:
             offset = jnp.where(first_y, cells_y - 3, 0)
             piece = lax.dynamic_slice_in_dim(field, offset, 3, axis=1)
@@ -184,7 +189,7 @@
         return lax.optimization_barrier(local_part(field))
 
     x_halos = (send_low(values[cells_x - 3 :], "gx"), send_high(values[:3], "gx"))
-    y_halos = y_halo(values)
+    y_halos = y_halo(values, whole=True)
     psi_grid = np.arange(n_psi).astype(np.float32) * np.float32(step_psi) - np.float32(math.pi)
     cos_table = np.cos(psi_grid.astype(np.float64)).astype(np.float32)
     sin_table = np.sin(psi_grid.astype(np.float64)).astype(np.float32)
@@ -213,7 +218,7 @@
     )
     local_bounds = jnp.max(terms, axis=(1, 2))
     locals_now = local_halves(values)
-    bounds = spread_max(local_bounds, ("gx", "gy"))
+    bounds = spread_max(spread_max(local_bounds, "gy", 0), "gx", 0)
     bound_one = bounds[0]
     bound_two = bounds[1]
     step_time = cfl_number / (

time: 205 us -> 205 us (level)
  waiting for transfers between devices: 51.9 us -> 54.2 us
    unnamed x59 -> x61, local copies, waits for them, and re-layouts: 1.58 us -> 4.66 us
    concatenate x3, other arithmetic: 2.51 us -> 0.43 us  [periodic_sided(): jnp.concatenate([lax.slice_in_dim(field, extent - 3, extent, axis=along),...]
  transfers between devices with their start and end apart: 15 -> 14, of which waited for: 6 -> 6; matrix products, arithmetic and copies ran while one was open for 24% -> 25% of each run, Pallas kernels for 0% -> 0%
where the time goes in v9:
time: 205 us; the launch traced here: 204 us
  other arithmetic  107 us (52%)
  waiting for transfers between devices  54.2 us (26%)
  starting transfers between devices  27.7 us (14%)
  local copies, waits for them, and re-layouts  9.11 us (4%)
  between operations  6.08 us (3%)
    add x4, other arithmetic, local_part(): partial + 0.5 * (alpha_three * (fore_three - back_three) + alpha_four * (...  41.1 us
    ppermute x3, waiting for transfers between devices, send_low(): lax.ppermute(piece, axis, [(i, (i + 1) % count) for i in range(count - 1)])  36.3 us
    add x2, other arithmetic, on_device(): 0.75 * cut(values, side) + 0.25 * (cut(first, side) + step_time * rate)  14.8 us
    add x2, other arithmetic, on_device(): cut(values, side) + step_time * rate  14.7 us
    add x1, other arithmetic, on_device(): cut(values, side) * (1.0 / 3.0)  14.1 us
    ppermute x3, starting transfers between devices, send_low(): lax.ppermute(piece, axis, [(i, (i + 1) % count) for i in range(count - 1)])  13.2 us
    ppermute x3, waiting for transfers between devices, send_high(): lax.ppermute(piece, axis, [((i + 1) % count, i) for i in range(count - 1)])  11.4 us
    ppermute x5, starting transfers between devices, spread_max(): lax.ppermute(local, axis, [(i, (i + k * span) % count) for i in range(cou...  9.71 us
  transfers between devices with their start and end apart: 14, of which 6 were waited for; matrix products, arithmetic and copies ran while one was open for 25% of the time, Pallas kernels for 0%

profile of v9, /device:TPU:0, one launch (start us, length us, event | category | flops | bytes accessed | tf_op | source)
XLA Modules:
  0.0 203.8 jit_solution(12061464017252119473)
XLA Ops:
  0.0 0.6 collective-permute-start.6
  0.6 1.3 fusion.128
  1.9 5.3 %collective-permute-start.5 = (f32[3,6,64,128]{3,2,1,0:T(8,128)S(1)}, f32[3,6,64,128]{3,2,1,0:T(8,128)}, u32[]{:S(2)}, u32[]{:S(2)}) collective-permute-start(f32[3,6,64,128]{3,2,1,0:T(8,128)S(1)} %get-tuple-element.74), channel_id=1, source_target_pairs={{0,2},{2,4},{4,6},{6,8},{8,10},{10,12},{12,14},{1,3},{3,5},{5,7},{... | collective-permute-start | bytes 1769480 | tf_op jit(solution)/shard_map/ppermute | solution.py:85
  7.2 1.3 collective-permute-start.7
  8.5 0.7 fusion.134
  9.2 0.6 abs_multiply_fusion
  9.8 0.6 abs_multiply_fusion.1
  11.7 1.2 copy_bitcast_fusion
  12.9 0.6 maximum_reduce_fusion
  13.7 0.4 subtract_multiply_fusion.1
  16.1 1.0 slice_bitcast_fusion.13
  17.0 0.9 slice_bitcast_fusion.5
  18.0 0.6 fusion.131
  18.8 0.6 slice_multiply_fusion.1
  19.4 0.6 broadcast_multiply_fusion
  20.1 0.7 broadcast_multiply_fusion.1
  20.8 0.4 fusion.129
  21.2 7.5 %multiply_add_fusion.2 = (f32[3,6,64,128]{3,2,1,0:T(8,128)}, f32[3,6,64,128]{3,2,1,0:T(8,128)S(1)}, f32[3,6,64,128]{3,2,1,0:T(8,128)S(1)}) fusion(f32[3,6,64,1]{3,2,1,0:T(8,128)S(1)} %get-tuple-element.125, f32[3,6,64,127]{3,2,1,0:T(8,128)S(1)} %get-tuple-element.72, f32[3,6,64,1]{3,2,1,0:T(8,128)S(1)} %get-tuple-element.126, f32[]{:T(128)S(6)} %add.2754, ...), kind=kLoop, calls=%fused_computation.189 | loop fusion | flops 40550400 | bytes 5902860 | tf_op jit(solution)/shard_map/add | solution.py:160
  28.8 0.7 add_multiply_fusion.8
  29.5 0.7 add_multiply_fusion.10
  30.2 0.7 broadcast_add_fusion
  30.9 7.5 %multiply_add_fusion.3 = (f32[3,6,64,128]{3,2,1,0:T(8,128)}, f32[3,6,64,128]{3,2,1,0:T(8,128)S(1)}, f32[3,6,64,128]{3,2,1,0:T(8,128)S(1)}) fusion(f32[3,6,64,1]{3,2,1,0:T(8,128)S(1)} %get-tuple-element.100, f32[3,6,64,127]{3,2,1,0:T(8,128)S(1)} %get-tuple-element.71, f32[3,6,64,1]{3,2,1,0:T(8,128)S(1)} %get-tuple-element.99, f32[]{:T(128)S(6)} %add.2754, ...), kind=kLoop, calls=%fused_computation.202 | loop fusion | flops 40550400 | bytes 5902860 | tf_op jit(solution)/shard_map/add | solution.py:160
  38.5 0.5 add_convert_fusion
  39.0 0.5 fusion.120
  39.5 1.3 copy.43
  41.4 1.3 copy.44
  42.7 0.5 fusion.121
  43.2 0.6 max.25
  43.9 2.7 %collective-permute-start.3 = (f32[2]{0:T(128)S(1)}, f32[2]{0:T(128)S(1)}, u32[]{:S(2)}, u32[]{:S(2)}) collective-permute-start(f32[2]{0:T(128)S(1)} %max.25), channel_id=1, source_target_pairs={{0,6},{2,8},{4,10},{6,12},{8,14},{10,0},{12,2},{14,4},{1,7},{3,9},... | collective-permute-start | bytes 32 | tf_op jit(solution)/shard_map/ppermute | solution.py:118
  46.6 1.6 collective-permute-start.2
  48.2 1.1 collective-permute-done.3
  49.2 3.4 %collective-permute-start.1 = (f32[2]{0:T(128)S(1)}, f32[2]{0:T(128)S(1)}, u32[]{:S(2)}, u32[]{:S(2)}) collective-permute-start(f32[2]{0:T(128)S(1)} %max.25), channel_id=1, source_target_pairs={{0,2},{2,4},{4,6},{6,8},{8,10},{10,12},{12,14},{14,0},{1,3},{3,5},... | collective-permute-start | bytes 32 | tf_op jit(solution)/shard_map/ppermute | solution.py:118
  52.6 2.9 %collective-permute-done.1 = f32[2]{0:T(128)S(1)} collective-permute-done((f32[2]{0:T(128)S(1)}, f32[2]{0:T(128)S(1)}, u32[]{:S(2)}, u32[]{:S(2)}) %collective-permute-start.1) | collective-permute-done | bytes 40 | tf_op jit(solution)/shard_map/ppermute | solution.py:118
  55.5 1.9 collective-permute-start.4
  57.4 2.6 %collective-permute-done.4 = f32[2]{0:T(128)S(1)} collective-permute-done((f32[2]{0:T(128)S(1)}, f32[2]{0:T(128)S(1)}, u32[]{:S(2)}, u32[]{:S(2)}) %collective-permute-start.4) | collective-permute-done | bytes 40 | tf_op jit(solution)/shard_map/ppermute | solution.py:118
  60.0 0.6 fusion.133
  61.9 1.2 add_select_fusion.7
  63.2 1.2 add_select_fusion.5
  64.5 0.5 fusion.7
  65.0 0.3 copy-done.6
  65.7 1.3 add_select_fusion.15
  67.0 0.3 pad_maximum_fusion.22
  67.5 0.9 copy-done.1
  68.5 7.4 %fusion.65 = f32[3,6,64,128]{3,2,1,0:T(8,128)S(1)} fusion(f32[3,6,64,128]{3,2,1,0:T(8,128)S(1)} %copy-done.1, f32[3,6,64,128]{3,2,1,0:T(8,128)S(1)} %add_multiply_fusion.6, f32[3,11,64,128]{3,2,1,0:T(8,128)S(1)} %fusion.42, f32[8,6,64,128]{3,2,1,0:T(8,128)S(1)} %get-tuple-element.52, f32[3]{0:T(128)S(1)} %copy-done.24, f32[3,6,64]{2,1,0:T(8,128)S(1)} %copy-done.14, ...), kind=kLoop, calls=%fused_computation.151 | loop fusion | flops 40108032 | bytes 9474684 | tf_op jit(solution)/shard_map/add | solution.py:310
  75.9 7.3 %fusion.51 = f32[3,6,64,128]{3,2,1,0:T(8,128)S(1)} fusion(f32[3,6,64,128]{3,2,1,0:T(8,128)S(1)} %copy-done.2, f32[3,6,64,128]{3,2,1,0:T(8,128)S(1)} %add_multiply_fusion.7, f32[3,11,64,128]{3,2,1,0:T(8,128)S(1)} %fusion.43, f32[8,6,64,128]{3,2,1,0:T(8,128)S(1)} %get-tuple-element.51, f32[]{:T(128)} %bitcast.3, f32[]{:T(128)} %bitcast.2, ...), kind=kLoop, calls=%fused_computation.137 | loop fusion | flops 40108032 | bytes 9474684 | tf_op jit(solution)/shard_map/add | solution.py:310
  83.2 0.4 fusion.14
  83.7 0.4 fusion.126
  84.6 13.0 %multiply_add_fusion.1 = (f32[6,6,64,128]{3,2,1,0:T(8,128)S(1)}, f32[6,6,64,128]{3,2,1,0:T(8,128)S(1)}, f32[6,6,64,128]{3,2,1,0:T(8,128)S(1)}) fusion(f32[6,6,64,1]{3,2,1,0:T(8,128)S(1)} %get-tuple-element.50, f32[6,6,64,127]{3,2,1,0:T(8,128)S(1)} %fusion.14, f32[6,6,64,1]{3,2,1,0:T(8,128)S(1)} %get-tuple-element.49, f32[]{:T(128)S(6)} %add.2754, ...), kind=kLoop, calls=%fused_computation.104 | loop fusion | flops 81100800 | bytes 11805708 | tf_op jit(solution)/shard_map/add | solution.py:160
  97.9 2.8 %collective-permute-start.8 = (f32[3,6,64,128]{3,2,1,0:T(8,128)S(1)}, f32[3,6,64,128]{3,2,1,0:T(8,128)S(1)}, u32[]{:S(2)}, u32[]{:S(2)}) collective-permute-start(f32[3,6,64,128]{3,2,1,0:T(8,128)S(1)} %fusion.65), channel_id=1, source_target_pairs={{0,2},{2,4},{4,6},{6,8},{8,10},{10,12},{12,14},{1,3},{3,5},{5,7},{... | collective-permute-start | bytes 1769480 | tf_op jit(solution)/shard_map/ppermute | solution.py:85
  100.7 1.5 collective-permute-start.10
  102.7 23.9 %collective-permute-done.8 = f32[3,6,64,128]{3,2,1,0:T(8,128)S(1)} collective-permute-done((f32[3,6,64,128]{3,2,1,0:T(8,128)S(1)}, f32[3,6,64,128]{3,2,1,0:T(8,128)S(1)}, u32[]{:S(2)}, u32[]{:S(2)}) %collective-permute-start.8) | collective-permute-done | bytes 589856 | tf_op jit(solution)/shard_map/ppermute | solution.py:85
  127.0 0.5 pad_maximum_fusion.3
  128.1 7.4 %fusion.73 = f32[3,6,64,128]{3,2,1,0:T(8,128)S(1)} fusion(f32[3,6,64,128]{3,2,1,0:T(8,128)S(1)} %fusion.65, f32[6,6,64,128]{3,2,1,0:T(8,128)S(1)} %get-tuple-element.18, f32[6,6,64,128]{3,2,1,0:T(8,128)S(1)} %add_multiply_fusion.1, f32[3,11,64,128]{3,2,1,0:T(8,128)S(1)} %fusion.40, f32[8,6,64,128]{3,2,1,0:T(8,128)S(1)} %fusion.8, f32[3]{0:T(128)S(1)} %copy-done.24, ...), kind=kLoop, calls=%fused_computation.159 | loop fusion | flops 40550400 | bytes 10064508 | tf_op jit(solution)/shard_map/add | solution.py:314
  135.5 7.4 %fusion.59 = f32[3,6,64,128]{3,2,1,0:T(8,128)S(1)} fusion(f32[3,6,64,128]{3,2,1,0:T(8,128)S(1)} %fusion.51, f32[6,6,64,128]{3,2,1,0:T(8,128)S(1)} %get-tuple-element.18, f32[6,6,64,128]{3,2,1,0:T(8,128)S(1)} %add_multiply_fusion.1, f32[3,11,64,128]{3,2,1,0:T(8,128)S(1)} %fusion.41, f32[8,6,64,128]{3,2,1,0:T(8,128)S(1)} %fusion.9, f32[]{:T(128)} %bitcast.3, ...), kind=kLoop, calls=%fused_computation.145 | loop fusion | flops 40550400 | bytes 10064508 | tf_op jit(solution)/shard_map/add | solution.py:314
  142.9 0.4 fusion.17
  143.4 0.4 fusion.125
  144.1 13.0 %multiply_add_fusion = (f32[6,6,64,128]{3,2,1,0:T(8,128)S(1)}, f32[6,6,64,128]{3,2,1,0:T(8,128)S(1)}, f32[6,6,64,128]{3,2,1,0:T(8,128)S(1)}) fusion(f32[6,6,64,1]{3,2,1,0:T(8,128)S(1)} %get-tuple-element.44, f32[6,6,64,127]{3,2,1,0:T(8,128)S(1)} %fusion.17, f32[6,6,64,1]{3,2,1,0:T(8,128)S(1)} %get-tuple-element.43, f32[]{:T(128)S(6)} %add.2754, f32[]{:T(128)} %bitcast.5, ...), kind=kLoop, calls=%fused_computation.94 | loop fusion | flops 81100800 | bytes 11805708 | tf_op jit(solution)/shard_map/add | solution.py:160
  157.5 1.3 collective-permute-start.12
  158.8 5.1 %collective-permute-start.11 = (f32[3,6,64,128]{3,2,1,0:T(8,128)S(1)}, f32[3,6,64,128]{3,2,1,0:T(8,128)S(1)}, u32[]{:S(2)}, u32[]{:S(2)}) collective-permute-start(f32[3,6,64,128]{3,2,1,0:T(8,128)S(1)} %fusion.73), channel_id=1, source_target_pairs={{0,2},{2,4},{4,6},{6,8},{8,10},{10,12},{12,14},{1,3},{3,5},{5,7},{... | collective-permute-start | bytes 1769480 | tf_op jit(solution)/shard_map/ppermute | solution.py:85
  164.0 0.3 add_select_fusion.1
  164.5 11.3 %collective-permute-done.12 = f32[3,6,64,128]{3,2,1,0:T(8,128)S(1)} collective-permute-done((f32[3,6,64,128]{3,2,1,0:T(8,128)S(1)}, f32[3,6,64,128]{3,2,1,0:T(8,128)S(1)}, u32[]{:S(2)}, u32[]{:S(2)}) %collective-permute-start.12) | collective-permute-done | bytes 589856 | tf_op jit(solution)/shard_map/ppermute | solution.py:90
  176.2 12.4 %collective-permute-done.11 = f32[3,6,64,128]{3,2,1,0:T(8,128)S(1)} collective-permute-done((f32[3,6,64,128]{3,2,1,0:T(8,128)S(1)}, f32[3,6,64,128]{3,2,1,0:T(8,128)S(1)}, u32[]{:S(2)}, u32[]{:S(2)}) %collective-permute-start.11) | collective-permute-done | bytes 589856 | tf_op jit(solution)/shard_map/ppermute | solution.py:85
  189.3 0.5 copy-done.15
  189.7 14.1 %fusion.21 = f32[6,6,64,128]{3,2,1,0:T(8,128)} fusion(f32[3,6,64,128]{3,2,1,0:T(8,128)S(1)} %fusion.73, f32[3,6,64,128]{3,2,1,0:T(8,128)S(1)} %fusion.59, f32[6,6,64,128]{3,2,1,0:T(8,128)S(1)} %get-tuple-element.20, f32[6,6,64,128]{3,2,1,0:T(8,128)S(1)} %add_multiply_fusion, f32[6,11,64,128]{3,2,1,0:T(8,128)S(1)} %fusion, f32[11,6,64,128]{3,2,1,0:T(8,128)S(1)} %fusion.1, ...), kind=kLoop, calls=%fused_computation.66 | loop fusion | flops 81395712 | bytes 20096208 | tf_op jit(solution)/shard_map/add | solution.py:319
  (112 shorter events, 5.5 us)
Async XLA Ops:
  0.0 13.7 %copy-start = (f32[6,6,64,128]{3,2,1,0:T(8,128)S(1)}, f32[6,6,64,128]{3,2,1,0:T(8,128)}, u32[]{:S(2)}) copy-start(f32[6,6,64,128]{3,2,1,0:T(8,128)} %param.6) | copy-start | bytes 3538948
  0.0 8.5 %copy-start.22 = (f32[4]{0:T(128)S(1)}, f32[4]{0:T(128)}, u32[]{:S(2)}) copy-start(f32[4]{0:T(128)} %param.8) | copy-start | bytes 52
  0.0 9.2 %copy-start.16 = (f32[2,6,6]{2,0,1:T(2,128)S(1)}, f32[2,6,6]{2,0,1:T(2,128)}, u32[]{:S(2)}) copy-start(f32[2,6,6]{2,0,1:T(2,128)} %param.7) | copy-start | bytes 868
  0.0 65.0 %collective-permute-start.6 = (f32[6,6,64,128]{3,2,1,0:T(8,128)}, f32[6,6,64,128]{3,2,1,0:T(8,128)}, u32[]{:S(2)}, u32[]{:S(2)}) collective-permute-start(f32[6,6,64,128]{3,2,1,0:T(8,128)} %param.6), channel_id=1, source_target_pairs={{0,1},{1,0},{2,3},{3,2},{4,5},{5,4},{6,7},{7,6},{8,9},{9,8},{10,11... | collective-permute-start | bytes 3538952 | tf_op jit(solution)/shard_map/ppermute | solution.py:175
  1.9 60.0 %collective-permute-start.5 = (f32[3,6,64,128]{3,2,1,0:T(8,128)S(1)}, f32[3,6,64,128]{3,2,1,0:T(8,128)}, u32[]{:S(2)}, u32[]{:S(2)}) collective-permute-start(f32[3,6,64,128]{3,2,1,0:T(8,128)S(1)} %get-tuple-element.74), channel_id=1, source_target_pairs={{0,2},{2,4},{4,6},{6,8},{8,10},{10,12},{12,14},{1,3},{3,5},{5,7},{... | collective-permute-start | bytes 1769480 | tf_op jit(solution)/shard_map/ppermute | solution.py:85
  7.2 55.9 %collective-permute-start.7 = (f32[3,6,64,128]{3,2,1,0:T(8,128)S(1)}, f32[3,6,64,128]{3,2,1,0:T(8,128)}, u32[]{:S(2)}, u32[]{:S(2)}) collective-permute-start(f32[3,6,64,128]{3,2,1,0:T(8,128)S(1)} %get-tuple-element.73), channel_id=1, source_target_pairs={{2,0},{4,2},{6,4},{8,6},{10,8},{12,10},{14,12},{3,1},{5,3},{7,5},{... | collective-permute-start | bytes 1769480 | tf_op jit(solution)/shard_map/ppermute | solution.py:90
  13.5 29.7 %collective-permute-start = (f32[2]{0:T(128)}, f32[2]{0:T(128)}, u32[]{:S(2)}, u32[]{:S(2)}) collective-permute-start(f32[2]{0:T(128)} %maximum_reduce_fusion), channel_id=1, source_target_pairs={{0,1},{1,0},{2,3},{3,2},{4,5},{5,4},{6,7},{7,6},{8,9},{9,8},{10,11... | collective-permute-start | bytes 32 | tf_op jit(solution)/shard_map/ppermute | solution.py:118
  18.7 0.7 copy-start.28
  18.7 1.4 copy-start.27
  28.7 1.4 copy-start.26
  43.9 5.4 %collective-permute-start.3 = (f32[2]{0:T(128)S(1)}, f32[2]{0:T(128)S(1)}, u32[]{:S(2)}, u32[]{:S(2)}) collective-permute-start(f32[2]{0:T(128)S(1)} %max.25), channel_id=1, source_target_pairs={{0,6},{2,8},{4,10},{6,12},{8,14},{10,0},{12,2},{14,4},{1,7},{3,9},... | collective-permute-start | bytes 32 | tf_op jit(solution)/shard_map/ppermute | solution.py:118
  46.6 6.1 %collective-permute-start.2 = (f32[2]{0:T(128)S(1)}, f32[2]{0:T(128)S(1)}, u32[]{:S(2)}, u32[]{:S(2)}) collective-permute-start(f32[2]{0:T(128)S(1)} %max.25), channel_id=1, source_target_pairs={{0,4},{2,6},{4,8},{6,10},{8,12},{10,14},{12,0},{14,2},{1,5},{3,7},... | collective-permute-start | bytes 32 | tf_op jit(solution)/shard_map/ppermute | solution.py:118
  49.2 6.3 %collective-permute-start.1 = (f32[2]{0:T(128)S(1)}, f32[2]{0:T(128)S(1)}, u32[]{:S(2)}, u32[]{:S(2)}) collective-permute-start(f32[2]{0:T(128)S(1)} %max.25), channel_id=1, source_target_pairs={{0,2},{2,4},{4,6},{6,8},{8,10},{10,12},{12,14},{14,0},{1,3},{3,5},... | collective-permute-start | bytes 32 | tf_op jit(solution)/shard_map/ppermute | solution.py:118
  55.5 4.5 %collective-permute-start.4 = (f32[2]{0:T(128)S(1)}, f32[2]{0:T(128)S(1)}, u32[]{:S(2)}, u32[]{:S(2)}) collective-permute-start(f32[2]{0:T(128)S(1)} %maximum_maximum_fusion), channel_id=1, source_target_pairs={{0,8},{2,10},{4,12},{6,14},{8,0},{10,2},{12,4},{14,6},{1,9},{3,11}... | collective-permute-start | bytes 32 | tf_op jit(solution)/shard_map/ppermute | solution.py:118
  61.9 1.3 copy-start.4
  61.9 1.3 copy-start.5
  61.9 1.3 copy-start.17
  64.4 0.9 copy-start.6
  64.4 0.9 copy-start.7
  64.5 1.0 copy-start.8
  64.5 1.0 copy-start.9
  64.5 1.1 copy-start.10
  64.5 1.1 copy-start.11
  64.5 1.1 copy-start.12
  64.5 1.2 copy-start.13
  67.4 1.1 copy-start.1
  67.4 1.1 copy-start.3
  67.4 1.1 copy-start.14
  67.4 1.0 copy-start.18
  67.4 1.0 copy-start.21
  67.4 1.0 copy-start.24
  68.5 7.4 %copy-start.2 = (f32[3,6,64,128]{3,2,1,0:T(8,128)S(1)}, f32[3,6,64,128]{3,2,1,0:T(8,128)}, u32[]{:S(2)}) copy-start(f32[3,6,64,128]{3,2,1,0:T(8,128)} %get-tuple-element.14) | copy-start | bytes 1769476
  68.5 7.4 %copy-start.19 = (f32[1,3,6]{2,1,0:T(4,128)S(1)}, f32[1,3,6]{2,1,0:T(4,128)}, u32[]{:S(2)}) copy-start(f32[1,3,6]{2,1,0:T(4,128)} %copy.44) | copy-start | bytes 220
  68.5 7.4 %copy-start.23 = (f32[3]{0:T(128)S(1)}, f32[3]{0:T(128)}, u32[]{:S(2)}) copy-start(f32[3]{0:T(128)} %get-tuple-element.115) | copy-start | bytes 40
  84.5 17.9 %collective-permute-start.9 = (f32[6,3,64,128]{3,2,1,0:T(8,128)S(1)}, f32[6,3,64,128]{3,2,1,0:T(8,128)S(1)}, u32[]{:S(2)}, u32[]{:S(2)}) collective-permute-start(f32[6,3,64,128]{3,2,1,0:T(8,128)S(1)} %fusion.74), channel_id=1, source_target_pairs={{0,1},{1,0},{2,3},{3,2},{4,5},{5,4},{6,7},{7,6},{8,9},{9,8},{10,11... | collective-permute-start | bytes 1769480 | tf_op jit(solution)/shard_map/ppermute | solution.py:183
  97.9 28.7 %collective-permute-start.8 = (f32[3,6,64,128]{3,2,1,0:T(8,128)S(1)}, f32[3,6,64,128]{3,2,1,0:T(8,128)S(1)}, u32[]{:S(2)}, u32[]{:S(2)}) collective-permute-start(f32[3,6,64,128]{3,2,1,0:T(8,128)S(1)} %fusion.65), channel_id=1, source_target_pairs={{0,2},{2,4},{4,6},{6,8},{8,10},{10,12},{12,14},{1,3},{3,5},{5,7},{... | collective-permute-start | bytes 1769480 | tf_op jit(solution)/shard_map/ppermute | solution.py:85
  100.7 26.1 %collective-permute-start.10 = (f32[3,6,64,128]{3,2,1,0:T(8,128)S(1)}, f32[3,6,64,128]{3,2,1,0:T(8,128)S(1)}, u32[]{:S(2)}, u32[]{:S(2)}) collective-permute-start(f32[3,6,64,128]{3,2,1,0:T(8,128)S(1)} %fusion.51), channel_id=1, source_target_pairs={{2,0},{4,2},{6,4},{8,6},{10,8},{12,10},{14,12},{3,1},{5,3},{7,5},{... | collective-permute-start | bytes 1769480 | tf_op jit(solution)/shard_map/ppermute | solution.py:90
  157.4 6.6 %collective-permute-start.13 = (f32[6,3,64,128]{3,2,1,0:T(8,128)S(1)}, f32[6,3,64,128]{3,2,1,0:T(8,128)S(1)}, u32[]{:S(2)}, u32[]{:S(2)}) collective-permute-start(f32[6,3,64,128]{3,2,1,0:T(8,128)S(1)} %fusion.75), channel_id=1, source_target_pairs={{0,1},{1,0},{2,3},{3,2},{4,5},{5,4},{6,7},{7,6},{8,9},{9,8},{10,11... | collective-permute-start | bytes 1769480 | tf_op jit(solution)/shard_map/ppermute | solution.py:183
  157.5 18.4 %collective-permute-start.12 = (f32[3,6,64,128]{3,2,1,0:T(8,128)S(1)}, f32[3,6,64,128]{3,2,1,0:T(8,128)S(1)}, u32[]{:S(2)}, u32[]{:S(2)}) collective-permute-start(f32[3,6,64,128]{3,2,1,0:T(8,128)S(1)} %fusion.59), channel_id=1, source_target_pairs={{2,0},{4,2},{6,4},{8,6},{10,8},{12,10},{14,12},{3,1},{5,3},{7,5},{... | collective-permute-start | bytes 1769480 | tf_op jit(solution)/shard_map/ppermute | solution.py:90
  158.8 29.9 %collective-permute-start.11 = (f32[3,6,64,128]{3,2,1,0:T(8,128)S(1)}, f32[3,6,64,128]{3,2,1,0:T(8,128)S(1)}, u32[]{:S(2)}, u32[]{:S(2)}) collective-permute-start(f32[3,6,64,128]{3,2,1,0:T(8,128)S(1)} %fusion.73), channel_id=1, source_target_pairs={{0,2},{2,4},{4,6},{6,8},{8,10},{10,12},{12,14},{1,3},{3,5},{5,7},{... | collective-permute-start | bytes 1769480 | tf_op jit(solution)/shard_map/ppermute | solution.py:85
  189.0 0.7 copy-start.15
  189.0 0.7 copy-start.20
  189.0 0.7 copy-start.25

commit v10 on v8

--- a/solution.py
+++ b/solution.py
@@ -109,20 +109,20 @@
     return jnp.where(at_high, inner + dist * (inner - before), halo)
 
 
-def spread_max(local, axes):
-    count = 1
-    for axis in axes:
-        count *= lax.axis_size(axis)
+def spread_max(local, axis, first_level, radix):
+    count = lax.axis_size(axis)
     span = 1
+    level = first_level
     while span < count:
         moved = [
-            lax.ppermute(local, axes, [(i, (i + k * span) % count) for i in range(count)])
-            for k in range(1, 4)
+            lax.ppermute(local, axis, [(i, (i + k * span) % count) for i in range(count)])
+            for k in range(1, radix)
             if k * span < count
         ]
         for item in moved:
             local = jnp.maximum(local, item)
-        span *= 4
+        span *= radix
+        level += 1
     return local
 
 
@@ -213,7 +213,7 @@
     )
     local_bounds = jnp.max(terms, axis=(1, 2))
     locals_now = local_halves(values)
-    bounds = spread_max(local_bounds, ("gx", "gy"))
+    bounds = spread_max(spread_max(local_bounds, "gy", 0, 4), "gx", 0, 2)
     bound_one = bounds[0]
     bound_two = bounds[1]
     step_time = cfl_number / (

time: 205 us -> 207 us (level)
  waiting for transfers between devices: 51.9 us -> 62.3 us
  starting transfers between devices: 28 us -> 19 us
    ppermute x6 -> x4, waiting for transfers between devices: 4.53 us -> 14.5 us  [spread_max(): lax.ppermute(local, axis, [(i, (i + k * span) % count) for i in range(cou...]
    ppermute x6 -> x4, starting transfers between devices: 9.98 us -> 2.65 us  [spread_max(): lax.ppermute(local, axis, [(i, (i + k * span) % count) for i in range(cou...]
    unnamed x59 -> x61, local copies, waits for them, and re-layouts: 1.58 us -> 5.01 us
    slice x1, local copies, waits for them, and re-layouts: 2.4 us -> 0.09 us  [cut(): return array[:half]]
  transfers between devices with their start and end apart: 15 -> 13, of which waited for: 6 -> 6; matrix products, arithmetic and copies ran while one was open for 24% -> 25% of each run, Pallas kernels for 0% -> 0%
where the time goes in v10:
time: 207 us; the launch traced here: 206 us
  other arithmetic  109 us (53%)
  waiting for transfers between devices  62.3 us (30%)
  starting transfers between devices  19 us (9%)
  local copies, waits for them, and re-layouts  10.2 us (5%)
  between operations  6.13 us (3%)
    add x4, other arithmetic, local_part(): partial + 0.5 * (alpha_three * (fore_three - back_three) + alpha_four * (...  40.8 us
    ppermute x3, waiting for transfers between devices, send_low(): lax.ppermute(piece, axis, [(i, (i + 1) % count) for i in range(count - 1)])  36.5 us
    add x2, other arithmetic, on_device(): 0.75 * cut(values, side) + 0.25 * (cut(first, side) + step_time * rate)  14.9 us
    add x2, other arithmetic, on_device(): cut(values, side) + step_time * rate  14.8 us
    ppermute x4, waiting for transfers between devices, spread_max(): lax.ppermute(local, axis, [(i, (i + k * span) % count) for i in range(cou...  14.5 us
    add x1, other arithmetic, on_device(): cut(values, side) * (1.0 / 3.0)  14.1 us
    ppermute x3, starting transfers between devices, send_low(): lax.ppermute(piece, axis, [(i, (i + 1) % count) for i in range(count - 1)])  11.6 us
    ppermute x3, waiting for transfers between devices, send_high(): lax.ppermute(piece, axis, [((i + 1) % count, i) for i in range(count - 1)])  11.3 us
  transfers between devices with their start and end apart: 13, of which 6 were waited for; matrix products, arithmetic and copies ran while one was open for 25% of the time, Pallas kernels for 0%

profile of v10, /device:TPU:0, one launch (start us, length us, event | category | flops | bytes accessed | tf_op | source)
XLA Modules:
  0.0 206.3 jit_solution(13790870613525424279)
XLA Ops:
  0.0 2.0 constant_dynamic-slice_fusion
  2.0 0.5 collective-permute-start.5
  2.6 5.2 %collective-permute-start.4 = (f32[3,6,64,128]{3,2,1,0:T(8,128)S(1)}, f32[3,6,64,128]{3,2,1,0:T(8,128)}, u32[]{:S(2)}, u32[]{:S(2)}) collective-permute-start(f32[3,6,64,128]{3,2,1,0:T(8,128)S(1)} %get-tuple-element.68), channel_id=1, source_target_pairs={{0,2},{2,4},{4,6},{6,8},{8,10},{10,12},{12,14},{1,3},{3,5},{5,7},{... | collective-permute-start | bytes 1769480 | tf_op jit(solution)/shard_map/ppermute | solution.py:85
  7.9 1.3 collective-permute-start.6
  9.2 0.7 fusion.134
  9.8 0.7 abs_multiply_fusion
  10.5 0.7 abs_multiply_fusion.1
  12.5 1.2 copy_bitcast_fusion
  13.8 0.6 maximum_reduce_fusion
  14.6 0.4 subtract_multiply_fusion.1
  17.1 0.9 slice_bitcast_fusion.13
  18.0 0.6 add_convert_fusion
  18.6 0.5 fusion.122
  19.2 0.6 fusion.131
  19.8 0.5 fusion.120
  20.6 0.5 copy-done.28
  21.1 0.6 broadcast_multiply_fusion
  21.8 0.7 broadcast_multiply_fusion.1
  22.6 0.4 fusion.129
  22.9 7.4 %multiply_add_fusion.2 = (f32[3,6,64,128]{3,2,1,0:T(8,128)}, f32[3,6,64,128]{3,2,1,0:T(8,128)S(1)}, f32[3,6,64,128]{3,2,1,0:T(8,128)S(1)}) fusion(f32[3,6,64,1]{3,2,1,0:T(8,128)S(1)} %get-tuple-element.125, f32[3,6,64,127]{3,2,1,0:T(8,128)S(1)} %get-tuple-element.66, f32[3,6,64,1]{3,2,1,0:T(8,128)S(1)} %get-tuple-element.126, f32[]{:T(128)S(6)} %add.2754, ...), kind=kLoop, calls=%fused_computation.189 | loop fusion | flops 40550400 | bytes 5902860 | tf_op jit(solution)/shard_map/add | solution.py:160
  30.5 0.7 add_multiply_fusion.8
  31.2 0.7 add_multiply_fusion.10
  31.8 0.7 broadcast_add_fusion
  32.5 7.4 %multiply_add_fusion.3 = (f32[3,6,64,128]{3,2,1,0:T(8,128)}, f32[3,6,64,128]{3,2,1,0:T(8,128)S(1)}, f32[3,6,64,128]{3,2,1,0:T(8,128)S(1)}) fusion(f32[3,6,64,1]{3,2,1,0:T(8,128)S(1)} %get-tuple-element.100, f32[3,6,64,127]{3,2,1,0:T(8,128)S(1)} %get-tuple-element.65, f32[3,6,64,1]{3,2,1,0:T(8,128)S(1)} %get-tuple-element.99, f32[]{:T(128)S(6)} %add.2754, ...), kind=kLoop, calls=%fused_computation.202 | loop fusion | flops 40550400 | bytes 5902860 | tf_op jit(solution)/shard_map/add | solution.py:160
  40.0 0.5 fusion.121
  40.6 1.3 copy.43
  42.4 1.3 copy.44
  43.7 0.9 slice_bitcast_fusion.5
  44.6 1.3 slice_multiply_fusion.1
  45.9 0.6 max.22
  46.5 2.4 %collective-permute-start.1 = (f32[2]{0:T(128)S(1)}, f32[2]{0:T(128)S(1)}, u32[]{:S(2)}, u32[]{:S(2)}) collective-permute-start(f32[2]{0:T(128)S(1)} %max.22), channel_id=1, source_target_pairs={{0,2},{2,4},{4,6},{6,8},{8,10},{10,12},{12,14},{14,0},{1,3},{3,5},... | collective-permute-start | bytes 32 | tf_op jit(solution)/shard_map/ppermute | solution.py:118
  48.9 4.6 %collective-permute-done.1 = f32[2]{0:T(128)S(1)} collective-permute-done((f32[2]{0:T(128)S(1)}, f32[2]{0:T(128)S(1)}, u32[]{:S(2)}, u32[]{:S(2)}) %collective-permute-start.1) | collective-permute-done | bytes 40 | tf_op jit(solution)/shard_map/ppermute | solution.py:118
  53.6 5.4 %collective-permute-done.2 = f32[2]{0:T(128)S(1)} collective-permute-done((f32[2]{0:T(128)S(1)}, f32[2]{0:T(128)S(1)}, u32[]{:S(2)}, u32[]{:S(2)}) %collective-permute-start.2) | collective-permute-done | bytes 40 | tf_op jit(solution)/shard_map/ppermute | solution.py:118
  58.9 4.5 %collective-permute-done.3 = f32[2]{0:T(128)S(1)} collective-permute-done((f32[2]{0:T(128)S(1)}, f32[2]{0:T(128)S(1)}, u32[]{:S(2)}, u32[]{:S(2)}) %collective-permute-start.3) | collective-permute-done | bytes 40 | tf_op jit(solution)/shard_map/ppermute | solution.py:118
  63.4 0.6 fusion.133
  65.3 1.3 add_select_fusion.7
  66.8 1.3 add_select_fusion.15
  68.6 0.8 copy-done.4
  69.5 1.2 add_select_fusion.5
  70.8 0.5 fusion.7
  71.3 0.5 copy-done.1
  71.9 7.5 %fusion.65 = f32[3,6,64,128]{3,2,1,0:T(8,128)S(1)} fusion(f32[3,6,64,128]{3,2,1,0:T(8,128)S(1)} %copy-done.1, f32[3,6,64,128]{3,2,1,0:T(8,128)S(1)} %add_multiply_fusion.6, f32[3,11,64,128]{3,2,1,0:T(8,128)S(1)} %fusion.42, f32[8,6,64,128]{3,2,1,0:T(8,128)S(1)} %get-tuple-element.48, f32[3]{0:T(128)S(1)} %copy-done.24, f32[3,6,64]{2,1,0:T(8,128)S(1)} %copy-done.14, ...), kind=kLoop, calls=%fused_computation.151 | loop fusion | flops 40108032 | bytes 9474684 | tf_op jit(solution)/shard_map/add | solution.py:305
  79.4 7.4 %fusion.51 = f32[3,6,64,128]{3,2,1,0:T(8,128)S(1)} fusion(f32[3,6,64,128]{3,2,1,0:T(8,128)S(1)} %copy-done.2, f32[3,6,64,128]{3,2,1,0:T(8,128)S(1)} %add_multiply_fusion.7, f32[3,11,64,128]{3,2,1,0:T(8,128)S(1)} %fusion.43, f32[8,6,64,128]{3,2,1,0:T(8,128)S(1)} %get-tuple-element.47, f32[]{:T(128)} %bitcast.3, f32[]{:T(128)} %bitcast.2, ...), kind=kLoop, calls=%fused_computation.137 | loop fusion | flops 40108032 | bytes 9474684 | tf_op jit(solution)/shard_map/add | solution.py:305
  86.8 0.4 fusion.14
  87.3 0.4 fusion.126
  88.1 13.0 %multiply_add_fusion.1 = (f32[6,6,64,128]{3,2,1,0:T(8,128)S(1)}, f32[6,6,64,128]{3,2,1,0:T(8,128)S(1)}, f32[6,6,64,128]{3,2,1,0:T(8,128)S(1)}) fusion(f32[6,6,64,1]{3,2,1,0:T(8,128)S(1)} %get-tuple-element.46, f32[6,6,64,127]{3,2,1,0:T(8,128)S(1)} %fusion.14, f32[6,6,64,1]{3,2,1,0:T(8,128)S(1)} %get-tuple-element.45, f32[]{:T(128)S(6)} %add.2754, ...), kind=kLoop, calls=%fused_computation.104 | loop fusion | flops 81100800 | bytes 11805708 | tf_op jit(solution)/shard_map/add | solution.py:160
  101.4 1.3 collective-permute-start.7
  102.7 1.5 collective-permute-start.9
  104.3 0.3 add_select_fusion.11
  104.7 24.1 %collective-permute-done.7 = f32[3,6,64,128]{3,2,1,0:T(8,128)S(1)} collective-permute-done((f32[3,6,64,128]{3,2,1,0:T(8,128)S(1)}, f32[3,6,64,128]{3,2,1,0:T(8,128)S(1)}, u32[]{:S(2)}, u32[]{:S(2)}) %collective-permute-start.7) | collective-permute-done | bytes 589856 | tf_op jit(solution)/shard_map/ppermute | solution.py:85
  129.3 0.5 pad_maximum_fusion.3
  130.4 7.5 %fusion.73 = f32[3,6,64,128]{3,2,1,0:T(8,128)S(1)} fusion(f32[3,6,64,128]{3,2,1,0:T(8,128)S(1)} %fusion.65, f32[6,6,64,128]{3,2,1,0:T(8,128)S(1)} %get-tuple-element.18, f32[6,6,64,128]{3,2,1,0:T(8,128)S(1)} %add_multiply_fusion.1, f32[3,11,64,128]{3,2,1,0:T(8,128)S(1)} %fusion.40, f32[8,6,64,128]{3,2,1,0:T(8,128)S(1)} %fusion.8, f32[3]{0:T(128)S(1)} %copy-done.24, ...), kind=kLoop, calls=%fused_computation.159 | loop fusion | flops 40550400 | bytes 10064508 | tf_op jit(solution)/shard_map/add | solution.py:309
  137.9 7.5 %fusion.59 = f32[3,6,64,128]{3,2,1,0:T(8,128)S(1)} fusion(f32[3,6,64,128]{3,2,1,0:T(8,128)S(1)} %fusion.51, f32[6,6,64,128]{3,2,1,0:T(8,128)S(1)} %get-tuple-element.18, f32[6,6,64,128]{3,2,1,0:T(8,128)S(1)} %add_multiply_fusion.1, f32[3,11,64,128]{3,2,1,0:T(8,128)S(1)} %fusion.41, f32[8,6,64,128]{3,2,1,0:T(8,128)S(1)} %fusion.9, f32[]{:T(128)} %bitcast.3, ...), kind=kLoop, calls=%fused_computation.145 | loop fusion | flops 40550400 | bytes 10064508 | tf_op jit(solution)/shard_map/add | solution.py:309
  145.3 0.4 fusion.17
  145.8 0.4 fusion.125
  146.6 13.0 %multiply_add_fusion = (f32[6,6,64,128]{3,2,1,0:T(8,128)S(1)}, f32[6,6,64,128]{3,2,1,0:T(8,128)S(1)}, f32[6,6,64,128]{3,2,1,0:T(8,128)S(1)}) fusion(f32[6,6,64,1]{3,2,1,0:T(8,128)S(1)} %get-tuple-element.40, f32[6,6,64,127]{3,2,1,0:T(8,128)S(1)} %fusion.17, f32[6,6,64,1]{3,2,1,0:T(8,128)S(1)} %get-tuple-element.39, f32[]{:T(128)S(6)} %add.2754, f32[]{:T(128)} %bitcast.5, ...), kind=kLoop, calls=%fused_computation.94 | loop fusion | flops 81100800 | bytes 11805708 | tf_op jit(solution)/shard_map/add | solution.py:160
  159.8 1.3 collective-permute-start.11
  161.1 5.1 %collective-permute-start.10 = (f32[3,6,64,128]{3,2,1,0:T(8,128)S(1)}, f32[3,6,64,128]{3,2,1,0:T(8,128)S(1)}, u32[]{:S(2)}, u32[]{:S(2)}) collective-permute-start(f32[3,6,64,128]{3,2,1,0:T(8,128)S(1)} %fusion.73), channel_id=1, source_target_pairs={{0,2},{2,4},{4,6},{6,8},{8,10},{10,12},{12,14},{1,3},{3,5},{5,7},{... | collective-permute-start | bytes 1769480 | tf_op jit(solution)/shard_map/ppermute | solution.py:85
  166.6 0.3 pad_maximum_fusion.2
  166.9 11.3 %collective-permute-done.11 = f32[3,6,64,128]{3,2,1,0:T(8,128)S(1)} collective-permute-done((f32[3,6,64,128]{3,2,1,0:T(8,128)S(1)}, f32[3,6,64,128]{3,2,1,0:T(8,128)S(1)}, u32[]{:S(2)}, u32[]{:S(2)}) %collective-permute-start.11) | collective-permute-done | bytes 589856 | tf_op jit(solution)/shard_map/ppermute | solution.py:90
  178.4 0.3 fusion
  178.6 12.4 %collective-permute-done.10 = f32[3,6,64,128]{3,2,1,0:T(8,128)S(1)} collective-permute-done((f32[3,6,64,128]{3,2,1,0:T(8,128)S(1)}, f32[3,6,64,128]{3,2,1,0:T(8,128)S(1)}, u32[]{:S(2)}, u32[]{:S(2)}) %collective-permute-start.10) | collective-permute-done | bytes 589856 | tf_op jit(solution)/shard_map/ppermute | solution.py:85
  191.7 0.5 copy-done.15
  192.1 14.1 %fusion.21 = f32[6,6,64,128]{3,2,1,0:T(8,128)} fusion(f32[3,6,64,128]{3,2,1,0:T(8,128)S(1)} %fusion.73, f32[3,6,64,128]{3,2,1,0:T(8,128)S(1)} %fusion.59, f32[6,6,64,128]{3,2,1,0:T(8,128)S(1)} %get-tuple-element.20, f32[6,6,64,128]{3,2,1,0:T(8,128)S(1)} %add_multiply_fusion, f32[6,11,64,128]{3,2,1,0:T(8,128)S(1)} %fusion, f32[11,6,64,128]{3,2,1,0:T(8,128)S(1)} %fusion.1, ...), kind=kLoop, calls=%fused_computation.66 | loop fusion | flops 81395712 | bytes 20096208 | tf_op jit(solution)/shard_map/add | solution.py:314
  (112 shorter events, 5.3 us)
Async XLA Ops:
  0.0 2.5 %copy-start = (f32[6,6,64,128]{3,2,1,0:T(8,128)S(1)}, f32[6,6,64,128]{3,2,1,0:T(8,128)}, u32[]{:S(2)}) copy-start(f32[6,6,64,128]{3,2,1,0:T(8,128)} %param.6) | copy-start | bytes 3538948
  2.0 7.1 %copy-start.22 = (f32[4]{0:T(128)S(1)}, f32[4]{0:T(128)}, u32[]{:S(2)}) copy-start(f32[4]{0:T(128)} %param.8) | copy-start | bytes 52
  2.0 7.8 %copy-start.16 = (f32[2,6,6]{2,0,1:T(2,128)S(1)}, f32[2,6,6]{2,0,1:T(2,128)}, u32[]{:S(2)}) copy-start(f32[2,6,6]{2,0,1:T(2,128)} %param.7) | copy-start | bytes 868
  2.0 64.7 %collective-permute-start.5 = (f32[6,3,64,128]{3,2,1,0:T(8,128)}, f32[6,3,64,128]{3,2,1,0:T(8,128)}, u32[]{:S(2)}, u32[]{:S(2)}) collective-permute-start(f32[6,3,64,128]{3,2,1,0:T(8,128)} %constant_dynamic-slice_fusion), channel_id=1, source_target_pairs={{0,1},{1,0},{2,3},{3,2},{4,5},{5,4},{6,7},{7,6},{8,9},{9,8},{10,11... | collective-permute-start | bytes 1769480 | tf_op jit(solution)/shard_map/ppermute | solution.py:178
  2.6 62.7 %collective-permute-start.4 = (f32[3,6,64,128]{3,2,1,0:T(8,128)S(1)}, f32[3,6,64,128]{3,2,1,0:T(8,128)}, u32[]{:S(2)}, u32[]{:S(2)}) collective-permute-start(f32[3,6,64,128]{3,2,1,0:T(8,128)S(1)} %get-tuple-element.68), channel_id=1, source_target_pairs={{0,2},{2,4},{4,6},{6,8},{8,10},{10,12},{12,14},{1,3},{3,5},{5,7},{... | collective-permute-start | bytes 1769480 | tf_op jit(solution)/shard_map/ppermute | solution.py:85
  7.9 60.8 %collective-permute-start.6 = (f32[3,6,64,128]{3,2,1,0:T(8,128)S(1)}, f32[3,6,64,128]{3,2,1,0:T(8,128)}, u32[]{:S(2)}, u32[]{:S(2)}) collective-permute-start(f32[3,6,64,128]{3,2,1,0:T(8,128)S(1)} %get-tuple-element.67), channel_id=1, source_target_pairs={{2,0},{4,2},{6,4},{8,6},{10,8},{12,10},{14,12},{3,1},{5,3},{7,5},{... | collective-permute-start | bytes 1769480 | tf_op jit(solution)/shard_map/ppermute | solution.py:90
  14.4 31.5 %collective-permute-start = (f32[2]{0:T(128)}, f32[2]{0:T(128)}, u32[]{:S(2)}, u32[]{:S(2)}) collective-permute-start(f32[2]{0:T(128)} %maximum_reduce_fusion), channel_id=1, source_target_pairs={{0,1},{1,0},{2,3},{3,2},{4,5},{5,4},{6,7},{7,6},{8,9},{9,8},{10,11... | collective-permute-start | bytes 32 | tf_op jit(solution)/shard_map/ppermute | solution.py:118
  20.5 0.7 copy-start.28
  20.5 1.3 copy-start.27
  30.4 1.4 copy-start.26
  46.5 7.0 %collective-permute-start.1 = (f32[2]{0:T(128)S(1)}, f32[2]{0:T(128)S(1)}, u32[]{:S(2)}, u32[]{:S(2)}) collective-permute-start(f32[2]{0:T(128)S(1)} %max.22), channel_id=1, source_target_pairs={{0,2},{2,4},{4,6},{6,8},{8,10},{10,12},{12,14},{14,0},{1,3},{3,5},... | collective-permute-start | bytes 32 | tf_op jit(solution)/shard_map/ppermute | solution.py:118
  53.6 5.4 %collective-permute-start.2 = (f32[2]{0:T(128)S(1)}, f32[2]{0:T(128)S(1)}, u32[]{:S(2)}, u32[]{:S(2)}) collective-permute-start(f32[2]{0:T(128)S(1)} %max.23), channel_id=1, source_target_pairs={{0,4},{2,6},{4,8},{6,10},{8,12},{10,14},{12,0},{14,2},{1,5},{3,7},... | collective-permute-start | bytes 32 | tf_op jit(solution)/shard_map/ppermute | solution.py:118
  58.9 4.5 %collective-permute-start.3 = (f32[2]{0:T(128)S(1)}, f32[2]{0:T(128)S(1)}, u32[]{:S(2)}, u32[]{:S(2)}) collective-permute-start(f32[2]{0:T(128)S(1)} %max.24), channel_id=1, source_target_pairs={{0,8},{2,10},{4,12},{6,14},{8,0},{10,2},{12,4},{14,6},{1,9},{3,11}... | collective-permute-start | bytes 32 | tf_op jit(solution)/shard_map/ppermute | solution.py:118
  65.3 1.4 copy-start.6
  65.3 1.4 copy-start.7
  65.3 1.4 copy-start.8
  65.3 1.4 copy-start.9
  65.3 1.4 copy-start.10
  65.3 1.4 copy-start.11
  65.3 1.4 copy-start.12
  65.3 1.4 copy-start.13
  68.5 0.9 copy-start.4
  68.5 1.0 copy-start.5
  68.5 1.0 copy-start.17
  70.7 1.1 copy-start.1
  70.8 1.1 copy-start.3
  70.8 1.1 copy-start.14
  70.8 1.0 copy-start.18
  70.8 1.0 copy-start.21
  70.8 1.0 copy-start.24
  71.8 7.5 %copy-start.2 = (f32[3,6,64,128]{3,2,1,0:T(8,128)S(1)}, f32[3,6,64,128]{3,2,1,0:T(8,128)}, u32[]{:S(2)}) copy-start(f32[3,6,64,128]{3,2,1,0:T(8,128)} %get-tuple-element.14) | copy-start | bytes 1769476
  71.8 7.5 %copy-start.19 = (f32[1,3,6]{2,1,0:T(4,128)S(1)}, f32[1,3,6]{2,1,0:T(4,128)}, u32[]{:S(2)}) copy-start(f32[1,3,6]{2,1,0:T(4,128)} %copy.44) | copy-start | bytes 220
  71.9 7.5 %copy-start.23 = (f32[3]{0:T(128)S(1)}, f32[3]{0:T(128)}, u32[]{:S(2)}) copy-start(f32[3]{0:T(128)} %get-tuple-element.115) | copy-start | bytes 40
  88.0 16.3 %collective-permute-start.8 = (f32[6,3,64,128]{3,2,1,0:T(8,128)S(1)}, f32[6,3,64,128]{3,2,1,0:T(8,128)S(1)}, u32[]{:S(2)}, u32[]{:S(2)}) collective-permute-start(f32[6,3,64,128]{3,2,1,0:T(8,128)S(1)} %fusion.74), channel_id=1, source_target_pairs={{0,1},{1,0},{2,3},{3,2},{4,5},{5,4},{6,7},{7,6},{8,9},{9,8},{10,11... | collective-permute-start | bytes 1769480 | tf_op jit(solution)/shard_map/ppermute | solution.py:178
  101.4 27.4 %collective-permute-start.7 = (f32[3,6,64,128]{3,2,1,0:T(8,128)S(1)}, f32[3,6,64,128]{3,2,1,0:T(8,128)S(1)}, u32[]{:S(2)}, u32[]{:S(2)}) collective-permute-start(f32[3,6,64,128]{3,2,1,0:T(8,128)S(1)} %fusion.65), channel_id=1, source_target_pairs={{0,2},{2,4},{4,6},{6,8},{8,10},{10,12},{12,14},{1,3},{3,5},{5,7},{... | collective-permute-start | bytes 1769480 | tf_op jit(solution)/shard_map/ppermute | solution.py:85
  102.7 26.4 %collective-permute-start.9 = (f32[3,6,64,128]{3,2,1,0:T(8,128)S(1)}, f32[3,6,64,128]{3,2,1,0:T(8,128)S(1)}, u32[]{:S(2)}, u32[]{:S(2)}) collective-permute-start(f32[3,6,64,128]{3,2,1,0:T(8,128)S(1)} %fusion.51), channel_id=1, source_target_pairs={{2,0},{4,2},{6,4},{8,6},{10,8},{12,10},{14,12},{3,1},{5,3},{7,5},{... | collective-permute-start | bytes 1769480 | tf_op jit(solution)/shard_map/ppermute | solution.py:90
  159.8 6.6 %collective-permute-start.12 = (f32[6,3,64,128]{3,2,1,0:T(8,128)S(1)}, f32[6,3,64,128]{3,2,1,0:T(8,128)S(1)}, u32[]{:S(2)}, u32[]{:S(2)}) collective-permute-start(f32[6,3,64,128]{3,2,1,0:T(8,128)S(1)} %fusion.75), channel_id=1, source_target_pairs={{0,1},{1,0},{2,3},{3,2},{4,5},{5,4},{6,7},{7,6},{8,9},{9,8},{10,11... | collective-permute-start | bytes 1769480 | tf_op jit(solution)/shard_map/ppermute | solution.py:178
  159.8 18.4 %collective-permute-start.11 = (f32[3,6,64,128]{3,2,1,0:T(8,128)S(1)}, f32[3,6,64,128]{3,2,1,0:T(8,128)S(1)}, u32[]{:S(2)}, u32[]{:S(2)}) collective-permute-start(f32[3,6,64,128]{3,2,1,0:T(8,128)S(1)} %fusion.59), channel_id=1, source_target_pairs={{2,0},{4,2},{6,4},{8,6},{10,8},{12,10},{14,12},{3,1},{5,3},{7,5},{... | collective-permute-start | bytes 1769480 | tf_op jit(solution)/shard_map/ppermute | solution.py:90
  161.1 29.9 %collective-permute-start.10 = (f32[3,6,64,128]{3,2,1,0:T(8,128)S(1)}, f32[3,6,64,128]{3,2,1,0:T(8,128)S(1)}, u32[]{:S(2)}, u32[]{:S(2)}) collective-permute-start(f32[3,6,64,128]{3,2,1,0:T(8,128)S(1)} %fusion.73), channel_id=1, source_target_pairs={{0,2},{2,4},{4,6},{6,8},{8,10},{10,12},{12,14},{1,3},{3,5},{5,7},{... | collective-permute-start | bytes 1769480 | tf_op jit(solution)/shard_map/ppermute | solution.py:85
  191.4 0.7 copy-start.15
  191.4 0.7 copy-start.20
  191.4 0.7 copy-start.25

commit v11 on v10

--- a/solution.py
+++ b/solution.py
@@ -109,19 +109,19 @@
     return jnp.where(at_high, inner + dist * (inner - before), halo)
 
 
-def spread_max(local, axis, first_level, radix):
+def spread_max(local, axis, first_level):
     count = lax.axis_size(axis)
     span = 1
     level = first_level
     while span < count:
         moved = [
             lax.ppermute(local, axis, [(i, (i + k * span) % count) for i in range(count)])
-            for k in range(1, radix)
+            for k in range(1, 4)
             if k * span < count
         ]
         for item in moved:
             local = jnp.maximum(local, item)
-        span *= radix
+        span *= 4
         level += 1
     return local
 
@@ -213,7 +213,7 @@
     )
     local_bounds = jnp.max(terms, axis=(1, 2))
     locals_now = local_halves(values)
-    bounds = spread_max(spread_max(local_bounds, "gy", 0, 4), "gx", 0, 2)
+    bounds = spread_max(spread_max(local_bounds, "gy", 0), "gx", 0)
     bound_one = bounds[0]
     bound_two = bounds[1]
     step_time = cfl_number / (
@@ -301,11 +301,11 @@
         return merged, (sent[1], sent[0]), next_y, next_pieces
 
     first, x_halos, y_halos, locals_now = stage(
-        values, x_halos, y_halos, locals_now, (1, 0),
+        values, x_halos, y_halos, locals_now, (0, 1),
         lambda side, rate: cut(values, side) + step_time * rate, False,
     )
     second, x_halos, y_halos, locals_now = stage(
-        first, x_halos, y_halos, locals_now, (0, 1),
+        first, x_halos, y_halos, locals_now, (1, 0),
         lambda side, rate: 0.75 * cut(values, side) + 0.25 * (cut(first, side) + step_time * rate),
         False,
     )

time: 207 us -> 205 us (level)
  starting transfers between devices: 19 us -> 27.3 us
  waiting for transfers between devices: 62.3 us -> 54.4 us
    ppermute x4 -> x5, waiting for transfers between devices: 14.5 us -> 6.79 us  [spread_max(): lax.ppermute(local, axis, [(i, (i + k * span) % count) for i in range(cou...]
    ppermute x4 -> x5, starting transfers between devices: 2.65 us -> 9.53 us  [spread_max(): lax.ppermute(local, axis, [(i, (i + k * span) % count) for i in range(cou...]
  transfers between devices with their start and end apart: 13 -> 14, of which waited for: 6 -> 6; matrix products, arithmetic and copies ran while one was open for 25% -> 24% of each run, Pallas kernels for 0% -> 0%
where the time goes in v11:
time: 205 us; the launch traced here: 204 us
  other arithmetic  107 us (52%)
  waiting for transfers between devices  54.4 us (27%)
  starting transfers between devices  27.3 us (13%)
  local copies, waits for them, and re-layouts  9.61 us (5%)
  between operations  5.83 us (3%)
    add x4, other arithmetic, local_part(): partial + 0.5 * (alpha_three * (fore_three - back_three) + alpha_four * (...  40.8 us
    ppermute x3, waiting for transfers between devices, send_low(): lax.ppermute(piece, axis, [(i, (i + 1) % count) for i in range(count - 1)])  36.2 us
    add x2, other arithmetic, on_device(): 0.75 * cut(values, side) + 0.25 * (cut(first, side) + step_time * rate)  14.8 us
    add x2, other arithmetic, on_device(): cut(values, side) + step_time * rate  14.7 us
    add x1, other arithmetic, on_device(): cut(values, side) * (1.0 / 3.0)  14.1 us
    ppermute x3, starting transfers between devices, send_low(): lax.ppermute(piece, axis, [(i, (i + 1) % count) for i in range(count - 1)])  13 us
    ppermute x3, waiting for transfers between devices, send_high(): lax.ppermute(piece, axis, [((i + 1) % count, i) for i in range(count - 1)])  11.3 us
    ppermute x5, starting transfers between devices, spread_max(): lax.ppermute(local, axis, [(i, (i + k * span) % count) for i in range(cou...  9.53 us
  transfers between devices with their start and end apart: 14, of which 6 were waited for; matrix products, arithmetic and copies ran while one was open for 24% of the time, Pallas kernels for 0%

profile of v11, /device:TPU:0, one launch (start us, length us, event | category | flops | bytes accessed | tf_op | source)
XLA Modules:
  0.0 204.1 jit_solution(13158740366360077513)
XLA Ops:
  0.0 2.0 constant_dynamic-slice_fusion
  2.0 0.5 collective-permute-start.6
  2.6 5.2 %collective-permute-start.5 = (f32[3,6,64,128]{3,2,1,0:T(8,128)S(1)}, f32[3,6,64,128]{3,2,1,0:T(8,128)}, u32[]{:S(2)}, u32[]{:S(2)}) collective-permute-start(f32[3,6,64,128]{3,2,1,0:T(8,128)S(1)} %get-tuple-element.68), channel_id=1, source_target_pairs={{0,2},{2,4},{4,6},{6,8},{8,10},{10,12},{12,14},{1,3},{3,5},{5,7},{... | collective-permute-start | bytes 1769480 | tf_op jit(solution)/shard_map/ppermute | solution.py:85
  7.9 1.3 collective-permute-start.7
  9.2 0.6 fusion.134
  9.8 0.6 abs_multiply_fusion
  10.4 0.6 abs_multiply_fusion.1
  12.3 1.2 copy_bitcast_fusion
  13.5 0.6 maximum_reduce_fusion
  14.3 0.4 subtract_multiply_fusion.1
  16.5 1.0 slice_bitcast_fusion.13
  17.4 0.5 add_convert_fusion
  18.0 0.6 fusion.131
  18.6 0.5 fusion.120
  19.4 0.6 slice_multiply_fusion.1
  20.0 0.6 broadcast_multiply_fusion
  20.7 0.7 broadcast_multiply_fusion.1
  21.4 0.4 fusion.129
  21.8 7.4 %multiply_add_fusion.2 = (f32[3,6,64,128]{3,2,1,0:T(8,128)}, f32[3,6,64,128]{3,2,1,0:T(8,128)S(1)}, f32[3,6,64,128]{3,2,1,0:T(8,128)S(1)}) fusion(f32[3,6,64,1]{3,2,1,0:T(8,128)S(1)} %get-tuple-element.125, f32[3,6,64,127]{3,2,1,0:T(8,128)S(1)} %get-tuple-element.66, f32[3,6,64,1]{3,2,1,0:T(8,128)S(1)} %get-tuple-element.126, f32[]{:T(128)S(6)} %add.2754, ...), kind=kLoop, calls=%fused_computation.189 | loop fusion | flops 40550400 | bytes 5902860 | tf_op jit(solution)/shard_map/add | solution.py:160
  29.4 0.7 add_multiply_fusion.8
  30.0 0.7 add_multiply_fusion.10
  30.7 0.7 broadcast_add_fusion
  31.4 7.4 %multiply_add_fusion.3 = (f32[3,6,64,128]{3,2,1,0:T(8,128)}, f32[3,6,64,128]{3,2,1,0:T(8,128)S(1)}, f32[3,6,64,128]{3,2,1,0:T(8,128)S(1)}) fusion(f32[3,6,64,1]{3,2,1,0:T(8,128)S(1)} %get-tuple-element.100, f32[3,6,64,127]{3,2,1,0:T(8,128)S(1)} %get-tuple-element.65, f32[3,6,64,1]{3,2,1,0:T(8,128)S(1)} %get-tuple-element.99, f32[]{:T(128)S(6)} %add.2754, ...), kind=kLoop, calls=%fused_computation.202 | loop fusion | flops 40550400 | bytes 5902860 | tf_op jit(solution)/shard_map/add | solution.py:160
  38.9 0.6 fusion.121
  39.5 1.3 copy.43
  41.4 1.2 copy.44
  42.6 1.0 slice_bitcast_fusion.5
  43.6 0.6 max.25
  44.2 2.6 %collective-permute-start.3 = (f32[2]{0:T(128)S(1)}, f32[2]{0:T(128)S(1)}, u32[]{:S(2)}, u32[]{:S(2)}) collective-permute-start(f32[2]{0:T(128)S(1)} %max.25), channel_id=1, source_target_pairs={{0,6},{2,8},{4,10},{6,12},{8,14},{10,0},{12,2},{14,4},{1,7},{3,9},... | collective-permute-start | bytes 32 | tf_op jit(solution)/shard_map/ppermute | solution.py:118
  46.8 1.6 collective-permute-start.2
  48.4 1.2 collective-permute-done.3
  49.6 3.3 %collective-permute-start.1 = (f32[2]{0:T(128)S(1)}, f32[2]{0:T(128)S(1)}, u32[]{:S(2)}, u32[]{:S(2)}) collective-permute-start(f32[2]{0:T(128)S(1)} %max.25), channel_id=1, source_target_pairs={{0,2},{2,4},{4,6},{6,8},{8,10},{10,12},{12,14},{14,0},{1,3},{3,5},... | collective-permute-start | bytes 32 | tf_op jit(solution)/shard_map/ppermute | solution.py:118
  52.9 2.9 %collective-permute-done.1 = f32[2]{0:T(128)S(1)} collective-permute-done((f32[2]{0:T(128)S(1)}, f32[2]{0:T(128)S(1)}, u32[]{:S(2)}, u32[]{:S(2)}) %collective-permute-start.1) | collective-permute-done | bytes 40 | tf_op jit(solution)/shard_map/ppermute | solution.py:118
  55.8 1.8 collective-permute-start.4
  57.6 2.7 %collective-permute-done.4 = f32[2]{0:T(128)S(1)} collective-permute-done((f32[2]{0:T(128)S(1)}, f32[2]{0:T(128)S(1)}, u32[]{:S(2)}, u32[]{:S(2)}) %collective-permute-start.4) | collective-permute-done | bytes 40 | tf_op jit(solution)/shard_map/ppermute | solution.py:118
  60.3 0.6 fusion.133
  62.3 1.3 add_select_fusion.7
  63.7 1.3 add_select_fusion.15
  65.6 0.8 copy-done.4
  66.5 1.2 add_select_fusion.5
  67.8 0.5 fusion.7
  68.3 0.5 copy-done.1
  68.8 7.4 %fusion.65 = f32[3,6,64,128]{3,2,1,0:T(8,128)S(1)} fusion(f32[3,6,64,128]{3,2,1,0:T(8,128)S(1)} %copy-done.1, f32[3,6,64,128]{3,2,1,0:T(8,128)S(1)} %add_multiply_fusion.6, f32[3,11,64,128]{3,2,1,0:T(8,128)S(1)} %fusion.42, f32[8,6,64,128]{3,2,1,0:T(8,128)S(1)} %get-tuple-element.48, f32[3]{0:T(128)S(1)} %copy-done.24, f32[3,6,64]{2,1,0:T(8,128)S(1)} %copy-done.14, ...), kind=kLoop, calls=%fused_computation.151 | loop fusion | flops 40108032 | bytes 9474684 | tf_op jit(solution)/shard_map/add | solution.py:305
  76.3 7.3 %fusion.51 = f32[3,6,64,128]{3,2,1,0:T(8,128)S(1)} fusion(f32[3,6,64,128]{3,2,1,0:T(8,128)S(1)} %copy-done.2, f32[3,6,64,128]{3,2,1,0:T(8,128)S(1)} %add_multiply_fusion.7, f32[3,11,64,128]{3,2,1,0:T(8,128)S(1)} %fusion.43, f32[8,6,64,128]{3,2,1,0:T(8,128)S(1)} %get-tuple-element.47, f32[]{:T(128)} %bitcast.3, f32[]{:T(128)} %bitcast.2, ...), kind=kLoop, calls=%fused_computation.137 | loop fusion | flops 40108032 | bytes 9474684 | tf_op jit(solution)/shard_map/add | solution.py:305
  83.6 0.4 fusion.14
  84.1 0.4 fusion.126
  85.0 13.0 %multiply_add_fusion.1 = (f32[6,6,64,128]{3,2,1,0:T(8,128)S(1)}, f32[6,6,64,128]{3,2,1,0:T(8,128)S(1)}, f32[6,6,64,128]{3,2,1,0:T(8,128)S(1)}) fusion(f32[6,6,64,1]{3,2,1,0:T(8,128)S(1)} %get-tuple-element.46, f32[6,6,64,127]{3,2,1,0:T(8,128)S(1)} %fusion.14, f32[6,6,64,1]{3,2,1,0:T(8,128)S(1)} %get-tuple-element.45, f32[]{:T(128)S(6)} %add.2754, ...), kind=kLoop, calls=%fused_computation.104 | loop fusion | flops 81100800 | bytes 11805708 | tf_op jit(solution)/shard_map/add | solution.py:160
  98.2 2.7 %collective-permute-start.8 = (f32[3,6,64,128]{3,2,1,0:T(8,128)S(1)}, f32[3,6,64,128]{3,2,1,0:T(8,128)S(1)}, u32[]{:S(2)}, u32[]{:S(2)}) collective-permute-start(f32[3,6,64,128]{3,2,1,0:T(8,128)S(1)} %fusion.65), channel_id=1, source_target_pairs={{0,2},{2,4},{4,6},{6,8},{8,10},{10,12},{12,14},{1,3},{3,5},{5,7},{... | collective-permute-start | bytes 1769480 | tf_op jit(solution)/shard_map/ppermute | solution.py:85
  101.0 1.5 collective-permute-start.10
  102.6 0.3 add_select_fusion.11
  103.0 23.8 %collective-permute-done.8 = f32[3,6,64,128]{3,2,1,0:T(8,128)S(1)} collective-permute-done((f32[3,6,64,128]{3,2,1,0:T(8,128)S(1)}, f32[3,6,64,128]{3,2,1,0:T(8,128)S(1)}, u32[]{:S(2)}, u32[]{:S(2)}) %collective-permute-start.8) | collective-permute-done | bytes 589856 | tf_op jit(solution)/shard_map/ppermute | solution.py:85
  127.3 0.5 pad_maximum_fusion.3
  128.4 7.4 %fusion.73 = f32[3,6,64,128]{3,2,1,0:T(8,128)S(1)} fusion(f32[3,6,64,128]{3,2,1,0:T(8,128)S(1)} %fusion.65, f32[6,6,64,128]{3,2,1,0:T(8,128)S(1)} %get-tuple-element.18, f32[6,6,64,128]{3,2,1,0:T(8,128)S(1)} %add_multiply_fusion.1, f32[3,11,64,128]{3,2,1,0:T(8,128)S(1)} %fusion.40, f32[8,6,64,128]{3,2,1,0:T(8,128)S(1)} %fusion.8, f32[3]{0:T(128)S(1)} %copy-done.24, ...), kind=kLoop, calls=%fused_computation.159 | loop fusion | flops 40550400 | bytes 10064508 | tf_op jit(solution)/shard_map/add | solution.py:309
  135.8 7.4 %fusion.59 = f32[3,6,64,128]{3,2,1,0:T(8,128)S(1)} fusion(f32[3,6,64,128]{3,2,1,0:T(8,128)S(1)} %fusion.51, f32[6,6,64,128]{3,2,1,0:T(8,128)S(1)} %get-tuple-element.18, f32[6,6,64,128]{3,2,1,0:T(8,128)S(1)} %add_multiply_fusion.1, f32[3,11,64,128]{3,2,1,0:T(8,128)S(1)} %fusion.41, f32[8,6,64,128]{3,2,1,0:T(8,128)S(1)} %fusion.9, f32[]{:T(128)} %bitcast.3, ...), kind=kLoop, calls=%fused_computation.145 | loop fusion | flops 40550400 | bytes 10064508 | tf_op jit(solution)/shard_map/add | solution.py:309
  143.2 0.4 fusion.17
  143.7 0.4 fusion.125
  144.5 13.0 %multiply_add_fusion = (f32[6,6,64,128]{3,2,1,0:T(8,128)S(1)}, f32[6,6,64,128]{3,2,1,0:T(8,128)S(1)}, f32[6,6,64,128]{3,2,1,0:T(8,128)S(1)}) fusion(f32[6,6,64,1]{3,2,1,0:T(8,128)S(1)} %get-tuple-element.40, f32[6,6,64,127]{3,2,1,0:T(8,128)S(1)} %fusion.17, f32[6,6,64,1]{3,2,1,0:T(8,128)S(1)} %get-tuple-element.39, f32[]{:T(128)S(6)} %add.2754, f32[]{:T(128)} %bitcast.5, ...), kind=kLoop, calls=%fused_computation.94 | loop fusion | flops 81100800 | bytes 11805708 | tf_op jit(solution)/shard_map/add | solution.py:160
  157.7 1.3 collective-permute-start.12
  159.0 5.1 %collective-permute-start.11 = (f32[3,6,64,128]{3,2,1,0:T(8,128)S(1)}, f32[3,6,64,128]{3,2,1,0:T(8,128)S(1)}, u32[]{:S(2)}, u32[]{:S(2)}) collective-permute-start(f32[3,6,64,128]{3,2,1,0:T(8,128)S(1)} %fusion.73), channel_id=1, source_target_pairs={{0,2},{2,4},{4,6},{6,8},{8,10},{10,12},{12,14},{1,3},{3,5},{5,7},{... | collective-permute-start | bytes 1769480 | tf_op jit(solution)/shard_map/ppermute | solution.py:85
  164.5 0.3 pad_maximum_fusion.2
  164.8 11.3 %collective-permute-done.12 = f32[3,6,64,128]{3,2,1,0:T(8,128)S(1)} collective-permute-done((f32[3,6,64,128]{3,2,1,0:T(8,128)S(1)}, f32[3,6,64,128]{3,2,1,0:T(8,128)S(1)}, u32[]{:S(2)}, u32[]{:S(2)}) %collective-permute-start.12) | collective-permute-done | bytes 589856 | tf_op jit(solution)/shard_map/ppermute | solution.py:90
  176.5 12.4 %collective-permute-done.11 = f32[3,6,64,128]{3,2,1,0:T(8,128)S(1)} collective-permute-done((f32[3,6,64,128]{3,2,1,0:T(8,128)S(1)}, f32[3,6,64,128]{3,2,1,0:T(8,128)S(1)}, u32[]{:S(2)}, u32[]{:S(2)}) %collective-permute-start.11) | collective-permute-done | bytes 589856 | tf_op jit(solution)/shard_map/ppermute | solution.py:85
  189.6 0.5 copy-done.15
  190.0 14.1 %fusion.21 = f32[6,6,64,128]{3,2,1,0:T(8,128)} fusion(f32[3,6,64,128]{3,2,1,0:T(8,128)S(1)} %fusion.73, f32[3,6,64,128]{3,2,1,0:T(8,128)S(1)} %fusion.59, f32[6,6,64,128]{3,2,1,0:T(8,128)S(1)} %get-tuple-element.20, f32[6,6,64,128]{3,2,1,0:T(8,128)S(1)} %add_multiply_fusion, f32[6,11,64,128]{3,2,1,0:T(8,128)S(1)} %fusion, f32[11,6,64,128]{3,2,1,0:T(8,128)S(1)} %fusion.1, ...), kind=kLoop, calls=%fused_computation.66 | loop fusion | flops 81395712 | bytes 20096208 | tf_op jit(solution)/shard_map/add | solution.py:314
  (113 shorter events, 5.5 us)
Async XLA Ops:
  0.0 2.5 %copy-start = (f32[6,6,64,128]{3,2,1,0:T(8,128)S(1)}, f32[6,6,64,128]{3,2,1,0:T(8,128)}, u32[]{:S(2)}) copy-start(f32[6,6,64,128]{3,2,1,0:T(8,128)} %param.6) | copy-start | bytes 3538948
  2.0 7.1 %copy-start.22 = (f32[4]{0:T(128)S(1)}, f32[4]{0:T(128)}, u32[]{:S(2)}) copy-start(f32[4]{0:T(128)} %param.8) | copy-start | bytes 52
  2.0 7.7 %copy-start.16 = (f32[2,6,6]{2,0,1:T(2,128)S(1)}, f32[2,6,6]{2,0,1:T(2,128)}, u32[]{:S(2)}) copy-start(f32[2,6,6]{2,0,1:T(2,128)} %param.7) | copy-start | bytes 868
  2.0 61.6 %collective-permute-start.6 = (f32[6,3,64,128]{3,2,1,0:T(8,128)}, f32[6,3,64,128]{3,2,1,0:T(8,128)}, u32[]{:S(2)}, u32[]{:S(2)}) collective-permute-start(f32[6,3,64,128]{3,2,1,0:T(8,128)} %constant_dynamic-slice_fusion), channel_id=1, source_target_pairs={{0,1},{1,0},{2,3},{3,2},{4,5},{5,4},{6,7},{7,6},{8,9},{9,8},{10,11... | collective-permute-start | bytes 1769480 | tf_op jit(solution)/shard_map/ppermute | solution.py:178
  2.6 59.7 %collective-permute-start.5 = (f32[3,6,64,128]{3,2,1,0:T(8,128)S(1)}, f32[3,6,64,128]{3,2,1,0:T(8,128)}, u32[]{:S(2)}, u32[]{:S(2)}) collective-permute-start(f32[3,6,64,128]{3,2,1,0:T(8,128)S(1)} %get-tuple-element.68), channel_id=1, source_target_pairs={{0,2},{2,4},{4,6},{6,8},{8,10},{10,12},{12,14},{1,3},{3,5},{5,7},{... | collective-permute-start | bytes 1769480 | tf_op jit(solution)/shard_map/ppermute | solution.py:85
  7.9 57.7 %collective-permute-start.7 = (f32[3,6,64,128]{3,2,1,0:T(8,128)S(1)}, f32[3,6,64,128]{3,2,1,0:T(8,128)}, u32[]{:S(2)}, u32[]{:S(2)}) collective-permute-start(f32[3,6,64,128]{3,2,1,0:T(8,128)S(1)} %get-tuple-element.67), channel_id=1, source_target_pairs={{2,0},{4,2},{6,4},{8,6},{10,8},{12,10},{14,12},{3,1},{5,3},{7,5},{... | collective-permute-start | bytes 1769480 | tf_op jit(solution)/shard_map/ppermute | solution.py:90
  14.1 29.4 %collective-permute-start = (f32[2]{0:T(128)}, f32[2]{0:T(128)}, u32[]{:S(2)}, u32[]{:S(2)}) collective-permute-start(f32[2]{0:T(128)} %maximum_reduce_fusion), channel_id=1, source_target_pairs={{0,1},{1,0},{2,3},{3,2},{4,5},{5,4},{6,7},{7,6},{8,9},{9,8},{10,11... | collective-permute-start | bytes 32 | tf_op jit(solution)/shard_map/ppermute | solution.py:118
  19.3 0.7 copy-start.28
  19.3 1.4 copy-start.27
  29.3 1.5 copy-start.26
  44.2 5.4 %collective-permute-start.3 = (f32[2]{0:T(128)S(1)}, f32[2]{0:T(128)S(1)}, u32[]{:S(2)}, u32[]{:S(2)}) collective-permute-start(f32[2]{0:T(128)S(1)} %max.25), channel_id=1, source_target_pairs={{0,6},{2,8},{4,10},{6,12},{8,14},{10,0},{12,2},{14,4},{1,7},{3,9},... | collective-permute-start | bytes 32 | tf_op jit(solution)/shard_map/ppermute | solution.py:118
  46.8 6.1 %collective-permute-start.2 = (f32[2]{0:T(128)S(1)}, f32[2]{0:T(128)S(1)}, u32[]{:S(2)}, u32[]{:S(2)}) collective-permute-start(f32[2]{0:T(128)S(1)} %max.25), channel_id=1, source_target_pairs={{0,4},{2,6},{4,8},{6,10},{8,12},{10,14},{12,0},{14,2},{1,5},{3,7},... | collective-permute-start | bytes 32 | tf_op jit(solution)/shard_map/ppermute | solution.py:118
  49.6 6.3 %collective-permute-start.1 = (f32[2]{0:T(128)S(1)}, f32[2]{0:T(128)S(1)}, u32[]{:S(2)}, u32[]{:S(2)}) collective-permute-start(f32[2]{0:T(128)S(1)} %max.25), channel_id=1, source_target_pairs={{0,2},{2,4},{4,6},{6,8},{8,10},{10,12},{12,14},{14,0},{1,3},{3,5},... | collective-permute-start | bytes 32 | tf_op jit(solution)/shard_map/ppermute | solution.py:118
  55.8 4.5 %collective-permute-start.4 = (f32[2]{0:T(128)S(1)}, f32[2]{0:T(128)S(1)}, u32[]{:S(2)}, u32[]{:S(2)}) collective-permute-start(f32[2]{0:T(128)S(1)} %maximum_maximum_fusion), channel_id=1, source_target_pairs={{0,8},{2,10},{4,12},{6,14},{8,0},{10,2},{12,4},{14,6},{1,9},{3,11}... | collective-permute-start | bytes 32 | tf_op jit(solution)/shard_map/ppermute | solution.py:118
  62.2 1.4 copy-start.6
  62.2 1.4 copy-start.7
  62.2 1.4 copy-start.8
  62.3 1.4 copy-start.9
  62.3 1.4 copy-start.10
  62.3 1.4 copy-start.11
  62.3 1.4 copy-start.12
  62.3 1.4 copy-start.13
  65.5 0.9 copy-start.4
  65.5 1.0 copy-start.5
  65.5 1.0 copy-start.17
  67.7 1.1 copy-start.1
  67.7 1.1 copy-start.3
  67.7 1.1 copy-start.14
  67.7 1.0 copy-start.18
  67.8 1.0 copy-start.21
  67.8 1.0 copy-start.24
  68.8 7.4 %copy-start.2 = (f32[3,6,64,128]{3,2,1,0:T(8,128)S(1)}, f32[3,6,64,128]{3,2,1,0:T(8,128)}, u32[]{:S(2)}) copy-start(f32[3,6,64,128]{3,2,1,0:T(8,128)} %get-tuple-element.14) | copy-start | bytes 1769476
  68.8 7.4 %copy-start.19 = (f32[1,3,6]{2,1,0:T(4,128)S(1)}, f32[1,3,6]{2,1,0:T(4,128)}, u32[]{:S(2)}) copy-start(f32[1,3,6]{2,1,0:T(4,128)} %copy.44) | copy-start | bytes 220
  68.8 7.4 %copy-start.23 = (f32[3]{0:T(128)S(1)}, f32[3]{0:T(128)}, u32[]{:S(2)}) copy-start(f32[3]{0:T(128)} %get-tuple-element.115) | copy-start | bytes 40
  84.9 17.7 %collective-permute-start.9 = (f32[6,3,64,128]{3,2,1,0:T(8,128)S(1)}, f32[6,3,64,128]{3,2,1,0:T(8,128)S(1)}, u32[]{:S(2)}, u32[]{:S(2)}) collective-permute-start(f32[6,3,64,128]{3,2,1,0:T(8,128)S(1)} %fusion.74), channel_id=1, source_target_pairs={{0,1},{1,0},{2,3},{3,2},{4,5},{5,4},{6,7},{7,6},{8,9},{9,8},{10,11... | collective-permute-start | bytes 1769480 | tf_op jit(solution)/shard_map/ppermute | solution.py:178
  98.2 28.6 %collective-permute-start.8 = (f32[3,6,64,128]{3,2,1,0:T(8,128)S(1)}, f32[3,6,64,128]{3,2,1,0:T(8,128)S(1)}, u32[]{:S(2)}, u32[]{:S(2)}) collective-permute-start(f32[3,6,64,128]{3,2,1,0:T(8,128)S(1)} %fusion.65), channel_id=1, source_target_pairs={{0,2},{2,4},{4,6},{6,8},{8,10},{10,12},{12,14},{1,3},{3,5},{5,7},{... | collective-permute-start | bytes 1769480 | tf_op jit(solution)/shard_map/ppermute | solution.py:85
  101.0 26.2 %collective-permute-start.10 = (f32[3,6,64,128]{3,2,1,0:T(8,128)S(1)}, f32[3,6,64,128]{3,2,1,0:T(8,128)S(1)}, u32[]{:S(2)}, u32[]{:S(2)}) collective-permute-start(f32[3,6,64,128]{3,2,1,0:T(8,128)S(1)} %fusion.51), channel_id=1, source_target_pairs={{2,0},{4,2},{6,4},{8,6},{10,8},{12,10},{14,12},{3,1},{5,3},{7,5},{... | collective-permute-start | bytes 1769480 | tf_op jit(solution)/shard_map/ppermute | solution.py:90
  157.6 6.6 %collective-permute-start.13 = (f32[6,3,64,128]{3,2,1,0:T(8,128)S(1)}, f32[6,3,64,128]{3,2,1,0:T(8,128)S(1)}, u32[]{:S(2)}, u32[]{:S(2)}) collective-permute-start(f32[6,3,64,128]{3,2,1,0:T(8,128)S(1)} %fusion.75), channel_id=1, source_target_pairs={{0,1},{1,0},{2,3},{3,2},{4,5},{5,4},{6,7},{7,6},{8,9},{9,8},{10,11... | collective-permute-start | bytes 1769480 | tf_op jit(solution)/shard_map/ppermute | solution.py:178
  157.7 18.4 %collective-permute-start.12 = (f32[3,6,64,128]{3,2,1,0:T(8,128)S(1)}, f32[3,6,64,128]{3,2,1,0:T(8,128)S(1)}, u32[]{:S(2)}, u32[]{:S(2)}) collective-permute-start(f32[3,6,64,128]{3,2,1,0:T(8,128)S(1)} %fusion.59), channel_id=1, source_target_pairs={{2,0},{4,2},{6,4},{8,6},{10,8},{12,10},{14,12},{3,1},{5,3},{7,5},{... | collective-permute-start | bytes 1769480 | tf_op jit(solution)/shard_map/ppermute | solution.py:90
  159.0 29.9 %collective-permute-start.11 = (f32[3,6,64,128]{3,2,1,0:T(8,128)S(1)}, f32[3,6,64,128]{3,2,1,0:T(8,128)S(1)}, u32[]{:S(2)}, u32[]{:S(2)}) collective-permute-start(f32[3,6,64,128]{3,2,1,0:T(8,128)S(1)} %fusion.73), channel_id=1, source_target_pairs={{0,2},{2,4},{4,6},{6,8},{8,10},{10,12},{12,14},{1,3},{3,5},{5,7},{... | collective-permute-start | bytes 1769480 | tf_op jit(solution)/shard_map/ppermute | solution.py:85
  189.3 0.7 copy-start.15
  189.3 0.7 copy-start.20
  189.3 0.7 copy-start.25

commit v12 on v11

--- a/solution.py
+++ b/solution.py
@@ -161,12 +161,6 @@
             alpha_three * (fore_three - back_three) + alpha_four * (fore_four - back_four)
         )
         return mean_three, partial
-
-    def local_halves(field):
-        pieces = []
-        for side in (0, 1):
-            pieces.append(lax.optimization_barrier(local_part(cut(field, side))))
-        return pieces
 
     def y_halo(field):
         tail = lax.slice_in_dim(field, cells_y - 3, cells_y, axis=1)
@@ -212,7 +206,7 @@
         ]
     )
     local_bounds = jnp.max(terms, axis=(1, 2))
-    locals_now = local_halves(values)
+    locals_now = local_whole(values)
     bounds = spread_max(spread_max(local_bounds, "gy", 0), "gx", 0)
     bound_one = bounds[0]
     bound_two = bounds[1]
@@ -300,8 +294,9 @@
         next_pieces = local_whole(merged)
         return merged, (sent[1], sent[0]), next_y, next_pieces
 
+    fresh = jnp.where(values == values, values, 0.0)
     first, x_halos, y_halos, locals_now = stage(
-        values, x_halos, y_halos, locals_now, (0, 1),
+        fresh, x_halos, y_halos, locals_now, (0, 1),
         lambda side, rate: cut(values, side) + step_time * rate, False,
     )
     second, x_halos, y_halos, locals_now = stage(

time: 205 us -> 207 us (level)
  local copies, waits for them, and re-layouts: 9.61 us -> 12.2 us
    slice x1 -> x2, local copies, waits for them, and re-layouts: 0.09 us -> 2.33 us  [the longest x1 1.18 us: half_parts(): part = field[start:stop]]
    add x4 -> x3, other arithmetic: 40.8 us -> 39.8 us  [local_part(): partial + 0.5 * (alpha_three * (fore_three - back_three) + alpha_four * (...]
    unnamed x61 -> x63, local copies, waits for them, and re-layouts: 4.44 us -> 4.64 us
  transfers between devices with their start and end apart: 14 -> 14, of which waited for: 6 -> 6; matrix products, arithmetic and copies ran while one was open for 24% -> 25% of each run, Pallas kernels for 0% -> 0%
where the time goes in v12:
time: 207 us
  other arithmetic  107 us (52%)
  waiting for transfers between devices  54.4 us (26%)
  starting transfers between devices  27.3 us (13%)
  local copies, waits for them, and re-layouts  12.2 us (6%)
  between operations  6.14 us (3%)
    add x3, other arithmetic, local_part(): partial + 0.5 * (alpha_three * (fore_three - back_three) + alpha_four * (...  39.8 us
    ppermute x3, waiting for transfers between devices, send_low(): lax.ppermute(piece, axis, [(i, (i + 1) % count) for i in range(count - 1)])  36.3 us
    add x2, other arithmetic, on_device(): 0.75 * cut(values, side) + 0.25 * (cut(first, side) + step_time * rate)  15 us
    add x2, other arithmetic, on_device(): cut(values, side) + step_time * rate  14.9 us
    add x1, other arithmetic, on_device(): cut(values, side) * (1.0 / 3.0)  14.2 us
    ppermute x3, starting transfers between devices, send_low(): lax.ppermute(piece, axis, [(i, (i + 1) % count) for i in range(count - 1)])  13 us
    ppermute x3, waiting for transfers between devices, send_high(): lax.ppermute(piece, axis, [((i + 1) % count, i) for i in range(count - 1)])  11.3 us
    ppermute x5, starting transfers between devices, spread_max(): lax.ppermute(local, axis, [(i, (i + k * span) % count) for i in range(cou...  9.53 us
  transfers between devices with their start and end apart: 14, of which 6 were waited for; matrix products, arithmetic and copies ran while one was open for 25% of the time, Pallas kernels for 0%

profile of v12, /device:TPU:0, one launch (start us, length us, event | category | flops | bytes accessed | tf_op | source)
XLA Modules:
  0.0 206.5 jit_solution(4072444421779332537)
XLA Ops:
  0.0 2.0 constant_dynamic-slice_fusion
  2.0 0.5 collective-permute-start.6
  2.5 1.2 fusion.123
  3.7 5.2 %collective-permute-start.5 = (f32[3,6,64,128]{3,2,1,0:T(8,128)}, f32[3,6,64,128]{3,2,1,0:T(8,128)}, u32[]{:S(2)}, u32[]{:S(2)}) collective-permute-start(f32[3,6,64,128]{3,2,1,0:T(8,128)} %get-tuple-element.46), channel_id=1, source_target_pairs={{0,2},{2,4},{4,6},{6,8},{8,10},{10,12},{12,14},{1,3},{3,5},{5,7},{... | collective-permute-start | bytes 1769480 | tf_op jit(solution)/shard_map/ppermute | solution.py:85
  8.9 1.3 collective-permute-start.7
  10.2 0.6 fusion.130
  10.9 0.6 abs_multiply_fusion
  11.5 0.6 abs_multiply_fusion.1
  13.4 1.2 copy_bitcast_fusion
  14.7 0.7 maximum_reduce_fusion
  15.6 0.4 subtract_multiply_fusion
  18.0 0.5 add_convert_fusion
  18.5 0.9 slice_bitcast_fusion.13
  19.4 1.2 fusion.124
  20.6 0.6 fusion.127
  21.2 0.5 fusion.116
  21.8 0.4 fusion.126
  22.6 0.6 slice_multiply_fusion.1
  23.2 0.6 broadcast_multiply_fusion
  23.8 0.7 broadcast_multiply_fusion.1
  24.5 13.7 %multiply_add_fusion.2 = (f32[6,6,64,128]{3,2,1,0:T(8,128)}, f32[6,6,64,128]{3,2,1,0:T(8,128)S(1)}, f32[6,6,64,128]{3,2,1,0:T(8,128)S(1)}) fusion(f32[6,6,64,1]{3,2,1,0:T(8,128)S(1)} %get-tuple-element.61, f32[6,6,64,127]{3,2,1,0:T(8,128)S(1)} %subtract_multiply_fusion, f32[6,6,64,1]{3,2,1,0:T(8,128)S(1)} %get-tuple-element.60, f32[]{:T(128)S(6)} %add.2511, ...), kind=kLoop, calls=%fused_computation.129 | loop fusion | flops 81100800 | bytes 11805708 | tf_op jit(solution)/shard_map/add | solution.py:160
  38.5 0.7 add_multiply_fusion.7
  39.1 0.7 add_multiply_fusion.9
  39.8 0.7 broadcast_add_fusion
  40.5 0.6 fusion.117
  41.1 1.2 copy.43
  42.9 1.2 copy.44
  44.2 0.9 slice_bitcast_fusion.5
  45.1 0.7 max.25
  45.8 2.6 %collective-permute-start.3 = (f32[2]{0:T(128)S(1)}, f32[2]{0:T(128)S(1)}, u32[]{:S(2)}, u32[]{:S(2)}) collective-permute-start(f32[2]{0:T(128)S(1)} %max.25), channel_id=1, source_target_pairs={{0,6},{2,8},{4,10},{6,12},{8,14},{10,0},{12,2},{14,4},{1,7},{3,9},... | collective-permute-start | bytes 32 | tf_op jit(solution)/shard_map/ppermute | solution.py:118
  48.4 1.6 collective-permute-start.2
  50.0 1.2 collective-permute-done.3
  51.1 3.3 %collective-permute-start.1 = (f32[2]{0:T(128)S(1)}, f32[2]{0:T(128)S(1)}, u32[]{:S(2)}, u32[]{:S(2)}) collective-permute-start(f32[2]{0:T(128)S(1)} %max.25), channel_id=1, source_target_pairs={{0,2},{2,4},{4,6},{6,8},{8,10},{10,12},{12,14},{14,0},{1,3},{3,5},... | collective-permute-start | bytes 32 | tf_op jit(solution)/shard_map/ppermute | solution.py:118
  54.5 2.9 %collective-permute-done.1 = f32[2]{0:T(128)S(1)} collective-permute-done((f32[2]{0:T(128)S(1)}, f32[2]{0:T(128)S(1)}, u32[]{:S(2)}, u32[]{:S(2)}) %collective-permute-start.1) | collective-permute-done | bytes 40 | tf_op jit(solution)/shard_map/ppermute | solution.py:118
  57.4 1.8 collective-permute-start.4
  59.2 2.7 %collective-permute-done.4 = f32[2]{0:T(128)S(1)} collective-permute-done((f32[2]{0:T(128)S(1)}, f32[2]{0:T(128)S(1)}, u32[]{:S(2)}, u32[]{:S(2)}) %collective-permute-start.4) | collective-permute-done | bytes 40 | tf_op jit(solution)/shard_map/ppermute | solution.py:118
  61.9 0.7 fusion.129
  64.0 1.3 add_select_fusion.7
  65.4 1.4 add_select_fusion.15
  66.9 0.3 pad_maximum_fusion.29
  67.4 0.8 copy-done.5
  68.3 1.2 add_select_fusion.5
  69.6 0.5 fusion.7
  70.0 0.8 copy-done.1
  70.8 7.4 %fusion.73 = f32[3,6,64,128]{3,2,1,0:T(8,128)S(1)} fusion(f32[6,6,64,128]{3,2,1,0:T(8,128)S(1)} %copy-done.1, f32[6,6,64,128]{3,2,1,0:T(8,128)S(1)} %add_multiply_fusion.2, f32[3,11,64,128]{3,2,1,0:T(8,128)S(1)} %fusion.52, f32[8,6,64,128]{3,2,1,0:T(8,128)S(1)} %get-tuple-element.41, f32[3]{0:T(128)S(1)} %copy-done.25, f32[3,6,64]{2,1,0:T(8,128)S(1)} %copy-done.15, ...), kind=kLoop, calls=%fused_computation.171 | loop fusion | flops 40108032 | bytes 9474684 | tf_op jit(solution)/shard_map/add | solution.py:300
  78.3 7.4 %fusion.59 = f32[3,6,64,128]{3,2,1,0:T(8,128)S(1)} fusion(f32[6,6,64,128]{3,2,1,0:T(8,128)S(1)} %copy-done.1, f32[6,6,64,128]{3,2,1,0:T(8,128)S(1)} %add_multiply_fusion.2, f32[3,11,64,128]{3,2,1,0:T(8,128)S(1)} %fusion.53, f32[8,6,64,128]{3,2,1,0:T(8,128)S(1)} %get-tuple-element.40, f32[]{:T(128)} %bitcast.3, f32[]{:T(128)} %bitcast.2, ...), kind=kLoop, calls=%fused_computation.157 | loop fusion | flops 40108032 | bytes 9474684 | tf_op jit(solution)/shard_map/add | solution.py:300
  85.7 0.4 fusion.15
  86.2 0.4 fusion.122
  87.1 13.0 %multiply_add_fusion.1 = (f32[6,6,64,128]{3,2,1,0:T(8,128)S(1)}, f32[6,6,64,128]{3,2,1,0:T(8,128)S(1)}, f32[6,6,64,128]{3,2,1,0:T(8,128)S(1)}) fusion(f32[6,6,64,1]{3,2,1,0:T(8,128)S(1)} %get-tuple-element.39, f32[6,6,64,127]{3,2,1,0:T(8,128)S(1)} %fusion.15, f32[6,6,64,1]{3,2,1,0:T(8,128)S(1)} %get-tuple-element.38, f32[]{:T(128)S(6)} %add.2511, ...), kind=kLoop, calls=%fused_computation.119 | loop fusion | flops 81100800 | bytes 11805708 | tf_op jit(solution)/shard_map/add | solution.py:160
  100.4 2.7 %collective-permute-start.8 = (f32[3,6,64,128]{3,2,1,0:T(8,128)S(1)}, f32[3,6,64,128]{3,2,1,0:T(8,128)S(1)}, u32[]{:S(2)}, u32[]{:S(2)}) collective-permute-start(f32[3,6,64,128]{3,2,1,0:T(8,128)S(1)} %fusion.73), channel_id=1, source_target_pairs={{0,2},{2,4},{4,6},{6,8},{8,10},{10,12},{12,14},{1,3},{3,5},{5,7},{... | collective-permute-start | bytes 1769480 | tf_op jit(solution)/shard_map/ppermute | solution.py:85
  103.1 1.5 collective-permute-start.10
  105.1 23.9 %collective-permute-done.8 = f32[3,6,64,128]{3,2,1,0:T(8,128)S(1)} collective-permute-done((f32[3,6,64,128]{3,2,1,0:T(8,128)S(1)}, f32[3,6,64,128]{3,2,1,0:T(8,128)S(1)}, u32[]{:S(2)}, u32[]{:S(2)}) %collective-permute-start.8) | collective-permute-done | bytes 589856 | tf_op jit(solution)/shard_map/ppermute | solution.py:85
  129.4 0.5 pad_maximum_fusion.3
  130.4 7.5 %fusion.81 = f32[3,6,64,128]{3,2,1,0:T(8,128)S(1)} fusion(f32[3,6,64,128]{3,2,1,0:T(8,128)S(1)} %fusion.73, f32[6,6,64,128]{3,2,1,0:T(8,128)S(1)} %get-tuple-element.14, f32[6,6,64,128]{3,2,1,0:T(8,128)S(1)} %add_multiply_fusion.1, f32[3,11,64,128]{3,2,1,0:T(8,128)S(1)} %fusion.50, f32[8,6,64,128]{3,2,1,0:T(8,128)S(1)} %fusion.8, f32[3]{0:T(128)S(1)} %copy-done.25, ...), kind=kLoop, calls=%fused_computation.179 | loop fusion | flops 40550400 | bytes 10064508 | tf_op jit(solution)/shard_map/add | solution.py:304
  138.0 7.5 %fusion.67 = f32[3,6,64,128]{3,2,1,0:T(8,128)S(1)} fusion(f32[3,6,64,128]{3,2,1,0:T(8,128)S(1)} %fusion.59, f32[6,6,64,128]{3,2,1,0:T(8,128)S(1)} %get-tuple-element.14, f32[6,6,64,128]{3,2,1,0:T(8,128)S(1)} %add_multiply_fusion.1, f32[3,11,64,128]{3,2,1,0:T(8,128)S(1)} %fusion.51, f32[8,6,64,128]{3,2,1,0:T(8,128)S(1)} %fusion.9, f32[]{:T(128)} %bitcast.3, ...), kind=kLoop, calls=%fused_computation.165 | loop fusion | flops 40550400 | bytes 10064508 | tf_op jit(solution)/shard_map/add | solution.py:304
  145.5 0.4 fusion.18
  146.0 0.4 fusion.121
  146.7 13.0 %multiply_add_fusion = (f32[6,6,64,128]{3,2,1,0:T(8,128)S(1)}, f32[6,6,64,128]{3,2,1,0:T(8,128)S(1)}, f32[6,6,64,128]{3,2,1,0:T(8,128)S(1)}) fusion(f32[6,6,64,1]{3,2,1,0:T(8,128)S(1)} %get-tuple-element.33, f32[6,6,64,127]{3,2,1,0:T(8,128)S(1)} %fusion.18, f32[6,6,64,1]{3,2,1,0:T(8,128)S(1)} %get-tuple-element.32, f32[]{:T(128)S(6)} %add.2511, f32[]{:T(128)} %bitcast.5, ...), kind=kLoop, calls=%fused_computation.109 | loop fusion | flops 81100800 | bytes 11805708 | tf_op jit(solution)/shard_map/add | solution.py:160
  160.0 1.3 collective-permute-start.12
  161.3 5.1 %collective-permute-start.11 = (f32[3,6,64,128]{3,2,1,0:T(8,128)S(1)}, f32[3,6,64,128]{3,2,1,0:T(8,128)S(1)}, u32[]{:S(2)}, u32[]{:S(2)}) collective-permute-start(f32[3,6,64,128]{3,2,1,0:T(8,128)S(1)} %fusion.81), channel_id=1, source_target_pairs={{0,2},{2,4},{4,6},{6,8},{8,10},{10,12},{12,14},{1,3},{3,5},{5,7},{... | collective-permute-start | bytes 1769480 | tf_op jit(solution)/shard_map/ppermute | solution.py:85
  167.1 11.3 %collective-permute-done.12 = f32[3,6,64,128]{3,2,1,0:T(8,128)S(1)} collective-permute-done((f32[3,6,64,128]{3,2,1,0:T(8,128)S(1)}, f32[3,6,64,128]{3,2,1,0:T(8,128)S(1)}, u32[]{:S(2)}, u32[]{:S(2)}) %collective-permute-start.12) | collective-permute-done | bytes 589856 | tf_op jit(solution)/shard_map/ppermute | solution.py:90
  178.8 12.4 %collective-permute-done.11 = f32[3,6,64,128]{3,2,1,0:T(8,128)S(1)} collective-permute-done((f32[3,6,64,128]{3,2,1,0:T(8,128)S(1)}, f32[3,6,64,128]{3,2,1,0:T(8,128)S(1)}, u32[]{:S(2)}, u32[]{:S(2)}) %collective-permute-start.11) | collective-permute-done | bytes 589856 | tf_op jit(solution)/shard_map/ppermute | solution.py:85
  191.9 0.5 copy-done.16
  192.3 14.2 %fusion.22 = f32[6,6,64,128]{3,2,1,0:T(8,128)} fusion(f32[3,6,64,128]{3,2,1,0:T(8,128)S(1)} %fusion.81, f32[3,6,64,128]{3,2,1,0:T(8,128)S(1)} %fusion.67, f32[6,6,64,128]{3,2,1,0:T(8,128)S(1)} %get-tuple-element.16, f32[6,6,64,128]{3,2,1,0:T(8,128)S(1)} %add_multiply_fusion, f32[6,11,64,128]{3,2,1,0:T(8,128)S(1)} %fusion, f32[11,6,64,128]{3,2,1,0:T(8,128)S(1)} %fusion.1, ...), kind=kLoop, calls=%fused_computation.70 | loop fusion | flops 81395712 | bytes 20096208 | tf_op jit(solution)/shard_map/add | solution.py:309
  (114 shorter events, 5.8 us)
Async XLA Ops:
  0.0 2.5 %copy-start = (f32[6,6,64,128]{3,2,1,0:T(8,128)S(1)}, f32[6,6,64,128]{3,2,1,0:T(8,128)}, u32[]{:S(2)}) copy-start(f32[6,6,64,128]{3,2,1,0:T(8,128)} %param.6) | copy-start | bytes 3538948
  2.0 8.2 %copy-start.23 = (f32[4]{0:T(128)S(1)}, f32[4]{0:T(128)}, u32[]{:S(2)}) copy-start(f32[4]{0:T(128)} %param.8) | copy-start | bytes 52
  2.0 8.8 %copy-start.17 = (f32[2,6,6]{2,0,1:T(2,128)S(1)}, f32[2,6,6]{2,0,1:T(2,128)}, u32[]{:S(2)}) copy-start(f32[2,6,6]{2,0,1:T(2,128)} %param.7) | copy-start | bytes 868
  2.0 63.3 %collective-permute-start.6 = (f32[6,3,64,128]{3,2,1,0:T(8,128)}, f32[6,3,64,128]{3,2,1,0:T(8,128)}, u32[]{:S(2)}, u32[]{:S(2)}) collective-permute-start(f32[6,3,64,128]{3,2,1,0:T(8,128)} %constant_dynamic-slice_fusion), channel_id=1, source_target_pairs={{0,1},{1,0},{2,3},{3,2},{4,5},{5,4},{6,7},{7,6},{8,9},{9,8},{10,11... | collective-permute-start | bytes 1769480 | tf_op jit(solution)/shard_map/ppermute | solution.py:172
  3.7 60.3 %collective-permute-start.5 = (f32[3,6,64,128]{3,2,1,0:T(8,128)}, f32[3,6,64,128]{3,2,1,0:T(8,128)}, u32[]{:S(2)}, u32[]{:S(2)}) collective-permute-start(f32[3,6,64,128]{3,2,1,0:T(8,128)} %get-tuple-element.46), channel_id=1, source_target_pairs={{0,2},{2,4},{4,6},{6,8},{8,10},{10,12},{12,14},{1,3},{3,5},{5,7},{... | collective-permute-start | bytes 1769480 | tf_op jit(solution)/shard_map/ppermute | solution.py:85
  8.9 58.5 %collective-permute-start.7 = (f32[3,6,64,128]{3,2,1,0:T(8,128)}, f32[3,6,64,128]{3,2,1,0:T(8,128)}, u32[]{:S(2)}, u32[]{:S(2)}) collective-permute-start(f32[3,6,64,128]{3,2,1,0:T(8,128)} %get-tuple-element.47), channel_id=1, source_target_pairs={{2,0},{4,2},{6,4},{8,6},{10,8},{12,10},{14,12},{3,1},{5,3},{7,5},{... | collective-permute-start | bytes 1769480 | tf_op jit(solution)/shard_map/ppermute | solution.py:90
  15.3 29.8 %collective-permute-start = (f32[2]{0:T(128)}, f32[2]{0:T(128)}, u32[]{:S(2)}, u32[]{:S(2)}) collective-permute-start(f32[2]{0:T(128)} %maximum_reduce_fusion), channel_id=1, source_target_pairs={{0,1},{1,0},{2,3},{3,2},{4,5},{5,4},{6,7},{7,6},{8,9},{9,8},{10,11... | collective-permute-start | bytes 32 | tf_op jit(solution)/shard_map/ppermute | solution.py:118
  22.3 0.8 copy-start.29
  22.4 1.5 copy-start.28
  38.2 1.6 copy-start.27
  45.8 5.4 %collective-permute-start.3 = (f32[2]{0:T(128)S(1)}, f32[2]{0:T(128)S(1)}, u32[]{:S(2)}, u32[]{:S(2)}) collective-permute-start(f32[2]{0:T(128)S(1)} %max.25), channel_id=1, source_target_pairs={{0,6},{2,8},{4,10},{6,12},{8,14},{10,0},{12,2},{14,4},{1,7},{3,9},... | collective-permute-start | bytes 32 | tf_op jit(solution)/shard_map/ppermute | solution.py:118
  48.4 6.1 %collective-permute-start.2 = (f32[2]{0:T(128)S(1)}, f32[2]{0:T(128)S(1)}, u32[]{:S(2)}, u32[]{:S(2)}) collective-permute-start(f32[2]{0:T(128)S(1)} %max.25), channel_id=1, source_target_pairs={{0,4},{2,6},{4,8},{6,10},{8,12},{10,14},{12,0},{14,2},{1,5},{3,7},... | collective-permute-start | bytes 32 | tf_op jit(solution)/shard_map/ppermute | solution.py:118
  51.1 6.3 %collective-permute-start.1 = (f32[2]{0:T(128)S(1)}, f32[2]{0:T(128)S(1)}, u32[]{:S(2)}, u32[]{:S(2)}) collective-permute-start(f32[2]{0:T(128)S(1)} %max.25), channel_id=1, source_target_pairs={{0,2},{2,4},{4,6},{6,8},{8,10},{10,12},{12,14},{14,0},{1,3},{3,5},... | collective-permute-start | bytes 32 | tf_op jit(solution)/shard_map/ppermute | solution.py:118
  57.4 4.5 %collective-permute-start.4 = (f32[2]{0:T(128)S(1)}, f32[2]{0:T(128)S(1)}, u32[]{:S(2)}, u32[]{:S(2)}) collective-permute-start(f32[2]{0:T(128)S(1)} %maximum_maximum_fusion), channel_id=1, source_target_pairs={{0,8},{2,10},{4,12},{6,14},{8,0},{10,2},{12,4},{14,6},{1,9},{3,11}... | collective-permute-start | bytes 32 | tf_op jit(solution)/shard_map/ppermute | solution.py:118
  63.9 1.4 copy-start.7
  63.9 1.4 copy-start.8
  63.9 1.4 copy-start.9
  63.9 1.4 copy-start.10
  63.9 1.4 copy-start.11
  64.0 1.4 copy-start.12
  64.0 1.4 copy-start.13
  64.0 1.4 copy-start.14
  65.4 1.5 copy-start.2
  65.4 1.5 copy-start.3
  67.3 0.9 copy-start.5
  67.3 1.0 copy-start.6
  67.3 1.0 copy-start.18
  69.5 1.3 copy-start.1
  69.5 1.3 copy-start.4
  69.5 1.3 copy-start.15
  69.5 1.2 copy-start.19
  69.6 1.2 copy-start.22
  69.6 1.2 copy-start.25
  70.8 7.5 %copy-start.20 = (f32[1,3,6]{2,1,0:T(4,128)S(1)}, f32[1,3,6]{2,1,0:T(4,128)}, u32[]{:S(2)}) copy-start(f32[1,3,6]{2,1,0:T(4,128)} %copy.44) | copy-start | bytes 220
  70.8 7.5 %copy-start.24 = (f32[3]{0:T(128)S(1)}, f32[3]{0:T(128)}, u32[]{:S(2)}) copy-start(f32[3]{0:T(128)} %get-tuple-element.104) | copy-start | bytes 40
  87.0 17.7 %collective-permute-start.9 = (f32[6,3,64,128]{3,2,1,0:T(8,128)S(1)}, f32[6,3,64,128]{3,2,1,0:T(8,128)S(1)}, u32[]{:S(2)}, u32[]{:S(2)}) collective-permute-start(f32[6,3,64,128]{3,2,1,0:T(8,128)S(1)} %fusion.82), channel_id=1, source_target_pairs={{0,1},{1,0},{2,3},{3,2},{4,5},{5,4},{6,7},{7,6},{8,9},{9,8},{10,11... | collective-permute-start | bytes 1769480 | tf_op jit(solution)/shard_map/ppermute | solution.py:172
  100.4 28.6 %collective-permute-start.8 = (f32[3,6,64,128]{3,2,1,0:T(8,128)S(1)}, f32[3,6,64,128]{3,2,1,0:T(8,128)S(1)}, u32[]{:S(2)}, u32[]{:S(2)}) collective-permute-start(f32[3,6,64,128]{3,2,1,0:T(8,128)S(1)} %fusion.73), channel_id=1, source_target_pairs={{0,2},{2,4},{4,6},{6,8},{8,10},{10,12},{12,14},{1,3},{3,5},{5,7},{... | collective-permute-start | bytes 1769480 | tf_op jit(solution)/shard_map/ppermute | solution.py:85
  103.1 26.1 %collective-permute-start.10 = (f32[3,6,64,128]{3,2,1,0:T(8,128)S(1)}, f32[3,6,64,128]{3,2,1,0:T(8,128)S(1)}, u32[]{:S(2)}, u32[]{:S(2)}) collective-permute-start(f32[3,6,64,128]{3,2,1,0:T(8,128)S(1)} %fusion.59), channel_id=1, source_target_pairs={{2,0},{4,2},{6,4},{8,6},{10,8},{12,10},{14,12},{3,1},{5,3},{7,5},{... | collective-permute-start | bytes 1769480 | tf_op jit(solution)/shard_map/ppermute | solution.py:90
  160.0 6.6 %collective-permute-start.13 = (f32[6,3,64,128]{3,2,1,0:T(8,128)S(1)}, f32[6,3,64,128]{3,2,1,0:T(8,128)S(1)}, u32[]{:S(2)}, u32[]{:S(2)}) collective-permute-start(f32[6,3,64,128]{3,2,1,0:T(8,128)S(1)} %fusion.83), channel_id=1, source_target_pairs={{0,1},{1,0},{2,3},{3,2},{4,5},{5,4},{6,7},{7,6},{8,9},{9,8},{10,11... | collective-permute-start | bytes 1769480 | tf_op jit(solution)/shard_map/ppermute | solution.py:172
  160.0 18.4 %collective-permute-start.12 = (f32[3,6,64,128]{3,2,1,0:T(8,128)S(1)}, f32[3,6,64,128]{3,2,1,0:T(8,128)S(1)}, u32[]{:S(2)}, u32[]{:S(2)}) collective-permute-start(f32[3,6,64,128]{3,2,1,0:T(8,128)S(1)} %fusion.67), channel_id=1, source_target_pairs={{2,0},{4,2},{6,4},{8,6},{10,8},{12,10},{14,12},{3,1},{5,3},{7,5},{... | collective-permute-start | bytes 1769480 | tf_op jit(solution)/shard_map/ppermute | solution.py:90
  161.3 29.9 %collective-permute-start.11 = (f32[3,6,64,128]{3,2,1,0:T(8,128)S(1)}, f32[3,6,64,128]{3,2,1,0:T(8,128)S(1)}, u32[]{:S(2)}, u32[]{:S(2)}) collective-permute-start(f32[3,6,64,128]{3,2,1,0:T(8,128)S(1)} %fusion.81), channel_id=1, source_target_pairs={{0,2},{2,4},{4,6},{6,8},{8,10},{10,12},{12,14},{1,3},{3,5},{5,7},{... | collective-permute-start | bytes 1769480 | tf_op jit(solution)/shard_map/ppermute | solution.py:85
  191.6 0.7 copy-start.16
  191.6 0.7 copy-start.21
  191.6 0.7 copy-start.26

commit v13 on v12

--- a/solution.py
+++ b/solution.py
@@ -123,6 +123,25 @@
             local = jnp.maximum(local, item)
         span *= 4
         level += 1
+    return local
+
+
+def spread_line(local, axis):
+    count = lax.axis_size(axis)
+    if count % 2:
+        return spread_max(local, axis, 0)
+    moved = lax.ppermute(local, axis, [(i, i ^ 1) for i in range(count)])
+    local = jnp.maximum(local, moved)
+    span = 2
+    while span < count:
+        moved = [
+            lax.ppermute(local, axis, [(i, (i + k * span) % count) for i in range(count)])
+            for k in range(1, 4)
+            if k * span < count
+        ]
+        for item in moved:
+            local = jnp.maximum(local, item)
+        span *= 4
     return local
 
 
@@ -207,7 +226,7 @@
     )
     local_bounds = jnp.max(terms, axis=(1, 2))
     locals_now = local_whole(values)
-    bounds = spread_max(spread_max(local_bounds, "gy", 0), "gx", 0)
+    bounds = spread_line(spread_max(local_bounds, "gy", 0), "gx")
     bound_one = bounds[0]
     bound_two = bounds[1]
     step_time = cfl_number / (
@@ -294,9 +313,8 @@
         next_pieces = local_whole(merged)
         return merged, (sent[1], sent[0]), next_y, next_pieces
 
-    fresh = jnp.where(values == values, values, 0.0)
     first, x_halos, y_halos, locals_now = stage(
-        fresh, x_halos, y_halos, locals_now, (0, 1),
+        values, x_halos, y_halos, locals_now, (0, 1),
         lambda side, rate: cut(values, side) + step_time * rate, False,
     )
     second, x_halos, y_halos, locals_now = stage(

time: 207 us -> 206 us (level)
    ppermute x5 -> x1, starting transfers between devices: 9.53 us -> 0.22 us  [spread_max(): lax.ppermute(local, axis, [(i, (i + k * span) % count) for i in range(cou...]
    ppermute x0 -> x4, waiting for transfers between devices: none -> 8.21 us  [the longest x3 6.66 us: spread_line(): lax.ppermute(local, axis, [(i, (i + k * span) % count) for i in range(cou...]
    ppermute x0 -> x4, starting transfers between devices: none -> 6.87 us  [the longest x3 4.44 us: spread_line(): lax.ppermute(local, axis, [(i, (i + k * span) % count) for i in range(cou...]
    ppermute x5 -> x1, waiting for transfers between devices: 6.79 us -> 0.01 us  [spread_max(): lax.ppermute(local, axis, [(i, (i + k * span) % count) for i in range(cou...]
    unnamed x63 -> x59, local copies, waits for them, and re-layouts: 4.64 us -> 4.6 us
  transfers between devices with their start and end apart: 14 -> 14, of which waited for: 6 -> 7; matrix products, arithmetic and copies ran while one was open for 25% -> 25% of each run, Pallas kernels for 0% -> 0%
where the time goes in v13:
time: 206 us; the launch traced here: 205 us
  other arithmetic  107 us (52%)
  waiting for transfers between devices  55.8 us (27%)
  starting transfers between devices  25.7 us (12%)
  local copies, waits for them, and re-layouts  10.9 us (5%)
  between operations  5.97 us (3%)
    add x3, other arithmetic, local_part(): partial + 0.5 * (alpha_three * (fore_three - back_three) + alpha_four * (...  39.3 us
    ppermute x3, waiting for transfers between devices, send_low(): lax.ppermute(piece, axis, [(i, (i + 1) % count) for i in range(count - 1)])  36.3 us
    add x2, other arithmetic, on_device(): 0.75 * cut(values, side) + 0.25 * (cut(first, side) + step_time * rate)  15 us
    add x2, other arithmetic, on_device(): cut(values, side) + step_time * rate  14.8 us
    add x1, other arithmetic, on_device(): cut(values, side) * (1.0 / 3.0)  14.1 us
    ppermute x3, starting transfers between devices, send_low(): lax.ppermute(piece, axis, [(i, (i + 1) % count) for i in range(count - 1)])  13.9 us
    ppermute x3, waiting for transfers between devices, send_high(): lax.ppermute(piece, axis, [((i + 1) % count, i) for i in range(count - 1)])  11.3 us
    ppermute x3, waiting for transfers between devices, spread_line(): lax.ppermute(local, axis, [(i, (i + k * span) % count) for i in range(cou...  6.66 us
  transfers between devices with their start and end apart: 14, of which 7 were waited for; matrix products, arithmetic and copies ran while one was open for 25% of the time, Pallas kernels for 0%

profile of v13, /device:TPU:0, one launch (start us, length us, event | category | flops | bytes accessed | tf_op | source)
XLA Modules:
  0.0 205.3 jit_solution(14681695520678846667)
XLA Ops:
  0.0 2.0 constant_dynamic-slice_fusion
  2.0 0.5 collective-permute-start.6
  2.5 1.2 fusion.117
  3.7 5.2 %collective-permute-start.5 = (f32[3,6,64,128]{3,2,1,0:T(8,128)}, f32[3,6,64,128]{3,2,1,0:T(8,128)}, u32[]{:S(2)}, u32[]{:S(2)}) collective-permute-start(f32[3,6,64,128]{3,2,1,0:T(8,128)} %get-tuple-element.55), channel_id=1, source_target_pairs={{0,2},{2,4},{4,6},{6,8},{8,10},{10,12},{12,14},{1,3},{3,5},{5,7},{... | collective-permute-start | bytes 1769480 | tf_op jit(solution)/shard_map/ppermute | solution.py:85
  8.9 1.3 collective-permute-start.7
  10.2 0.7 fusion.123
  10.9 0.6 abs_multiply_fusion
  11.6 0.6 abs_multiply_fusion.1
  13.5 1.2 copy_bitcast_fusion
  14.7 0.7 maximum_reduce_fusion
  15.6 0.4 subtract_multiply_fusion
  17.8 0.9 slice_bitcast_fusion.13
  18.8 0.5 add_convert_fusion
  19.3 0.6 fusion.120
  19.9 0.5 fusion.110
  20.4 0.4 fusion.119
  21.2 0.7 slice_multiply_fusion.1
  21.9 0.6 broadcast_multiply_fusion
  22.5 0.6 broadcast_multiply_fusion.1
  23.2 13.1 %multiply_add_fusion.2 = (f32[6,6,64,128]{3,2,1,0:T(8,128)S(1)}, f32[6,6,64,128]{3,2,1,0:T(8,128)S(1)}, f32[6,6,64,128]{3,2,1,0:T(8,128)S(1)}) fusion(f32[6,6,64,1]{3,2,1,0:T(8,128)S(1)} %get-tuple-element.59, f32[6,6,64,127]{3,2,1,0:T(8,128)S(1)} %subtract_multiply_fusion, f32[6,6,64,1]{3,2,1,0:T(8,128)S(1)} %get-tuple-element.58, f32[]{:T(128)S(6)} %add.2511, ...), kind=kLoop, calls=%fused_computation.128 | loop fusion | flops 81100800 | bytes 11805708 | tf_op jit(solution)/shard_map/add | solution.py:179
  36.5 0.4 copy-done.19
  36.9 0.7 add_multiply_fusion.7
  37.6 0.7 add_multiply_fusion.9
  38.3 0.7 broadcast_add_fusion
  39.0 0.5 fusion.111
  39.5 1.3 copy.43
  41.5 1.3 copy.44
  42.7 0.9 slice_bitcast_fusion.5
  43.6 0.7 max.25
  44.3 2.4 %collective-permute-start.1 = (f32[2]{0:T(128)S(1)}, f32[2]{0:T(128)S(1)}, u32[]{:S(2)}, u32[]{:S(2)}) collective-permute-start(f32[2]{0:T(128)S(1)} %max.25), channel_id=1, source_target_pairs={{0,2},{2,0},{4,6},{6,4},{8,10},{10,8},{12,14},{14,12},{1,3},{3,1},... | collective-permute-start | bytes 32 | tf_op jit(solution)/shard_map/ppermute | solution.py:133
  46.7 1.5 collective-permute-done.1
  48.3 4.2 %collective-permute-start.4 = (f32[2]{0:T(128)S(1)}, f32[2]{0:T(128)S(1)}, u32[]{:S(2)}, u32[]{:S(2)}) collective-permute-start(f32[2]{0:T(128)S(1)} %max.26), channel_id=1, source_target_pairs={{0,12},{2,14},{4,0},{6,2},{8,4},{10,6},{12,8},{14,10},{1,13},{3,15... | collective-permute-start | bytes 32 | tf_op jit(solution)/shard_map/ppermute | solution.py:138
  52.5 1.3 collective-permute-done.4
  54.0 2.9 %collective-permute-done.3 = f32[2]{0:T(128)S(1)} collective-permute-done((f32[2]{0:T(128)S(1)}, f32[2]{0:T(128)S(1)}, u32[]{:S(2)}, u32[]{:S(2)}) %collective-permute-start.3) | collective-permute-done | bytes 40 | tf_op jit(solution)/shard_map/ppermute | solution.py:138
  56.9 2.4 %collective-permute-done.2 = f32[2]{0:T(128)S(1)} collective-permute-done((f32[2]{0:T(128)S(1)}, f32[2]{0:T(128)S(1)}, u32[]{:S(2)}, u32[]{:S(2)}) %collective-permute-start.2) | collective-permute-done | bytes 40 | tf_op jit(solution)/shard_map/ppermute | solution.py:138
  59.4 0.6 fusion.122
  61.4 1.3 add_select_fusion.7
  62.8 1.3 add_select_fusion.15
  64.2 1.5 pad_maximum_fusion.29
  65.9 0.8 copy-done.2
  66.8 1.2 add_select_fusion.5
  68.0 0.5 fusion.7
  68.8 7.4 %fusion.73 = f32[3,6,64,128]{3,2,1,0:T(8,128)S(1)} fusion(f32[6,6,64,128]{3,2,1,0:T(8,128)S(1)} %get-tuple-element.12, f32[6,6,64,128]{3,2,1,0:T(8,128)S(1)} %add_multiply_fusion.2, f32[3,11,64,128]{3,2,1,0:T(8,128)S(1)} %fusion.52, f32[8,6,64,128]{3,2,1,0:T(8,128)S(1)} %get-tuple-element.41, f32[3]{0:T(128)S(1)} %copy-done.23, ...), kind=kLoop, calls=%fused_computation.170 | loop fusion | flops 40108032 | bytes 9474684 | tf_op jit(solution)/shard_map/add | solution.py:318
  76.2 7.4 %fusion.59 = f32[3,6,64,128]{3,2,1,0:T(8,128)S(1)} fusion(f32[6,6,64,128]{3,2,1,0:T(8,128)S(1)} %get-tuple-element.12, f32[6,6,64,128]{3,2,1,0:T(8,128)S(1)} %add_multiply_fusion.2, f32[3,11,64,128]{3,2,1,0:T(8,128)S(1)} %fusion.53, f32[8,6,64,128]{3,2,1,0:T(8,128)S(1)} %get-tuple-element.40, f32[]{:T(128)} %bitcast.3, f32[]{:T(128)} %bitcast.2, ...), kind=kLoop, calls=%fused_computation.156 | loop fusion | flops 40108032 | bytes 9474684 | tf_op jit(solution)/shard_map/add | solution.py:318
  83.6 0.4 fusion.15
  84.1 0.4 fusion.116
  85.0 13.1 %multiply_add_fusion.1 = (f32[6,6,64,128]{3,2,1,0:T(8,128)S(1)}, f32[6,6,64,128]{3,2,1,0:T(8,128)S(1)}, f32[6,6,64,128]{3,2,1,0:T(8,128)S(1)}) fusion(f32[6,6,64,1]{3,2,1,0:T(8,128)S(1)} %get-tuple-element.39, f32[6,6,64,127]{3,2,1,0:T(8,128)S(1)} %fusion.15, f32[6,6,64,1]{3,2,1,0:T(8,128)S(1)} %get-tuple-element.38, f32[]{:T(128)S(6)} %add.2511, ...), kind=kLoop, calls=%fused_computation.118 | loop fusion | flops 81100800 | bytes 11805708 | tf_op jit(solution)/shard_map/add | solution.py:179
  98.3 3.6 %collective-permute-start.8 = (f32[3,6,64,128]{3,2,1,0:T(8,128)S(1)}, f32[3,6,64,128]{3,2,1,0:T(8,128)S(1)}, u32[]{:S(2)}, u32[]{:S(2)}) collective-permute-start(f32[3,6,64,128]{3,2,1,0:T(8,128)S(1)} %fusion.73), channel_id=1, source_target_pairs={{0,2},{2,4},{4,6},{6,8},{8,10},{10,12},{12,14},{1,3},{3,5},{5,7},{... | collective-permute-start | bytes 1769480 | tf_op jit(solution)/shard_map/ppermute | solution.py:85
  101.9 1.5 collective-permute-start.10
  103.8 23.9 %collective-permute-done.8 = f32[3,6,64,128]{3,2,1,0:T(8,128)S(1)} collective-permute-done((f32[3,6,64,128]{3,2,1,0:T(8,128)S(1)}, f32[3,6,64,128]{3,2,1,0:T(8,128)S(1)}, u32[]{:S(2)}, u32[]{:S(2)}) %collective-permute-start.8) | collective-permute-done | bytes 589856 | tf_op jit(solution)/shard_map/ppermute | solution.py:85
  128.2 0.5 pad_maximum_fusion.3
  129.2 7.5 %fusion.81 = f32[3,6,64,128]{3,2,1,0:T(8,128)S(1)} fusion(f32[3,6,64,128]{3,2,1,0:T(8,128)S(1)} %fusion.73, f32[6,6,64,128]{3,2,1,0:T(8,128)S(1)} %get-tuple-element.14, f32[6,6,64,128]{3,2,1,0:T(8,128)S(1)} %add_multiply_fusion.1, f32[3,11,64,128]{3,2,1,0:T(8,128)S(1)} %fusion.50, f32[8,6,64,128]{3,2,1,0:T(8,128)S(1)} %fusion.8, f32[3]{0:T(128)S(1)} %copy-done.23, ...), kind=kLoop, calls=%fused_computation.178 | loop fusion | flops 40550400 | bytes 10064508 | tf_op jit(solution)/shard_map/add | solution.py:322
  136.7 7.5 %fusion.67 = f32[3,6,64,128]{3,2,1,0:T(8,128)S(1)} fusion(f32[3,6,64,128]{3,2,1,0:T(8,128)S(1)} %fusion.59, f32[6,6,64,128]{3,2,1,0:T(8,128)S(1)} %get-tuple-element.14, f32[6,6,64,128]{3,2,1,0:T(8,128)S(1)} %add_multiply_fusion.1, f32[3,11,64,128]{3,2,1,0:T(8,128)S(1)} %fusion.51, f32[8,6,64,128]{3,2,1,0:T(8,128)S(1)} %fusion.9, f32[]{:T(128)} %bitcast.3, ...), kind=kLoop, calls=%fused_computation.164 | loop fusion | flops 40550400 | bytes 10064508 | tf_op jit(solution)/shard_map/add | solution.py:322
  144.2 0.4 fusion.18
  144.7 0.4 fusion.115
  145.5 13.1 %multiply_add_fusion = (f32[6,6,64,128]{3,2,1,0:T(8,128)S(1)}, f32[6,6,64,128]{3,2,1,0:T(8,128)S(1)}, f32[6,6,64,128]{3,2,1,0:T(8,128)S(1)}) fusion(f32[6,6,64,1]{3,2,1,0:T(8,128)S(1)} %get-tuple-element.33, f32[6,6,64,127]{3,2,1,0:T(8,128)S(1)} %fusion.18, f32[6,6,64,1]{3,2,1,0:T(8,128)S(1)} %get-tuple-element.32, f32[]{:T(128)S(6)} %add.2511, f32[]{:T(128)} %bitcast.5, ...), kind=kLoop, calls=%fused_computation.108 | loop fusion | flops 81100800 | bytes 11805708 | tf_op jit(solution)/shard_map/add | solution.py:179
  158.8 1.3 collective-permute-start.12
  160.1 5.1 %collective-permute-start.11 = (f32[3,6,64,128]{3,2,1,0:T(8,128)S(1)}, f32[3,6,64,128]{3,2,1,0:T(8,128)S(1)}, u32[]{:S(2)}, u32[]{:S(2)}) collective-permute-start(f32[3,6,64,128]{3,2,1,0:T(8,128)S(1)} %fusion.81), channel_id=1, source_target_pairs={{0,2},{2,4},{4,6},{6,8},{8,10},{10,12},{12,14},{1,3},{3,5},{5,7},{... | collective-permute-start | bytes 1769480 | tf_op jit(solution)/shard_map/ppermute | solution.py:85
  165.6 0.3 pad_maximum_fusion.2
  165.9 11.3 %collective-permute-done.12 = f32[3,6,64,128]{3,2,1,0:T(8,128)S(1)} collective-permute-done((f32[3,6,64,128]{3,2,1,0:T(8,128)S(1)}, f32[3,6,64,128]{3,2,1,0:T(8,128)S(1)}, u32[]{:S(2)}, u32[]{:S(2)}) %collective-permute-start.12) | collective-permute-done | bytes 589856 | tf_op jit(solution)/shard_map/ppermute | solution.py:90
  177.4 0.3 fusion
  177.6 12.4 %collective-permute-done.11 = f32[3,6,64,128]{3,2,1,0:T(8,128)S(1)} collective-permute-done((f32[3,6,64,128]{3,2,1,0:T(8,128)S(1)}, f32[3,6,64,128]{3,2,1,0:T(8,128)S(1)}, u32[]{:S(2)}, u32[]{:S(2)}) %collective-permute-start.11) | collective-permute-done | bytes 589856 | tf_op jit(solution)/shard_map/ppermute | solution.py:85
  190.6 0.5 copy-done.13
  191.1 14.1 %fusion.22 = f32[6,6,64,128]{3,2,1,0:T(8,128)} fusion(f32[3,6,64,128]{3,2,1,0:T(8,128)S(1)} %fusion.81, f32[3,6,64,128]{3,2,1,0:T(8,128)S(1)} %fusion.67, f32[6,6,64,128]{3,2,1,0:T(8,128)S(1)} %get-tuple-element.16, f32[6,6,64,128]{3,2,1,0:T(8,128)S(1)} %add_multiply_fusion, f32[6,11,64,128]{3,2,1,0:T(8,128)S(1)} %fusion, f32[11,6,64,128]{3,2,1,0:T(8,128)S(1)} %fusion.1, ...), kind=kLoop, calls=%fused_computation.69 | loop fusion | flops 81395712 | bytes 20096208 | tf_op jit(solution)/shard_map/add | solution.py:327
  (108 shorter events, 5.6 us)
Async XLA Ops:
  0.0 2.5 %copy-start = (f32[6,6,64,128]{3,2,1,0:T(8,128)S(1)}, f32[6,6,64,128]{3,2,1,0:T(8,128)}, u32[]{:S(2)}) copy-start(f32[6,6,64,128]{3,2,1,0:T(8,128)} %param.6) | copy-start | bytes 3538948
  2.0 8.2 %copy-start.21 = (f32[4]{0:T(128)S(1)}, f32[4]{0:T(128)}, u32[]{:S(2)}) copy-start(f32[4]{0:T(128)} %param.8) | copy-start | bytes 52
  2.0 8.9 %copy-start.14 = (f32[2,6,6]{2,0,1:T(2,128)S(1)}, f32[2,6,6]{2,0,1:T(2,128)}, u32[]{:S(2)}) copy-start(f32[2,6,6]{2,0,1:T(2,128)} %param.7) | copy-start | bytes 868
  2.0 60.7 %collective-permute-start.6 = (f32[6,3,64,128]{3,2,1,0:T(8,128)}, f32[6,3,64,128]{3,2,1,0:T(8,128)}, u32[]{:S(2)}, u32[]{:S(2)}) collective-permute-start(f32[6,3,64,128]{3,2,1,0:T(8,128)} %constant_dynamic-slice_fusion), channel_id=1, source_target_pairs={{0,1},{1,0},{2,3},{3,2},{4,5},{5,4},{6,7},{7,6},{8,9},{9,8},{10,11... | collective-permute-start | bytes 1769480 | tf_op jit(solution)/shard_map/ppermute | solution.py:191
  3.7 57.7 %collective-permute-start.5 = (f32[3,6,64,128]{3,2,1,0:T(8,128)}, f32[3,6,64,128]{3,2,1,0:T(8,128)}, u32[]{:S(2)}, u32[]{:S(2)}) collective-permute-start(f32[3,6,64,128]{3,2,1,0:T(8,128)} %get-tuple-element.55), channel_id=1, source_target_pairs={{0,2},{2,4},{4,6},{6,8},{8,10},{10,12},{12,14},{1,3},{3,5},{5,7},{... | collective-permute-start | bytes 1769480 | tf_op jit(solution)/shard_map/ppermute | solution.py:85
  8.9 56.9 %collective-permute-start.7 = (f32[3,6,64,128]{3,2,1,0:T(8,128)}, f32[3,6,64,128]{3,2,1,0:T(8,128)}, u32[]{:S(2)}, u32[]{:S(2)}) collective-permute-start(f32[3,6,64,128]{3,2,1,0:T(8,128)} %get-tuple-element.54), channel_id=1, source_target_pairs={{2,0},{4,2},{6,4},{8,6},{10,8},{12,10},{14,12},{3,1},{5,3},{7,5},{... | collective-permute-start | bytes 1769480 | tf_op jit(solution)/shard_map/ppermute | solution.py:90
  15.4 28.2 %collective-permute-start = (f32[2]{0:T(128)}, f32[2]{0:T(128)}, u32[]{:S(2)}, u32[]{:S(2)}) collective-permute-start(f32[2]{0:T(128)} %maximum_reduce_fusion), channel_id=1, source_target_pairs={{0,1},{1,0},{2,3},{3,2},{4,5},{5,4},{6,7},{7,6},{8,9},{9,8},{10,11... | collective-permute-start | bytes 32 | tf_op jit(solution)/shard_map/ppermute | solution.py:118
  21.0 0.9 copy-start.27
  21.0 1.5 copy-start.26
  36.3 0.7 copy-start.19
  36.3 2.0 copy-start.25
  44.3 4.0 %collective-permute-start.1 = (f32[2]{0:T(128)S(1)}, f32[2]{0:T(128)S(1)}, u32[]{:S(2)}, u32[]{:S(2)}) collective-permute-start(f32[2]{0:T(128)S(1)} %max.25), channel_id=1, source_target_pairs={{0,2},{2,0},{4,6},{6,4},{8,10},{10,8},{12,14},{14,12},{1,3},{3,1},... | collective-permute-start | bytes 32 | tf_op jit(solution)/shard_map/ppermute | solution.py:133
  48.3 5.5 %collective-permute-start.4 = (f32[2]{0:T(128)S(1)}, f32[2]{0:T(128)S(1)}, u32[]{:S(2)}, u32[]{:S(2)}) collective-permute-start(f32[2]{0:T(128)S(1)} %max.26), channel_id=1, source_target_pairs={{0,12},{2,14},{4,0},{6,2},{8,4},{10,6},{12,8},{14,10},{1,13},{3,15... | collective-permute-start | bytes 32 | tf_op jit(solution)/shard_map/ppermute | solution.py:138
  52.5 4.5 %collective-permute-start.3 = (f32[2]{0:T(128)S(1)}, f32[2]{0:T(128)S(1)}, u32[]{:S(2)}, u32[]{:S(2)}) collective-permute-start(f32[2]{0:T(128)S(1)} %max.26), channel_id=1, source_target_pairs={{0,8},{2,10},{4,12},{6,14},{8,0},{10,2},{12,4},{14,6},{1,9},{3,11}... | collective-permute-start | bytes 32 | tf_op jit(solution)/shard_map/ppermute | solution.py:138
  53.8 5.6 %collective-permute-start.2 = (f32[2]{0:T(128)S(1)}, f32[2]{0:T(128)S(1)}, u32[]{:S(2)}, u32[]{:S(2)}) collective-permute-start(f32[2]{0:T(128)S(1)} %max.26), channel_id=1, source_target_pairs={{0,4},{2,6},{4,8},{6,10},{8,12},{10,14},{12,0},{14,2},{1,5},{3,7},... | collective-permute-start | bytes 32 | tf_op jit(solution)/shard_map/ppermute | solution.py:138
  61.3 1.4 copy-start.4
  61.3 1.4 copy-start.5
  61.3 1.4 copy-start.6
  61.3 1.4 copy-start.7
  61.4 1.4 copy-start.8
  61.4 1.4 copy-start.9
  61.4 1.4 copy-start.10
  61.4 1.4 copy-start.11
  65.7 0.9 copy-start.2
  65.7 1.0 copy-start.3
  65.8 1.0 copy-start.15
  68.0 0.8 copy-start.1
  68.0 0.8 copy-start.12
  68.0 0.7 copy-start.16
  68.0 0.7 copy-start.20
  68.0 0.7 copy-start.23
  68.8 7.4 %copy-start.17 = (f32[1,3,6]{2,1,0:T(4,128)S(1)}, f32[1,3,6]{2,1,0:T(4,128)}, u32[]{:S(2)}) copy-start(f32[1,3,6]{2,1,0:T(4,128)} %copy.44) | copy-start | bytes 220
  68.8 7.4 %copy-start.22 = (f32[3]{0:T(128)S(1)}, f32[3]{0:T(128)}, u32[]{:S(2)}) copy-start(f32[3]{0:T(128)} %get-tuple-element.102) | copy-start | bytes 40
  84.9 18.6 %collective-permute-start.9 = (f32[6,3,64,128]{3,2,1,0:T(8,128)S(1)}, f32[6,3,64,128]{3,2,1,0:T(8,128)S(1)}, u32[]{:S(2)}, u32[]{:S(2)}) collective-permute-start(f32[6,3,64,128]{3,2,1,0:T(8,128)S(1)} %fusion.82), channel_id=1, source_target_pairs={{0,1},{1,0},{2,3},{3,2},{4,5},{5,4},{6,7},{7,6},{8,9},{9,8},{10,11... | collective-permute-start | bytes 1769480 | tf_op jit(solution)/shard_map/ppermute | solution.py:191
  98.3 29.4 %collective-permute-start.8 = (f32[3,6,64,128]{3,2,1,0:T(8,128)S(1)}, f32[3,6,64,128]{3,2,1,0:T(8,128)S(1)}, u32[]{:S(2)}, u32[]{:S(2)}) collective-permute-start(f32[3,6,64,128]{3,2,1,0:T(8,128)S(1)} %fusion.73), channel_id=1, source_target_pairs={{0,2},{2,4},{4,6},{6,8},{8,10},{10,12},{12,14},{1,3},{3,5},{5,7},{... | collective-permute-start | bytes 1769480 | tf_op jit(solution)/shard_map/ppermute | solution.py:85
  101.9 26.1 %collective-permute-start.10 = (f32[3,6,64,128]{3,2,1,0:T(8,128)S(1)}, f32[3,6,64,128]{3,2,1,0:T(8,128)S(1)}, u32[]{:S(2)}, u32[]{:S(2)}) collective-permute-start(f32[3,6,64,128]{3,2,1,0:T(8,128)S(1)} %fusion.59), channel_id=1, source_target_pairs={{2,0},{4,2},{6,4},{8,6},{10,8},{12,10},{14,12},{3,1},{5,3},{7,5},{... | collective-permute-start | bytes 1769480 | tf_op jit(solution)/shard_map/ppermute | solution.py:90
  158.8 6.6 %collective-permute-start.13 = (f32[6,3,64,128]{3,2,1,0:T(8,128)S(1)}, f32[6,3,64,128]{3,2,1,0:T(8,128)S(1)}, u32[]{:S(2)}, u32[]{:S(2)}) collective-permute-start(f32[6,3,64,128]{3,2,1,0:T(8,128)S(1)} %fusion.83), channel_id=1, source_target_pairs={{0,1},{1,0},{2,3},{3,2},{4,5},{5,4},{6,7},{7,6},{8,9},{9,8},{10,11... | collective-permute-start | bytes 1769480 | tf_op jit(solution)/shard_map/ppermute | solution.py:191
  158.8 18.4 %collective-permute-start.12 = (f32[3,6,64,128]{3,2,1,0:T(8,128)S(1)}, f32[3,6,64,128]{3,2,1,0:T(8,128)S(1)}, u32[]{:S(2)}, u32[]{:S(2)}) collective-permute-start(f32[3,6,64,128]{3,2,1,0:T(8,128)S(1)} %fusion.67), channel_id=1, source_target_pairs={{2,0},{4,2},{6,4},{8,6},{10,8},{12,10},{14,12},{3,1},{5,3},{7,5},{... | collective-permute-start | bytes 1769480 | tf_op jit(solution)/shard_map/ppermute | solution.py:90
  160.1 29.9 %collective-permute-start.11 = (f32[3,6,64,128]{3,2,1,0:T(8,128)S(1)}, f32[3,6,64,128]{3,2,1,0:T(8,128)S(1)}, u32[]{:S(2)}, u32[]{:S(2)}) collective-permute-start(f32[3,6,64,128]{3,2,1,0:T(8,128)S(1)} %fusion.81), channel_id=1, source_target_pairs={{0,2},{2,4},{4,6},{6,8},{8,10},{10,12},{12,14},{1,3},{3,5},{5,7},{... | collective-permute-start | bytes 1769480 | tf_op jit(solution)/shard_map/ppermute | solution.py:85
  190.4 0.7 copy-start.13
  190.4 0.7 copy-start.18
  190.4 0.7 copy-start.24

commit v14 on v12

--- a/solution.py
+++ b/solution.py
@@ -162,10 +162,10 @@
         )
         return mean_three, partial
 
-    def y_halo(field):
+    def y_halo(field, paired=False):
         tail = lax.slice_in_dim(field, cells_y - 3, cells_y, axis=1)
         head = lax.slice_in_dim(field, 0, 3, axis=1)
-        if devices_y == 2:
+        if devices_y == 2 and not paired:
             offset = jnp.where(first_y, cells_y - 3, 0)
             piece = lax.dynamic_slice_in_dim(field, offset, 3, axis=1)
             piece = lax.optimization_barrier(piece)
@@ -178,7 +178,7 @@
         return lax.optimization_barrier(local_part(field))
 
     x_halos = (send_low(values[cells_x - 3 :], "gx"), send_high(values[:3], "gx"))
-    y_halos = y_halo(values)
+    y_halos = y_halo(values, paired=True)
     psi_grid = np.arange(n_psi).astype(np.float32) * np.float32(step_psi) - np.float32(math.pi)
     cos_table = np.cos(psi_grid.astype(np.float64)).astype(np.float32)
     sin_table = np.sin(psi_grid.astype(np.float64)).astype(np.float32)
@@ -294,9 +294,8 @@
         next_pieces = local_whole(merged)
         return merged, (sent[1], sent[0]), next_y, next_pieces
 
-    fresh = jnp.where(values == values, values, 0.0)
     first, x_halos, y_halos, locals_now = stage(
-        fresh, x_halos, y_halos, locals_now, (0, 1),
+        values, x_halos, y_halos, locals_now, (0, 1),
         lambda side, rate: cut(values, side) + step_time * rate, False,
     )
     second, x_halos, y_halos, locals_now = stage(

time: 207 us -> 219 us (1.058)
  waiting for transfers between devices: 54.4 us -> 62 us
  starting transfers between devices: 27.3 us -> 31.5 us
    ppermute x5, waiting for transfers between devices: 6.79 us -> 14.3 us  [spread_max(): lax.ppermute(local, axis, [(i, (i + k * span) % count) for i in range(cou...]
    ppermute x3 -> x4, starting transfers between devices: 13 us -> 17.7 us  [send_low(): lax.ppermute(piece, axis, [(i, (i + 1) % count) for i in range(count - 1)])]
    ppermute x3 -> x4, starting transfers between devices: 4.08 us -> 5.5 us  [send_high(): lax.ppermute(piece, axis, [((i + 1) % count, i) for i in range(count - 1)])]
    unnamed x63 -> x53, local copies, waits for them, and re-layouts: 4.64 us -> 4.92 us
    ppermute x3 -> x4, waiting for transfers between devices: 11.3 us -> 11.4 us  [send_high(): lax.ppermute(piece, axis, [((i + 1) % count, i) for i in range(count - 1)])]
    ppermute x3 -> x4, waiting for transfers between devices: 36.3 us -> 36.3 us  [send_low(): lax.ppermute(piece, axis, [(i, (i + 1) % count) for i in range(count - 1)])]
  transfers between devices with their start and end apart: 14 -> 15, of which waited for: 6 -> 7; matrix products, arithmetic and copies ran while one was open for 25% -> 23% of each run, Pallas kernels for 0% -> 0%
where the time goes in v14:
time: 219 us; the launch traced here: 218 us
  other arithmetic  107 us (49%)
  waiting for transfers between devices  62 us (28%)
  starting transfers between devices  31.5 us (14%)
  local copies, waits for them, and re-layouts  11.7 us (5%)
  between operations  5.91 us (3%)
    add x3, other arithmetic, local_part(): partial + 0.5 * (alpha_three * (fore_three - back_three) + alpha_four * (...  39.1 us
    ppermute x4, waiting for transfers between devices, send_low(): lax.ppermute(piece, axis, [(i, (i + 1) % count) for i in range(count - 1)])  36.3 us
    ppermute x4, starting transfers between devices, send_low(): lax.ppermute(piece, axis, [(i, (i + 1) % count) for i in range(count - 1)])  17.7 us
    add x2, other arithmetic, on_device(): 0.75 * cut(values, side) + 0.25 * (cut(first, side) + step_time * rate)  15.2 us
    add x2, other arithmetic, on_device(): cut(values, side) + step_time * rate  15.1 us
    ppermute x5, waiting for transfers between devices, spread_max(): lax.ppermute(local, axis, [(i, (i + k * span) % count) for i in range(cou...  14.3 us
    add x1, other arithmetic, on_device(): cut(values, side) * (1.0 / 3.0)  14.3 us
    ppermute x4, waiting for transfers between devices, send_high(): lax.ppermute(piece, axis, [((i + 1) % count, i) for i in range(count - 1)])  11.4 us
  transfers between devices with their start and end apart: 15, of which 7 were waited for; matrix products, arithmetic and copies ran while one was open for 23% of the time, Pallas kernels for 0%

profile of v14, /device:TPU:0, one launch (start us, length us, event | category | flops | bytes accessed | tf_op | source)
XLA Modules:
  0.0 218.1 jit_solution(1652037968356825017)
XLA Ops:
  0.0 2.5 %fusion.118 = (f32[6,3,64,128]{3,2,1,0:T(8,128)}, f32[6,3,64,128]{3,2,1,0:T(8,128)}) fusion(f32[6,6,64,128]{3,2,1,0:T(8,128)} %param.6), kind=kLoop, calls=%fused_computation.285 | loop fusion | bytes 2359296 | tf_op jit(solution)/shard_map/slice | solution.py:167
  2.5 1.4 collective-permute-start.7
  3.9 4.7 %collective-permute-start.6 = (f32[6,3,64,128]{3,2,1,0:T(8,128)}, f32[6,3,64,128]{3,2,1,0:T(8,128)}, u32[]{:S(2)}, u32[]{:S(2)}) collective-permute-start(f32[6,3,64,128]{3,2,1,0:T(8,128)} %get-tuple-element.13), channel_id=1, source_target_pairs={{0,1},{2,3},{4,5},{6,7},{8,9},{10,11},{12,13},{14,15},{16,17},{18,... | collective-permute-start | bytes 1769480 | tf_op jit(solution)/shard_map/ppermute | solution.py:85
  8.6 1.2 fusion.117
  9.8 5.7 %collective-permute-start.5 = (f32[3,6,64,128]{3,2,1,0:T(8,128)}, f32[3,6,64,128]{3,2,1,0:T(8,128)}, u32[]{:S(2)}, u32[]{:S(2)}) collective-permute-start(f32[3,6,64,128]{3,2,1,0:T(8,128)} %get-tuple-element.59), channel_id=1, source_target_pairs={{0,2},{2,4},{4,6},{6,8},{8,10},{10,12},{12,14},{1,3},{3,5},{5,7},{... | collective-permute-start | bytes 1769480 | tf_op jit(solution)/shard_map/ppermute | solution.py:85
  15.5 1.3 collective-permute-start.8
  16.8 0.7 fusion.124
  17.5 0.6 abs_multiply_fusion
  18.1 0.6 abs_multiply_fusion.1
  19.8 1.1 copy_bitcast_fusion
  21.0 0.7 maximum_reduce_fusion
  21.7 0.4 subtract_multiply_fusion
  24.0 1.0 slice_bitcast_fusion.13
  24.9 0.6 add_convert_fusion
  25.5 0.6 fusion.121
  26.1 0.5 fusion.110
  26.7 0.4 fusion.120
  27.4 0.6 slice_multiply_fusion.1
  28.1 0.5 broadcast_multiply_fusion
  28.6 0.5 broadcast_multiply_fusion.1
  29.2 13.0 %multiply_add_fusion.2 = (f32[6,6,64,128]{3,2,1,0:T(8,128)S(1)}, f32[6,6,64,128]{3,2,1,0:T(8,128)S(1)}, f32[6,6,64,128]{3,2,1,0:T(8,128)S(1)}) fusion(f32[6,6,64,1]{3,2,1,0:T(8,128)S(1)} %get-tuple-element.65, f32[6,6,64,127]{3,2,1,0:T(8,128)S(1)} %subtract_multiply_fusion, f32[6,6,64,1]{3,2,1,0:T(8,128)S(1)} %get-tuple-element.64, f32[]{:T(128)S(6)} %add.2510, ...), kind=kLoop, calls=%fused_computation.128 | loop fusion | flops 81100800 | bytes 11805708 | tf_op jit(solution)/shard_map/add | solution.py:160
  42.4 0.7 add_multiply_fusion.7
  43.1 0.7 add_multiply_fusion.9
  43.8 0.7 broadcast_add_fusion
  44.5 0.5 fusion.111
  45.0 1.2 copy.43
  46.9 1.2 copy.44
  48.1 1.0 slice_bitcast_fusion.5
  49.1 0.7 max.25
  49.8 2.8 %collective-permute-start.3 = (f32[2]{0:T(128)S(1)}, f32[2]{0:T(128)S(1)}, u32[]{:S(2)}, u32[]{:S(2)}) collective-permute-start(f32[2]{0:T(128)S(1)} %max.25), channel_id=1, source_target_pairs={{0,6},{2,8},{4,10},{6,12},{8,14},{10,0},{12,2},{14,4},{1,7},{3,9},... | collective-permute-start | bytes 32 | tf_op jit(solution)/shard_map/ppermute | solution.py:118
  52.6 2.6 %collective-permute-done.3 = f32[2]{0:T(128)S(1)} collective-permute-done((f32[2]{0:T(128)S(1)}, f32[2]{0:T(128)S(1)}, u32[]{:S(2)}, u32[]{:S(2)}) %collective-permute-start.3) | collective-permute-done | bytes 40 | tf_op jit(solution)/shard_map/ppermute | solution.py:118
  55.2 2.8 %collective-permute-start.2 = (f32[2]{0:T(128)S(1)}, f32[2]{0:T(128)S(1)}, u32[]{:S(2)}, u32[]{:S(2)}) collective-permute-start(f32[2]{0:T(128)S(1)} %max.25), channel_id=1, source_target_pairs={{0,4},{2,6},{4,8},{6,10},{8,12},{10,14},{12,0},{14,2},{1,5},{3,7},... | collective-permute-start | bytes 32 | tf_op jit(solution)/shard_map/ppermute | solution.py:118
  57.9 3.6 %collective-permute-done.2 = f32[2]{0:T(128)S(1)} collective-permute-done((f32[2]{0:T(128)S(1)}, f32[2]{0:T(128)S(1)}, u32[]{:S(2)}, u32[]{:S(2)}) %collective-permute-start.2) | collective-permute-done | bytes 40 | tf_op jit(solution)/shard_map/ppermute | solution.py:118
  61.5 2.6 %collective-permute-start.1 = (f32[2]{0:T(128)S(1)}, f32[2]{0:T(128)S(1)}, u32[]{:S(2)}, u32[]{:S(2)}) collective-permute-start(f32[2]{0:T(128)S(1)} %max.25), channel_id=1, source_target_pairs={{0,2},{2,4},{4,6},{6,8},{8,10},{10,12},{12,14},{14,0},{1,3},{3,5},... | collective-permute-start | bytes 32 | tf_op jit(solution)/shard_map/ppermute | solution.py:118
  64.0 3.7 %collective-permute-done.1 = f32[2]{0:T(128)S(1)} collective-permute-done((f32[2]{0:T(128)S(1)}, f32[2]{0:T(128)S(1)}, u32[]{:S(2)}, u32[]{:S(2)}) %collective-permute-start.1) | collective-permute-done | bytes 40 | tf_op jit(solution)/shard_map/ppermute | solution.py:118
  67.8 4.5 %collective-permute-done.4 = f32[2]{0:T(128)S(1)} collective-permute-done((f32[2]{0:T(128)S(1)}, f32[2]{0:T(128)S(1)}, u32[]{:S(2)}, u32[]{:S(2)}) %collective-permute-start.4) | collective-permute-done | bytes 40 | tf_op jit(solution)/shard_map/ppermute | solution.py:118
  72.2 0.7 fusion.123
  74.4 1.4 slice_select_fusion.3
  76.0 0.6 copy-done.6
  76.8 1.2 slice_select_fusion.2
  78.0 1.5 pad_maximum_fusion.29
  79.8 0.7 copy-done.2
  80.6 1.2 add_select_fusion.5
  81.9 0.5 fusion.7
  82.7 7.5 %fusion.73 = f32[3,6,64,128]{3,2,1,0:T(8,128)S(1)} fusion(f32[6,6,64,128]{3,2,1,0:T(8,128)S(1)} %get-tuple-element.16, f32[6,6,64,128]{3,2,1,0:T(8,128)S(1)} %add_multiply_fusion.2, f32[3,11,64,128]{3,2,1,0:T(8,128)S(1)} %fusion.52, f32[8,6,64,128]{3,2,1,0:T(8,128)S(1)} %get-tuple-element.45, f32[3]{0:T(128)S(1)} %copy-done.20, ...), kind=kLoop, calls=%fused_computation.170 | loop fusion | flops 40108032 | bytes 9474684 | tf_op jit(solution)/shard_map/add | solution.py:299
  90.2 7.5 %fusion.59 = f32[3,6,64,128]{3,2,1,0:T(8,128)S(1)} fusion(f32[6,6,64,128]{3,2,1,0:T(8,128)S(1)} %get-tuple-element.16, f32[6,6,64,128]{3,2,1,0:T(8,128)S(1)} %add_multiply_fusion.2, f32[3,11,64,128]{3,2,1,0:T(8,128)S(1)} %fusion.53, f32[8,6,64,128]{3,2,1,0:T(8,128)S(1)} %get-tuple-element.44, f32[]{:T(128)} %bitcast.3, f32[]{:T(128)} %bitcast.2, ...), kind=kLoop, calls=%fused_computation.156 | loop fusion | flops 40108032 | bytes 9474684 | tf_op jit(solution)/shard_map/add | solution.py:299
  97.7 0.4 fusion.15
  98.2 0.4 fusion.116
  99.1 13.0 %multiply_add_fusion.1 = (f32[6,6,64,128]{3,2,1,0:T(8,128)S(1)}, f32[6,6,64,128]{3,2,1,0:T(8,128)S(1)}, f32[6,6,64,128]{3,2,1,0:T(8,128)S(1)}) fusion(f32[6,6,64,1]{3,2,1,0:T(8,128)S(1)} %get-tuple-element.43, f32[6,6,64,127]{3,2,1,0:T(8,128)S(1)} %fusion.15, f32[6,6,64,1]{3,2,1,0:T(8,128)S(1)} %get-tuple-element.42, f32[]{:T(128)S(6)} %add.2510, ...), kind=kLoop, calls=%fused_computation.118 | loop fusion | flops 81100800 | bytes 11805708 | tf_op jit(solution)/shard_map/add | solution.py:160
  112.4 2.2 %collective-permute-start.9 = (f32[3,6,64,128]{3,2,1,0:T(8,128)S(1)}, f32[3,6,64,128]{3,2,1,0:T(8,128)S(1)}, u32[]{:S(2)}, u32[]{:S(2)}) collective-permute-start(f32[3,6,64,128]{3,2,1,0:T(8,128)S(1)} %fusion.73), channel_id=1, source_target_pairs={{0,2},{2,4},{4,6},{6,8},{8,10},{10,12},{12,14},{1,3},{3,5},{5,7},{... | collective-permute-start | bytes 1769480 | tf_op jit(solution)/shard_map/ppermute | solution.py:85
  114.6 1.5 collective-permute-start.11
  116.5 23.9 %collective-permute-done.9 = f32[3,6,64,128]{3,2,1,0:T(8,128)S(1)} collective-permute-done((f32[3,6,64,128]{3,2,1,0:T(8,128)S(1)}, f32[3,6,64,128]{3,2,1,0:T(8,128)S(1)}, u32[]{:S(2)}, u32[]{:S(2)}) %collective-permute-start.9) | collective-permute-done | bytes 589856 | tf_op jit(solution)/shard_map/ppermute | solution.py:85
  140.8 0.4 pad_maximum_fusion.3
  141.8 7.6 %fusion.81 = f32[3,6,64,128]{3,2,1,0:T(8,128)S(1)} fusion(f32[3,6,64,128]{3,2,1,0:T(8,128)S(1)} %fusion.73, f32[6,6,64,128]{3,2,1,0:T(8,128)S(1)} %get-tuple-element.18, f32[6,6,64,128]{3,2,1,0:T(8,128)S(1)} %add_multiply_fusion.1, f32[3,11,64,128]{3,2,1,0:T(8,128)S(1)} %fusion.50, f32[8,6,64,128]{3,2,1,0:T(8,128)S(1)} %fusion.8, f32[3]{0:T(128)S(1)} %copy-done.20, ...), kind=kLoop, calls=%fused_computation.178 | loop fusion | flops 40550400 | bytes 10064508 | tf_op jit(solution)/shard_map/add | solution.py:303
  149.4 7.6 %fusion.67 = f32[3,6,64,128]{3,2,1,0:T(8,128)S(1)} fusion(f32[3,6,64,128]{3,2,1,0:T(8,128)S(1)} %fusion.59, f32[6,6,64,128]{3,2,1,0:T(8,128)S(1)} %get-tuple-element.18, f32[6,6,64,128]{3,2,1,0:T(8,128)S(1)} %add_multiply_fusion.1, f32[3,11,64,128]{3,2,1,0:T(8,128)S(1)} %fusion.51, f32[8,6,64,128]{3,2,1,0:T(8,128)S(1)} %fusion.9, f32[]{:T(128)} %bitcast.3, ...), kind=kLoop, calls=%fused_computation.164 | loop fusion | flops 40550400 | bytes 10064508 | tf_op jit(solution)/shard_map/add | solution.py:303
  157.0 0.4 fusion.18
  157.5 0.4 fusion.115
  158.2 13.0 %multiply_add_fusion = (f32[6,6,64,128]{3,2,1,0:T(8,128)S(1)}, f32[6,6,64,128]{3,2,1,0:T(8,128)S(1)}, f32[6,6,64,128]{3,2,1,0:T(8,128)S(1)}) fusion(f32[6,6,64,1]{3,2,1,0:T(8,128)S(1)} %get-tuple-element.37, f32[6,6,64,127]{3,2,1,0:T(8,128)S(1)} %fusion.18, f32[6,6,64,1]{3,2,1,0:T(8,128)S(1)} %get-tuple-element.36, f32[]{:T(128)S(6)} %add.2510, f32[]{:T(128)} %bitcast.5, ...), kind=kLoop, calls=%fused_computation.108 | loop fusion | flops 81100800 | bytes 11805708 | tf_op jit(solution)/shard_map/add | solution.py:160
  171.5 1.3 collective-permute-start.13
  172.8 5.1 %collective-permute-start.12 = (f32[3,6,64,128]{3,2,1,0:T(8,128)S(1)}, f32[3,6,64,128]{3,2,1,0:T(8,128)S(1)}, u32[]{:S(2)}, u32[]{:S(2)}) collective-permute-start(f32[3,6,64,128]{3,2,1,0:T(8,128)S(1)} %fusion.81), channel_id=1, source_target_pairs={{0,2},{2,4},{4,6},{6,8},{8,10},{10,12},{12,14},{1,3},{3,5},{5,7},{... | collective-permute-start | bytes 1769480 | tf_op jit(solution)/shard_map/ppermute | solution.py:85
  178.5 11.4 %collective-permute-done.13 = f32[3,6,64,128]{3,2,1,0:T(8,128)S(1)} collective-permute-done((f32[3,6,64,128]{3,2,1,0:T(8,128)S(1)}, f32[3,6,64,128]{3,2,1,0:T(8,128)S(1)}, u32[]{:S(2)}, u32[]{:S(2)}) %collective-permute-start.13) | collective-permute-done | bytes 589856 | tf_op jit(solution)/shard_map/ppermute | solution.py:90
  190.3 12.4 %collective-permute-done.12 = f32[3,6,64,128]{3,2,1,0:T(8,128)S(1)} collective-permute-done((f32[3,6,64,128]{3,2,1,0:T(8,128)S(1)}, f32[3,6,64,128]{3,2,1,0:T(8,128)S(1)}, u32[]{:S(2)}, u32[]{:S(2)}) %collective-permute-start.12) | collective-permute-done | bytes 589856 | tf_op jit(solution)/shard_map/ppermute | solution.py:85
  203.4 0.5 copy-done.11
  203.8 14.3 %fusion.22 = f32[6,6,64,128]{3,2,1,0:T(8,128)} fusion(f32[3,6,64,128]{3,2,1,0:T(8,128)S(1)} %fusion.81, f32[3,6,64,128]{3,2,1,0:T(8,128)S(1)} %fusion.67, f32[6,6,64,128]{3,2,1,0:T(8,128)S(1)} %get-tuple-element.20, f32[6,6,64,128]{3,2,1,0:T(8,128)S(1)} %add_multiply_fusion, f32[6,11,64,128]{3,2,1,0:T(8,128)S(1)} %fusion, f32[11,6,64,128]{3,2,1,0:T(8,128)S(1)} %fusion.1, ...), kind=kLoop, calls=%fused_computation.69 | loop fusion | flops 81395712 | bytes 20096208 | tf_op jit(solution)/shard_map/add | solution.py:308
  (105 shorter events, 6.0 us)
Async XLA Ops:
  0.0 8.6 %copy-start = (f32[6,6,64,128]{3,2,1,0:T(8,128)S(1)}, f32[6,6,64,128]{3,2,1,0:T(8,128)}, u32[]{:S(2)}) copy-start(f32[6,6,64,128]{3,2,1,0:T(8,128)} %param.6) | copy-start | bytes 3538948
  2.5 14.3 %copy-start.18 = (f32[4]{0:T(128)S(1)}, f32[4]{0:T(128)}, u32[]{:S(2)}) copy-start(f32[4]{0:T(128)} %param.8) | copy-start | bytes 52
  2.5 15.0 %copy-start.12 = (f32[2,6,6]{2,0,1:T(2,128)S(1)}, f32[2,6,6]{2,0,1:T(2,128)}, u32[]{:S(2)}) copy-start(f32[2,6,6]{2,0,1:T(2,128)} %param.7) | copy-start | bytes 868
  2.5 73.5 %collective-permute-start.7 = (f32[6,3,64,128]{3,2,1,0:T(8,128)}, f32[6,3,64,128]{3,2,1,0:T(8,128)}, u32[]{:S(2)}, u32[]{:S(2)}) collective-permute-start(f32[6,3,64,128]{3,2,1,0:T(8,128)} %get-tuple-element.14), channel_id=1, source_target_pairs={{1,0},{3,2},{5,4},{7,6},{9,8},{11,10},{13,12},{15,14},{17,16},{19,... | collective-permute-start | bytes 1769480 | tf_op jit(solution)/shard_map/ppermute | solution.py:90
  3.9 70.5 %collective-permute-start.6 = (f32[6,3,64,128]{3,2,1,0:T(8,128)}, f32[6,3,64,128]{3,2,1,0:T(8,128)}, u32[]{:S(2)}, u32[]{:S(2)}) collective-permute-start(f32[6,3,64,128]{3,2,1,0:T(8,128)} %get-tuple-element.13), channel_id=1, source_target_pairs={{0,1},{2,3},{4,5},{6,7},{8,9},{10,11},{12,13},{14,15},{16,17},{18,... | collective-permute-start | bytes 1769480 | tf_op jit(solution)/shard_map/ppermute | solution.py:85
  9.8 66.0 %collective-permute-start.5 = (f32[3,6,64,128]{3,2,1,0:T(8,128)}, f32[3,6,64,128]{3,2,1,0:T(8,128)}, u32[]{:S(2)}, u32[]{:S(2)}) collective-permute-start(f32[3,6,64,128]{3,2,1,0:T(8,128)} %get-tuple-element.59), channel_id=1, source_target_pairs={{0,2},{2,4},{4,6},{6,8},{8,10},{10,12},{12,14},{1,3},{3,5},{5,7},{... | collective-permute-start | bytes 1769480 | tf_op jit(solution)/shard_map/ppermute | solution.py:85
  15.5 64.3 %collective-permute-start.8 = (f32[3,6,64,128]{3,2,1,0:T(8,128)}, f32[3,6,64,128]{3,2,1,0:T(8,128)}, u32[]{:S(2)}, u32[]{:S(2)}) collective-permute-start(f32[3,6,64,128]{3,2,1,0:T(8,128)} %get-tuple-element.58), channel_id=1, source_target_pairs={{2,0},{4,2},{6,4},{8,6},{10,8},{12,10},{14,12},{3,1},{5,3},{7,5},{... | collective-permute-start | bytes 1769480 | tf_op jit(solution)/shard_map/ppermute | solution.py:90
  21.7 27.4 %collective-permute-start = (f32[2]{0:T(128)}, f32[2]{0:T(128)}, u32[]{:S(2)}, u32[]{:S(2)}) collective-permute-start(f32[2]{0:T(128)} %maximum_reduce_fusion), channel_id=1, source_target_pairs={{0,1},{1,0},{2,3},{3,2},{4,5},{5,4},{6,7},{7,6},{8,9},{9,8},{10,11... | collective-permute-start | bytes 32 | tf_op jit(solution)/shard_map/ppermute | solution.py:118
  27.2 0.8 copy-start.24
  27.2 1.4 copy-start.23
  42.2 1.6 copy-start.22
  49.8 5.4 %collective-permute-start.3 = (f32[2]{0:T(128)S(1)}, f32[2]{0:T(128)S(1)}, u32[]{:S(2)}, u32[]{:S(2)}) collective-permute-start(f32[2]{0:T(128)S(1)} %max.25), channel_id=1, source_target_pairs={{0,6},{2,8},{4,10},{6,12},{8,14},{10,0},{12,2},{14,4},{1,7},{3,9},... | collective-permute-start | bytes 32 | tf_op jit(solution)/shard_map/ppermute | solution.py:118
  55.2 6.3 %collective-permute-start.2 = (f32[2]{0:T(128)S(1)}, f32[2]{0:T(128)S(1)}, u32[]{:S(2)}, u32[]{:S(2)}) collective-permute-start(f32[2]{0:T(128)S(1)} %max.25), channel_id=1, source_target_pairs={{0,4},{2,6},{4,8},{6,10},{8,12},{10,14},{12,0},{14,2},{1,5},{3,7},... | collective-permute-start | bytes 32 | tf_op jit(solution)/shard_map/ppermute | solution.py:118
  61.5 6.3 %collective-permute-start.1 = (f32[2]{0:T(128)S(1)}, f32[2]{0:T(128)S(1)}, u32[]{:S(2)}, u32[]{:S(2)}) collective-permute-start(f32[2]{0:T(128)S(1)} %max.25), channel_id=1, source_target_pairs={{0,2},{2,4},{4,6},{6,8},{8,10},{10,12},{12,14},{14,0},{1,3},{3,5},... | collective-permute-start | bytes 32 | tf_op jit(solution)/shard_map/ppermute | solution.py:118
  67.8 4.5 %collective-permute-start.4 = (f32[2]{0:T(128)S(1)}, f32[2]{0:T(128)S(1)}, u32[]{:S(2)}, u32[]{:S(2)}) collective-permute-start(f32[2]{0:T(128)S(1)} %maximum_maximum_fusion), channel_id=1, source_target_pairs={{0,8},{2,10},{4,12},{6,14},{8,0},{10,2},{12,4},{14,6},{1,9},{3,11}... | collective-permute-start | bytes 32 | tf_op jit(solution)/shard_map/ppermute | solution.py:118
  74.3 1.5 copy-start.4
  74.3 1.5 copy-start.5
  75.7 0.9 copy-start.6
  75.8 0.9 copy-start.7
  75.8 1.0 copy-start.8
  75.8 1.0 copy-start.9
  75.8 1.0 copy-start.13
  79.6 0.9 copy-start.2
  79.6 1.0 copy-start.3
  81.9 0.8 copy-start.1
  81.9 0.8 copy-start.10
  81.9 0.7 copy-start.14
  81.9 0.7 copy-start.17
  81.9 0.7 copy-start.20
  82.6 7.6 %copy-start.15 = (f32[1,3,6]{2,1,0:T(4,128)S(1)}, f32[1,3,6]{2,1,0:T(4,128)}, u32[]{:S(2)}) copy-start(f32[1,3,6]{2,1,0:T(4,128)} %copy.44) | copy-start | bytes 220
  82.6 7.6 %copy-start.19 = (f32[3]{0:T(128)S(1)}, f32[3]{0:T(128)}, u32[]{:S(2)}) copy-start(f32[3]{0:T(128)} %get-tuple-element.106) | copy-start | bytes 40
  99.0 17.2 %collective-permute-start.10 = (f32[6,3,64,128]{3,2,1,0:T(8,128)S(1)}, f32[6,3,64,128]{3,2,1,0:T(8,128)S(1)}, u32[]{:S(2)}, u32[]{:S(2)}) collective-permute-start(f32[6,3,64,128]{3,2,1,0:T(8,128)S(1)} %fusion.82), channel_id=1, source_target_pairs={{0,1},{1,0},{2,3},{3,2},{4,5},{5,4},{6,7},{7,6},{8,9},{9,8},{10,11... | collective-permute-start | bytes 1769480 | tf_op jit(solution)/shard_map/ppermute | solution.py:172
  112.4 28.1 %collective-permute-start.9 = (f32[3,6,64,128]{3,2,1,0:T(8,128)S(1)}, f32[3,6,64,128]{3,2,1,0:T(8,128)S(1)}, u32[]{:S(2)}, u32[]{:S(2)}) collective-permute-start(f32[3,6,64,128]{3,2,1,0:T(8,128)S(1)} %fusion.73), channel_id=1, source_target_pairs={{0,2},{2,4},{4,6},{6,8},{8,10},{10,12},{12,14},{1,3},{3,5},{5,7},{... | collective-permute-start | bytes 1769480 | tf_op jit(solution)/shard_map/ppermute | solution.py:85
  114.6 26.1 %collective-permute-start.11 = (f32[3,6,64,128]{3,2,1,0:T(8,128)S(1)}, f32[3,6,64,128]{3,2,1,0:T(8,128)S(1)}, u32[]{:S(2)}, u32[]{:S(2)}) collective-permute-start(f32[3,6,64,128]{3,2,1,0:T(8,128)S(1)} %fusion.59), channel_id=1, source_target_pairs={{2,0},{4,2},{6,4},{8,6},{10,8},{12,10},{14,12},{3,1},{5,3},{7,5},{... | collective-permute-start | bytes 1769480 | tf_op jit(solution)/shard_map/ppermute | solution.py:90
  171.5 6.6 %collective-permute-start.14 = (f32[6,3,64,128]{3,2,1,0:T(8,128)S(1)}, f32[6,3,64,128]{3,2,1,0:T(8,128)S(1)}, u32[]{:S(2)}, u32[]{:S(2)}) collective-permute-start(f32[6,3,64,128]{3,2,1,0:T(8,128)S(1)} %fusion.83), channel_id=1, source_target_pairs={{0,1},{1,0},{2,3},{3,2},{4,5},{5,4},{6,7},{7,6},{8,9},{9,8},{10,11... | collective-permute-start | bytes 1769480 | tf_op jit(solution)/shard_map/ppermute | solution.py:172
  171.5 18.4 %collective-permute-start.13 = (f32[3,6,64,128]{3,2,1,0:T(8,128)S(1)}, f32[3,6,64,128]{3,2,1,0:T(8,128)S(1)}, u32[]{:S(2)}, u32[]{:S(2)}) collective-permute-start(f32[3,6,64,128]{3,2,1,0:T(8,128)S(1)} %fusion.67), channel_id=1, source_target_pairs={{2,0},{4,2},{6,4},{8,6},{10,8},{12,10},{14,12},{3,1},{5,3},{7,5},{... | collective-permute-start | bytes 1769480 | tf_op jit(solution)/shard_map/ppermute | solution.py:90
  172.8 29.9 %collective-permute-start.12 = (f32[3,6,64,128]{3,2,1,0:T(8,128)S(1)}, f32[3,6,64,128]{3,2,1,0:T(8,128)S(1)}, u32[]{:S(2)}, u32[]{:S(2)}) collective-permute-start(f32[3,6,64,128]{3,2,1,0:T(8,128)S(1)} %fusion.81), channel_id=1, source_target_pairs={{0,2},{2,4},{4,6},{6,8},{8,10},{10,12},{12,14},{1,3},{3,5},{5,7},{... | collective-permute-start | bytes 1769480 | tf_op jit(solution)/shard_map/ppermute | solution.py:85
  203.1 0.7 copy-start.11
  203.1 0.7 copy-start.16
  203.1 0.7 copy-start.21

commit v15 on v12

--- a/solution.py
+++ b/solution.py
@@ -279,10 +279,10 @@
 
         def send(side):
             if side == 0:
-                piece = lax.optimization_barrier(results[side][:3])
+                piece = results[side][:3]
                 sent[side] = send_high(piece, "gx")
             else:
-                piece = lax.optimization_barrier(results[side][results[side].shape[0] - 3 :])
+                piece = results[side][results[side].shape[0] - 3 :]
                 sent[side] = send_low(piece, "gx")
 
         half(order[0])
@@ -294,9 +294,8 @@
         next_pieces = local_whole(merged)
         return merged, (sent[1], sent[0]), next_y, next_pieces
 
-    fresh = jnp.where(values == values, values, 0.0)
     first, x_halos, y_halos, locals_now = stage(
-        fresh, x_halos, y_halos, locals_now, (0, 1),
+        values, x_halos, y_halos, locals_now, (0, 1),
         lambda side, rate: cut(values, side) + step_time * rate, False,
     )
     second, x_halos, y_halos, locals_now = stage(

time: 207 us -> 174 us (0.84); the launches traced: 207 us -> 170 us
  waiting for transfers between devices: 54.4 us -> 19.2 us
    ppermute x3, waiting for transfers between devices: 36.3 us -> 10.6 us  [send_low(): lax.ppermute(piece, axis, [(i, (i + 1) % count) for i in range(count - 1)])]
    ppermute x3, waiting for transfers between devices: 11.3 us -> 0.01 us  [send_high(): lax.ppermute(piece, axis, [((i + 1) % count, i) for i in range(count - 1)])]
    unnamed x63 -> x59, local copies, waits for them, and re-layouts: 4.64 us -> 4.6 us
  transfers between devices with their start and end apart: 14 -> 14, of which waited for: 6 -> 6; matrix products, arithmetic and copies ran while one was open for 25% -> 38% of each run, Pallas kernels for 0% -> 0%
where the time goes in v15:
time: 174 us; the launch traced here: 170 us
  other arithmetic  107 us (61%)
  starting transfers between devices  27.5 us (16%)
  waiting for transfers between devices  19.2 us (11%)
  local copies, waits for them, and re-layouts  10.9 us (6%)
  between operations  5.97 us (3%)
    add x3, other arithmetic, local_part(): partial + 0.5 * (alpha_three * (fore_three - back_three) + alpha_four * (...  39.3 us
    add x2, other arithmetic, on_device(): 0.75 * cut(values, side) + 0.25 * (cut(first, side) + step_time * rate)  15 us
    add x2, other arithmetic, on_device(): cut(values, side) + step_time * rate  14.8 us
    add x1, other arithmetic, on_device(): cut(values, side) * (1.0 / 3.0)  14.1 us
    ppermute x3, starting transfers between devices, send_low(): lax.ppermute(piece, axis, [(i, (i + 1) % count) for i in range(count - 1)])  13.3 us
    ppermute x3, waiting for transfers between devices, send_low(): lax.ppermute(piece, axis, [(i, (i + 1) % count) for i in range(count - 1)])  10.6 us
    ppermute x5, starting transfers between devices, spread_max(): lax.ppermute(local, axis, [(i, (i + k * span) % count) for i in range(cou...  9.53 us
    ppermute x5, waiting for transfers between devices, spread_max(): lax.ppermute(local, axis, [(i, (i + k * span) % count) for i in range(cou...  6.8 us
  transfers between devices with their start and end apart: 14, of which 6 were waited for; matrix products, arithmetic and copies ran while one was open for 38% of the time, Pallas kernels for 0%

profile of v15, /device:TPU:0, one launch (start us, length us, event | category | flops | bytes accessed | tf_op | source)
XLA Modules:
  0.0 170.4 jit_solution(5392983770786062325)
XLA Ops:
  0.0 2.0 %constant_dynamic-slice_fusion = f32[6,3,64,128]{3,2,1,0:T(8,128)} fusion(f32[6,6,64,128]{3,2,1,0:T(8,128)} %param.6, s32[]{:T(128)S(6)} %select_n.94), kind=kLoop, calls=%fused_computation.266 | loop fusion | bytes 1179652 | tf_op jit(solution)/shard_map/dynamic_slice | solution.py:170
  2.0 0.5 collective-permute-start.6
  2.5 1.2 fusion.117
  3.7 5.2 %collective-permute-start.5 = (f32[3,6,64,128]{3,2,1,0:T(8,128)}, f32[3,6,64,128]{3,2,1,0:T(8,128)}, u32[]{:S(2)}, u32[]{:S(2)}) collective-permute-start(f32[3,6,64,128]{3,2,1,0:T(8,128)} %get-tuple-element.55), channel_id=1, source_target_pairs={{0,2},{2,4},{4,6},{6,8},{8,10},{10,12},{12,14},{1,3},{3,5},{5,7},{... | collective-permute-start | bytes 1769480 | tf_op jit(solution)/shard_map/ppermute | solution.py:85
  8.9 1.3 collective-permute-start.7
  10.2 0.7 fusion.123
  10.9 0.6 abs_multiply_fusion
  11.6 0.6 abs_multiply_fusion.1
  13.5 1.2 copy_bitcast_fusion
  14.7 0.7 maximum_reduce_fusion
  15.6 0.4 subtract_multiply_fusion
  17.8 0.9 slice_bitcast_fusion.13
  18.8 0.5 add_convert_fusion
  19.3 0.6 fusion.120
  19.9 0.5 fusion.110
  20.4 0.4 fusion.119
  21.2 0.7 slice_multiply_fusion.1
  21.9 0.6 broadcast_multiply_fusion
  22.5 0.6 broadcast_multiply_fusion.1
  23.2 13.1 %multiply_add_fusion.2 = (f32[6,6,64,128]{3,2,1,0:T(8,128)S(1)}, f32[6,6,64,128]{3,2,1,0:T(8,128)S(1)}, f32[6,6,64,128]{3,2,1,0:T(8,128)S(1)}) fusion(f32[6,6,64,1]{3,2,1,0:T(8,128)S(1)} %get-tuple-element.59, f32[6,6,64,127]{3,2,1,0:T(8,128)S(1)} %subtract_multiply_fusion, f32[6,6,64,1]{3,2,1,0:T(8,128)S(1)} %get-tuple-element.58, f32[]{:T(128)S(6)} %add.2511, ...), kind=kLoop, calls=%fused_computation.128 | loop fusion | flops 81100800 | bytes 11805708 | tf_op jit(solution)/shard_map/add | solution.py:160
  36.5 0.4 copy-done.19
  36.9 0.7 add_multiply_fusion.7
  37.6 0.7 add_multiply_fusion.9
  38.3 0.7 broadcast_add_fusion
  39.0 0.5 fusion.111
  39.5 1.3 copy.43
  41.5 1.3 copy.44
  42.7 0.9 slice_bitcast_fusion.5
  43.6 0.7 max.25
  44.3 2.6 %collective-permute-start.3 = (f32[2]{0:T(128)S(1)}, f32[2]{0:T(128)S(1)}, u32[]{:S(2)}, u32[]{:S(2)}) collective-permute-start(f32[2]{0:T(128)S(1)} %max.25), channel_id=1, source_target_pairs={{0,6},{2,8},{4,10},{6,12},{8,14},{10,0},{12,2},{14,4},{1,7},{3,9},... | collective-permute-start | bytes 32 | tf_op jit(solution)/shard_map/ppermute | solution.py:118
  46.9 1.6 collective-permute-start.2
  48.5 1.2 collective-permute-done.3
  49.7 3.3 %collective-permute-start.1 = (f32[2]{0:T(128)S(1)}, f32[2]{0:T(128)S(1)}, u32[]{:S(2)}, u32[]{:S(2)}) collective-permute-start(f32[2]{0:T(128)S(1)} %max.25), channel_id=1, source_target_pairs={{0,2},{2,4},{4,6},{6,8},{8,10},{10,12},{12,14},{14,0},{1,3},{3,5},... | collective-permute-start | bytes 32 | tf_op jit(solution)/shard_map/ppermute | solution.py:118
  53.0 2.9 %collective-permute-done.1 = f32[2]{0:T(128)S(1)} collective-permute-done((f32[2]{0:T(128)S(1)}, f32[2]{0:T(128)S(1)}, u32[]{:S(2)}, u32[]{:S(2)}) %collective-permute-start.1) | collective-permute-done | bytes 40 | tf_op jit(solution)/shard_map/ppermute | solution.py:118
  56.0 1.8 %collective-permute-start.4 = (f32[2]{0:T(128)S(1)}, f32[2]{0:T(128)S(1)}, u32[]{:S(2)}, u32[]{:S(2)}) collective-permute-start(f32[2]{0:T(128)S(1)} %maximum_maximum_fusion), channel_id=1, source_target_pairs={{0,8},{2,10},{4,12},{6,14},{8,0},{10,2},{12,4},{14,6},{1,9},{3,11}... | collective-permute-start | bytes 32 | tf_op jit(solution)/shard_map/ppermute | solution.py:118
  57.7 2.7 %collective-permute-done.4 = f32[2]{0:T(128)S(1)} collective-permute-done((f32[2]{0:T(128)S(1)}, f32[2]{0:T(128)S(1)}, u32[]{:S(2)}, u32[]{:S(2)}) %collective-permute-start.4) | collective-permute-done | bytes 40 | tf_op jit(solution)/shard_map/ppermute | solution.py:118
  60.4 0.6 fusion.122
  62.4 1.3 add_select_fusion.7
  63.8 1.3 add_select_fusion.15
  65.2 1.5 pad_maximum_fusion.29
  66.9 0.8 copy-done.2
  67.8 1.2 add_select_fusion.5
  69.1 0.5 fusion.7
  69.8 7.4 %fusion.73 = f32[3,6,64,128]{3,2,1,0:T(8,128)S(1)} fusion(f32[6,6,64,128]{3,2,1,0:T(8,128)S(1)} %get-tuple-element.12, f32[6,6,64,128]{3,2,1,0:T(8,128)S(1)} %add_multiply_fusion.2, f32[3,11,64,128]{3,2,1,0:T(8,128)S(1)} %fusion.52, f32[8,6,64,128]{3,2,1,0:T(8,128)S(1)} %get-tuple-element.41, f32[3]{0:T(128)S(1)} %copy-done.23, ...), kind=kLoop, calls=%fused_computation.170 | loop fusion | flops 40108032 | bytes 9474684 | tf_op jit(solution)/shard_map/add | solution.py:299
  77.2 7.4 %fusion.59 = f32[3,6,64,128]{3,2,1,0:T(8,128)S(1)} fusion(f32[6,6,64,128]{3,2,1,0:T(8,128)S(1)} %get-tuple-element.12, f32[6,6,64,128]{3,2,1,0:T(8,128)S(1)} %add_multiply_fusion.2, f32[3,11,64,128]{3,2,1,0:T(8,128)S(1)} %fusion.53, f32[8,6,64,128]{3,2,1,0:T(8,128)S(1)} %get-tuple-element.40, f32[]{:T(128)} %bitcast.3, f32[]{:T(128)} %bitcast.2, ...), kind=kLoop, calls=%fused_computation.156 | loop fusion | flops 40108032 | bytes 9474684 | tf_op jit(solution)/shard_map/add | solution.py:299
  84.7 0.4 fusion.15
  85.2 2.7 %collective-permute-start.8 = (f32[3,6,64,128]{3,2,1,0:T(8,128)S(1)}, f32[3,6,64,128]{3,2,1,0:T(8,128)S(1)}, u32[]{:S(2)}, u32[]{:S(2)}) collective-permute-start(f32[3,6,64,128]{3,2,1,0:T(8,128)S(1)} %fusion.73), channel_id=1, source_target_pairs={{0,2},{2,4},{4,6},{6,8},{8,10},{10,12},{12,14},{1,3},{3,5},{5,7},{... | collective-permute-start | bytes 1769480 | tf_op jit(solution)/shard_map/ppermute | solution.py:85
  88.0 1.5 collective-permute-start.10
  89.4 0.4 fusion.116
  90.3 13.1 %multiply_add_fusion.1 = (f32[6,6,64,128]{3,2,1,0:T(8,128)S(1)}, f32[6,6,64,128]{3,2,1,0:T(8,128)S(1)}, f32[6,6,64,128]{3,2,1,0:T(8,128)S(1)}) fusion(f32[6,6,64,1]{3,2,1,0:T(8,128)S(1)} %get-tuple-element.39, f32[6,6,64,127]{3,2,1,0:T(8,128)S(1)} %fusion.15, f32[6,6,64,1]{3,2,1,0:T(8,128)S(1)} %get-tuple-element.38, f32[]{:T(128)S(6)} %add.2511, ...), kind=kLoop, calls=%fused_computation.118 | loop fusion | flops 81100800 | bytes 11805708 | tf_op jit(solution)/shard_map/add | solution.py:160
  104.0 6.3 %collective-permute-done.8 = f32[3,6,64,128]{3,2,1,0:T(8,128)S(1)} collective-permute-done((f32[3,6,64,128]{3,2,1,0:T(8,128)S(1)}, f32[3,6,64,128]{3,2,1,0:T(8,128)S(1)}, u32[]{:S(2)}, u32[]{:S(2)}) %collective-permute-start.8) | collective-permute-done | bytes 589856 | tf_op jit(solution)/shard_map/ppermute | solution.py:85
  110.8 0.5 pad_maximum_fusion.3
  111.8 7.5 %fusion.81 = f32[3,6,64,128]{3,2,1,0:T(8,128)S(1)} fusion(f32[3,6,64,128]{3,2,1,0:T(8,128)S(1)} %fusion.73, f32[6,6,64,128]{3,2,1,0:T(8,128)S(1)} %get-tuple-element.14, f32[6,6,64,128]{3,2,1,0:T(8,128)S(1)} %add_multiply_fusion.1, f32[3,11,64,128]{3,2,1,0:T(8,128)S(1)} %fusion.50, f32[8,6,64,128]{3,2,1,0:T(8,128)S(1)} %fusion.8, f32[3]{0:T(128)S(1)} %copy-done.23, ...), kind=kLoop, calls=%fused_computation.178 | loop fusion | flops 40550400 | bytes 10064508 | tf_op jit(solution)/shard_map/add | solution.py:303
  119.3 7.5 %fusion.67 = f32[3,6,64,128]{3,2,1,0:T(8,128)S(1)} fusion(f32[3,6,64,128]{3,2,1,0:T(8,128)S(1)} %fusion.59, f32[6,6,64,128]{3,2,1,0:T(8,128)S(1)} %get-tuple-element.14, f32[6,6,64,128]{3,2,1,0:T(8,128)S(1)} %add_multiply_fusion.1, f32[3,11,64,128]{3,2,1,0:T(8,128)S(1)} %fusion.51, f32[8,6,64,128]{3,2,1,0:T(8,128)S(1)} %fusion.9, f32[]{:T(128)} %bitcast.3, ...), kind=kLoop, calls=%fused_computation.164 | loop fusion | flops 40550400 | bytes 10064508 | tf_op jit(solution)/shard_map/add | solution.py:303
  126.8 0.4 fusion.18
  127.3 1.3 collective-permute-start.12
  128.6 5.3 %collective-permute-start.11 = (f32[3,6,64,128]{3,2,1,0:T(8,128)S(1)}, f32[3,6,64,128]{3,2,1,0:T(8,128)S(1)}, u32[]{:S(2)}, u32[]{:S(2)}) collective-permute-start(f32[3,6,64,128]{3,2,1,0:T(8,128)S(1)} %fusion.81), channel_id=1, source_target_pairs={{0,2},{2,4},{4,6},{6,8},{8,10},{10,12},{12,14},{1,3},{3,5},{5,7},{... | collective-permute-start | bytes 1769480 | tf_op jit(solution)/shard_map/ppermute | solution.py:85
  133.8 0.4 fusion.115
  134.6 13.1 %multiply_add_fusion = (f32[6,6,64,128]{3,2,1,0:T(8,128)S(1)}, f32[6,6,64,128]{3,2,1,0:T(8,128)S(1)}, f32[6,6,64,128]{3,2,1,0:T(8,128)S(1)}) fusion(f32[6,6,64,1]{3,2,1,0:T(8,128)S(1)} %get-tuple-element.33, f32[6,6,64,127]{3,2,1,0:T(8,128)S(1)} %fusion.18, f32[6,6,64,1]{3,2,1,0:T(8,128)S(1)} %get-tuple-element.32, f32[]{:T(128)S(6)} %add.2511, f32[]{:T(128)} %bitcast.5, ...), kind=kLoop, calls=%fused_computation.108 | loop fusion | flops 81100800 | bytes 11805708 | tf_op jit(solution)/shard_map/add | solution.py:160
  148.1 1.9 %collective-permute-done.13 = f32[6,3,64,128]{3,2,1,0:T(8,128)S(1)} collective-permute-done((f32[6,3,64,128]{3,2,1,0:T(8,128)S(1)}, f32[6,3,64,128]{3,2,1,0:T(8,128)S(1)}, u32[]{:S(2)}, u32[]{:S(2)}) %collective-permute-start.13) | collective-permute-done | bytes 589856 | tf_op jit(solution)/shard_map/ppermute | solution.py:172
  150.2 0.3 pad_maximum_fusion.2
  150.9 4.2 %collective-permute-done.11 = f32[3,6,64,128]{3,2,1,0:T(8,128)S(1)} collective-permute-done((f32[3,6,64,128]{3,2,1,0:T(8,128)S(1)}, f32[3,6,64,128]{3,2,1,0:T(8,128)S(1)}, u32[]{:S(2)}, u32[]{:S(2)}) %collective-permute-start.11) | collective-permute-done | bytes 589856 | tf_op jit(solution)/shard_map/ppermute | solution.py:85
  155.8 0.5 copy-done.13
  156.3 14.1 %fusion.22 = f32[6,6,64,128]{3,2,1,0:T(8,128)} fusion(f32[3,6,64,128]{3,2,1,0:T(8,128)S(1)} %fusion.81, f32[3,6,64,128]{3,2,1,0:T(8,128)S(1)} %fusion.67, f32[6,6,64,128]{3,2,1,0:T(8,128)S(1)} %get-tuple-element.16, f32[6,6,64,128]{3,2,1,0:T(8,128)S(1)} %add_multiply_fusion, f32[6,11,64,128]{3,2,1,0:T(8,128)S(1)} %fusion, f32[11,6,64,128]{3,2,1,0:T(8,128)S(1)} %fusion.1, ...), kind=kLoop, calls=%fused_computation.69 | loop fusion | flops 81395712 | bytes 20096208 | tf_op jit(solution)/shard_map/add | solution.py:308
  (108 shorter events, 5.6 us)
Async XLA Ops:
  0.0 2.5 %copy-start = (f32[6,6,64,128]{3,2,1,0:T(8,128)S(1)}, f32[6,6,64,128]{3,2,1,0:T(8,128)}, u32[]{:S(2)}) copy-start(f32[6,6,64,128]{3,2,1,0:T(8,128)} %param.6) | copy-start | bytes 3538948
  2.0 8.2 %copy-start.21 = (f32[4]{0:T(128)S(1)}, f32[4]{0:T(128)}, u32[]{:S(2)}) copy-start(f32[4]{0:T(128)} %param.8) | copy-start | bytes 52
  2.0 8.9 %copy-start.14 = (f32[2,6,6]{2,0,1:T(2,128)S(1)}, f32[2,6,6]{2,0,1:T(2,128)}, u32[]{:S(2)}) copy-start(f32[2,6,6]{2,0,1:T(2,128)} %param.7) | copy-start | bytes 868
  2.0 61.7 %collective-permute-start.6 = (f32[6,3,64,128]{3,2,1,0:T(8,128)}, f32[6,3,64,128]{3,2,1,0:T(8,128)}, u32[]{:S(2)}, u32[]{:S(2)}) collective-permute-start(f32[6,3,64,128]{3,2,1,0:T(8,128)} %constant_dynamic-slice_fusion), channel_id=1, source_target_pairs={{0,1},{1,0},{2,3},{3,2},{4,5},{5,4},{6,7},{7,6},{8,9},{9,8},{10,11... | collective-permute-start | bytes 1769480 | tf_op jit(solution)/shard_map/ppermute | solution.py:172
  3.7 58.7 %collective-permute-start.5 = (f32[3,6,64,128]{3,2,1,0:T(8,128)}, f32[3,6,64,128]{3,2,1,0:T(8,128)}, u32[]{:S(2)}, u32[]{:S(2)}) collective-permute-start(f32[3,6,64,128]{3,2,1,0:T(8,128)} %get-tuple-element.55), channel_id=1, source_target_pairs={{0,2},{2,4},{4,6},{6,8},{8,10},{10,12},{12,14},{1,3},{3,5},{5,7},{... | collective-permute-start | bytes 1769480 | tf_op jit(solution)/shard_map/ppermute | solution.py:85
  8.9 58.0 %collective-permute-start.7 = (f32[3,6,64,128]{3,2,1,0:T(8,128)}, f32[3,6,64,128]{3,2,1,0:T(8,128)}, u32[]{:S(2)}, u32[]{:S(2)}) collective-permute-start(f32[3,6,64,128]{3,2,1,0:T(8,128)} %get-tuple-element.54), channel_id=1, source_target_pairs={{2,0},{4,2},{6,4},{8,6},{10,8},{12,10},{14,12},{3,1},{5,3},{7,5},{... | collective-permute-start | bytes 1769480 | tf_op jit(solution)/shard_map/ppermute | solution.py:90
  15.4 28.2 %collective-permute-start = (f32[2]{0:T(128)}, f32[2]{0:T(128)}, u32[]{:S(2)}, u32[]{:S(2)}) collective-permute-start(f32[2]{0:T(128)} %maximum_reduce_fusion), channel_id=1, source_target_pairs={{0,1},{1,0},{2,3},{3,2},{4,5},{5,4},{6,7},{7,6},{8,9},{9,8},{10,11... | collective-permute-start | bytes 32 | tf_op jit(solution)/shard_map/ppermute | solution.py:118
  21.0 0.9 copy-start.27
  21.0 1.5 copy-start.26
  36.3 0.7 copy-start.19
  36.3 2.0 %copy-start.25 = (f32[128]{0:T(128)S(1)}, f32[128]{0:T(128)}, u32[]{:S(2)}) copy-start(f32[128]{0:T(128)} %constant.462) | copy-start | bytes 1540
  44.3 5.4 %collective-permute-start.3 = (f32[2]{0:T(128)S(1)}, f32[2]{0:T(128)S(1)}, u32[]{:S(2)}, u32[]{:S(2)}) collective-permute-start(f32[2]{0:T(128)S(1)} %max.25), channel_id=1, source_target_pairs={{0,6},{2,8},{4,10},{6,12},{8,14},{10,0},{12,2},{14,4},{1,7},{3,9},... | collective-permute-start | bytes 32 | tf_op jit(solution)/shard_map/ppermute | solution.py:118
  46.9 6.1 %collective-permute-start.2 = (f32[2]{0:T(128)S(1)}, f32[2]{0:T(128)S(1)}, u32[]{:S(2)}, u32[]{:S(2)}) collective-permute-start(f32[2]{0:T(128)S(1)} %max.25), channel_id=1, source_target_pairs={{0,4},{2,6},{4,8},{6,10},{8,12},{10,14},{12,0},{14,2},{1,5},{3,7},... | collective-permute-start | bytes 32 | tf_op jit(solution)/shard_map/ppermute | solution.py:118
  49.7 6.3 %collective-permute-start.1 = (f32[2]{0:T(128)S(1)}, f32[2]{0:T(128)S(1)}, u32[]{:S(2)}, u32[]{:S(2)}) collective-permute-start(f32[2]{0:T(128)S(1)} %max.25), channel_id=1, source_target_pairs={{0,2},{2,4},{4,6},{6,8},{8,10},{10,12},{12,14},{14,0},{1,3},{3,5},... | collective-permute-start | bytes 32 | tf_op jit(solution)/shard_map/ppermute | solution.py:118
  56.0 4.5 %collective-permute-start.4 = (f32[2]{0:T(128)S(1)}, f32[2]{0:T(128)S(1)}, u32[]{:S(2)}, u32[]{:S(2)}) collective-permute-start(f32[2]{0:T(128)S(1)} %maximum_maximum_fusion), channel_id=1, source_target_pairs={{0,8},{2,10},{4,12},{6,14},{8,0},{10,2},{12,4},{14,6},{1,9},{3,11}... | collective-permute-start | bytes 32 | tf_op jit(solution)/shard_map/ppermute | solution.py:118
  62.3 1.4 copy-start.4
  62.4 1.4 copy-start.5
  62.4 1.4 copy-start.6
  62.4 1.4 copy-start.7
  62.4 1.4 copy-start.8
  62.4 1.4 copy-start.9
  62.4 1.4 copy-start.10
  62.4 1.4 copy-start.11
  66.8 0.9 copy-start.2
  66.8 1.0 copy-start.3
  66.8 1.0 copy-start.15
  69.0 0.8 copy-start.1
  69.0 0.8 copy-start.12
  69.0 0.7 copy-start.16
  69.0 0.7 copy-start.20
  69.0 0.7 copy-start.23
  69.8 7.4 %copy-start.17 = (f32[1,3,6]{2,1,0:T(4,128)S(1)}, f32[1,3,6]{2,1,0:T(4,128)}, u32[]{:S(2)}) copy-start(f32[1,3,6]{2,1,0:T(4,128)} %copy.44) | copy-start | bytes 220
  69.8 7.4 %copy-start.22 = (f32[3]{0:T(128)S(1)}, f32[3]{0:T(128)}, u32[]{:S(2)}) copy-start(f32[3]{0:T(128)} %get-tuple-element.102) | copy-start | bytes 40
  85.2 25.1 %collective-permute-start.8 = (f32[3,6,64,128]{3,2,1,0:T(8,128)S(1)}, f32[3,6,64,128]{3,2,1,0:T(8,128)S(1)}, u32[]{:S(2)}, u32[]{:S(2)}) collective-permute-start(f32[3,6,64,128]{3,2,1,0:T(8,128)S(1)} %fusion.73), channel_id=1, source_target_pairs={{0,2},{2,4},{4,6},{6,8},{8,10},{10,12},{12,14},{1,3},{3,5},{5,7},{... | collective-permute-start | bytes 1769480 | tf_op jit(solution)/shard_map/ppermute | solution.py:85
  88.0 22.6 %collective-permute-start.10 = (f32[3,6,64,128]{3,2,1,0:T(8,128)S(1)}, f32[3,6,64,128]{3,2,1,0:T(8,128)S(1)}, u32[]{:S(2)}, u32[]{:S(2)}) collective-permute-start(f32[3,6,64,128]{3,2,1,0:T(8,128)S(1)} %fusion.59), channel_id=1, source_target_pairs={{2,0},{4,2},{6,4},{8,6},{10,8},{12,10},{14,12},{3,1},{5,3},{7,5},{... | collective-permute-start | bytes 1769480 | tf_op jit(solution)/shard_map/ppermute | solution.py:90
  90.2 13.4 %collective-permute-start.9 = (f32[6,3,64,128]{3,2,1,0:T(8,128)S(1)}, f32[6,3,64,128]{3,2,1,0:T(8,128)S(1)}, u32[]{:S(2)}, u32[]{:S(2)}) collective-permute-start(f32[6,3,64,128]{3,2,1,0:T(8,128)S(1)} %fusion.82), channel_id=1, source_target_pairs={{0,1},{1,0},{2,3},{3,2},{4,5},{5,4},{6,7},{7,6},{8,9},{9,8},{10,11... | collective-permute-start | bytes 1769480 | tf_op jit(solution)/shard_map/ppermute | solution.py:172
  127.3 23.2 %collective-permute-start.12 = (f32[3,6,64,128]{3,2,1,0:T(8,128)S(1)}, f32[3,6,64,128]{3,2,1,0:T(8,128)S(1)}, u32[]{:S(2)}, u32[]{:S(2)}) collective-permute-start(f32[3,6,64,128]{3,2,1,0:T(8,128)S(1)} %fusion.67), channel_id=1, source_target_pairs={{2,0},{4,2},{6,4},{8,6},{10,8},{12,10},{14,12},{3,1},{5,3},{7,5},{... | collective-permute-start | bytes 1769480 | tf_op jit(solution)/shard_map/ppermute | solution.py:90
  128.6 26.6 %collective-permute-start.11 = (f32[3,6,64,128]{3,2,1,0:T(8,128)S(1)}, f32[3,6,64,128]{3,2,1,0:T(8,128)S(1)}, u32[]{:S(2)}, u32[]{:S(2)}) collective-permute-start(f32[3,6,64,128]{3,2,1,0:T(8,128)S(1)} %fusion.81), channel_id=1, source_target_pairs={{0,2},{2,4},{4,6},{6,8},{8,10},{10,12},{12,14},{1,3},{3,5},{5,7},{... | collective-permute-start | bytes 1769480 | tf_op jit(solution)/shard_map/ppermute | solution.py:85
  147.9 2.1 %collective-permute-start.13 = (f32[6,3,64,128]{3,2,1,0:T(8,128)S(1)}, f32[6,3,64,128]{3,2,1,0:T(8,128)S(1)}, u32[]{:S(2)}, u32[]{:S(2)}) collective-permute-start(f32[6,3,64,128]{3,2,1,0:T(8,128)S(1)} %fusion.83), channel_id=1, source_target_pairs={{0,1},{1,0},{2,3},{3,2},{4,5},{5,4},{6,7},{7,6},{8,9},{9,8},{10,11... | collective-permute-start | bytes 1769480 | tf_op jit(solution)/shard_map/ppermute | solution.py:172
  155.5 0.7 copy-start.13
  155.5 0.7 copy-start.18
  155.5 0.7 copy-start.24
